TPU v7x, 128 devices: a whole 4x4x4 slice. The times are simulated.
128 devices in a mesh: ctx: 16 (over x_lo, z, core), tp: 8 (over y, x_hi).
Axes of the slice: x: 4 (x_hi: 2, x_lo: 2; x = x_hi * 2 + x_lo), y: 4, z: 4, core: 2. Of those that a mesh axis runs over, the one named last changes fastest.
Arguments:
- queries: bfloat16 [8192, 4096], P('ctx', 'tp'), may hold values from -6 to 6
- key_rows: bfloat16 [8192, 4096], P('ctx', 'tp'), may hold values from -6 to 6
- value_rows: bfloat16 [8192, 4096], P('ctx', 'tp'), may hold values from -30 to 30
- selection: int32 [16, 3], replicated, may hold values from 0 to 15, as said below
- out_weight: bfloat16 [4096, 7168], P('tp'), may hold values from -0.125 to 0.125
Outputs:
- mixed: bfloat16 [8192, 7168], P('ctx', 'tp')
Inputs may be any that keep to these rules, and one draw needn't show every extreme that they name: Row q of selection lists q first, then 3 - 1 distinct blocks below q; where fewer than that lie below q, the remaining entries are q.
All inputs are finite; a program needn't handle non-finite values.
Results may differ from a plain program's by a relative error of at most 0.013.
Values may be sent and summed in bfloat16 or wider, within the bound.
No kernel may reach another device: no remote copies, remote signals or barrier semaphores. Data moves between devices by JAX's collectives and lax.ppermute only.
A program may use at most 192 MiB of HBM per device.

v0:
```python
import jax
import jax.numpy as jnp
from jax import lax
from jax.sharding import PartitionSpec as P

HD = 128
BLOCK = 512


neg_fill = -1e30


def per_device(queries, key_rows, value_rows, selection, out_weight):
    row_count, feat_width = queries.shape
    head_count = feat_width // HD
    blocks_here = row_count // BLOCK
    block_total = selection.shape[0]
    ctx_place = lax.axis_index("ctx")
    first_row = ctx_place * row_count
    scaling = 1.0 / jnp.sqrt(jnp.float32(HD))
    query_heads = queries.reshape(row_count, head_count, HD).transpose(1, 0, 2)
    own_choice = lax.dynamic_slice_in_dim(selection, ctx_place * blocks_here, blocks_here, 0)
    repeated = jnp.concatenate(
        [jnp.zeros((blocks_here, 1), bool), own_choice[:, 1:] == own_choice[:, :1]], axis=1
    )
    block_ids = jnp.arange(block_total, dtype=jnp.int32)
    chosen = jnp.any(
        (own_choice[:, :, None] == block_ids[None, None, :])
        & jnp.logical_not(repeated)[:, :, None],
        axis=1,
    )
    query_pos = first_row + jnp.arange(row_count, dtype=jnp.int32)
    initial = (
        jnp.full((head_count, row_count), neg_fill, jnp.float32),
        jnp.zeros((head_count, row_count), jnp.float32),
        jnp.zeros((head_count, row_count, HD), jnp.float32),
    )
    key_piece = lax.all_gather(key_rows, "ctx", axis=0, tiled=True)
    value_piece = lax.all_gather(value_rows, "ctx", axis=0, tiled=True)
    piece_rows = key_piece.shape[0]
    key_pos = jnp.arange(piece_rows, dtype=jnp.int32)
    in_block = (key_pos // BLOCK)[None, :] == block_ids[:, None]
    blockwise = jnp.any(chosen[:, :, None] & in_block[None, :, :], axis=1)
    allowed = jnp.broadcast_to(blockwise[:, None, :], (blocks_here, BLOCK, piece_rows)).reshape(
        row_count, piece_rows
    )
    allowed = allowed & (key_pos[None, :] <= query_pos[:, None])

    def compute(state):
        run_max, run_sum, run_acc = state
        key_heads = key_piece.reshape(piece_rows, head_count, HD).transpose(1, 0, 2)
        value_heads = value_piece.reshape(piece_rows, head_count, HD).transpose(1, 0, 2)
        scores = (
            jnp.einsum("htd,hsd->hts", query_heads, key_heads, preferred_element_type=jnp.float32)
            * scaling
        )
        new_max = jnp.maximum(run_max, jnp.max(jnp.where(allowed[None], scores, neg_fill), axis=-1))
        expo = jnp.where(allowed[None], jnp.exp(scores - new_max[..., None]), 0.0)
        new_sum = jnp.sum(expo, axis=-1)
        weights = expo.astype(jnp.bfloat16)
        new_acc = jnp.einsum(
            "hts,hsd->htd", weights, value_heads, preferred_element_type=jnp.float32
        )
        return (new_max, new_sum, new_acc)

    run_max, run_sum, run_acc = lax.cond(jnp.any(allowed), compute, lambda state: state, initial)
    attended = (
        (run_acc / run_sum[..., None])
        .astype(jnp.bfloat16)
        .transpose(1, 0, 2)
        .reshape(row_count, feat_width)
    )
    shares = lax.psum_scatter(
        lax.dot_general(
            out_weight, attended, (((0,), (1,)), ((), ())), preferred_element_type=jnp.float32
        ).astype(jnp.bfloat16),
        "tp",
        scatter_dimension=0,
        tiled=True,
    ).astype(jnp.float32)
    mixed_out = jnp.transpose(shares)
    return mixed_out.astype(jnp.bfloat16)


def solution(mesh):
    placed = (P("ctx", "tp"), P("ctx", "tp"), P("ctx", "tp"), P(), P("tp", None))
    return jax.shard_map(
        per_device, mesh=mesh, in_specs=placed, out_specs=P("ctx", "tp"), check_vma=False
    )
```

profile of v0, /device:TPU:0, one launch (start us, length us, event | category | flops | bytes accessed | tf_op | source)
XLA Modules:
  0.0 339.5 jit_solution(13768091969145868570)
XLA Ops:
  6.5 0.7 all-gather.3.cloned.1.call-update
  7.3 0.0 all-gather.5.cloned.1.call-start
  7.3 0.7 all-gather.5.cloned.1.call-update
  8.0 0.0 reduce-scatter.4.cloned.1.call-start
  8.1 0.9 fusion.20
  8.9 0.5 slice.7
  9.4 1.3 copy.20
  10.7 0.8 compare_reduce_fusion
  11.5 0.1 add_not_fusion
  11.6 0.1 fusion.18
  11.6 0.2 fusion.13
  11.8 7.3 %fusion.10 = (pred[512,8192]{1,0:T(8,128)(4,1)}, pred[]{:T(512)}) fusion(s32[512]{0:T(512)S(1)} %iota_add_fusion, pred[8192]{0:T(1024)(128)(4,1)S(1)} %fusion.13), kind=kLoop, calls=%fused_computation.15 | loop fusion | flops 12582911 | bytes 4204545 | tf_op jit(solution)/shard_map/and | solution.py:47
  19.8 44.0 %all-gather.3.cloned.1.call-done = bf16[8192,512]{1,0:T(8,128)(2,1)} async-done(((bf16[512,512]{1,0:T(8,128)(2,1)}), bf16[8192,512]{1,0:T(8,128)(2,1)}) %all-gather.3.cloned.1.call-update) | async-done | bytes 8388624 | tf_op jit(solution)/shard_map/all_gather | solution.py:38
  63.7 54.9 %all-gather.5.cloned.1.call-done = bf16[8192,512]{1,0:T(8,128)(2,1)} async-done(((bf16[512,512]{1,0:T(8,128)(2,1)}), bf16[8192,512]{1,0:T(8,128)(2,1)}) %all-gather.5.cloned.1.call-update) | async-done | bytes 8388624 | tf_op jit(solution)/shard_map/all_gather | solution.py:39
  118.6 84.5 %conditional.1 = (f32[4,512]{1,0:T(4,128)S(1)}, f32[4,512,128]{1,2,0:T(8,128)S(1)}) conditional(s32[]{:T(128)} %convert_element_type.20, () %tuple.13, (pred[512,8192]{1,0:T(8,128)(4,1)}, bf16[8192,512]{1,0:T(8,128)(2,1)}, bf16[4,512,128]{1,2,0:T(8,128)(2,1)S(1)}, bf16[8192,512]{1,0:T(8,128)(2,1)}) %tuple.31), branch_computations={%region_3.4_spmd, %region_4.7_spmd} | conditional | flops 8774481920 | bytes 232308752 | solution.py:66
  118.6 29.7 %select_reduce_fusion = (f32[4,512]{1,0:T(4,128)S(1)}, f32[4,512,8192]{2,1,0:T(8,128)}) fusion(pred[512,8192]{1,0:T(8,128)(4,1)} %get-tuple-element.13, bf16[4,512,128]{1,2,0:T(8,128)(2,1)S(1)} %get-tuple-element.31, bf16[8192,512]{1,0:T(8,128)(2,1)} %get-tuple-element.15), kind=kOutput, calls=%fused_computation.1 | convolution fusion | flops 4345296896 | bytes 80224256 | tf_op jit(solution)/shard_map/cond/branch_1_fun/htd,hsd->hts/dot_general | solution.py:54
  148.3 31.8 %fusion.2 = f32[4,512,128]{1,2,0:T(8,128)S(1)} fusion(f32[4,512,8192]{2,1,0:T(8,128)} %get-tuple-element.37, f32[4,512]{1,0:T(4,128)S(1)} %broadcast_maximum_fusion, pred[512,8192]{1,0:T(8,128)(4,1)} %get-tuple-element.13, bf16[8192,512]{1,0:T(8,128)(2,1)} %get-tuple-element.16), kind=kOutput, calls=%fused_computation.4 | convolution fusion | flops 4362076160 | bytes 80748544 | tf_op jit(solution)/shard_map/cond | solution.py:66
  180.1 22.7 %fusion.1 = f32[4,512]{1,0:T(4,128)S(1)} fusion(f32[4,512,8192]{2,1,0:T(8,128)} %get-tuple-element.37, f32[4,512]{1,0:T(4,128)S(1)} %broadcast_maximum_fusion, pred[512,8192]{1,0:T(8,128)(4,1)} %get-tuple-element.13), kind=kLoop, calls=%fused_computation.3 | loop fusion | flops 67106816 | bytes 71319552 | tf_op jit(solution)/shard_map/cond/branch_1_fun/reduce_sum | solution.py:59
  203.1 0.1 divide_convert_fusion
  203.2 9.2 %fusion.11 = bf16[7168,512]{0,1:T(8,128)(2,1)} fusion(bf16[512,512]{0,1:T(8,128)(2,1)S(1)} %bitcast.38, bf16[512,7168]{1,0:T(8,128)(2,1)} %param.11), kind=kOutput, calls=%fused_computation.17 | convolution fusion | flops 3761766400 | bytes 15204352 | tf_op jit(solution)/shard_map/dot_general | solution.py:74
  212.4 10.4 %copy.24 = bf16[7168,512]{1,0:T(8,128)(2,1)} copy(bf16[7168,512]{0,1:T(8,128)(2,1)} %fusion.11) | data formatting | bytes 14680064
  222.9 0.0 reduce-scatter.4.cloned.1.call-update
  222.9 107.9 %reduce-scatter.4.cloned.1.call-done = bf16[896,512]{1,0:T(8,128)(2,1)} async-done(((bf16[7168,512]{1,0:T(8,128)(2,1)}), bf16[896,512]{1,0:T(8,128)(2,1)}) %reduce-scatter.4.cloned.1.call-update) | async-done | bytes 917520
  330.8 2.2 copy.25
  (4 shorter events, 0.0 us)
Async XLA Ops:
  6.5 57.2 %all-gather.3.cloned.1.call-start = ((), (), s32[]{:S(2)}) async-start(), calls=%async_computation.1 | async-start | bytes 8912896 | tf_op jit(solution)/shard_map/all_gather | solution.py:38
  7.3 111.3 %all-gather.5.cloned.1.call-start = ((), (), s32[]{:S(2)}) async-start(), calls=%async_computation.2 | async-start | bytes 8912896 | tf_op jit(solution)/shard_map/all_gather | solution.py:39
  8.0 322.8 %reduce-scatter.4.cloned.1.call-start = ((), (), s32[]{:S(2)}) async-start(), calls=%async_computation.3 | async-start | bytes 8257536
Sparse Core Ops, SparseCore 0:
  9.1 54.6 all-gather.2
  65.4 53.1 all-gather.4
  223.0 107.7 reduce-scatter.3
where the time goes:
time: 340 us
  waiting for transfers between devices  208 us (61%)
  matrix products  70.8 us (21%)
  other arithmetic  31.3 us (9%)
  local copies, waits for them, and re-layouts  15.3 us (4%)
  between operations  13.8 us (4%)
    unnamed x4, waiting for transfers between devices  109 us
    all_gather x1, waiting for transfers between devices, per_device(): value_piece = lax.all_gather(value_rows, 'ctx', axis=0, tiled=True)  54.9 us
    all_gather x1, waiting for transfers between devices, per_device(): key_piece = lax.all_gather(key_rows, 'ctx', axis=0, tiled=True)  44 us
    cond x1, matrix products, per_device(): lax.cond(jnp.any(allowed), compute, lambda state: state, initial)  31.8 us
    dot_general x1, matrix products, compute(): jnp.einsum('htd,hsd->hts', query_heads, key_heads, preferred_element_type...  29.7 us
    reduce_sum x1, other arithmetic, compute(): new_sum = jnp.sum(expo, axis=-1)  22.7 us
    unnamed x3, local copies, waits for them, and re-layouts  13.9 us
    dot_general x1, matrix products, per_device(): lax.dot_general(out_weight, attended, (((0,), (1,)), ((), ())), preferred...  9.24 us
  transfers between devices with their start and end apart: 3, of which 3 were waited for; matrix products, arithmetic and copies ran while one was open for 3% of the time, Pallas kernels for 0%

commit v1 on v0

v1 whole, which is shorter than its diff:
```python
import jax
import jax.numpy as jnp
from jax import lax
from jax.sharding import PartitionSpec as P

HD = 128
BLOCK = 512

neg_fill = -1e30


def per_device(queries, key_rows, value_rows, selection, out_weight):
    row_count, feat_width = queries.shape
    head_count = feat_width // HD
    topk = selection.shape[1]
    ctx_place = lax.axis_index("ctx")
    first_row = ctx_place * row_count
    scaling = 1.0 / jnp.sqrt(jnp.float32(HD))
    query_heads = queries.reshape(row_count, head_count, HD).transpose(1, 0, 2)
    own_choice = lax.dynamic_slice_in_dim(selection, ctx_place, 1, 0)[0]
    usable = jnp.concatenate([jnp.ones((1,), bool), own_choice[1:] != own_choice[0]])
    kv_piece = lax.all_gather(
        jnp.concatenate([key_rows, value_rows], axis=1), "ctx", axis=0, tiled=True
    )
    picked = jnp.stack(
        [lax.dynamic_slice_in_dim(kv_piece, own_choice[s] * BLOCK, BLOCK, 0) for s in range(topk)]
    ).reshape(topk * BLOCK, 2, head_count, HD)
    key_heads = picked[:, 0].transpose(1, 0, 2)
    value_heads = picked[:, 1].transpose(1, 0, 2)
    query_pos = first_row + jnp.arange(row_count, dtype=jnp.int32)
    key_pos = (own_choice[:, None] * BLOCK + jnp.arange(BLOCK, dtype=jnp.int32)[None, :]).reshape(-1)
    slot_ok = jnp.repeat(usable, BLOCK)
    allowed = (key_pos[None, :] <= query_pos[:, None]) & slot_ok[None, :]
    scores = (
        jnp.einsum("htd,hsd->hts", query_heads, key_heads, preferred_element_type=jnp.float32)
        * scaling
    )
    run_max = jnp.max(jnp.where(allowed[None], scores, neg_fill), axis=-1)
    expo = jnp.where(allowed[None], jnp.exp(scores - run_max[..., None]), 0.0)
    run_sum = jnp.sum(expo, axis=-1)
    weights = expo.astype(jnp.bfloat16)
    run_acc = jnp.einsum("hts,hsd->htd", weights, value_heads, preferred_element_type=jnp.float32)
    attended = (
        (run_acc / run_sum[..., None])
        .astype(jnp.bfloat16)
        .transpose(1, 0, 2)
        .reshape(row_count, feat_width)
    )
    shares = lax.psum_scatter(
        lax.dot_general(
            out_weight, attended, (((0,), (1,)), ((), ())), preferred_element_type=jnp.float32
        ).astype(jnp.bfloat16),
        "tp",
        scatter_dimension=0,
        tiled=True,
    ).astype(jnp.float32)
    mixed_out = jnp.transpose(shares)
    return mixed_out.astype(jnp.bfloat16)


def solution(mesh):
    placed = (P("ctx", "tp"), P("ctx", "tp"), P("ctx", "tp"), P(), P("tp", None))
    return jax.shard_map(
        per_device, mesh=mesh, in_specs=placed, out_specs=P("ctx", "tp"), check_vma=False
    )
```

time: 340 us -> 272 us (0.80)
  matrix products: 70.8 us -> 16.7 us
  other arithmetic: 31.3 us -> 15.4 us
  local copies, waits for them, and re-layouts: 15.3 us -> 27.5 us
  waiting for transfers between devices: 208 us -> 197 us
    cond x1 -> x0, matrix products: 31.8 us -> none  [per_device(): lax.cond(jnp.any(allowed), compute, lambda state: state, initial)]
    reduce_sum x1 -> x0, other arithmetic: 22.7 us -> none  [compute(): new_sum = jnp.sum(expo, axis=-1)]
    dot_general x1 -> x2, matrix products: 29.7 us -> 7.45 us  [the longest x1 4.25 us: per_device(): jnp.einsum('hts,hsd->htd', weights, value_heads, preferred_element_type=j...]
    all_gather x2 -> x1, waiting for transfers between devices: 98.8 us -> 88.8 us  [per_device(): lax.all_gather(jnp.concatenate([key_rows, value_rows], axis=1), 'ctx', ax...]
    sub x0 -> x1, other arithmetic: none -> 8.07 us  [per_device(): expo = jnp.where(allowed[None], jnp.exp(scores - run_max[..., None]), 0.0)]
    and x1, other arithmetic: 7.28 us -> 1.12 us  [per_device(): allowed = (key_pos[None, :] <= query_pos[:, None]) & slot_ok[None, :]]
    reshape x0 -> x1, local copies, waits for them, and re-layouts: none -> 6.08 us  [per_device(): picked = jnp.stack([lax.dynamic_slice_in_dim(kv_piece, own_choice[s] * BL...]
    slice x1 -> x2, local copies, waits for them, and re-layouts: 0.51 us -> 3.94 us  [the longest x1 3.35 us: per_device(): value_heads = picked[:, 1].transpose(1, 0, 2)]
  transfers between devices with their start and end apart: 3 -> 2, of which waited for: 3 -> 2; matrix products, arithmetic and copies ran while one was open for 3% -> 1% of each run, Pallas kernels for 0% -> 0%
where the time goes in v1:
time: 272 us; the launch traced here: 271 us
  waiting for transfers between devices  197 us (72%)
  local copies, waits for them, and re-layouts  27.5 us (10%)
  matrix products  16.7 us (6%)
  other arithmetic  15.4 us (6%)
  between operations  15.3 us (6%)
    unnamed x3, waiting for transfers between devices  108 us
    all_gather x1, waiting for transfers between devices, per_device(): lax.all_gather(jnp.concatenate([key_rows, value_rows], axis=1), 'ctx', ax...  88.8 us
    unnamed x7, local copies, waits for them, and re-layouts  15 us
    dot_general x1, matrix products, per_device(): lax.dot_general(out_weight, attended, (((0,), (1,)), ((), ())), preferred...  9.24 us
    sub x1, other arithmetic, per_device(): expo = jnp.where(allowed[None], jnp.exp(scores - run_max[..., None]), 0.0)  8.07 us
    reshape x1, local copies, waits for them, and re-layouts, per_device(): picked = jnp.stack([lax.dynamic_slice_in_dim(kv_piece, own_choice[s] * BL...  6.08 us
  transfers between devices with their start and end apart: 2, of which 2 were waited for; matrix products, arithmetic and copies ran while one was open for 1% of the time, Pallas kernels for 0%

profile of v1, /device:TPU:0, one launch (start us, length us, event | category | flops | bytes accessed | tf_op | source)
XLA Modules:
  0.0 271.5 jit_solution(3721377676455916608)
XLA Ops:
  6.5 2.4 pad_maximum_fusion.1
  8.9 0.0 all-gather.2.cloned.1.call-update
  8.9 0.0 reduce-scatter.4.cloned.1.call-start
  9.0 0.9 multiply_reduce_fusion
  9.8 0.6 fusion.32
  12.3 0.8 compare_reduce_fusion
  13.0 0.1 pad_add_fusion
  13.1 0.1 broadcast_in_dim.27
  13.2 0.1 iota_add_fusion
  13.3 1.1 compare_and_fusion
  14.4 88.8 %all-gather.2.cloned.1.call-done = bf16[8192,1024]{1,0:T(8,128)(2,1)} async-done(((bf16[512,1024]{1,0:T(8,128)(2,1)}), bf16[8192,1024]{1,0:T(8,128)(2,1)}) %all-gather.2.cloned.1.call-update) | async-done | bytes 16777232 | tf_op jit(solution)/shard_map/all_gather | solution.py:22
  103.2 2.3 dynamic-slice_bitcast_fusion.2
  105.6 2.0 pad_maximum_fusion
  107.6 6.1 %reshape.97 = bf16[1536,2,4,128]{3,2,1,0:T(4,128)(2,1)} reshape(bf16[3,512,1024]{2,1,0:T(8,128)(2,1)} %pad_maximum_fusion) | data formatting | bytes 6291456 | tf_op jit(solution)/shard_map/reshape | solution.py:27
  113.7 3.4 %fusion.31 = (bf16[1536,1,4,128]{3,2,1,0:T(4,128)(2,1)S(1)}, bf16[1536,1,4,128]{3,2,1,0:T(4,128)(2,1)}) fusion(bf16[1536,2,4,128]{3,2,1,0:T(4,128)(2,1)} %reshape.97), kind=kLoop, calls=%fused_computation.36 | loop fusion | bytes 6291456 | tf_op jit(solution)/shard_map/slice | solution.py:29
  117.0 2.3 copy.20
  119.4 3.2 %fusion.11 = f32[4,1536,512]{2,1,0:T(8,128)S(1)} fusion(bf16[1536,1,4,128]{3,2,1,0:T(4,128)(2,1)} %get-tuple-element.11, bf16[512,512]{1,0:T(8,128)(2,1)S(1)} %copy-done), kind=kOutput, calls=%fused_computation.17 | convolution fusion | flops 805306368 | bytes 14680064 | tf_op jit(solution)/shard_map/htd,hsd->hts/dot_general | solution.py:35
  122.6 8.1 %fusion.33 = (f32[4,512]{1,0:T(4,128)S(1)}, bf16[4,512,1536]{1,2,0:T(8,128)(2,1)}) fusion(f32[4,1536,512]{2,1,0:T(8,128)S(1)} %fusion.11, pred[512,1536]{0,1:T(8,128)(4,1)S(1)} %compare_and_fusion), kind=kOutput, calls=%fused_computation.38 | output fusion | flops 22021632 | bytes 19668992 | tf_op jit(solution)/shard_map/sub | solution.py:39
  130.6 4.3 %fusion.23 = bf16[512,4,128]{0,2,1:T(8,128)(2,1)S(1)} fusion(bf16[4,512,1536]{1,2,0:T(8,128)(2,1)} %get-tuple-element.16, bf16[1536,1,4,128]{0,3,2,1:T(8,128)(2,1)} %copy.20, f32[512,4]{0,1:T(4,128)S(1)} %bitcast.65), kind=kOutput, calls=%fused_computation.21 | convolution fusion | flops 805830656 | bytes 8396800 | tf_op jit(solution)/shard_map/hts,hsd->htd/dot_general | solution.py:42
  134.9 9.2 %fusion.5 = bf16[7168,512]{0,1:T(8,128)(2,1)} fusion(bf16[512,512]{0,1:T(8,128)(2,1)S(1)} %bitcast.64, bf16[512,7168]{1,0:T(8,128)(2,1)} %param.9), kind=kOutput, calls=%fused_computation.8 | convolution fusion | flops 3761766400 | bytes 15204352 | tf_op jit(solution)/shard_map/dot_general | solution.py:50
  144.1 10.5 %copy.18 = bf16[7168,512]{1,0:T(8,128)(2,1)} copy(bf16[7168,512]{0,1:T(8,128)(2,1)} %fusion.5) | data formatting | bytes 14680064
  154.6 0.0 reduce-scatter.4.cloned.1.call-update
  154.6 107.8 %reduce-scatter.4.cloned.1.call-done = bf16[896,512]{1,0:T(8,128)(2,1)} async-done(((bf16[7168,512]{1,0:T(8,128)(2,1)}), bf16[896,512]{1,0:T(8,128)(2,1)}) %reduce-scatter.4.cloned.1.call-update) | async-done | bytes 917520
  262.4 2.2 copy.19
  (8 shorter events, 0.0 us)
Async XLA Ops:
  6.5 112.8 %copy-start = (bf16[512,512]{1,0:T(8,128)(2,1)S(1)}, bf16[512,512]{1,0:T(8,128)(2,1)}, u32[]{:S(2)}) copy-start(bf16[512,512]{1,0:T(8,128)(2,1)} %param.5) | copy-start | bytes 1572868
  6.5 96.7 %all-gather.2.cloned.1.call-start = ((), (), s32[]{:S(2)}) async-start(), calls=%async_computation.1 | async-start | bytes 17825792 | tf_op jit(solution)/shard_map/all_gather | solution.py:22
  8.9 253.5 %reduce-scatter.4.cloned.1.call-start = ((), (), s32[]{:S(2)}) async-start(), calls=%async_computation.2 | async-start | bytes 8257536
  144.1 120.5 %copy-start.1 = (bf16[512,512]{1,0:T(8,128)(2,1)S(1)}, bf16[512,512]{1,0:T(8,128)(2,1)}, u32[]{:S(2)}) copy-start(bf16[512,512]{1,0:T(8,128)(2,1)} %param.5) | copy-start | bytes 1572868
Sparse Core Ops, SparseCore 0:
  9.1 94.1 all-gather.1
  154.8 107.6 reduce-scatter.3

commit v2 on v1

--- a/solution.py
+++ b/solution.py
@@ -22,6 +22,23 @@
     kv_piece = lax.all_gather(
         jnp.concatenate([key_rows, value_rows], axis=1), "ctx", axis=0, tiled=True
     )
+    tp_size = lax.axis_size("tp")
+    tp_place = lax.axis_index("tp")
+    col_width = out_weight.shape[1] // tp_size
+    w_cols = jnp.zeros((out_weight.shape[0] * tp_size, col_width), out_weight.dtype)
+    w_cols = lax.dynamic_update_slice_in_dim(
+        w_cols,
+        lax.dynamic_slice_in_dim(out_weight, tp_place * col_width, col_width, 1),
+        tp_place * out_weight.shape[0],
+        0,
+    )
+    for shift in range(1, tp_size):
+        dest = (tp_place + shift) % tp_size
+        sent = lax.dynamic_slice_in_dim(out_weight, dest * col_width, col_width, 1)
+        got = lax.ppermute(sent, "tp", [(i, (i + shift) % tp_size) for i in range(tp_size)])
+        src = (tp_place - shift) % tp_size
+        w_cols = lax.dynamic_update_slice_in_dim(w_cols, got, src * out_weight.shape[0], 0)
+    kv_piece, w_cols = lax.optimization_barrier((kv_piece, w_cols))
     picked = jnp.stack(
         [lax.dynamic_slice_in_dim(kv_piece, own_choice[s] * BLOCK, BLOCK, 0) for s in range(topk)]
     ).reshape(topk * BLOCK, 2, head_count, HD)
@@ -46,15 +63,8 @@
         .transpose(1, 0, 2)
         .reshape(row_count, feat_width)
     )
-    shares = lax.psum_scatter(
-        lax.dot_general(
-            out_weight, attended, (((0,), (1,)), ((), ())), preferred_element_type=jnp.float32
-        ).astype(jnp.bfloat16),
-        "tp",
-        scatter_dimension=0,
-        tiled=True,
-    ).astype(jnp.float32)
-    mixed_out = jnp.transpose(shares)
+    att_full = lax.all_gather(attended, "tp", axis=1, tiled=True)
+    mixed_out = jnp.dot(att_full, w_cols, preferred_element_type=jnp.float32)
     return mixed_out.astype(jnp.bfloat16)
 
 

time: 272 us -> 305 us (1.12)
  starting transfers between devices: 0.04 us -> 18.8 us
  local copies, waits for them, and re-layouts: 27.5 us -> 38.9 us
    ppermute x0 -> x7, waiting for transfers between devices: none -> 125 us  [per_device(): lax.ppermute(sent, 'tp', [(i, (i + shift) % tp_size) for i in range(tp_si...]
    unnamed x3 -> x2, waiting for transfers between devices: 108 us -> 0.03 us
    all_gather x1, waiting for transfers between devices: 88.8 us -> 0.01 us  [per_device(): lax.all_gather(jnp.concatenate([key_rows, value_rows], axis=1), 'ctx', ax...]
    all_gather x0 -> x1, waiting for transfers between devices: none -> 72.3 us  [per_device(): att_full = lax.all_gather(attended, 'tp', axis=1, tiled=True)]
    ppermute x0 -> x7, starting transfers between devices: none -> 18.8 us  [per_device(): lax.ppermute(sent, 'tp', [(i, (i + shift) % tp_size) for i in range(tp_si...]
    dynamic_update_slice x0 -> x7, local copies, waits for them, and re-layouts: none -> 15.6 us  [per_device(): lax.dynamic_update_slice_in_dim(w_cols, got, src * out_weight.shape[0], 0)]
    unnamed x7 -> x13, local copies, waits for them, and re-layouts: 15 us -> 7.77 us
  transfers between devices with their start and end apart: 2 -> 9, of which waited for: 2 -> 5; matrix products, arithmetic and copies ran while one was open for 1% -> 7% of each run, Pallas kernels for 0% -> 0%
where the time goes in v2:
time: 305 us; the launch traced here: 304 us
  waiting for transfers between devices  197 us (65%)
  local copies, waits for them, and re-layouts  38.9 us (13%)
  starting transfers between devices  18.8 us (6%)
  matrix products  18.1 us (6%)
  between operations  15.5 us (5%)
  other arithmetic  15.4 us (5%)
    ppermute x7, waiting for transfers between devices, per_device(): lax.ppermute(sent, 'tp', [(i, (i + shift) % tp_size) for i in range(tp_si...  125 us
    all_gather x1, waiting for transfers between devices, per_device(): att_full = lax.all_gather(attended, 'tp', axis=1, tiled=True)  72.3 us
    ppermute x7, starting transfers between devices, per_device(): lax.ppermute(sent, 'tp', [(i, (i + shift) % tp_size) for i in range(tp_si...  18.8 us
    dynamic_update_slice x7, local copies, waits for them, and re-layouts, per_device(): lax.dynamic_update_slice_in_dim(w_cols, got, src * out_weight.shape[0], 0)  15.6 us
    dot_general x1, matrix products, per_device(): mixed_out = jnp.dot(att_full, w_cols, preferred_element_type=jnp.float32)  9.79 us
    sub x1, other arithmetic, per_device(): expo = jnp.where(allowed[None], jnp.exp(scores - run_max[..., None]), 0.0)  8.06 us
    unnamed x13, local copies, waits for them, and re-layouts  7.77 us
  transfers between devices with their start and end apart: 9, of which 5 were waited for; matrix products, arithmetic and copies ran while one was open for 7% of the time, Pallas kernels for 0%

profile of v2, /device:TPU:0, one launch (start us, length us, event | category | flops | bytes accessed | tf_op | source)
XLA Modules:
  0.0 304.0 jit_solution(923836337490062315)
XLA Ops:
  6.5 2.4 pad_maximum_fusion.1
  9.7 2.5 copy-done.2
  12.2 2.6 constant_dynamic-slice_fusion
  14.8 2.9 copy-done.3
  17.7 3.1 %collective-permute-start = (bf16[512,896]{1,0:T(8,128)(2,1)}, bf16[512,896]{1,0:T(8,128)(2,1)}, u32[]{:S(2)}, u32[]{:S(2)}) collective-permute-start(bf16[512,896]{1,0:T(8,128)(2,1)} %get-tuple-element.19), channel_id=1, source_target_pairs={{0,1},{1,2},{2,3},{3,4},{4,5},{5,6},{6,7},{7,0},{8,9},{9,10},{10,1... | collective-permute-start | bytes 2752520 | tf_op jit(solution)/shard_map/ppermute | solution.py:38
  22.4 2.2 collective-permute-start.2
  26.5 4.8 %collective-permute-start.4 = (bf16[512,896]{1,0:T(8,128)(2,1)S(1)}, bf16[512,896]{1,0:T(8,128)(2,1)}, u32[]{:S(2)}, u32[]{:S(2)}) collective-permute-start(bf16[512,896]{1,0:T(8,128)(2,1)S(1)} %get-tuple-element.15), channel_id=1, source_target_pairs={{0,5},{1,6},{2,7},{3,0},{4,1},{5,2},{6,3},{7,4},{8,13},{9,14},{10,... | collective-permute-start | bytes 2752520 | tf_op jit(solution)/shard_map/ppermute | solution.py:38
  33.0 30.2 %collective-permute-done = bf16[512,896]{1,0:T(8,128)(2,1)} collective-permute-done((bf16[512,896]{1,0:T(8,128)(2,1)}, bf16[512,896]{1,0:T(8,128)(2,1)}, u32[]{:S(2)}, u32[]{:S(2)}) %collective-permute-start) | collective-permute-done | bytes 917536 | tf_op jit(solution)/shard_map/ppermute | solution.py:38
  63.2 3.0 collective-permute-start.5
  76.6 28.4 %collective-permute-done.2 = bf16[512,896]{1,0:T(8,128)(2,1)} collective-permute-done((bf16[512,896]{1,0:T(8,128)(2,1)}, bf16[512,896]{1,0:T(8,128)(2,1)}, u32[]{:S(2)}, u32[]{:S(2)}) %collective-permute-start.2) | collective-permute-done | bytes 917536 | tf_op jit(solution)/shard_map/ppermute | solution.py:38
  105.0 2.2 constant_dynamic-update-slice_fusion.4
  107.3 2.3 constant_dynamic-update-slice_fusion.3
  109.6 33.5 %collective-permute-done.4 = bf16[512,896]{1,0:T(8,128)(2,1)} collective-permute-done((bf16[512,896]{1,0:T(8,128)(2,1)S(1)}, bf16[512,896]{1,0:T(8,128)(2,1)}, u32[]{:S(2)}, u32[]{:S(2)}) %collective-permute-start.4) | collective-permute-done | bytes 917536 | tf_op jit(solution)/shard_map/ppermute | solution.py:38
  147.5 32.8 %collective-permute-done.6 = bf16[512,896]{1,0:T(8,128)(2,1)} collective-permute-done((bf16[512,896]{1,0:T(8,128)(2,1)S(1)}, bf16[512,896]{1,0:T(8,128)(2,1)}, u32[]{:S(2)}, u32[]{:S(2)}) %collective-permute-start.6) | collective-permute-done | bytes 917536 | tf_op jit(solution)/shard_map/ppermute | solution.py:38
  180.3 2.2 constant_dynamic-update-slice_fusion
  182.6 2.3 dynamic-slice_bitcast_fusion.2
  186.9 6.1 %reshape.97 = bf16[1536,2,4,128]{3,2,1,0:T(4,128)(2,1)} reshape(bf16[3,512,1024]{2,1,0:T(8,128)(2,1)} %pad_maximum_fusion) | data formatting | bytes 6291456 | tf_op jit(solution)/shard_map/reshape | solution.py:44
  193.0 3.3 %fusion.30 = (bf16[1536,1,4,128]{3,2,1,0:T(4,128)(2,1)S(1)}, bf16[1536,1,4,128]{3,2,1,0:T(4,128)(2,1)}) fusion(bf16[1536,2,4,128]{3,2,1,0:T(4,128)(2,1)} %reshape.97), kind=kLoop, calls=%fused_computation.50 | loop fusion | bytes 6291456 | tf_op jit(solution)/shard_map/slice | solution.py:46
  196.3 2.3 copy.14
  198.6 3.3 %fusion.10 = f32[4,1536,512]{2,1,0:T(8,128)S(1)} fusion(bf16[1536,1,4,128]{3,2,1,0:T(4,128)(2,1)} %get-tuple-element.23, bf16[512,512]{1,0:T(8,128)(2,1)S(1)} %copy-done), kind=kOutput, calls=%fused_computation.15 | convolution fusion | flops 805306368 | bytes 14680064 | tf_op jit(solution)/shard_map/htd,hsd->hts/dot_general | solution.py:52
  201.9 8.1 %fusion.32 = (f32[4,512]{1,0:T(4,128)S(1)}, bf16[4,512,1536]{1,2,0:T(8,128)(2,1)}) fusion(f32[4,1536,512]{2,1,0:T(8,128)S(1)} %fusion.10, pred[512,1536]{0,1:T(8,128)(4,1)S(1)} %copy-done.4), kind=kOutput, calls=%fused_computation.52 | output fusion | flops 22021632 | bytes 19668992 | tf_op jit(solution)/shard_map/sub | solution.py:56
  210.0 5.1 %fusion.22 = bf16[512,4,128]{0,2,1:T(8,128)(2,1)} fusion(bf16[4,512,1536]{1,2,0:T(8,128)(2,1)} %get-tuple-element.28, bf16[1536,1,4,128]{0,3,2,1:T(8,128)(2,1)} %copy.14, f32[512,4]{0,1:T(4,128)S(1)} %bitcast.61), kind=kOutput, calls=%fused_computation.20 | convolution fusion | flops 805830656 | bytes 8396800 | tf_op jit(solution)/shard_map/hts,hsd->htd/dot_general | solution.py:59
  215.1 72.3 %all-gather.5.cloned.1.call-done = bf16[512,4096]{0,1:T(8,128)(2,1)} async-done(((bf16[512,512]{0,1:T(8,128)(2,1)}), bf16[512,4096]{0,1:T(8,128)(2,1)}) %all-gather.5.cloned.1.call-update) | async-done | bytes 4194320 | tf_op jit(solution)/shard_map/all_gather | solution.py:66
  287.3 9.8 %convolution_convert_fusion = bf16[512,896]{1,0:T(8,128)(2,1)} fusion(bf16[512,4096]{0,1:T(8,128)(2,1)} %all-gather.5.cloned.1.call-done, bf16[4096,896]{1,0:T(8,128)(2,1)} %constant_dynamic-update-slice_fusion), kind=kOutput, calls=%fused_computation.17 | convolution fusion | flops 3758555136 | bytes 12451840 | tf_op jit(solution)/shard_map/dot_general | solution.py:67
  (37 shorter events, 20.7 us)
Async XLA Ops:
  6.5 192.1 %copy-start = (bf16[512,512]{1,0:T(8,128)(2,1)S(1)}, bf16[512,512]{1,0:T(8,128)(2,1)}, u32[]{:S(2)}) copy-start(bf16[512,512]{1,0:T(8,128)(2,1)} %param.5) | copy-start | bytes 1572868
  6.5 176.0 %all-gather.3.cloned.1.call-start = ((), (), s32[]{:S(2)}) async-start(), calls=%async_computation | async-start | bytes 17825792 | tf_op jit(solution)/shard_map/all_gather | solution.py:22
  8.9 278.4 %all-gather.5.cloned.1.call-start = ((), (), s32[]{:S(2)}) async-start(), calls=%async_computation.1 | async-start | bytes 4718592 | tf_op jit(solution)/shard_map/all_gather | solution.py:66
  9.1 3.1 %copy-start.2 = (bf16[512,7168]{1,0:T(8,128)(2,1)S(1)}, bf16[512,7168]{1,0:T(8,128)(2,1)}, u32[]{:S(2)}) copy-start(bf16[512,7168]{1,0:T(8,128)(2,1)} %param.9) | copy-start | bytes 22020100
  12.2 19.0 %copy-start.5 = (s32[16,3]{0,1:T(4,128)S(1)}, s32[16,3]{0,1:T(4,128)}, u32[]{:S(2)}) copy-start(s32[16,3]{0,1:T(4,128)} %param.8) | copy-start | bytes 580
  14.8 2.9 copy-start.3
  17.7 45.5 %collective-permute-start = (bf16[512,896]{1,0:T(8,128)(2,1)}, bf16[512,896]{1,0:T(8,128)(2,1)}, u32[]{:S(2)}, u32[]{:S(2)}) collective-permute-start(bf16[512,896]{1,0:T(8,128)(2,1)} %get-tuple-element.19), channel_id=1, source_target_pairs={{0,1},{1,2},{2,3},{3,4},{4,5},{5,6},{6,7},{7,0},{8,9},{9,10},{10,1... | collective-permute-start | bytes 2752520 | tf_op jit(solution)/shard_map/ppermute | solution.py:38
  20.8 45.5 %collective-permute-start.1 = (bf16[512,896]{1,0:T(8,128)(2,1)}, bf16[512,896]{1,0:T(8,128)(2,1)}, u32[]{:S(2)}, u32[]{:S(2)}) collective-permute-start(bf16[512,896]{1,0:T(8,128)(2,1)} %get-tuple-element.18), channel_id=1, source_target_pairs={{0,2},{1,3},{2,4},{3,5},{4,6},{5,7},{6,0},{7,1},{8,10},{9,11},{10,... | collective-permute-start | bytes 2752520 | tf_op jit(solution)/shard_map/ppermute | solution.py:38
  22.4 82.7 %collective-permute-start.2 = (bf16[512,896]{1,0:T(8,128)(2,1)}, bf16[512,896]{1,0:T(8,128)(2,1)}, u32[]{:S(2)}, u32[]{:S(2)}) collective-permute-start(bf16[512,896]{1,0:T(8,128)(2,1)} %get-tuple-element.17), channel_id=1, source_target_pairs={{0,3},{1,4},{2,5},{3,6},{4,7},{5,0},{6,1},{7,2},{8,11},{9,12},{10,... | collective-permute-start | bytes 2752520 | tf_op jit(solution)/shard_map/ppermute | solution.py:38
  24.6 82.6 %collective-permute-start.3 = (bf16[512,896]{1,0:T(8,128)(2,1)}, bf16[512,896]{1,0:T(8,128)(2,1)}, u32[]{:S(2)}, u32[]{:S(2)}) collective-permute-start(bf16[512,896]{1,0:T(8,128)(2,1)} %get-tuple-element.16), channel_id=1, source_target_pairs={{0,4},{1,5},{2,6},{3,7},{4,0},{5,1},{6,2},{7,3},{8,12},{9,13},{10,... | collective-permute-start | bytes 2752520 | tf_op jit(solution)/shard_map/ppermute | solution.py:38
  26.5 116.6 %collective-permute-start.4 = (bf16[512,896]{1,0:T(8,128)(2,1)S(1)}, bf16[512,896]{1,0:T(8,128)(2,1)}, u32[]{:S(2)}, u32[]{:S(2)}) collective-permute-start(bf16[512,896]{1,0:T(8,128)(2,1)S(1)} %get-tuple-element.15), channel_id=1, source_target_pairs={{0,5},{1,6},{2,7},{3,0},{4,1},{5,2},{6,3},{7,4},{8,13},{9,14},{10,... | collective-permute-start | bytes 2752520 | tf_op jit(solution)/shard_map/ppermute | solution.py:38
  63.2 82.0 %collective-permute-start.5 = (bf16[512,896]{1,0:T(8,128)(2,1)S(1)}, bf16[512,896]{1,0:T(8,128)(2,1)}, u32[]{:S(2)}, u32[]{:S(2)}) collective-permute-start(bf16[512,896]{1,0:T(8,128)(2,1)S(1)} %get-tuple-element.21), channel_id=1, source_target_pairs={{0,6},{1,7},{2,0},{3,1},{4,2},{5,3},{6,4},{7,5},{8,14},{9,15},{10,... | collective-permute-start | bytes 2752520 | tf_op jit(solution)/shard_map/ppermute | solution.py:38
  66.3 114.0 %collective-permute-start.6 = (bf16[512,896]{1,0:T(8,128)(2,1)S(1)}, bf16[512,896]{1,0:T(8,128)(2,1)}, u32[]{:S(2)}, u32[]{:S(2)}) collective-permute-start(bf16[512,896]{1,0:T(8,128)(2,1)S(1)} %get-tuple-element.14), channel_id=1, source_target_pairs={{0,7},{1,0},{2,1},{3,2},{4,3},{5,4},{6,5},{7,6},{8,15},{9,8},{10,9... | collective-permute-start | bytes 2752520 | tf_op jit(solution)/shard_map/ppermute | solution.py:38
  198.6 3.3 %copy-start.4 = (pred[512,1536]{0,1:T(8,128)(4,1)S(1)}, pred[512,1536]{0,1:T(8,128)(4,1)}, u32[]{:S(2)}) copy-start(pred[512,1536]{0,1:T(8,128)(4,1)} %compare_and_fusion) | copy-start | bytes 2359300
  215.1 82.1 %copy-start.1 = (bf16[512,512]{1,0:T(8,128)(2,1)S(1)}, bf16[512,512]{1,0:T(8,128)(2,1)}, u32[]{:S(2)}) copy-start(bf16[512,512]{1,0:T(8,128)(2,1)} %param.5) | copy-start | bytes 1572868
Sparse Core Ops, SparseCore 0:
  9.1 171.9 all-gather.2
  215.2 72.0 all-gather.4

commit v3 on v1

v3 whole, which is shorter than its diff:
```python
import functools

import jax
import jax.numpy as jnp
from jax import lax
from jax.experimental import pallas as pl
from jax.experimental.pallas import tpu as pltpu
from jax.sharding import PartitionSpec as P

HD = 128
BLOCK = 512

neg_fill = -1e30


def attend_kernel(meta_ref, q_ref, k0_ref, k1_ref, k2_ref, v0_ref, v1_ref, v2_ref, o_ref, *, topk):
    scaling = 1.0 / jnp.sqrt(jnp.float32(HD))
    q = q_ref[...]
    query_pos = meta_ref[topk] * BLOCK + lax.broadcasted_iota(jnp.int32, (BLOCK, BLOCK), 0)
    key_off = lax.broadcasted_iota(jnp.int32, (BLOCK, BLOCK), 1)
    k_refs = (k0_ref, k1_ref, k2_ref)
    v_refs = (v0_ref, v1_ref, v2_ref)
    scores = []
    masks = []
    for s in range(topk):
        sc = lax.dot_general(
            q, k_refs[s][...], (((1,), (1,)), ((), ())), preferred_element_type=jnp.float32
        ) * scaling
        ok = (meta_ref[s] * BLOCK + key_off) <= query_pos
        if s > 0:
            ok = ok & (meta_ref[s] != meta_ref[0])
        scores.append(sc)
        masks.append(ok)
    row_max = jnp.max(jnp.where(masks[0], scores[0], neg_fill), axis=1, keepdims=True)
    for s in range(1, topk):
        row_max = jnp.maximum(
            row_max, jnp.max(jnp.where(masks[s], scores[s], neg_fill), axis=1, keepdims=True)
        )
    row_sum = jnp.zeros((BLOCK, 1), jnp.float32)
    acc = jnp.zeros((BLOCK, HD), jnp.float32)
    for s in range(topk):
        e = jnp.where(masks[s], jnp.exp(scores[s] - row_max), 0.0)
        row_sum = row_sum + jnp.sum(e, axis=1, keepdims=True)
        acc = acc + jnp.dot(
            e.astype(jnp.bfloat16), v_refs[s][...], preferred_element_type=jnp.float32
        )
    o_ref[...] = (acc / row_sum).astype(o_ref.dtype)


def attend(meta, queries, kv_piece, head_count, topk):
    def k_map(s):
        return lambda h, m: (m[s], h)

    def v_map(s):
        return lambda h, m: (m[s], head_count + h)

    blk = (BLOCK, HD)
    grid_spec = pltpu.PrefetchScalarGridSpec(
        num_scalar_prefetch=1,
        grid=(head_count,),
        in_specs=[pl.BlockSpec(blk, lambda h, m: (0, h))]
        + [pl.BlockSpec(blk, k_map(s)) for s in range(topk)]
        + [pl.BlockSpec(blk, v_map(s)) for s in range(topk)],
        out_specs=pl.BlockSpec(blk, lambda h, m: (0, h)),
    )
    return pl.pallas_call(
        functools.partial(attend_kernel, topk=topk),
        grid_spec=grid_spec,
        out_shape=jax.ShapeDtypeStruct(queries.shape, queries.dtype),
        cost_estimate=pl.CostEstimate(
            flops=4 * head_count * BLOCK * topk * BLOCK * HD,
            transcendentals=head_count * BLOCK * topk * BLOCK,
            bytes_accessed=2 * queries.size * 2 + 2 * topk * BLOCK * head_count * HD * 2,
        ),
    )(meta, queries, *([kv_piece] * (2 * topk)))


def per_device(queries, key_rows, value_rows, selection, out_weight):
    row_count, feat_width = queries.shape
    head_count = feat_width // HD
    topk = selection.shape[1]
    tp_size = lax.axis_size("tp")
    ctx_place = lax.axis_index("ctx")
    own_choice = lax.dynamic_slice_in_dim(selection, ctx_place, 1, 0)[0]
    meta = jnp.concatenate([own_choice, ctx_place.astype(jnp.int32)[None]])
    kv_piece = lax.all_gather(
        jnp.concatenate([key_rows, value_rows], axis=1), "ctx", axis=0, tiled=True
    )
    attended = attend(meta, queries, kv_piece, head_count, topk)
    col_width = out_weight.shape[1] // tp_size
    partial = jnp.einsum(
        "tk,kjc->jtc",
        attended,
        out_weight.reshape(out_weight.shape[0], tp_size, col_width),
        preferred_element_type=jnp.float32,
    ).astype(jnp.bfloat16)
    shares = lax.psum_scatter(partial, "tp", scatter_dimension=0, tiled=True)
    return shares.reshape(row_count, col_width)


def solution(mesh):
    placed = (P("ctx", "tp"), P("ctx", "tp"), P("ctx", "tp"), P(), P("tp", None))
    return jax.shard_map(
        per_device, mesh=mesh, in_specs=placed, out_specs=P("ctx", "tp"), check_vma=False
    )
```

time: 272 us -> 242 us (0.89)
  local copies, waits for them, and re-layouts: 27.5 us -> 0.19 us
  Pallas kernels: 0 us -> 13.4 us
  other arithmetic: 15.4 us -> 2.96 us
  matrix products: 16.7 us -> 10.2 us
  waiting for transfers between devices: 197 us -> 202 us
    reduce_scatter x0 -> x1, waiting for transfers between devices: none -> 108 us  [per_device(): shares = lax.psum_scatter(partial, 'tp', scatter_dimension=0, tiled=True)]
    unnamed x3 -> x2, waiting for transfers between devices: 108 us -> 0.03 us
    unnamed x7 -> x2, local copies, waits for them, and re-layouts: 15 us -> 0.01 us
    pallas_call x0 -> x1, Pallas kernels: none -> 13.4 us  [attend(): pl.pallas_call(functools.partial(attend_kernel, topk=topk), grid_spec=gri...]
    sub x1 -> x0, other arithmetic: 8.07 us -> none  [per_device(): expo = jnp.where(allowed[None], jnp.exp(scores - run_max[..., None]), 0.0)]
    dot_general x3 -> x1, matrix products: 16.7 us -> 10.2 us  [per_device(): jnp.einsum('tk,kjc->jtc', attended, out_weight.reshape(out_weight.shape[0...]
    reshape x1 -> x0, local copies, waits for them, and re-layouts: 6.08 us -> none  [per_device(): picked = jnp.stack([lax.dynamic_slice_in_dim(kv_piece, own_choice[s] * BL...]
    all_gather x1, waiting for transfers between devices: 88.8 us -> 93.5 us  [per_device(): lax.all_gather(jnp.concatenate([key_rows, value_rows], axis=1), 'ctx', ax...]
  transfers between devices with their start and end apart: 2 -> 2, of which waited for: 2 -> 2; matrix products, arithmetic and copies ran while one was open for 1% -> 0% of each run, Pallas kernels for 0% -> 0%
where the time goes in v3:
time: 242 us
  waiting for transfers between devices  202 us (83%)
  Pallas kernels  13.4 us (6%)
  between operations  13.4 us (6%)
  matrix products  10.2 us (4%)
  other arithmetic  2.96 us (1%)
    reduce_scatter x1, waiting for transfers between devices, per_device(): shares = lax.psum_scatter(partial, 'tp', scatter_dimension=0, tiled=True)  108 us
    all_gather x1, waiting for transfers between devices, per_device(): lax.all_gather(jnp.concatenate([key_rows, value_rows], axis=1), 'ctx', ax...  93.5 us
    pallas_call x1, Pallas kernels, attend(): pl.pallas_call(functools.partial(attend_kernel, topk=topk), grid_spec=gri...  13.4 us
    dot_general x1, matrix products, per_device(): jnp.einsum('tk,kjc->jtc', attended, out_weight.reshape(out_weight.shape[0...  10.2 us
  transfers between devices with their start and end apart: 2, of which 2 were waited for; matrix products, arithmetic and copies ran while one was open for 0% of the time, Pallas kernels for 0%

profile of v3, /device:TPU:0, one launch (start us, length us, event | category | flops | bytes accessed | tf_op | source)
XLA Modules:
  0.0 241.8 jit_solution(194516054713875909)
XLA Ops:
  6.5 0.0 copy-start
  6.5 0.0 all-gather.2.cloned.1.call-start
  6.5 2.3 pad_maximum_fusion
  8.8 0.0 all-gather.2.cloned.1.call-update
  8.9 0.0 reduce-scatter.2.cloned.1.call-start
  8.9 0.0 copy-done
  8.9 0.2 dynamic-slice_reduce_fusion
  9.1 0.7 pad_add_fusion.meta_ref
  9.8 93.5 %all-gather.2.cloned.1.call-done.k0_ref.k1_ref.k2_ref.v0_ref.v1_ref.v2_ref = bf16[8192,1024]{1,0:T(8,128)(2,1)} async-done(((bf16[512,1024]{1,0:T(8,128)(2,1)}), bf16[8192,1024]{1,0:T(8,128)(2,1)}) %all-gather.2.cloned.1.call-update) | async-done | bytes 16777232 | tf_op jit(solution)/shard_map/all_gather | solution.py:86
  103.2 13.4 %shard_map.55 = bf16[512,512]{1,0:T(8,128)(2,1)} custom-call(s32[4]{0:T(128)} %pad_add_fusion.meta_ref, bf16[512,512]{1,0:T(8,128)(2,1)} %q_ref.1, bf16[8192,1024]{1,0:T(8,128)(2,1)} %all-gather.2.cloned.1.call-done.k0_ref.k1_ref.k2_ref.v0_ref.v1_ref.v2_ref, bf16[8192,1024]{1,0:T(8,128)(2,1)} %all-gather.2.cloned.1.call-done.k0_ref.k1_ref.k2_ref.v0_ref.v1_ref.v2_ref, ...), custom_call_target="tpu_custom_call" | custom-call | flops 1610612736 | bytes 4194304 | tf_op jit(solution)/shard_map/pallas_call | solution.py:66
  116.6 10.2 %convert_bitcast_fusion = bf16[8,512,896]{2,1,0:T(8,128)(2,1)} fusion(bf16[64,8,8,896]{3,2,1,0:T(8,128)(2,1)} %bitcast.13, bf16[512,512]{1,0:T(8,128)(2,1)} %shard_map.55), kind=kOutput, calls=%fused_computation.3 | convolution fusion | flops 3761766400 | bytes 15204352 | tf_op jit(solution)/shard_map/tk,kjc->jtc/dot_general | solution.py:91
  126.8 0.0 reduce-scatter.2.cloned.1.call-update
  126.9 108.1 %reduce-scatter.2.cloned.1.call-done = bf16[1,512,896]{2,1,0:T(8,128)(2,1)} async-done(((bf16[8,512,896]{2,1,0:T(8,128)(2,1)}), bf16[1,512,896]{2,1,0:T(8,128)(2,1)}) %reduce-scatter.2.cloned.1.call-update) | async-done | bytes 917520 | tf_op jit(solution)/shard_map/reduce_scatter | solution.py:97
Async XLA Ops:
  6.5 2.4 copy-start
  6.5 96.7 %all-gather.2.cloned.1.call-start = ((), (), s32[]{:S(2)}) async-start(), calls=%async_computation.1 | async-start | bytes 17825792 | tf_op jit(solution)/shard_map/all_gather | solution.py:86
  8.9 226.1 %reduce-scatter.2.cloned.1.call-start = ((), (), s32[]{:S(2)}) async-start(), calls=%async_computation.2 | async-start | bytes 8257536 | tf_op jit(solution)/shard_map/reduce_scatter | solution.py:97
Sparse Core Ops, SparseCore 0:
  9.1 94.1 all-gather.1
  127.0 107.9 reduce-scatter.1

commit v4 on v3

v4 whole, which is shorter than its diff:
```python
import functools

import jax
import jax.numpy as jnp
from jax import lax
from jax.experimental import pallas as pl
from jax.experimental.pallas import tpu as pltpu
from jax.sharding import PartitionSpec as P

HD = 128
BLOCK = 512

neg_fill = -1e30


def layer_kernel(meta_ref, q_ref, *refs, topk, head_count):
    k_refs = refs[:topk]
    v_refs = refs[topk : 2 * topk]
    w_ref, o_ref, att_ref = refs[2 * topk :]

    @pl.when(pl.program_id(0) == 0)
    def _():
        scaling = 1.0 / jnp.sqrt(jnp.float32(HD))
        q_block = meta_ref[topk]
        query_pos = q_block * BLOCK + lax.broadcasted_iota(jnp.int32, (BLOCK, BLOCK), 0)
        key_pos = meta_ref[0] * BLOCK + lax.broadcasted_iota(jnp.int32, (BLOCK, BLOCK), 1)
        causal = key_pos <= query_pos
        usable = [None] + [
            (meta_ref[s] != meta_ref[0]) & (meta_ref[s] < q_block) for s in range(1, topk)
        ]
        for h in range(head_count):
            cols = slice(h * HD, (h + 1) * HD)
            q = q_ref[:, cols]
            scores = []
            for s in range(topk):
                sc = lax.dot_general(
                    q, k_refs[s][:, cols], (((1,), (1,)), ((), ())),
                    preferred_element_type=jnp.float32,
                ) * scaling
                if s == 0:
                    sc = jnp.where(causal, sc, neg_fill)
                else:
                    sc = jnp.where(usable[s], sc, neg_fill)
                scores.append(sc)
            row_max = jnp.max(scores[0], axis=1, keepdims=True)
            for s in range(1, topk):
                row_max = jnp.maximum(row_max, jnp.max(scores[s], axis=1, keepdims=True))
            row_sum = jnp.zeros((BLOCK, 1), jnp.float32)
            acc = jnp.zeros((BLOCK, HD), jnp.float32)
            for s in range(topk):
                e = jnp.exp(scores[s] - row_max)
                row_sum = row_sum + jnp.sum(e, axis=1, keepdims=True)
                acc = acc + jnp.dot(
                    e.astype(jnp.bfloat16), v_refs[s][:, cols],
                    preferred_element_type=jnp.float32,
                )
            att_ref[:, cols] = (acc / row_sum).astype(att_ref.dtype)

    o_ref[0] = jnp.dot(att_ref[...], w_ref[...], preferred_element_type=jnp.float32).astype(
        o_ref.dtype
    )


def layer(meta, queries, kv_piece, out_weight, topk, chunks):
    row_count, feat_width = queries.shape
    head_count = feat_width // HD
    col_width = out_weight.shape[1] // chunks

    def k_map(s):
        return lambda j, m: (m[s], 0)

    def v_map(s):
        return lambda j, m: (m[s], 1)

    blk = (BLOCK, feat_width)
    grid_spec = pltpu.PrefetchScalarGridSpec(
        num_scalar_prefetch=1,
        grid=(chunks,),
        in_specs=[pl.BlockSpec(blk, lambda j, m: (0, 0))]
        + [pl.BlockSpec(blk, k_map(s)) for s in range(topk)]
        + [pl.BlockSpec(blk, v_map(s)) for s in range(topk)]
        + [pl.BlockSpec((out_weight.shape[0], col_width), lambda j, m: (0, j))],
        out_specs=pl.BlockSpec((1, row_count, col_width), lambda j, m: (j, 0, 0)),
        scratch_shapes=[pltpu.VMEM((row_count, feat_width), queries.dtype)],
    )
    attn_flops = 4 * head_count * BLOCK * topk * BLOCK * HD
    proj_flops = 2 * row_count * feat_width * out_weight.shape[1]
    return pl.pallas_call(
        functools.partial(layer_kernel, topk=topk, head_count=head_count),
        grid_spec=grid_spec,
        out_shape=jax.ShapeDtypeStruct((chunks, row_count, col_width), queries.dtype),
        compiler_params=pltpu.CompilerParams(dimension_semantics=("arbitrary",)),
        cost_estimate=pl.CostEstimate(
            flops=attn_flops + proj_flops,
            transcendentals=head_count * BLOCK * topk * BLOCK,
            bytes_accessed=queries.size * 2 * (1 + 2 * topk) + out_weight.size * 2 * 2,
        ),
    )(meta, queries, *([kv_piece] * (2 * topk)), out_weight)


def per_device(queries, key_rows, value_rows, selection, out_weight):
    row_count, feat_width = queries.shape
    topk = selection.shape[1]
    tp_size = lax.axis_size("tp")
    ctx_place = lax.axis_index("ctx")
    own_choice = lax.dynamic_slice_in_dim(selection, ctx_place, 1, 0)[0]
    meta = jnp.concatenate([own_choice, ctx_place.astype(jnp.int32)[None]])
    kv_piece = lax.all_gather(
        jnp.concatenate([key_rows, value_rows], axis=1), "ctx", axis=0, tiled=True
    )
    partial = layer(meta, queries, kv_piece, out_weight, topk, tp_size)
    shares = lax.psum_scatter(partial, "tp", scatter_dimension=0, tiled=True)
    return shares.reshape(row_count, out_weight.shape[1] // tp_size)


def solution(mesh):
    placed = (P("ctx", "tp"), P("ctx", "tp"), P("ctx", "tp"), P(), P("tp", None))
    return jax.shard_map(
        per_device, mesh=mesh, in_specs=placed, out_specs=P("ctx", "tp"), check_vma=False
    )
```

time: 242 us -> 236 us (0.975)
  matrix products: 10.2 us -> 0 us
  Pallas kernels: 13.4 us -> 17.8 us
    dot_general x1 -> x0, matrix products: 10.2 us -> none  [per_device(): jnp.einsum('tk,kjc->jtc', attended, out_weight.reshape(out_weight.shape[0...]
    pallas_call x1, Pallas kernels: 13.4 us -> 17.8 us  [layer(): pl.pallas_call(functools.partial(layer_kernel, topk=topk, head_count=head...]
where the time goes in v4:
time: 236 us
  waiting for transfers between devices  201 us (85%)
  Pallas kernels  17.8 us (8%)
  between operations  13.4 us (6%)
  other arithmetic  2.95 us (1%)
    reduce_scatter x1, waiting for transfers between devices, per_device(): shares = lax.psum_scatter(partial, 'tp', scatter_dimension=0, tiled=True)  108 us
    all_gather x1, waiting for transfers between devices, per_device(): lax.all_gather(jnp.concatenate([key_rows, value_rows], axis=1), 'ctx', ax...  93.5 us
    pallas_call x1, Pallas kernels, layer(): pl.pallas_call(functools.partial(layer_kernel, topk=topk, head_count=head...  17.8 us
  transfers between devices with their start and end apart: 2, of which 2 were waited for; matrix products, arithmetic and copies ran while one was open for 0% of the time, Pallas kernels for 0%

profile of v4, /device:TPU:0, one launch (start us, length us, event | category | flops | bytes accessed | tf_op | source)
XLA Modules:
  0.0 235.7 jit_solution(14712913958076291096)
XLA Ops:
  6.5 0.0 copy-start
  6.5 0.0 all-gather.2.cloned.1.call-start
  6.5 2.3 pad_maximum_fusion
  8.8 0.0 all-gather.2.cloned.1.call-update
  8.9 0.0 reduce-scatter.2.cloned.1.call-start
  8.9 0.0 copy-done
  8.9 0.2 dynamic-slice_reduce_fusion
  9.1 0.7 pad_add_fusion.meta_ref
  9.8 93.5 %all-gather.2.cloned.1.call-done.refs_0_.refs_1_.refs_2_.refs_3_.refs_4_.refs_5_ = bf16[8192,1024]{1,0:T(8,128)(2,1)} async-done(((bf16[512,1024]{1,0:T(8,128)(2,1)}), bf16[8192,1024]{1,0:T(8,128)(2,1)}) %all-gather.2.cloned.1.call-update) | async-done | bytes 16777232 | tf_op jit(solution)/shard_map/all_gather | solution.py:108
  103.2 17.8 %shard_map.55 = bf16[8,512,896]{2,1,0:T(8,128)(2,1)} custom-call(s32[4]{0:T(128)} %pad_add_fusion.meta_ref, bf16[512,512]{1,0:T(8,128)(2,1)} %q_ref.1, bf16[8192,1024]{1,0:T(8,128)(2,1)} %all-gather.2.cloned.1.call-done.refs_0_.refs_1_.refs_2_.refs_3_.refs_4_.refs_5_, ...), custom_call_target="tpu_custom_call" | custom-call | flops 5368709120 | bytes 18350080 | tf_op jit(solution)/shard_map/pallas_call | solution.py:88
  121.0 0.0 reduce-scatter.2.cloned.1.call-update
  121.0 107.8 %reduce-scatter.2.cloned.1.call-done = bf16[1,512,896]{2,1,0:T(8,128)(2,1)} async-done(((bf16[8,512,896]{2,1,0:T(8,128)(2,1)}), bf16[1,512,896]{2,1,0:T(8,128)(2,1)}) %reduce-scatter.2.cloned.1.call-update) | async-done | bytes 917520 | tf_op jit(solution)/shard_map/reduce_scatter | solution.py:112
Async XLA Ops:
  6.5 2.4 %copy-start = (s32[16,3]{0,1:T(4,128)S(1)}, s32[16,3]{0,1:T(4,128)}, u32[]{:S(2)}) copy-start(s32[16,3]{0,1:T(4,128)} %param.8) | copy-start | bytes 580
  6.5 96.7 %all-gather.2.cloned.1.call-start = ((), (), s32[]{:S(2)}) async-start(), calls=%async_computation.1 | async-start | bytes 17825792 | tf_op jit(solution)/shard_map/all_gather | solution.py:108
  8.9 220.0 %reduce-scatter.2.cloned.1.call-start = ((), (), s32[]{:S(2)}) async-start(), calls=%async_computation.2 | async-start | bytes 8257536 | tf_op jit(solution)/shard_map/reduce_scatter | solution.py:112
Sparse Core Ops, SparseCore 0:
  9.1 94.1 all-gather.1
  121.2 107.6 reduce-scatter.1

commit v5 on v4

v5 whole, which is shorter than its diff:
```python
import functools

import jax
import jax.numpy as jnp
from jax import lax
from jax.experimental import pallas as pl
from jax.experimental.pallas import tpu as pltpu
from jax.sharding import Mesh, PartitionSpec as P

HD = 128
BLOCK = 512

neg_fill = -1e30


def attend_kernel(meta_ref, q_ref, *refs, topk, head_count):
    k_refs = refs[:topk]
    v_refs = refs[topk : 2 * topk]
    att_ref = refs[2 * topk]
    if True:
        scaling = 1.0 / jnp.sqrt(jnp.float32(HD))
        q_block = meta_ref[topk]
        query_pos = q_block * BLOCK + lax.broadcasted_iota(jnp.int32, (BLOCK, BLOCK), 0)
        key_pos = meta_ref[0] * BLOCK + lax.broadcasted_iota(jnp.int32, (BLOCK, BLOCK), 1)
        causal = key_pos <= query_pos
        usable = [None] + [
            (meta_ref[s] != meta_ref[0]) & (meta_ref[s] < q_block) for s in range(1, topk)
        ]
        for h in range(head_count):
            cols = slice(h * HD, (h + 1) * HD)
            q = q_ref[:, cols]
            scores = []
            for s in range(topk):
                sc = lax.dot_general(
                    q, k_refs[s][:, cols], (((1,), (1,)), ((), ())),
                    preferred_element_type=jnp.float32,
                ) * scaling
                if s == 0:
                    sc = jnp.where(causal, sc, neg_fill)
                else:
                    sc = jnp.where(usable[s], sc, neg_fill)
                scores.append(sc)
            row_max = jnp.max(scores[0], axis=1, keepdims=True)
            for s in range(1, topk):
                row_max = jnp.maximum(row_max, jnp.max(scores[s], axis=1, keepdims=True))
            row_sum = jnp.zeros((BLOCK, 1), jnp.float32)
            acc = jnp.zeros((BLOCK, HD), jnp.float32)
            for s in range(topk):
                e = jnp.exp(scores[s] - row_max)
                row_sum = row_sum + jnp.sum(e, axis=1, keepdims=True)
                acc = acc + jnp.dot(
                    e.astype(jnp.bfloat16), v_refs[s][:, cols],
                    preferred_element_type=jnp.float32,
                )
            att_ref[:, cols] = (acc / row_sum).astype(att_ref.dtype)


def project_kernel(a_ref, w_ref, o_ref):
    o_ref[0] = jnp.dot(a_ref[...], w_ref[...], preferred_element_type=jnp.float32).astype(
        o_ref.dtype
    )


def attend(meta, queries, kv_piece, topk):
    row_count, feat_width = queries.shape
    head_count = feat_width // HD

    def k_map(s):
        return lambda j, m: (m[s], 0)

    def v_map(s):
        return lambda j, m: (m[s], 1)

    blk = (BLOCK, feat_width)
    grid_spec = pltpu.PrefetchScalarGridSpec(
        num_scalar_prefetch=1,
        grid=(1,),
        in_specs=[pl.BlockSpec(blk, lambda j, m: (0, 0))]
        + [pl.BlockSpec(blk, k_map(s)) for s in range(topk)]
        + [pl.BlockSpec(blk, v_map(s)) for s in range(topk)],
        out_specs=pl.BlockSpec(blk, lambda j, m: (0, 0)),
    )
    return pl.pallas_call(
        functools.partial(attend_kernel, topk=topk, head_count=head_count),
        grid_spec=grid_spec,
        out_shape=jax.ShapeDtypeStruct((row_count, feat_width), queries.dtype),
        cost_estimate=pl.CostEstimate(
            flops=4 * head_count * BLOCK * topk * BLOCK * HD,
            transcendentals=head_count * BLOCK * topk * BLOCK,
            bytes_accessed=queries.size * 2 * (2 + 2 * topk),
        ),
    )(meta, queries, *([kv_piece] * (2 * topk)))


def project(att_full, w_group, halves):
    rows, inner = att_full.shape
    col_width = w_group.shape[1] // halves
    return pl.pallas_call(
        project_kernel,
        grid=(halves,),
        in_specs=[
            pl.BlockSpec((rows, inner), lambda k: (0, 0)),
            pl.BlockSpec((inner, col_width), lambda k: (0, k)),
        ],
        out_specs=pl.BlockSpec((1, rows, col_width), lambda k: (k, 0, 0)),
        out_shape=jax.ShapeDtypeStruct((halves, rows, col_width), att_full.dtype),
        cost_estimate=pl.CostEstimate(
            flops=2 * rows * inner * w_group.shape[1],
            transcendentals=0,
            bytes_accessed=att_full.size * 2 + w_group.size * 2 + rows * w_group.shape[1] * 2,
        ),
    )(att_full, w_group)


CTX = ("xl", "z", "core")
TP = ("y", "xh")


def per_device(queries, key_rows, value_rows, selection, out_weight):
    row_count, feat_width = queries.shape
    topk = selection.shape[1]
    y_size = lax.axis_size("y")
    xh_size = lax.axis_size("xh")
    y_place = lax.axis_index("y")
    ctx_place = lax.axis_index(CTX)
    own_choice = lax.dynamic_slice_in_dim(selection, ctx_place, 1, 0)[0]
    meta = jnp.concatenate([own_choice, ctx_place.astype(jnp.int32)[None]])
    kv_piece = lax.all_gather(
        jnp.concatenate([key_rows, value_rows], axis=1), CTX, axis=0, tiled=True
    )
    group_width = out_weight.shape[1] // y_size
    pieces = [lax.dynamic_slice_in_dim(out_weight, y_place * group_width, group_width, 1)]
    for shift in range(1, y_size):
        dest = (y_place + shift) % y_size
        sent = lax.dynamic_slice_in_dim(out_weight, dest * group_width, group_width, 1)
        pieces.append(lax.ppermute(sent, "y", [(i, (i + shift) % y_size) for i in range(y_size)]))
    by_shift = jnp.stack(pieces)
    order = (y_place - jnp.arange(y_size, dtype=jnp.int32)) % y_size
    w_group = jnp.take(by_shift, order, axis=0).reshape(y_size * out_weight.shape[0], group_width)
    kv_piece, w_group = lax.optimization_barrier((kv_piece, w_group))
    attended = attend(meta, queries, kv_piece, topk)
    att_full = lax.all_gather(attended, "y", axis=1, tiled=True)
    partial = project(att_full, w_group, xh_size)
    shares = lax.psum_scatter(partial, "xh", scatter_dimension=0, tiled=True)
    return shares.reshape(row_count, group_width // xh_size)


def solution(mesh):
    ctx_size, tp_size = mesh.devices.shape
    view = Mesh(
        mesh.devices.reshape(2, ctx_size // 4, 2, tp_size // 2, 2), ("xl", "z", "core", "y", "xh")
    )
    placed = (P(CTX, TP), P(CTX, TP), P(CTX, TP), P(), P(TP, None))
    return jax.shard_map(
        per_device, mesh=view, in_specs=placed, out_specs=P(CTX, TP), check_vma=False
    )
```

time: 236 us -> 209 us (0.89)
  waiting for transfers between devices: 201 us -> 143 us
  local copies, waits for them, and re-layouts: 0.19 us -> 13.1 us
  other arithmetic: 2.95 us -> 15.8 us
  starting transfers between devices: 0.04 us -> 5.99 us
    ppermute x0 -> x3, waiting for transfers between devices: none -> 77.1 us  [per_device(): lax.ppermute(sent, 'y', [(i, (i + shift) % y_size) for i in range(y_size)])]
    reduce_scatter x1, waiting for transfers between devices: 108 us -> 33.1 us  [per_device(): shares = lax.psum_scatter(partial, 'xh', scatter_dimension=0, tiled=True)]
    all_gather x1 -> x2, waiting for transfers between devices: 93.5 us -> 32.5 us  [the longest x1 32.5 us: per_device(): att_full = lax.all_gather(attended, 'y', axis=1, tiled=True)]
    gather x0 -> x1, local copies, waits for them, and re-layouts: none -> 7.1 us  [per_device(): jnp.take(by_shift, order, axis=0)]
    select_n x0 -> x2, other arithmetic: none -> 6.78 us  [per_device(): jnp.take(by_shift, order, axis=0)]
    another operation x0 -> x1, other arithmetic: none -> 6.13 us  [per_device(): by_shift = jnp.stack(pieces)]
    ppermute x0 -> x3, starting transfers between devices: none -> 5.91 us  [per_device(): lax.ppermute(sent, 'y', [(i, (i + shift) % y_size) for i in range(y_size)])]
    another operation x0 -> x1, local copies, waits for them, and re-layouts: none -> 5.71 us  [per_device(): by_shift = jnp.stack(pieces)]
  transfers between devices with their start and end apart: 2 -> 6, of which waited for: 2 -> 4; matrix products, arithmetic and copies ran while one was open for 0% -> 13% of each run, Pallas kernels for 0% -> 0%
where the time goes in v5:
time: 209 us; the launch traced here: 208 us
  waiting for transfers between devices  143 us (68%)
  Pallas kernels  17.4 us (8%)
  other arithmetic  15.8 us (8%)
  between operations  13.2 us (6%)
  local copies, waits for them, and re-layouts  13.1 us (6%)
  starting transfers between devices  5.99 us (3%)
    ppermute x3, waiting for transfers between devices, per_device(): lax.ppermute(sent, 'y', [(i, (i + shift) % y_size) for i in range(y_size)])  77.1 us
    reduce_scatter x1, waiting for transfers between devices, per_device(): shares = lax.psum_scatter(partial, 'xh', scatter_dimension=0, tiled=True)  33.1 us
    all_gather x1, waiting for transfers between devices, per_device(): att_full = lax.all_gather(attended, 'y', axis=1, tiled=True)  32.5 us
    pallas_call x1, Pallas kernels, attend(): pl.pallas_call(functools.partial(attend_kernel, topk=topk, head_count=hea...  9.03 us
    pallas_call x1, Pallas kernels, project(): pl.pallas_call(project_kernel, grid=(halves,), in_specs=[pl.BlockSpec((ro...  8.32 us
    gather x1, local copies, waits for them, and re-layouts, per_device(): jnp.take(by_shift, order, axis=0)  7.1 us
    select_n x2, other arithmetic, per_device(): jnp.take(by_shift, order, axis=0)  6.78 us
    another operation x1, other arithmetic, per_device(): by_shift = jnp.stack(pieces)  6.13 us
  transfers between devices with their start and end apart: 6, of which 4 were waited for; matrix products, arithmetic and copies ran while one was open for 13% of the time, Pallas kernels for 0%

profile of v5, /device:TPU:0, one launch (start us, length us, event | category | flops | bytes accessed | tf_op | source)
XLA Modules:
  0.0 208.2 jit_solution(8087081301218329174)
XLA Ops:
  6.5 2.3 %pad_maximum_fusion.1 = bf16[512,1024]{1,0:T(8,128)(2,1)} fusion(bf16[512,512]{1,0:T(8,128)(2,1)} %param.7, bf16[512,512]{1,0:T(8,128)(2,1)} %param.6), kind=kLoop, calls=%fused_computation.4 | loop fusion | flops 2097152 | bytes 2097152 | tf_op jit(solution)/shard_map/concatenate | solution.py:129
  8.8 0.0 all-gather.3.cloned.1.call-update
  8.9 0.0 all-gather.5.cloned.1.call-start
  9.0 5.7 %dynamic-slice_bitcast_fusion = (bf16[1,512,1792]{2,1,0:T(8,128)(2,1)S(1)}, bf16[512,1792]{1,0:T(8,128)(2,1)}, bf16[512,1792]{1,0:T(8,128)(2,1)}, bf16[512,1792]{1,0:T(8,128)(2,1)}) fusion(bf16[512,7168]{1,0:T(8,128)(2,1)} %param.9, s32[]{:T(128)S(6)} %select_n.71, s32[]{:T(128)S(6)} %select_n.73, s32[]{:T(128)S(6)} %select_n.77, s32[]{:T(128)S(6)} %select_n.75), kind=kLoop, calls=%fused_computation.3 | loop fusion | bytes 14680080 | tf_op jit(solution)/shard_map/stack | solution.py:137
  14.7 1.7 collective-permute-start
  16.3 2.9 %collective-permute-start.1 = (bf16[512,1792]{1,0:T(8,128)(2,1)}, bf16[512,1792]{1,0:T(8,128)(2,1)}, u32[]{:S(2)}, u32[]{:S(2)}) collective-permute-start(bf16[512,1792]{1,0:T(8,128)(2,1)} %get-tuple-element.12), channel_id=1, source_target_pairs={{0,4},{2,6},{4,0},{6,2},{1,5},{3,7},{5,1},{7,3},{8,12},{10,14},{12... | collective-permute-start | bytes 5505032 | tf_op jit(solution)/shard_map/ppermute | solution.py:136
  19.2 1.3 collective-permute-start.2
  20.6 0.1 broadcast_bitcast_fusion
  20.7 0.0 copy-done
  20.7 0.2 dynamic-slice_reduce_fusion
  20.9 0.6 pad_add_fusion.meta_ref
  21.5 36.6 %collective-permute-done = bf16[512,1792]{1,0:T(8,128)(2,1)} collective-permute-done((bf16[512,1792]{1,0:T(8,128)(2,1)}, bf16[512,1792]{1,0:T(8,128)(2,1)}, u32[]{:S(2)}, u32[]{:S(2)}) %collective-permute-start) | collective-permute-done | bytes 1835040 | tf_op jit(solution)/shard_map/ppermute | solution.py:136
  58.1 40.5 %collective-permute-done.1 = bf16[512,1792]{1,0:T(8,128)(2,1)} collective-permute-done((bf16[512,1792]{1,0:T(8,128)(2,1)}, bf16[512,1792]{1,0:T(8,128)(2,1)}, u32[]{:S(2)}, u32[]{:S(2)}) %collective-permute-start.1) | collective-permute-done | bytes 1835040 | tf_op jit(solution)/shard_map/ppermute | solution.py:136
  98.6 0.0 collective-permute-done.2
  98.6 6.1 %pad_maximum_fusion = bf16[4,512,1792]{2,1,0:T(8,128)(2,1)} fusion(bf16[1,512,1792]{2,1,0:T(8,128)(2,1)} %bitcast.4, bf16[1,512,1792]{2,1,0:T(8,128)(2,1)} %bitcast.3, bf16[1,512,1792]{2,1,0:T(8,128)(2,1)} %bitcast.2, bf16[1,512,1792]{2,1,0:T(8,128)(2,1)S(1)} %get-tuple-element.9), kind=kLoop, calls=%fused_computation.1 | loop fusion | flops 11010048 | bytes 14680064 | tf_op jit(solution)/shard_map/stack | solution.py:137
  104.7 7.1 %gather_fusion = bf16[4,512,1792]{2,1,0:T(8,128)(2,1)} fusion(bf16[4,512,1792]{2,1,0:T(8,128)(2,1)} %pad_maximum_fusion, s32[1024]{0:T(1024)S(1)} %pad_clamp_fusion), kind=kCustom, calls=%fused_computation | custom fusion | bytes 14680080 | tf_op jit(solution)/shard_map/jit(_take)/gather | solution.py:139
  111.8 6.8 %bitcast_select_fusion.w_ref = bf16[2048,1792]{1,0:T(8,128)(2,1)} fusion(bf16[4,512,1792]{2,1,0:T(8,128)(2,1)} %gather_fusion, pred[2048]{0:T(1024)(128)(4,1)S(1)} %bitcast.14), kind=kLoop, calls=%fused_computation.2 | loop fusion | flops 3670016 | bytes 14682112 | tf_op jit(solution)/shard_map/jit(_take)/select_n | solution.py:139
  118.6 9.0 %shard_map.55 = bf16[512,512]{1,0:T(8,128)(2,1)} custom-call(s32[4]{0:T(128)} %pad_add_fusion.meta_ref, bf16[512,512]{1,0:T(8,128)(2,1)} %q_ref.1, bf16[8192,1024]{1,0:T(8,128)(2,1)} %all-gather.3.cloned.1.call-done.refs_0_.refs_1_.refs_2_.refs_3_.refs_4_.refs_5_, ...), custom_call_target="tpu_custom_call" | custom-call | flops 1610612736 | bytes 4194304 | tf_op jit(solution)/shard_map/pallas_call | solution.py:83
  127.6 0.0 all-gather.5.cloned.1.call-update
  127.7 0.0 reduce-scatter.2.cloned.1.call-start
  127.7 32.5 %all-gather.5.cloned.1.call-done.a_ref = bf16[512,2048]{1,0:T(8,128)(2,1)} async-done(((bf16[512,512]{1,0:T(8,128)(2,1)}), bf16[512,2048]{1,0:T(8,128)(2,1)}) %all-gather.5.cloned.1.call-update) | async-done | bytes 2097168 | tf_op jit(solution)/shard_map/all_gather | solution.py:142
  160.2 8.3 %shard_map.56 = bf16[2,512,896]{2,1,0:T(8,128)(2,1)} custom-call(bf16[512,2048]{1,0:T(8,128)(2,1)} %all-gather.5.cloned.1.call-done.a_ref, bf16[2048,1792]{1,0:T(8,128)(2,1)} %bitcast_select_fusion.w_ref), custom_call_target="tpu_custom_call" | custom-call | flops 3758096384 | bytes 11272192 | tf_op jit(solution)/shard_map/pallas_call | solution.py:98
  168.5 0.0 reduce-scatter.2.cloned.1.call-update
  168.5 33.1 %reduce-scatter.2.cloned.1.call-done = bf16[1,512,896]{2,1,0:T(8,128)(2,1)} async-done(((bf16[2,512,896]{2,1,0:T(8,128)(2,1)}), bf16[1,512,896]{2,1,0:T(8,128)(2,1)}) %reduce-scatter.2.cloned.1.call-update) | async-done | bytes 917520 | tf_op jit(solution)/shard_map/reduce_scatter | solution.py:144
  (7 shorter events, 0.0 us)
Async XLA Ops:
  6.5 14.2 %copy-start = (s32[16,3]{0,1:T(4,128)S(1)}, s32[16,3]{0,1:T(4,128)}, u32[]{:S(2)}) copy-start(s32[16,3]{0,1:T(4,128)} %param.8) | copy-start | bytes 580
  6.5 112.1 %all-gather.3.cloned.1.call-start = ((), (), s32[]{:S(2)}) async-start(), calls=%async_computation.1 | async-start | bytes 17825792 | tf_op jit(solution)/shard_map/all_gather | solution.py:128
  8.9 151.3 %all-gather.5.cloned.1.call-start = ((), (), s32[]{:S(2)}) async-start(), calls=%async_computation.2 | async-start | bytes 2621440 | tf_op jit(solution)/shard_map/all_gather | solution.py:142
  14.7 43.4 %collective-permute-start = (bf16[512,1792]{1,0:T(8,128)(2,1)}, bf16[512,1792]{1,0:T(8,128)(2,1)}, u32[]{:S(2)}, u32[]{:S(2)}) collective-permute-start(bf16[512,1792]{1,0:T(8,128)(2,1)} %get-tuple-element.10), channel_id=1, source_target_pairs={{0,2},{2,4},{4,6},{6,0},{1,3},{3,5},{5,7},{7,1},{8,10},{10,12},{12... | collective-permute-start | bytes 5505032 | tf_op jit(solution)/shard_map/ppermute | solution.py:136
  16.3 82.3 %collective-permute-start.1 = (bf16[512,1792]{1,0:T(8,128)(2,1)}, bf16[512,1792]{1,0:T(8,128)(2,1)}, u32[]{:S(2)}, u32[]{:S(2)}) collective-permute-start(bf16[512,1792]{1,0:T(8,128)(2,1)} %get-tuple-element.12), channel_id=1, source_target_pairs={{0,4},{2,6},{4,0},{6,2},{1,5},{3,7},{5,1},{7,3},{8,12},{10,14},{12... | collective-permute-start | bytes 5505032 | tf_op jit(solution)/shard_map/ppermute | solution.py:136
  19.2 79.4 %collective-permute-start.2 = (bf16[512,1792]{1,0:T(8,128)(2,1)}, bf16[512,1792]{1,0:T(8,128)(2,1)}, u32[]{:S(2)}, u32[]{:S(2)}) collective-permute-start(bf16[512,1792]{1,0:T(8,128)(2,1)} %get-tuple-element.11), channel_id=1, source_target_pairs={{0,6},{2,0},{4,2},{6,4},{1,7},{3,1},{5,3},{7,5},{8,14},{10,8},{12,... | collective-permute-start | bytes 5505032 | tf_op jit(solution)/shard_map/ppermute | solution.py:136
  127.7 74.0 %reduce-scatter.2.cloned.1.call-start = ((), (), s32[]{:S(2)}) async-start(), calls=%async_computation.3 | async-start | bytes 2752512 | tf_op jit(solution)/shard_map/reduce_scatter | solution.py:144
Sparse Core Ops, SparseCore 0:
  9.1 94.1 all-gather.2
  127.8 32.3 all-gather.4
  168.6 32.9 reduce-scatter.1

commit v6 on v5

--- a/solution.py
+++ b/solution.py
@@ -55,10 +55,14 @@
             att_ref[:, cols] = (acc / row_sum).astype(att_ref.dtype)
 
 
-def project_kernel(a_ref, w_ref, o_ref):
-    o_ref[0] = jnp.dot(a_ref[...], w_ref[...], preferred_element_type=jnp.float32).astype(
-        o_ref.dtype
-    )
+def project_kernel(y_ref, *refs, shifts):
+    a_refs = refs[:shifts]
+    w_refs = refs[shifts : 2 * shifts]
+    o_ref = refs[2 * shifts]
+    acc = jnp.dot(a_refs[0][...], w_refs[0][...], preferred_element_type=jnp.float32)
+    for sh in range(1, shifts):
+        acc = acc + jnp.dot(a_refs[sh][...], w_refs[sh][...], preferred_element_type=jnp.float32)
+    o_ref[0] = acc.astype(o_ref.dtype)
 
 
 def attend(meta, queries, kv_piece, topk):
@@ -92,24 +96,34 @@
     )(meta, queries, *([kv_piece] * (2 * topk)))
 
 
-def project(att_full, w_group, halves):
-    rows, inner = att_full.shape
-    col_width = w_group.shape[1] // halves
+def project(y_meta, att_full, out_weight, received, halves):
+    rows = att_full.shape[0]
+    shifts = len(received) + 1
+    inner = att_full.shape[1] // shifts
+    col_width = received[0].shape[1] // halves
+
+    def a_map(sh):
+        return lambda k, m: (0, (m[0] + shifts - sh) % shifts)
+
+    grid_spec = pltpu.PrefetchScalarGridSpec(
+        num_scalar_prefetch=1,
+        grid=(halves,),
+        in_specs=[pl.BlockSpec((rows, inner), a_map(sh)) for sh in range(shifts)]
+        + [pl.BlockSpec((inner, col_width), lambda k, m: (0, m[0] * halves + k))]
+        + [pl.BlockSpec((inner, col_width), lambda k, m: (0, k)) for _ in received],
+        out_specs=pl.BlockSpec((1, rows, col_width), lambda k, m: (k, 0, 0)),
+    )
     return pl.pallas_call(
-        project_kernel,
-        grid=(halves,),
-        in_specs=[
-            pl.BlockSpec((rows, inner), lambda k: (0, 0)),
-            pl.BlockSpec((inner, col_width), lambda k: (0, k)),
-        ],
-        out_specs=pl.BlockSpec((1, rows, col_width), lambda k: (k, 0, 0)),
+        functools.partial(project_kernel, shifts=shifts),
+        grid_spec=grid_spec,
         out_shape=jax.ShapeDtypeStruct((halves, rows, col_width), att_full.dtype),
         cost_estimate=pl.CostEstimate(
-            flops=2 * rows * inner * w_group.shape[1],
+            flops=2 * rows * att_full.shape[1] * col_width * halves,
             transcendentals=0,
-            bytes_accessed=att_full.size * 2 + w_group.size * 2 + rows * w_group.shape[1] * 2,
+            bytes_accessed=att_full.size * 2 + shifts * inner * col_width * halves * 2
+            + rows * col_width * halves * 2,
         ),
-    )(att_full, w_group)
+    )(y_meta, *([att_full] * shifts), out_weight, *received)
 
 
 CTX = ("xl", "z", "core")
@@ -129,18 +143,18 @@
         jnp.concatenate([key_rows, value_rows], axis=1), CTX, axis=0, tiled=True
     )
     group_width = out_weight.shape[1] // y_size
-    pieces = [lax.dynamic_slice_in_dim(out_weight, y_place * group_width, group_width, 1)]
+    received = []
     for shift in range(1, y_size):
         dest = (y_place + shift) % y_size
         sent = lax.dynamic_slice_in_dim(out_weight, dest * group_width, group_width, 1)
-        pieces.append(lax.ppermute(sent, "y", [(i, (i + shift) % y_size) for i in range(y_size)]))
-    by_shift = jnp.stack(pieces)
-    order = (y_place - jnp.arange(y_size, dtype=jnp.int32)) % y_size
-    w_group = jnp.take(by_shift, order, axis=0).reshape(y_size * out_weight.shape[0], group_width)
-    kv_piece, w_group = lax.optimization_barrier((kv_piece, w_group))
+        received.append(
+            lax.ppermute(sent, "y", [(i, (i + shift) % y_size) for i in range(y_size)])
+        )
+    kv_piece, received = lax.optimization_barrier((kv_piece, received))
     attended = attend(meta, queries, kv_piece, topk)
     att_full = lax.all_gather(attended, "y", axis=1, tiled=True)
-    partial = project(att_full, w_group, xh_size)
+    y_meta = y_place.astype(jnp.int32)[None]
+    partial = project(y_meta, att_full, out_weight, received, xh_size)
     shares = lax.psum_scatter(partial, "xh", scatter_dimension=0, tiled=True)
     return shares.reshape(row_count, group_width // xh_size)
 

time: 209 us -> 193 us (0.923)
  other arithmetic: 15.8 us -> 2.84 us
  local copies, waits for them, and re-layouts: 13.1 us -> 5.38 us
  waiting for transfers between devices: 143 us -> 147 us
    gather x1 -> x0, local copies, waits for them, and re-layouts: 7.1 us -> none  [per_device(): jnp.take(by_shift, order, axis=0)]
    select_n x2 -> x0, other arithmetic: 6.78 us -> none  [per_device(): jnp.take(by_shift, order, axis=0)]
    another operation x1 -> x0, other arithmetic: 6.13 us -> none  [per_device(): by_shift = jnp.stack(pieces)]
    another operation x1 -> x0, local copies, waits for them, and re-layouts: 5.71 us -> none  [per_device(): by_shift = jnp.stack(pieces)]
    dynamic_slice x0 -> x1, local copies, waits for them, and re-layouts: none -> 5.19 us  [per_device(): lax.dynamic_slice_in_dim(out_weight, dest * group_width, group_width, 1)]
    all_gather x1, waiting for transfers between devices: 0.01 us -> 5.17 us  [per_device(): lax.all_gather(jnp.concatenate([key_rows, value_rows], axis=1), CTX, axis...]
  transfers between devices with their start and end apart: 6 -> 6, of which waited for: 4 -> 5; matrix products, arithmetic and copies ran while one was open for 13% -> 3% of each run, Pallas kernels for 0% -> 0%
where the time goes in v6:
time: 193 us; the launch traced here: 192 us
  waiting for transfers between devices  147 us (76%)
  Pallas kernels  17.5 us (9%)
  between operations  13.2 us (7%)
  starting transfers between devices  5.99 us (3%)
  local copies, waits for them, and re-layouts  5.38 us (3%)
  other arithmetic  2.84 us (1%)
    ppermute x3, waiting for transfers between devices, per_device(): lax.ppermute(sent, 'y', [(i, (i + shift) % y_size) for i in range(y_size)])  77.3 us
    reduce_scatter x1, waiting for transfers between devices, per_device(): shares = lax.psum_scatter(partial, 'xh', scatter_dimension=0, tiled=True)  33.1 us
    all_gather x1, waiting for transfers between devices, per_device(): att_full = lax.all_gather(attended, 'y', axis=1, tiled=True)  31.8 us
    pallas_call x1, Pallas kernels, attend(): pl.pallas_call(functools.partial(attend_kernel, topk=topk, head_count=hea...  8.96 us
    pallas_call x1, Pallas kernels, project(): pl.pallas_call(functools.partial(project_kernel, shifts=shifts), grid_spe...  8.57 us
    ppermute x3, starting transfers between devices, per_device(): lax.ppermute(sent, 'y', [(i, (i + shift) % y_size) for i in range(y_size)])  5.91 us
    dynamic_slice x1, local copies, waits for them, and re-layouts, per_device(): lax.dynamic_slice_in_dim(out_weight, dest * group_width, group_width, 1)  5.19 us
    all_gather x1, waiting for transfers between devices, per_device(): lax.all_gather(jnp.concatenate([key_rows, value_rows], axis=1), CTX, axis...  5.17 us
  transfers between devices with their start and end apart: 6, of which 5 were waited for; matrix products, arithmetic and copies ran while one was open for 3% of the time, Pallas kernels for 0%

profile of v6, /device:TPU:0, one launch (start us, length us, event | category | flops | bytes accessed | tf_op | source)
XLA Modules:
  0.0 192.3 jit_solution(8925247376835516600)
XLA Ops:
  6.5 0.0 copy-start
  6.5 0.0 all-gather.3.cloned.1.call-start
  6.5 2.3 %pad_maximum_fusion = bf16[512,1024]{1,0:T(8,128)(2,1)} fusion(bf16[512,512]{1,0:T(8,128)(2,1)} %param.7, bf16[512,512]{1,0:T(8,128)(2,1)} %param.6), kind=kLoop, calls=%fused_computation | loop fusion | flops 2097152 | bytes 2097152 | tf_op jit(solution)/shard_map/concatenate | solution.py:143
  8.8 0.0 all-gather.3.cloned.1.call-update
  8.8 0.0 all-gather.5.cloned.1.call-start
  8.9 5.2 %constant_dynamic-slice_fusion = (bf16[512,1792]{1,0:T(8,128)(2,1)}, bf16[512,1792]{1,0:T(8,128)(2,1)}, bf16[512,1792]{1,0:T(8,128)(2,1)}) fusion(bf16[512,7168]{1,0:T(8,128)(2,1)} %refs_4_.1, s32[]{:T(128)S(6)} %select_n.33, s32[]{:T(128)S(6)} %select_n.31, s32[]{:T(128)S(6)} %select_n.29), kind=kLoop, calls=%fused_computation.2 | loop fusion | bytes 11010060 | tf_op jit(solution)/shard_map/dynamic_slice | solution.py:149
  14.1 1.7 collective-permute-start
  15.8 2.9 %collective-permute-start.1 = (bf16[512,1792]{1,0:T(8,128)(2,1)}, bf16[512,1792]{1,0:T(8,128)(2,1)}, u32[]{:S(2)}, u32[]{:S(2)}) collective-permute-start(bf16[512,1792]{1,0:T(8,128)(2,1)} %get-tuple-element.14), channel_id=1, source_target_pairs={{0,4},{2,6},{4,0},{6,2},{1,5},{3,7},{5,1},{7,3},{8,12},{10,14},{12... | collective-permute-start | bytes 5505032 | tf_op jit(solution)/shard_map/ppermute | solution.py:151
  18.7 1.3 collective-permute-start.2
  20.0 0.0 copy-done
  20.0 0.2 dynamic-slice_reduce_fusion
  20.2 0.6 pad_add_fusion.meta_ref
  20.8 36.7 %collective-permute-done.refs_5_ = bf16[512,1792]{1,0:T(8,128)(2,1)S(1)} collective-permute-done((bf16[512,1792]{1,0:T(8,128)(2,1)}, bf16[512,1792]{1,0:T(8,128)(2,1)S(1)}, u32[]{:S(2)}, u32[]{:S(2)}) %collective-permute-start) | collective-permute-done | bytes 1835040 | tf_op jit(solution)/shard_map/ppermute | solution.py:151
  57.4 40.6 %collective-permute-done.1.refs_6_ = bf16[512,1792]{1,0:T(8,128)(2,1)} collective-permute-done((bf16[512,1792]{1,0:T(8,128)(2,1)}, bf16[512,1792]{1,0:T(8,128)(2,1)}, u32[]{:S(2)}, u32[]{:S(2)}) %collective-permute-start.1) | collective-permute-done | bytes 1835040 | tf_op jit(solution)/shard_map/ppermute | solution.py:151
  98.1 0.0 collective-permute-done.2.refs_7_
  98.1 5.2 %all-gather.3.cloned.1.call-done.refs_0_.refs_1_.refs_2_.refs_3_.refs_4_.refs_5_ = bf16[8192,1024]{1,0:T(8,128)(2,1)} async-done(((bf16[512,1024]{1,0:T(8,128)(2,1)}), bf16[8192,1024]{1,0:T(8,128)(2,1)}) %all-gather.3.cloned.1.call-update) | async-done | bytes 16777232 | tf_op jit(solution)/shard_map/all_gather | solution.py:142
  103.2 9.0 %shard_map.55 = bf16[512,512]{1,0:T(8,128)(2,1)} custom-call(s32[4]{0:T(128)} %pad_add_fusion.meta_ref, bf16[512,512]{1,0:T(8,128)(2,1)} %q_ref.1, bf16[8192,1024]{1,0:T(8,128)(2,1)} %all-gather.3.cloned.1.call-done.refs_0_.refs_1_.refs_2_.refs_3_.refs_4_.refs_5_, ...), custom_call_target="tpu_custom_call" | custom-call | flops 1610612736 | bytes 4194304 | tf_op jit(solution)/shard_map/pallas_call | solution.py:87
  112.2 0.0 copy-done.1
  112.2 0.0 all-gather.5.cloned.1.call-update
  112.2 0.0 reduce-scatter.2.cloned.1.call-start
  112.3 31.8 %all-gather.5.cloned.1.call-done.refs_0_.refs_1_.refs_2_.refs_3_ = bf16[512,2048]{1,0:T(8,128)(2,1)} async-done(((bf16[512,512]{1,0:T(8,128)(2,1)}), bf16[512,2048]{1,0:T(8,128)(2,1)}) %all-gather.5.cloned.1.call-update) | async-done | bytes 2097168 | tf_op jit(solution)/shard_map/all_gather | solution.py:155
  144.0 8.6 %shard_map.56 = bf16[2,512,896]{2,1,0:T(8,128)(2,1)} custom-call(s32[1]{0:T(128)} %bitcast.y_ref, bf16[512,2048]{1,0:T(8,128)(2,1)} %all-gather.5.cloned.1.call-done.refs_0_.refs_1_.refs_2_.refs_3_, bf16[512,2048]{1,0:T(8,128)(2,1)} %all-gather.5.cloned.1.call-done.refs_0_.refs_1_.refs_2_.refs_3_, ...), custom_call_target="tpu_custom_call" | custom-call | flops 3758096384 | bytes 11272192 | tf_op jit(solution)/shard_map/pallas_call | solution.py:116
  152.6 0.0 reduce-scatter.2.cloned.1.call-update
  152.6 33.1 %reduce-scatter.2.cloned.1.call-done = bf16[1,512,896]{2,1,0:T(8,128)(2,1)} async-done(((bf16[2,512,896]{2,1,0:T(8,128)(2,1)}), bf16[1,512,896]{2,1,0:T(8,128)(2,1)}) %reduce-scatter.2.cloned.1.call-update) | async-done | bytes 917520 | tf_op jit(solution)/shard_map/reduce_scatter | solution.py:158
  (1 shorter events, 0.0 us)
Async XLA Ops:
  6.5 13.5 %copy-start = (s32[16,3]{0,1:T(4,128)S(1)}, s32[16,3]{0,1:T(4,128)}, u32[]{:S(2)}) copy-start(s32[16,3]{0,1:T(4,128)} %param.8) | copy-start | bytes 580
  6.5 96.7 %all-gather.3.cloned.1.call-start = ((), (), s32[]{:S(2)}) async-start(), calls=%async_computation.1 | async-start | bytes 17825792 | tf_op jit(solution)/shard_map/all_gather | solution.py:142
  8.8 135.2 %all-gather.5.cloned.1.call-start = ((), (), s32[]{:S(2)}) async-start(), calls=%async_computation.2 | async-start | bytes 2621440 | tf_op jit(solution)/shard_map/all_gather | solution.py:155
  14.1 43.3 %collective-permute-start = (bf16[512,1792]{1,0:T(8,128)(2,1)}, bf16[512,1792]{1,0:T(8,128)(2,1)S(1)}, u32[]{:S(2)}, u32[]{:S(2)}) collective-permute-start(bf16[512,1792]{1,0:T(8,128)(2,1)} %get-tuple-element.15), channel_id=1, source_target_pairs={{0,2},{2,4},{4,6},{6,0},{1,3},{3,5},{5,7},{7,1},{8,10},{10,12},{12... | collective-permute-start | bytes 5505032 | tf_op jit(solution)/shard_map/ppermute | solution.py:151
  15.8 82.3 %collective-permute-start.1 = (bf16[512,1792]{1,0:T(8,128)(2,1)}, bf16[512,1792]{1,0:T(8,128)(2,1)}, u32[]{:S(2)}, u32[]{:S(2)}) collective-permute-start(bf16[512,1792]{1,0:T(8,128)(2,1)} %get-tuple-element.14), channel_id=1, source_target_pairs={{0,4},{2,6},{4,0},{6,2},{1,5},{3,7},{5,1},{7,3},{8,12},{10,14},{12... | collective-permute-start | bytes 5505032 | tf_op jit(solution)/shard_map/ppermute | solution.py:151
  18.7 79.4 %collective-permute-start.2 = (bf16[512,1792]{1,0:T(8,128)(2,1)}, bf16[512,1792]{1,0:T(8,128)(2,1)}, u32[]{:S(2)}, u32[]{:S(2)}) collective-permute-start(bf16[512,1792]{1,0:T(8,128)(2,1)} %get-tuple-element.13), channel_id=1, source_target_pairs={{0,6},{2,0},{4,2},{6,4},{1,7},{3,1},{5,3},{7,5},{8,14},{10,8},{12,... | collective-permute-start | bytes 5505032 | tf_op jit(solution)/shard_map/ppermute | solution.py:151
  57.4 54.7 %copy-start.1 = (bf16[512,1792]{1,0:T(8,128)(2,1)}, bf16[512,1792]{1,0:T(8,128)(2,1)S(1)}, u32[]{:S(2)}) copy-start(bf16[512,1792]{1,0:T(8,128)(2,1)S(1)} %collective-permute-done.refs_5_) | copy-start | bytes 5505028
  112.2 73.6 %reduce-scatter.2.cloned.1.call-start = ((), (), s32[]{:S(2)}) async-start(), calls=%async_computation.3 | async-start | bytes 2752512 | tf_op jit(solution)/shard_map/reduce_scatter | solution.py:158
Sparse Core Ops, SparseCore 0:
  9.1 94.1 all-gather.2
  112.3 31.6 all-gather.4
  152.7 32.9 reduce-scatter.1

commit v7 on v6

--- a/solution.py
+++ b/solution.py
@@ -62,7 +62,7 @@
     acc = jnp.dot(a_refs[0][...], w_refs[0][...], preferred_element_type=jnp.float32)
     for sh in range(1, shifts):
         acc = acc + jnp.dot(a_refs[sh][...], w_refs[sh][...], preferred_element_type=jnp.float32)
-    o_ref[0] = acc.astype(o_ref.dtype)
+    o_ref[...] = acc.astype(o_ref.dtype)
 
 
 def attend(meta, queries, kv_piece, topk):
@@ -96,34 +96,34 @@
     )(meta, queries, *([kv_piece] * (2 * topk)))
 
 
-def project(y_meta, att_full, out_weight, received, halves):
+def project(meta, att_full, out_weight, received, halves, out_dtype):
     rows = att_full.shape[0]
     shifts = len(received) + 1
     inner = att_full.shape[1] // shifts
     col_width = received[0].shape[1] // halves
 
     def a_map(sh):
-        return lambda k, m: (0, (m[0] + shifts - sh) % shifts)
+        return lambda i, m: (0, (m[0] + shifts - sh) % shifts)
 
     grid_spec = pltpu.PrefetchScalarGridSpec(
         num_scalar_prefetch=1,
-        grid=(halves,),
+        grid=(1,),
         in_specs=[pl.BlockSpec((rows, inner), a_map(sh)) for sh in range(shifts)]
-        + [pl.BlockSpec((inner, col_width), lambda k, m: (0, m[0] * halves + k))]
-        + [pl.BlockSpec((inner, col_width), lambda k, m: (0, k)) for _ in received],
-        out_specs=pl.BlockSpec((1, rows, col_width), lambda k, m: (k, 0, 0)),
+        + [pl.BlockSpec((inner, col_width), lambda i, m: (0, m[0] * halves + m[1]))]
+        + [pl.BlockSpec((inner, col_width), lambda i, m: (0, m[1])) for _ in received],
+        out_specs=pl.BlockSpec((rows, col_width), lambda i, m: (0, 0)),
     )
     return pl.pallas_call(
         functools.partial(project_kernel, shifts=shifts),
         grid_spec=grid_spec,
-        out_shape=jax.ShapeDtypeStruct((halves, rows, col_width), att_full.dtype),
+        out_shape=jax.ShapeDtypeStruct((rows, col_width), out_dtype),
         cost_estimate=pl.CostEstimate(
-            flops=2 * rows * att_full.shape[1] * col_width * halves,
+            flops=2 * rows * att_full.shape[1] * col_width,
             transcendentals=0,
-            bytes_accessed=att_full.size * 2 + shifts * inner * col_width * halves * 2
-            + rows * col_width * halves * 2,
+            bytes_accessed=att_full.size * 2 + shifts * inner * col_width * 2
+            + rows * col_width * jnp.dtype(out_dtype).itemsize,
         ),
-    )(y_meta, *([att_full] * shifts), out_weight, *received)
+    )(meta, *([att_full] * shifts), out_weight, *received)
 
 
 CTX = ("xl", "z", "core")
@@ -153,10 +153,13 @@
     kv_piece, received = lax.optimization_barrier((kv_piece, received))
     attended = attend(meta, queries, kv_piece, topk)
     att_full = lax.all_gather(attended, "y", axis=1, tiled=True)
-    y_meta = y_place.astype(jnp.int32)[None]
-    partial = project(y_meta, att_full, out_weight, received, xh_size)
-    shares = lax.psum_scatter(partial, "xh", scatter_dimension=0, tiled=True)
-    return shares.reshape(row_count, group_width // xh_size)
+    xh_place = lax.axis_index("xh")
+    other = jnp.stack([y_place, xh_size - 1 - xh_place]).astype(jnp.int32)
+    mine = jnp.stack([y_place, xh_place]).astype(jnp.int32)
+    sent = project(other, att_full, out_weight, received, xh_size, queries.dtype)
+    got = lax.ppermute(sent, "xh", [(i, xh_size - 1 - i) for i in range(xh_size)])
+    own = project(mine, att_full, out_weight, received, xh_size, jnp.float32)
+    return (own + got.astype(jnp.float32)).astype(queries.dtype)
 
 
 def solution(mesh):

time: 193 us -> 184 us (0.953)
  waiting for transfers between devices: 147 us -> 127 us
  Pallas kernels: 17.5 us -> 22.4 us
  other arithmetic: 2.84 us -> 6.77 us
  starting transfers between devices: 5.99 us -> 8.93 us
    reduce_scatter x1 -> x0, waiting for transfers between devices: 33.1 us -> none  [per_device(): shares = lax.psum_scatter(partial, 'xh', scatter_dimension=0, tiled=True)]
    ppermute x0 -> x1, waiting for transfers between devices: none -> 13.3 us  [per_device(): lax.ppermute(sent, 'xh', [(i, xh_size - 1 - i) for i in range(xh_size)])]
    pallas_call x1 -> x2, Pallas kernels: 8.57 us -> 13.5 us  [project(): pl.pallas_call(functools.partial(project_kernel, shifts=shifts), grid_spe...]
    ppermute x0 -> x1, starting transfers between devices: none -> 2.98 us  [per_device(): lax.ppermute(sent, 'xh', [(i, xh_size - 1 - i) for i in range(xh_size)])]
    convert_element_type x0 -> x1, other arithmetic: none -> 2.64 us  [per_device(): return (own + got.astype(jnp.float32)).astype(queries.dtype)]
  transfers between devices with their start and end apart: 6 -> 6, of which waited for: 5 -> 5; matrix products, arithmetic and copies ran while one was open for 3% -> 4% of each run, Pallas kernels for 0% -> 4%
where the time goes in v7:
time: 184 us
  waiting for transfers between devices  127 us (69%)
  Pallas kernels  22.4 us (12%)
  between operations  13.5 us (7%)
  starting transfers between devices  8.93 us (5%)
  other arithmetic  6.77 us (4%)
  local copies, waits for them, and re-layouts  5.38 us (3%)
    ppermute x3, waiting for transfers between devices, per_device(): lax.ppermute(sent, 'y', [(i, (i + shift) % y_size) for i in range(y_size)])  77.2 us
    all_gather x1, waiting for transfers between devices, per_device(): att_full = lax.all_gather(attended, 'y', axis=1, tiled=True)  31.2 us
    pallas_call x2, Pallas kernels, project(): pl.pallas_call(functools.partial(project_kernel, shifts=shifts), grid_spe...  13.5 us
    ppermute x1, waiting for transfers between devices, per_device(): lax.ppermute(sent, 'xh', [(i, xh_size - 1 - i) for i in range(xh_size)])  13.3 us
    pallas_call x1, Pallas kernels, attend(): pl.pallas_call(functools.partial(attend_kernel, topk=topk, head_count=hea...  8.96 us
    ppermute x3, starting transfers between devices, per_device(): lax.ppermute(sent, 'y', [(i, (i + shift) % y_size) for i in range(y_size)])  5.91 us
    dynamic_slice x1, local copies, waits for them, and re-layouts, per_device(): lax.dynamic_slice_in_dim(out_weight, dest * group_width, group_width, 1)  5.18 us
    all_gather x1, waiting for transfers between devices, per_device(): lax.all_gather(jnp.concatenate([key_rows, value_rows], axis=1), CTX, axis...  5.16 us
  transfers between devices with their start and end apart: 6, of which 5 were waited for; matrix products, arithmetic and copies ran while one was open for 4% of the time, Pallas kernels for 4%

profile of v7, /device:TPU:0, one launch (start us, length us, event | category | flops | bytes accessed | tf_op | source)
XLA Modules:
  0.0 183.9 jit_solution(4674684576846336251)
XLA Ops:
  6.5 0.0 copy-start
  6.5 2.3 %pad_maximum_fusion = bf16[512,1024]{1,0:T(8,128)(2,1)} fusion(bf16[512,512]{1,0:T(8,128)(2,1)} %param.7, bf16[512,512]{1,0:T(8,128)(2,1)} %param.6), kind=kLoop, calls=%fused_computation.1 | loop fusion | flops 2097152 | bytes 2097152 | tf_op jit(solution)/shard_map/concatenate | solution.py:143
  8.8 0.0 all-gather.3.cloned.1.call-update
  8.9 0.0 all-gather.5.cloned.1.call-start
  9.0 5.2 %constant_dynamic-slice_fusion = (bf16[512,1792]{1,0:T(8,128)(2,1)}, bf16[512,1792]{1,0:T(8,128)(2,1)}, bf16[512,1792]{1,0:T(8,128)(2,1)}) fusion(bf16[512,7168]{1,0:T(8,128)(2,1)} %refs_4_.3, s32[]{:T(128)S(6)} %select_n.33, s32[]{:T(128)S(6)} %select_n.31, s32[]{:T(128)S(6)} %select_n.29), kind=kLoop, calls=%fused_computation.3 | loop fusion | bytes 11010060 | tf_op jit(solution)/shard_map/dynamic_slice | solution.py:149
  14.1 1.7 collective-permute-start
  15.8 2.9 %collective-permute-start.1 = (bf16[512,1792]{1,0:T(8,128)(2,1)}, bf16[512,1792]{1,0:T(8,128)(2,1)}, u32[]{:S(2)}, u32[]{:S(2)}) collective-permute-start(bf16[512,1792]{1,0:T(8,128)(2,1)} %get-tuple-element.14), channel_id=1, source_target_pairs={{0,4},{2,6},{4,0},{6,2},{1,5},{3,7},{5,1},{7,3},{8,12},{10,14},{12... | collective-permute-start | bytes 5505032 | tf_op jit(solution)/shard_map/ppermute | solution.py:151
  18.7 1.3 collective-permute-start.2
  20.1 0.2 dynamic-slice_reduce_fusion
  20.2 0.6 pad_add_fusion.1.meta_ref
  20.8 36.6 %collective-permute-done.refs_5_ = bf16[512,1792]{1,0:T(8,128)(2,1)S(1)} collective-permute-done((bf16[512,1792]{1,0:T(8,128)(2,1)}, bf16[512,1792]{1,0:T(8,128)(2,1)S(1)}, u32[]{:S(2)}, u32[]{:S(2)}) %collective-permute-start) | collective-permute-done | bytes 1835040 | tf_op jit(solution)/shard_map/ppermute | solution.py:151
  57.5 40.6 %collective-permute-done.1.refs_6_ = bf16[512,1792]{1,0:T(8,128)(2,1)} collective-permute-done((bf16[512,1792]{1,0:T(8,128)(2,1)}, bf16[512,1792]{1,0:T(8,128)(2,1)}, u32[]{:S(2)}, u32[]{:S(2)}) %collective-permute-start.1) | collective-permute-done | bytes 1835040 | tf_op jit(solution)/shard_map/ppermute | solution.py:151
  98.1 0.0 collective-permute-done.2.refs_7_
  98.1 5.2 %all-gather.3.cloned.1.call-done.refs_0_.refs_1_.refs_2_.refs_3_.refs_4_.refs_5_ = bf16[8192,1024]{1,0:T(8,128)(2,1)} async-done(((bf16[512,1024]{1,0:T(8,128)(2,1)}), bf16[8192,1024]{1,0:T(8,128)(2,1)}) %all-gather.3.cloned.1.call-update) | async-done | bytes 16777232 | tf_op jit(solution)/shard_map/all_gather | solution.py:142
  103.2 9.0 %shard_map.55 = bf16[512,512]{1,0:T(8,128)(2,1)} custom-call(s32[4]{0:T(128)} %pad_add_fusion.1.meta_ref, bf16[512,512]{1,0:T(8,128)(2,1)} %q_ref.1, bf16[8192,1024]{1,0:T(8,128)(2,1)} %all-gather.3.cloned.1.call-done.refs_0_.refs_1_.refs_2_.refs_3_.refs_4_.refs_5_, ...), custom_call_target="tpu_custom_call" | custom-call | flops 1610612736 | bytes 4194304 | tf_op jit(solution)/shard_map/pallas_call | solution.py:87
  112.2 0.0 all-gather.5.cloned.1.call-update
  112.2 0.6 pad_add_fusion.2.y_ref
  112.8 31.2 %all-gather.5.cloned.1.call-done.refs_0_.refs_1_.refs_2_.refs_3_ = bf16[512,2048]{1,0:T(8,128)(2,1)} async-done(((bf16[512,512]{1,0:T(8,128)(2,1)}), bf16[512,2048]{1,0:T(8,128)(2,1)}) %all-gather.5.cloned.1.call-update) | async-done | bytes 2097168 | tf_op jit(solution)/shard_map/all_gather | solution.py:155
  144.0 6.6 %shard_map.57 = bf16[512,896]{1,0:T(8,128)(2,1)} custom-call(s32[2]{0:T(128)} %pad_add_fusion.2.y_ref, bf16[512,2048]{1,0:T(8,128)(2,1)} %all-gather.5.cloned.1.call-done.refs_0_.refs_1_.refs_2_.refs_3_, bf16[512,2048]{1,0:T(8,128)(2,1)} %all-gather.5.cloned.1.call-done.refs_0_.refs_1_.refs_2_.refs_3_, ...), custom_call_target="tpu_custom_call" | custom-call | flops 1879048192 | bytes 6684672 | tf_op jit(solution)/shard_map/pallas_call | solution.py:116
  150.6 3.0 %collective-permute-start.3 = (bf16[512,896]{1,0:T(8,128)(2,1)}, bf16[512,896]{1,0:T(8,128)(2,1)S(1)}, u32[]{:S(2)}, u32[]{:S(2)}) collective-permute-start(bf16[512,896]{1,0:T(8,128)(2,1)} %shard_map.57), channel_id=1, source_target_pairs={{0,1},{1,0},{2,3},{3,2},{4,5},{5,4},{6,7},{7,6},{8,9},{9,8},{10,11... | collective-permute-start | bytes 2752520 | tf_op jit(solution)/shard_map/ppermute | solution.py:160
  153.6 0.7 pad_add_fusion.y_ref
  154.3 6.9 %shard_map.56 = f32[512,896]{1,0:T(8,128)} custom-call(s32[2]{0:T(128)} %pad_add_fusion.y_ref, bf16[512,2048]{1,0:T(8,128)(2,1)} %all-gather.5.cloned.1.call-done.refs_0_.refs_1_.refs_2_.refs_3_, bf16[512,2048]{1,0:T(8,128)(2,1)} %all-gather.5.cloned.1.call-done.refs_0_.refs_1_.refs_2_.refs_3_, ...), custom_call_target="tpu_custom_call" | custom-call | flops 1879048192 | bytes 7602176 | tf_op jit(solution)/shard_map/pallas_call | solution.py:116
  161.2 13.3 %collective-permute-done.3 = bf16[512,896]{1,0:T(8,128)(2,1)S(1)} collective-permute-done((bf16[512,896]{1,0:T(8,128)(2,1)}, bf16[512,896]{1,0:T(8,128)(2,1)S(1)}, u32[]{:S(2)}, u32[]{:S(2)}) %collective-permute-start.3) | collective-permute-done | bytes 917536 | tf_op jit(solution)/shard_map/ppermute | solution.py:160
  174.4 2.6 %add_convert_fusion = bf16[512,896]{1,0:T(8,128)(2,1)} fusion(f32[512,896]{1,0:T(8,128)} %shard_map.56, bf16[512,896]{1,0:T(8,128)(2,1)S(1)} %collective-permute-done.3), kind=kLoop, calls=%fused_computation | loop fusion | flops 1376256 | bytes 3670016 | tf_op jit(solution)/shard_map/convert_element_type | solution.py:162
  (4 shorter events, 0.0 us)
Async XLA Ops:
  6.5 13.5 %copy-start = (s32[16,3]{0,1:T(4,128)S(1)}, s32[16,3]{0,1:T(4,128)}, u32[]{:S(2)}) copy-start(s32[16,3]{0,1:T(4,128)} %param.8) | copy-start | bytes 580
  6.5 96.7 %all-gather.3.cloned.1.call-start = ((), (), s32[]{:S(2)}) async-start(), calls=%async_computation | async-start | bytes 17825792 | tf_op jit(solution)/shard_map/all_gather | solution.py:142
  8.9 135.2 %all-gather.5.cloned.1.call-start = ((), (), s32[]{:S(2)}) async-start(), calls=%async_computation.1 | async-start | bytes 2621440 | tf_op jit(solution)/shard_map/all_gather | solution.py:155
  14.1 43.3 %collective-permute-start = (bf16[512,1792]{1,0:T(8,128)(2,1)}, bf16[512,1792]{1,0:T(8,128)(2,1)S(1)}, u32[]{:S(2)}, u32[]{:S(2)}) collective-permute-start(bf16[512,1792]{1,0:T(8,128)(2,1)} %get-tuple-element.15), channel_id=1, source_target_pairs={{0,2},{2,4},{4,6},{6,0},{1,3},{3,5},{5,7},{7,1},{8,10},{10,12},{12... | collective-permute-start | bytes 5505032 | tf_op jit(solution)/shard_map/ppermute | solution.py:151
  15.8 82.3 %collective-permute-start.1 = (bf16[512,1792]{1,0:T(8,128)(2,1)}, bf16[512,1792]{1,0:T(8,128)(2,1)}, u32[]{:S(2)}, u32[]{:S(2)}) collective-permute-start(bf16[512,1792]{1,0:T(8,128)(2,1)} %get-tuple-element.14), channel_id=1, source_target_pairs={{0,4},{2,6},{4,0},{6,2},{1,5},{3,7},{5,1},{7,3},{8,12},{10,14},{12... | collective-permute-start | bytes 5505032 | tf_op jit(solution)/shard_map/ppermute | solution.py:151
  18.7 79.4 %collective-permute-start.2 = (bf16[512,1792]{1,0:T(8,128)(2,1)}, bf16[512,1792]{1,0:T(8,128)(2,1)}, u32[]{:S(2)}, u32[]{:S(2)}) collective-permute-start(bf16[512,1792]{1,0:T(8,128)(2,1)} %get-tuple-element.13), channel_id=1, source_target_pairs={{0,6},{2,0},{4,2},{6,4},{1,7},{3,1},{5,3},{7,5},{8,14},{10,8},{12,... | collective-permute-start | bytes 5505032 | tf_op jit(solution)/shard_map/ppermute | solution.py:151
  57.5 54.7 %copy-start.1 = (bf16[512,1792]{1,0:T(8,128)(2,1)}, bf16[512,1792]{1,0:T(8,128)(2,1)S(1)}, u32[]{:S(2)}) copy-start(bf16[512,1792]{1,0:T(8,128)(2,1)S(1)} %collective-permute-done.refs_5_) | copy-start | bytes 5505028
  150.6 23.8 %collective-permute-start.3 = (bf16[512,896]{1,0:T(8,128)(2,1)}, bf16[512,896]{1,0:T(8,128)(2,1)S(1)}, u32[]{:S(2)}, u32[]{:S(2)}) collective-permute-start(bf16[512,896]{1,0:T(8,128)(2,1)} %shard_map.57), channel_id=1, source_target_pairs={{0,1},{1,0},{2,3},{3,2},{4,5},{5,4},{6,7},{7,6},{8,9},{9,8},{10,11... | collective-permute-start | bytes 2752520 | tf_op jit(solution)/shard_map/ppermute | solution.py:160
Sparse Core Ops, SparseCore 0:
  9.1 94.1 all-gather.2
  112.3 31.6 all-gather.4

commit v8 on v7

v8 whole, which is shorter than its diff:
```python
import functools

import jax
import jax.numpy as jnp
from jax import lax
from jax.experimental import pallas as pl
from jax.experimental.pallas import tpu as pltpu
from jax.sharding import Mesh, PartitionSpec as P

HD = 128
BLOCK = 512

neg_fill = -1e30


def attend_kernel(meta_ref, q_ref, *refs, topk):
    k_refs = refs[:topk]
    v_refs = refs[topk : 2 * topk]
    att_ref = refs[2 * topk]
    scaling = 1.0 / jnp.sqrt(jnp.float32(HD))
    q_block = meta_ref[topk]
    query_pos = q_block * BLOCK + lax.broadcasted_iota(jnp.int32, (BLOCK, BLOCK), 0)
    key_pos = meta_ref[0] * BLOCK + lax.broadcasted_iota(jnp.int32, (BLOCK, BLOCK), 1)
    causal = key_pos <= query_pos
    q = q_ref[...]
    scores = []
    for s in range(topk):
        sc = lax.dot_general(
            q, k_refs[s][...], (((1,), (1,)), ((), ())), preferred_element_type=jnp.float32
        ) * scaling
        if s == 0:
            sc = jnp.where(causal, sc, neg_fill)
        else:
            usable = (meta_ref[s] != meta_ref[0]) & (meta_ref[s] < q_block)
            sc = jnp.where(usable, sc, neg_fill)
        scores.append(sc)
    row_max = jnp.max(scores[0], axis=1, keepdims=True)
    for s in range(1, topk):
        row_max = jnp.maximum(row_max, jnp.max(scores[s], axis=1, keepdims=True))
    row_sum = jnp.zeros((BLOCK, 1), jnp.float32)
    acc = jnp.zeros((BLOCK, HD), jnp.float32)
    for s in range(topk):
        e = jnp.exp(scores[s] - row_max)
        row_sum = row_sum + jnp.sum(e, axis=1, keepdims=True)
        acc = acc + jnp.dot(e.astype(jnp.bfloat16), v_refs[s][...], preferred_element_type=jnp.float32)
    att_ref[...] = (acc / row_sum).astype(att_ref.dtype)


def project_kernel(meta_ref, a_ref, w0_ref, w_ref, o_ref, acc_ref):
    sh = pl.program_id(0)

    @pl.when(sh == 0)
    def _():
        acc_ref[...] = jnp.dot(a_ref[...], w0_ref[...], preferred_element_type=jnp.float32)

    @pl.when(sh > 0)
    def _():
        acc_ref[...] += jnp.dot(a_ref[...], w_ref[0], preferred_element_type=jnp.float32)

    @pl.when(sh == pl.num_programs(0) - 1)
    def _():
        o_ref[...] = acc_ref[...].astype(o_ref.dtype)


def attend(meta, queries, kv_piece, topk):
    row_count, feat_width = queries.shape
    head_count = feat_width // HD

    def k_map(s):
        return lambda h, m: (m[s], h)

    def v_map(s):
        return lambda h, m: (m[s], head_count + h)

    blk = (BLOCK, HD)
    grid_spec = pltpu.PrefetchScalarGridSpec(
        num_scalar_prefetch=1,
        grid=(head_count,),
        in_specs=[pl.BlockSpec(blk, lambda h, m: (0, h))]
        + [pl.BlockSpec(blk, k_map(s)) for s in range(topk)]
        + [pl.BlockSpec(blk, v_map(s)) for s in range(topk)],
        out_specs=pl.BlockSpec(blk, lambda h, m: (0, h)),
    )
    return pl.pallas_call(
        functools.partial(attend_kernel, topk=topk),
        grid_spec=grid_spec,
        out_shape=jax.ShapeDtypeStruct((row_count, feat_width), queries.dtype),
        cost_estimate=pl.CostEstimate(
            flops=4 * head_count * BLOCK * topk * BLOCK * HD,
            transcendentals=head_count * BLOCK * topk * BLOCK,
            bytes_accessed=queries.size * 2 * (2 + 2 * topk),
        ),
    )(meta, queries, *([kv_piece] * (2 * topk)))


def project(meta, att_full, out_weight, received, halves, out_dtype):
    rows = att_full.shape[0]
    shifts = received.shape[0] + 1
    inner = att_full.shape[1] // shifts
    col_width = received.shape[2] // halves
    grid_spec = pltpu.PrefetchScalarGridSpec(
        num_scalar_prefetch=1,
        grid=(shifts,),
        in_specs=[
            pl.BlockSpec((rows, inner), lambda sh, m: (0, (m[0] + shifts - sh) % shifts)),
            pl.BlockSpec((inner, col_width), lambda sh, m: (0, m[0] * halves + m[1])),
            pl.BlockSpec(
                (1, inner, col_width), lambda sh, m: (jnp.maximum(sh - 1, 0), 0, m[1])
            ),
        ],
        out_specs=pl.BlockSpec((rows, col_width), lambda sh, m: (0, 0)),
        scratch_shapes=[pltpu.VMEM((rows, col_width), jnp.float32)],
    )
    return pl.pallas_call(
        project_kernel,
        grid_spec=grid_spec,
        out_shape=jax.ShapeDtypeStruct((rows, col_width), out_dtype),
        compiler_params=pltpu.CompilerParams(dimension_semantics=("arbitrary",)),
        cost_estimate=pl.CostEstimate(
            flops=2 * rows * att_full.shape[1] * col_width,
            transcendentals=0,
            bytes_accessed=att_full.size * 2 + shifts * inner * col_width * 2
            + rows * col_width * jnp.dtype(out_dtype).itemsize,
        ),
    )(meta, att_full, out_weight, received)


CTX = ("xl", "z", "core")
TP = ("y", "xh")


def per_device(queries, key_rows, value_rows, selection, out_weight):
    row_count, feat_width = queries.shape
    topk = selection.shape[1]
    y_size = lax.axis_size("y")
    xh_size = lax.axis_size("xh")
    y_place = lax.axis_index("y")
    ctx_place = lax.axis_index(CTX)
    own_choice = lax.dynamic_slice_in_dim(selection, ctx_place, 1, 0)[0]
    meta = jnp.concatenate([own_choice, ctx_place.astype(jnp.int32)[None]])
    kv_piece = lax.all_gather(
        jnp.concatenate([key_rows, value_rows], axis=1), CTX, axis=0, tiled=True
    )
    group_width = out_weight.shape[1] // y_size
    received = []
    for shift in range(1, y_size):
        dest = (y_place + shift) % y_size
        sent = lax.dynamic_slice_in_dim(out_weight, dest * group_width, group_width, 1)
        received.append(
            lax.ppermute(sent, "y", [(i, (i + shift) % y_size) for i in range(y_size)])
        )
    kv_piece, received = lax.optimization_barrier((kv_piece, jnp.stack(received)))
    attended = attend(meta, queries, kv_piece, topk)
    att_full = lax.all_gather(attended, "y", axis=1, tiled=True)
    xh_place = lax.axis_index("xh")
    other = jnp.stack([y_place, xh_size - 1 - xh_place]).astype(jnp.int32)
    mine = jnp.stack([y_place, xh_place]).astype(jnp.int32)
    sent = project(other, att_full, out_weight, received, xh_size, queries.dtype)
    got = lax.ppermute(sent, "xh", [(i, xh_size - 1 - i) for i in range(xh_size)])
    own = project(mine, att_full, out_weight, received, xh_size, jnp.float32)
    return (own + got.astype(jnp.float32)).astype(queries.dtype)


def solution(mesh):
    ctx_size, tp_size = mesh.devices.shape
    view = Mesh(
        mesh.devices.reshape(2, ctx_size // 4, 2, tp_size // 2, 2), ("xl", "z", "core", "y", "xh")
    )
    placed = (P(CTX, TP), P(CTX, TP), P(CTX, TP), P(), P(TP, None))
    return jax.shard_map(
        per_device, mesh=view, in_specs=placed, out_specs=P(CTX, TP), check_vma=False
    )
```

time: 184 us -> 188 us (1.022)
  other arithmetic: 6.77 us -> 12.6 us
  waiting for transfers between devices: 127 us -> 122 us
  Pallas kernels: 22.4 us -> 25.7 us
    another operation x0 -> x1, other arithmetic: none -> 5.67 us  [per_device(): jnp.stack(received)]
    all_gather x1, waiting for transfers between devices: 5.16 us -> 0.01 us  [per_device(): lax.all_gather(jnp.concatenate([key_rows, value_rows], axis=1), CTX, axis...]
    pallas_call x3, Pallas kernels: 22.4 us -> 25.7 us  [the longest x2 14.3 us: project(): pl.pallas_call(project_kernel, grid_spec=grid_spec, out_shape=jax.ShapeDt...]
  transfers between devices with their start and end apart: 6 -> 6, of which waited for: 5 -> 4; matrix products, arithmetic and copies ran while one was open for 4% -> 7% of each run, Pallas kernels for 4% -> 4%
where the time goes in v8:
time: 188 us
  waiting for transfers between devices  122 us (65%)
  Pallas kernels  25.7 us (14%)
  between operations  13.5 us (7%)
  other arithmetic  12.6 us (7%)
  starting transfers between devices  8.93 us (5%)
  local copies, waits for them, and re-layouts  4.96 us (3%)
    ppermute x3, waiting for transfers between devices, per_device(): lax.ppermute(sent, 'y', [(i, (i + shift) % y_size) for i in range(y_size)])  77.2 us
    all_gather x1, waiting for transfers between devices, per_device(): att_full = lax.all_gather(attended, 'y', axis=1, tiled=True)  32.1 us
    pallas_call x2, Pallas kernels, project(): pl.pallas_call(project_kernel, grid_spec=grid_spec, out_shape=jax.ShapeDt...  14.3 us
    ppermute x1, waiting for transfers between devices, per_device(): lax.ppermute(sent, 'xh', [(i, xh_size - 1 - i) for i in range(xh_size)])  12.8 us
    pallas_call x1, Pallas kernels, attend(): pl.pallas_call(functools.partial(attend_kernel, topk=topk), grid_spec=gri...  11.4 us
    ppermute x3, starting transfers between devices, per_device(): lax.ppermute(sent, 'y', [(i, (i + shift) % y_size) for i in range(y_size)])  5.91 us
    another operation x1, other arithmetic, per_device(): jnp.stack(received)  5.67 us
    dynamic_slice x1, local copies, waits for them, and re-layouts, per_device(): lax.dynamic_slice_in_dim(out_weight, dest * group_width, group_width, 1)  4.78 us
  transfers between devices with their start and end apart: 6, of which 4 were waited for; matrix products, arithmetic and copies ran while one was open for 7% of the time, Pallas kernels for 4%

profile of v8, /device:TPU:0, one launch (start us, length us, event | category | flops | bytes accessed | tf_op | source)
XLA Modules:
  0.0 187.8 jit_solution(7342878882152641005)
XLA Ops:
  6.5 0.0 all-gather.3.cloned.1.call-start
  6.5 2.3 %pad_maximum_fusion.1 = bf16[512,1024]{1,0:T(8,128)(2,1)} fusion(bf16[512,512]{1,0:T(8,128)(2,1)} %param.7, bf16[512,512]{1,0:T(8,128)(2,1)} %param.6), kind=kLoop, calls=%fused_computation.2 | loop fusion | flops 2097152 | bytes 2097152 | tf_op jit(solution)/shard_map/concatenate | solution.py:142
  8.8 0.0 all-gather.3.cloned.1.call-update
  8.8 0.0 all-gather.5.cloned.1.call-start
  8.9 4.8 %constant_dynamic-slice_fusion.2 = (bf16[512,1792]{1,0:T(8,128)(2,1)}, bf16[512,1792]{1,0:T(8,128)(2,1)S(1)}, bf16[512,1792]{1,0:T(8,128)(2,1)}) fusion(bf16[512,7168]{1,0:T(8,128)(2,1)} %w0_ref.3, s32[]{:T(128)S(6)} %select_n.29, s32[]{:T(128)S(6)} %select_n.33, s32[]{:T(128)S(6)} %select_n.31), kind=kLoop, calls=%fused_computation.6 | loop fusion | bytes 11010060 | tf_op jit(solution)/shard_map/dynamic_slice | solution.py:148
  13.7 1.7 collective-permute-start
  15.4 2.9 %collective-permute-start.1 = (bf16[512,1792]{1,0:T(8,128)(2,1)}, bf16[512,1792]{1,0:T(8,128)(2,1)}, u32[]{:S(2)}, u32[]{:S(2)}) collective-permute-start(bf16[512,1792]{1,0:T(8,128)(2,1)} %get-tuple-element.11), channel_id=1, source_target_pairs={{0,4},{2,6},{4,0},{6,2},{1,5},{3,7},{5,1},{7,3},{8,12},{10,14},{12... | collective-permute-start | bytes 5505032 | tf_op jit(solution)/shard_map/ppermute | solution.py:150
  18.3 1.3 collective-permute-start.2
  19.6 0.2 dynamic-slice_reduce_fusion
  19.8 0.7 pad_add_fusion.1.meta_ref
  20.5 36.7 %collective-permute-done = bf16[512,1792]{1,0:T(8,128)(2,1)} collective-permute-done((bf16[512,1792]{1,0:T(8,128)(2,1)}, bf16[512,1792]{1,0:T(8,128)(2,1)}, u32[]{:S(2)}, u32[]{:S(2)}) %collective-permute-start) | collective-permute-done | bytes 1835040 | tf_op jit(solution)/shard_map/ppermute | solution.py:150
  57.1 40.5 %collective-permute-done.1 = bf16[512,1792]{1,0:T(8,128)(2,1)} collective-permute-done((bf16[512,1792]{1,0:T(8,128)(2,1)}, bf16[512,1792]{1,0:T(8,128)(2,1)}, u32[]{:S(2)}, u32[]{:S(2)}) %collective-permute-start.1) | collective-permute-done | bytes 1835040 | tf_op jit(solution)/shard_map/ppermute | solution.py:150
  97.6 0.0 collective-permute-done.2
  97.6 5.7 %pad_maximum_fusion.w_ref = bf16[3,512,1792]{2,1,0:T(8,128)(2,1)} fusion(bf16[1,512,1792]{2,1,0:T(8,128)(2,1)} %bitcast.5, bf16[1,512,1792]{2,1,0:T(8,128)(2,1)} %bitcast.4, bf16[1,512,1792]{2,1,0:T(8,128)(2,1)} %bitcast.3), kind=kLoop, calls=%fused_computation | loop fusion | flops 5505024 | bytes 11010048 | tf_op jit(solution)/shard_map/stack | solution.py:152
  103.3 11.4 %shard_map.55 = bf16[512,512]{1,0:T(8,128)(2,1)} custom-call(s32[4]{0:T(128)} %pad_add_fusion.1.meta_ref, bf16[512,512]{1,0:T(8,128)(2,1)} %q_ref.1, bf16[8192,1024]{1,0:T(8,128)(2,1)} %all-gather.3.cloned.1.call-done.refs_0_.refs_1_.refs_2_.refs_3_.refs_4_.refs_5_, ...), custom_call_target="tpu_custom_call" | custom-call | flops 1610612736 | bytes 4194304 | tf_op jit(solution)/shard_map/pallas_call | solution.py:84
  114.7 0.0 all-gather.5.cloned.1.call-update
  114.8 0.7 pad_add_fusion.2.meta_ref
  115.4 32.1 %all-gather.5.cloned.1.call-done.a_ref = bf16[512,2048]{1,0:T(8,128)(2,1)} async-done(((bf16[512,512]{1,0:T(8,128)(2,1)}), bf16[512,2048]{1,0:T(8,128)(2,1)}) %all-gather.5.cloned.1.call-update) | async-done | bytes 2097168 | tf_op jit(solution)/shard_map/all_gather | solution.py:154
  147.6 7.0 %shard_map.57 = bf16[512,896]{1,0:T(8,128)(2,1)} custom-call(s32[2]{0:T(128)} %pad_add_fusion.2.meta_ref, bf16[512,2048]{1,0:T(8,128)(2,1)} %all-gather.5.cloned.1.call-done.a_ref, bf16[512,7168]{1,0:T(8,128)(2,1)} %w0_ref.3, bf16[3,512,1792]{2,1,0:T(8,128)(2,1)} %pad_maximum_fusion.w_ref), custom_call_target="tpu_custom_call" | custom-call | flops 1879048192 | bytes 6684672 | tf_op jit(solution)/shard_map/pallas_call | solution.py:114
  154.6 3.0 %collective-permute-start.3 = (bf16[512,896]{1,0:T(8,128)(2,1)}, bf16[512,896]{1,0:T(8,128)(2,1)S(1)}, u32[]{:S(2)}, u32[]{:S(2)}) collective-permute-start(bf16[512,896]{1,0:T(8,128)(2,1)} %shard_map.57), channel_id=1, source_target_pairs={{0,1},{1,0},{2,3},{3,2},{4,5},{5,4},{6,7},{7,6},{8,9},{9,8},{10,11... | collective-permute-start | bytes 2752520 | tf_op jit(solution)/shard_map/ppermute | solution.py:159
  157.5 0.7 pad_add_fusion.meta_ref
  158.2 7.3 %shard_map.56 = f32[512,896]{1,0:T(8,128)} custom-call(s32[2]{0:T(128)} %pad_add_fusion.meta_ref, bf16[512,2048]{1,0:T(8,128)(2,1)} %all-gather.5.cloned.1.call-done.a_ref, bf16[512,7168]{1,0:T(8,128)(2,1)} %w0_ref.3, bf16[3,512,1792]{2,1,0:T(8,128)(2,1)} %pad_maximum_fusion.w_ref), custom_call_target="tpu_custom_call" | custom-call | flops 1879048192 | bytes 7602176 | tf_op jit(solution)/shard_map/pallas_call | solution.py:114
  165.5 12.8 %collective-permute-done.3 = bf16[512,896]{1,0:T(8,128)(2,1)S(1)} collective-permute-done((bf16[512,896]{1,0:T(8,128)(2,1)}, bf16[512,896]{1,0:T(8,128)(2,1)S(1)}, u32[]{:S(2)}, u32[]{:S(2)}) %collective-permute-start.3) | collective-permute-done | bytes 917536 | tf_op jit(solution)/shard_map/ppermute | solution.py:159
  178.4 2.6 %add_convert_fusion = bf16[512,896]{1,0:T(8,128)(2,1)} fusion(f32[512,896]{1,0:T(8,128)} %shard_map.56, bf16[512,896]{1,0:T(8,128)(2,1)S(1)} %collective-permute-done.3), kind=kLoop, calls=%fused_computation.1 | loop fusion | flops 1376256 | bytes 3670016 | tf_op jit(solution)/shard_map/convert_element_type | solution.py:161
  (3 shorter events, 0.0 us)
Async XLA Ops:
  6.5 13.1 %copy-start = (s32[16,3]{0,1:T(4,128)S(1)}, s32[16,3]{0,1:T(4,128)}, u32[]{:S(2)}) copy-start(s32[16,3]{0,1:T(4,128)} %param.8) | copy-start | bytes 580
  6.5 96.8 %all-gather.3.cloned.1.call-start = ((), (), s32[]{:S(2)}) async-start(), calls=%async_computation | async-start | bytes 17825792 | tf_op jit(solution)/shard_map/all_gather | solution.py:141
  8.8 138.7 %all-gather.5.cloned.1.call-start = ((), (), s32[]{:S(2)}) async-start(), calls=%async_computation.1 | async-start | bytes 2621440 | tf_op jit(solution)/shard_map/all_gather | solution.py:154
  13.7 43.4 %collective-permute-start = (bf16[512,1792]{1,0:T(8,128)(2,1)}, bf16[512,1792]{1,0:T(8,128)(2,1)}, u32[]{:S(2)}, u32[]{:S(2)}) collective-permute-start(bf16[512,1792]{1,0:T(8,128)(2,1)} %get-tuple-element.9), channel_id=1, source_target_pairs={{0,2},{2,4},{4,6},{6,0},{1,3},{3,5},{5,7},{7,1},{8,10},{10,12},{12... | collective-permute-start | bytes 5505032 | tf_op jit(solution)/shard_map/ppermute | solution.py:150
  15.4 82.3 %collective-permute-start.1 = (bf16[512,1792]{1,0:T(8,128)(2,1)}, bf16[512,1792]{1,0:T(8,128)(2,1)}, u32[]{:S(2)}, u32[]{:S(2)}) collective-permute-start(bf16[512,1792]{1,0:T(8,128)(2,1)} %get-tuple-element.11), channel_id=1, source_target_pairs={{0,4},{2,6},{4,0},{6,2},{1,5},{3,7},{5,1},{7,3},{8,12},{10,14},{12... | collective-permute-start | bytes 5505032 | tf_op jit(solution)/shard_map/ppermute | solution.py:150
  18.3 79.4 %collective-permute-start.2 = (bf16[512,1792]{1,0:T(8,128)(2,1)S(1)}, bf16[512,1792]{1,0:T(8,128)(2,1)}, u32[]{:S(2)}, u32[]{:S(2)}) collective-permute-start(bf16[512,1792]{1,0:T(8,128)(2,1)S(1)} %get-tuple-element.10), channel_id=1, source_target_pairs={{0,6},{2,0},{4,2},{6,4},{1,7},{3,1},{5,3},{7,5},{8,14},{10,8},{12,... | collective-permute-start | bytes 5505032 | tf_op jit(solution)/shard_map/ppermute | solution.py:150
  154.6 23.8 %collective-permute-start.3 = (bf16[512,896]{1,0:T(8,128)(2,1)}, bf16[512,896]{1,0:T(8,128)(2,1)S(1)}, u32[]{:S(2)}, u32[]{:S(2)}) collective-permute-start(bf16[512,896]{1,0:T(8,128)(2,1)} %shard_map.57), channel_id=1, source_target_pairs={{0,1},{1,0},{2,3},{3,2},{4,5},{5,4},{6,7},{7,6},{8,9},{9,8},{10,11... | collective-permute-start | bytes 2752520 | tf_op jit(solution)/shard_map/ppermute | solution.py:159
Sparse Core Ops, SparseCore 0:
  9.1 94.1 all-gather.2
  114.9 32.6 all-gather.4

commit v9 on v7

--- a/solution.py
+++ b/solution.py
@@ -96,19 +96,14 @@
     )(meta, queries, *([kv_piece] * (2 * topk)))
 
 
-def project(meta, att_full, out_weight, received, halves, out_dtype):
-    rows = att_full.shape[0]
+def project(meta, pieces, out_weight, received, halves, out_dtype):
+    rows, inner = pieces[0].shape
     shifts = len(received) + 1
-    inner = att_full.shape[1] // shifts
     col_width = received[0].shape[1] // halves
-
-    def a_map(sh):
-        return lambda i, m: (0, (m[0] + shifts - sh) % shifts)
-
     grid_spec = pltpu.PrefetchScalarGridSpec(
         num_scalar_prefetch=1,
         grid=(1,),
-        in_specs=[pl.BlockSpec((rows, inner), a_map(sh)) for sh in range(shifts)]
+        in_specs=[pl.BlockSpec((rows, inner), lambda i, m: (0, 0)) for _ in range(shifts)]
         + [pl.BlockSpec((inner, col_width), lambda i, m: (0, m[0] * halves + m[1]))]
         + [pl.BlockSpec((inner, col_width), lambda i, m: (0, m[1])) for _ in received],
         out_specs=pl.BlockSpec((rows, col_width), lambda i, m: (0, 0)),
@@ -118,12 +113,12 @@
         grid_spec=grid_spec,
         out_shape=jax.ShapeDtypeStruct((rows, col_width), out_dtype),
         cost_estimate=pl.CostEstimate(
-            flops=2 * rows * att_full.shape[1] * col_width,
+            flops=2 * rows * inner * shifts * col_width,
             transcendentals=0,
-            bytes_accessed=att_full.size * 2 + shifts * inner * col_width * 2
+            bytes_accessed=rows * inner * shifts * 2 + shifts * inner * col_width * 2
             + rows * col_width * jnp.dtype(out_dtype).itemsize,
         ),
-    )(meta, *([att_full] * shifts), out_weight, *received)
+    )(meta, *pieces, out_weight, *received)
 
 
 CTX = ("xl", "z", "core")
@@ -152,13 +147,16 @@
         )
     kv_piece, received = lax.optimization_barrier((kv_piece, received))
     attended = attend(meta, queries, kv_piece, topk)
-    att_full = lax.all_gather(attended, "y", axis=1, tiled=True)
+    pieces = [attended] + [
+        lax.ppermute(attended, "y", [(i, (i + shift) % y_size) for i in range(y_size)])
+        for shift in range(1, y_size)
+    ]
     xh_place = lax.axis_index("xh")
     other = jnp.stack([y_place, xh_size - 1 - xh_place]).astype(jnp.int32)
     mine = jnp.stack([y_place, xh_place]).astype(jnp.int32)
-    sent = project(other, att_full, out_weight, received, xh_size, queries.dtype)
+    sent = project(other, pieces, out_weight, received, xh_size, queries.dtype)
     got = lax.ppermute(sent, "xh", [(i, xh_size - 1 - i) for i in range(xh_size)])
-    own = project(mine, att_full, out_weight, received, xh_size, jnp.float32)
+    own = project(mine, pieces, out_weight, received, xh_size, jnp.float32)
     return (own + got.astype(jnp.float32)).astype(queries.dtype)
 
 

time: 184 us -> 181 us (0.984)
  waiting for transfers between devices: 127 us -> 116 us
  starting transfers between devices: 8.93 us -> 14.5 us
    all_gather x1 -> x0, waiting for transfers between devices: 31.2 us -> none  [per_device(): att_full = lax.all_gather(attended, 'y', axis=1, tiled=True)]
    ppermute x0 -> x3, waiting for transfers between devices: none -> 21.2 us  [per_device(): lax.ppermute(attended, 'y', [(i, (i + shift) % y_size) for i in range(y_s...]
    ppermute x0 -> x3, starting transfers between devices: none -> 5.65 us  [per_device(): lax.ppermute(attended, 'y', [(i, (i + shift) % y_size) for i in range(y_s...]
  transfers between devices with their start and end apart: 6 -> 8, of which waited for: 5 -> 6; matrix products, arithmetic and copies ran while one was open for 4% -> 4% of each run, Pallas kernels for 4% -> 4%
where the time goes in v9:
time: 181 us
  waiting for transfers between devices  116 us (64%)
  Pallas kernels  22.5 us (12%)
  starting transfers between devices  14.5 us (8%)
  between operations  13.5 us (7%)
  local copies, waits for them, and re-layouts  6.98 us (4%)
  other arithmetic  6.8 us (4%)
    ppermute x3, waiting for transfers between devices, per_device(): lax.ppermute(sent, 'y', [(i, (i + shift) % y_size) for i in range(y_size)])  77.2 us
    ppermute x3, waiting for transfers between devices, per_device(): lax.ppermute(attended, 'y', [(i, (i + shift) % y_size) for i in range(y_s...  21.2 us
    pallas_call x2, Pallas kernels, project(): pl.pallas_call(functools.partial(project_kernel, shifts=shifts), grid_spe...  13.5 us
    ppermute x1, waiting for transfers between devices, per_device(): lax.ppermute(sent, 'xh', [(i, xh_size - 1 - i) for i in range(xh_size)])  12.7 us
    pallas_call x1, Pallas kernels, attend(): pl.pallas_call(functools.partial(attend_kernel, topk=topk, head_count=hea...  9.02 us
    ppermute x3, starting transfers between devices, per_device(): lax.ppermute(sent, 'y', [(i, (i + shift) % y_size) for i in range(y_size)])  5.91 us
    ppermute x3, starting transfers between devices, per_device(): lax.ppermute(attended, 'y', [(i, (i + shift) % y_size) for i in range(y_s...  5.65 us
    all_gather x1, waiting for transfers between devices, per_device(): lax.all_gather(jnp.concatenate([key_rows, value_rows], axis=1), CTX, axis...  5.21 us
  transfers between devices with their start and end apart: 8, of which 6 were waited for; matrix products, arithmetic and copies ran while one was open for 4% of the time, Pallas kernels for 4%

profile of v9, /device:TPU:0, one launch (start us, length us, event | category | flops | bytes accessed | tf_op | source)
XLA Modules:
  0.0 180.6 jit_solution(3290449686040531467)
XLA Ops:
  6.5 2.3 %pad_maximum_fusion = bf16[512,1024]{1,0:T(8,128)(2,1)} fusion(bf16[512,512]{1,0:T(8,128)(2,1)} %param.7, bf16[512,512]{1,0:T(8,128)(2,1)} %param.6), kind=kLoop, calls=%fused_computation.1 | loop fusion | flops 2097152 | bytes 2097152 | tf_op jit(solution)/shard_map/concatenate | solution.py:138
  8.9 5.2 %constant_dynamic-slice_fusion = (bf16[512,1792]{1,0:T(8,128)(2,1)}, bf16[512,1792]{1,0:T(8,128)(2,1)}, bf16[512,1792]{1,0:T(8,128)(2,1)}) fusion(bf16[512,7168]{1,0:T(8,128)(2,1)} %refs_4_.3, s32[]{:T(128)S(6)} %select_n.33, s32[]{:T(128)S(6)} %select_n.31, s32[]{:T(128)S(6)} %select_n.29), kind=kLoop, calls=%fused_computation.3 | loop fusion | bytes 11010060 | tf_op jit(solution)/shard_map/dynamic_slice | solution.py:144
  14.1 1.7 collective-permute-start
  15.7 2.9 %collective-permute-start.1 = (bf16[512,1792]{1,0:T(8,128)(2,1)}, bf16[512,1792]{1,0:T(8,128)(2,1)}, u32[]{:S(2)}, u32[]{:S(2)}) collective-permute-start(bf16[512,1792]{1,0:T(8,128)(2,1)} %get-tuple-element.14), channel_id=1, source_target_pairs={{0,4},{2,6},{4,0},{6,2},{1,5},{3,7},{5,1},{7,3},{8,12},{10,14},{12... | collective-permute-start | bytes 5505032 | tf_op jit(solution)/shard_map/ppermute | solution.py:146
  18.6 1.3 collective-permute-start.2
  20.2 0.6 pad_add_fusion.1.meta_ref
  20.8 36.6 %collective-permute-done.refs_5_ = bf16[512,1792]{1,0:T(8,128)(2,1)S(1)} collective-permute-done((bf16[512,1792]{1,0:T(8,128)(2,1)}, bf16[512,1792]{1,0:T(8,128)(2,1)S(1)}, u32[]{:S(2)}, u32[]{:S(2)}) %collective-permute-start) | collective-permute-done | bytes 1835040 | tf_op jit(solution)/shard_map/ppermute | solution.py:146
  57.4 40.6 %collective-permute-done.1.refs_6_ = bf16[512,1792]{1,0:T(8,128)(2,1)} collective-permute-done((bf16[512,1792]{1,0:T(8,128)(2,1)}, bf16[512,1792]{1,0:T(8,128)(2,1)}, u32[]{:S(2)}, u32[]{:S(2)}) %collective-permute-start.1) | collective-permute-done | bytes 1835040 | tf_op jit(solution)/shard_map/ppermute | solution.py:146
  98.0 5.2 %all-gather.2.cloned.1.call-done.refs_0_.refs_1_.refs_2_.refs_3_.refs_4_.refs_5_ = bf16[8192,1024]{1,0:T(8,128)(2,1)} async-done(((bf16[512,1024]{1,0:T(8,128)(2,1)}), bf16[8192,1024]{1,0:T(8,128)(2,1)}) %all-gather.2.cloned.1.call-update) | async-done | bytes 16777232 | tf_op jit(solution)/shard_map/all_gather | solution.py:137
  103.2 9.0 %shard_map.55.refs_0_ = bf16[512,512]{1,0:T(8,128)(2,1)} custom-call(s32[4]{0:T(128)} %pad_add_fusion.1.meta_ref, bf16[512,512]{1,0:T(8,128)(2,1)} %q_ref.1, bf16[8192,1024]{1,0:T(8,128)(2,1)} %all-gather.2.cloned.1.call-done.refs_0_.refs_1_.refs_2_.refs_3_.refs_4_.refs_5_, ...), custom_call_target="tpu_custom_call" | custom-call | flops 1610612736 | bytes 4194304 | tf_op jit(solution)/shard_map/pallas_call | solution.py:87
  112.2 1.5 collective-permute-start.3
  113.7 2.7 %collective-permute-start.4 = (bf16[512,512]{1,0:T(8,128)(2,1)}, bf16[512,512]{1,0:T(8,128)(2,1)S(1)}, u32[]{:S(2)}, u32[]{:S(2)}) collective-permute-start(bf16[512,512]{1,0:T(8,128)(2,1)} %shard_map.55.refs_0_), channel_id=1, source_target_pairs={{0,4},{2,6},{4,0},{6,2},{1,5},{3,7},{5,1},{7,3},{8,12},{10,14},{12... | collective-permute-start | bytes 1572872 | tf_op jit(solution)/shard_map/ppermute | solution.py:151
  116.5 1.4 collective-permute-start.5
  117.9 0.6 pad_add_fusion.2.y_ref
  118.5 9.0 %collective-permute-done.3.refs_1_ = bf16[512,512]{1,0:T(8,128)(2,1)S(1)} collective-permute-done((bf16[512,512]{1,0:T(8,128)(2,1)}, bf16[512,512]{1,0:T(8,128)(2,1)S(1)}, u32[]{:S(2)}, u32[]{:S(2)}) %collective-permute-start.3) | collective-permute-done | bytes 524320 | tf_op jit(solution)/shard_map/ppermute | solution.py:151
  127.5 12.2 %collective-permute-done.4.refs_2_ = bf16[512,512]{1,0:T(8,128)(2,1)S(1)} collective-permute-done((bf16[512,512]{1,0:T(8,128)(2,1)}, bf16[512,512]{1,0:T(8,128)(2,1)S(1)}, u32[]{:S(2)}, u32[]{:S(2)}) %collective-permute-start.4) | collective-permute-done | bytes 524320 | tf_op jit(solution)/shard_map/ppermute | solution.py:151
  139.8 0.8 copy-done.3
  140.6 0.8 copy-done.4
  141.4 6.6 %shard_map.57 = bf16[512,896]{1,0:T(8,128)(2,1)} custom-call(s32[2]{0:T(128)} %pad_add_fusion.2.y_ref, bf16[512,512]{1,0:T(8,128)(2,1)} %shard_map.55.refs_0_, bf16[512,512]{1,0:T(8,128)(2,1)} %copy-done.2, bf16[512,512]{1,0:T(8,128)(2,1)} %copy-done.3, bf16[512,512]{1,0:T(8,128)(2,1)} %copy-done.4, bf16[512,7168]{1,0:T(8,128)(2,1)} %refs_4_.3, ...), custom_call_target="tpu_custom_call" | custom-call | flops 1879048192 | bytes 6684672 | tf_op jit(solution)/shard_map/pallas_call | solution.py:111
  147.9 3.0 %collective-permute-start.6 = (bf16[512,896]{1,0:T(8,128)(2,1)}, bf16[512,896]{1,0:T(8,128)(2,1)S(1)}, u32[]{:S(2)}, u32[]{:S(2)}) collective-permute-start(bf16[512,896]{1,0:T(8,128)(2,1)} %shard_map.57), channel_id=1, source_target_pairs={{0,1},{1,0},{2,3},{3,2},{4,5},{5,4},{6,7},{7,6},{8,9},{9,8},{10,11... | collective-permute-start | bytes 2752520 | tf_op jit(solution)/shard_map/ppermute | solution.py:158
  150.9 0.6 pad_add_fusion.y_ref
  151.5 6.9 %shard_map.56 = f32[512,896]{1,0:T(8,128)} custom-call(s32[2]{0:T(128)} %pad_add_fusion.y_ref, bf16[512,512]{1,0:T(8,128)(2,1)} %shard_map.55.refs_0_, bf16[512,512]{1,0:T(8,128)(2,1)} %copy-done.2, bf16[512,512]{1,0:T(8,128)(2,1)} %copy-done.3, bf16[512,512]{1,0:T(8,128)(2,1)} %copy-done.4, bf16[512,7168]{1,0:T(8,128)(2,1)} %refs_4_.3, ...), custom_call_target="tpu_custom_call" | custom-call | flops 1879048192 | bytes 7602176 | tf_op jit(solution)/shard_map/pallas_call | solution.py:111
  158.4 12.7 %collective-permute-done.6 = bf16[512,896]{1,0:T(8,128)(2,1)S(1)} collective-permute-done((bf16[512,896]{1,0:T(8,128)(2,1)}, bf16[512,896]{1,0:T(8,128)(2,1)S(1)}, u32[]{:S(2)}, u32[]{:S(2)}) %collective-permute-start.6) | collective-permute-done | bytes 917536 | tf_op jit(solution)/shard_map/ppermute | solution.py:158
  171.1 2.6 %add_convert_fusion = bf16[512,896]{1,0:T(8,128)(2,1)} fusion(f32[512,896]{1,0:T(8,128)} %shard_map.56, bf16[512,896]{1,0:T(8,128)(2,1)S(1)} %collective-permute-done.6), kind=kLoop, calls=%fused_computation | loop fusion | flops 1376256 | bytes 3670016 | tf_op jit(solution)/shard_map/convert_element_type | solution.py:160
  (13 shorter events, 0.2 us)
Async XLA Ops:
  6.5 13.5 %copy-start = (s32[16,3]{0,1:T(4,128)S(1)}, s32[16,3]{0,1:T(4,128)}, u32[]{:S(2)}) copy-start(s32[16,3]{0,1:T(4,128)} %param.8) | copy-start | bytes 580
  6.5 96.7 %all-gather.2.cloned.1.call-start = ((), (), s32[]{:S(2)}) async-start(), calls=%async_computation | async-start | bytes 17825792 | tf_op jit(solution)/shard_map/all_gather | solution.py:137
  14.1 43.3 %collective-permute-start = (bf16[512,1792]{1,0:T(8,128)(2,1)}, bf16[512,1792]{1,0:T(8,128)(2,1)S(1)}, u32[]{:S(2)}, u32[]{:S(2)}) collective-permute-start(bf16[512,1792]{1,0:T(8,128)(2,1)} %get-tuple-element.15), channel_id=1, source_target_pairs={{0,2},{2,4},{4,6},{6,0},{1,3},{3,5},{5,7},{7,1},{8,10},{10,12},{12... | collective-permute-start | bytes 5505032 | tf_op jit(solution)/shard_map/ppermute | solution.py:146
  15.7 82.3 %collective-permute-start.1 = (bf16[512,1792]{1,0:T(8,128)(2,1)}, bf16[512,1792]{1,0:T(8,128)(2,1)}, u32[]{:S(2)}, u32[]{:S(2)}) collective-permute-start(bf16[512,1792]{1,0:T(8,128)(2,1)} %get-tuple-element.14), channel_id=1, source_target_pairs={{0,4},{2,6},{4,0},{6,2},{1,5},{3,7},{5,1},{7,3},{8,12},{10,14},{12... | collective-permute-start | bytes 5505032 | tf_op jit(solution)/shard_map/ppermute | solution.py:146
  18.6 79.4 %collective-permute-start.2 = (bf16[512,1792]{1,0:T(8,128)(2,1)}, bf16[512,1792]{1,0:T(8,128)(2,1)}, u32[]{:S(2)}, u32[]{:S(2)}) collective-permute-start(bf16[512,1792]{1,0:T(8,128)(2,1)} %get-tuple-element.13), channel_id=1, source_target_pairs={{0,6},{2,0},{4,2},{6,4},{1,7},{3,1},{5,3},{7,5},{8,14},{10,8},{12,... | collective-permute-start | bytes 5505032 | tf_op jit(solution)/shard_map/ppermute | solution.py:146
  57.4 54.8 %copy-start.1 = (bf16[512,1792]{1,0:T(8,128)(2,1)}, bf16[512,1792]{1,0:T(8,128)(2,1)S(1)}, u32[]{:S(2)}) copy-start(bf16[512,1792]{1,0:T(8,128)(2,1)S(1)} %collective-permute-done.refs_5_) | copy-start | bytes 5505028
  112.2 15.3 %collective-permute-start.3 = (bf16[512,512]{1,0:T(8,128)(2,1)}, bf16[512,512]{1,0:T(8,128)(2,1)S(1)}, u32[]{:S(2)}, u32[]{:S(2)}) collective-permute-start(bf16[512,512]{1,0:T(8,128)(2,1)} %shard_map.55.refs_0_), channel_id=1, source_target_pairs={{0,2},{2,4},{4,6},{6,0},{1,3},{3,5},{5,7},{7,1},{8,10},{10,12},{12... | collective-permute-start | bytes 1572872 | tf_op jit(solution)/shard_map/ppermute | solution.py:151
  113.7 26.0 %collective-permute-start.4 = (bf16[512,512]{1,0:T(8,128)(2,1)}, bf16[512,512]{1,0:T(8,128)(2,1)S(1)}, u32[]{:S(2)}, u32[]{:S(2)}) collective-permute-start(bf16[512,512]{1,0:T(8,128)(2,1)} %shard_map.55.refs_0_), channel_id=1, source_target_pairs={{0,4},{2,6},{4,0},{6,2},{1,5},{3,7},{5,1},{7,3},{8,12},{10,14},{12... | collective-permute-start | bytes 1572872 | tf_op jit(solution)/shard_map/ppermute | solution.py:151
  116.5 23.3 %collective-permute-start.5 = (bf16[512,512]{1,0:T(8,128)(2,1)}, bf16[512,512]{1,0:T(8,128)(2,1)S(1)}, u32[]{:S(2)}, u32[]{:S(2)}) collective-permute-start(bf16[512,512]{1,0:T(8,128)(2,1)} %shard_map.55.refs_0_), channel_id=1, source_target_pairs={{0,6},{2,0},{4,2},{6,4},{1,7},{3,1},{5,3},{7,5},{8,14},{10,8},{12,... | collective-permute-start | bytes 1572872 | tf_op jit(solution)/shard_map/ppermute | solution.py:151
  127.5 12.2 %copy-start.2 = (bf16[512,512]{1,0:T(8,128)(2,1)}, bf16[512,512]{1,0:T(8,128)(2,1)S(1)}, u32[]{:S(2)}) copy-start(bf16[512,512]{1,0:T(8,128)(2,1)S(1)} %collective-permute-done.3.refs_1_) | copy-start | bytes 1572868
  139.8 0.8 copy-start.3
  140.6 0.8 copy-start.4
  147.9 23.2 %collective-permute-start.6 = (bf16[512,896]{1,0:T(8,128)(2,1)}, bf16[512,896]{1,0:T(8,128)(2,1)S(1)}, u32[]{:S(2)}, u32[]{:S(2)}) collective-permute-start(bf16[512,896]{1,0:T(8,128)(2,1)} %shard_map.57), channel_id=1, source_target_pairs={{0,1},{1,0},{2,3},{3,2},{4,5},{5,4},{6,7},{7,6},{8,9},{9,8},{10,11... | collective-permute-start | bytes 2752520 | tf_op jit(solution)/shard_map/ppermute | solution.py:158
Sparse Core Ops, SparseCore 0:
  9.1 94.1 all-gather.1

commit v10 on v9

--- a/solution.py
+++ b/solution.py
@@ -13,46 +13,58 @@
 neg_fill = -1e30
 
 
+def own_kernel(meta_ref, q_ref, k_ref, v_ref, acc_ref, max_ref, sum_ref, *, head_count):
+    scaling = 1.0 / jnp.sqrt(jnp.float32(HD))
+    query_pos = meta_ref[0] * BLOCK + lax.broadcasted_iota(jnp.int32, (BLOCK, BLOCK), 0)
+    key_pos = meta_ref[1] * BLOCK + lax.broadcasted_iota(jnp.int32, (BLOCK, BLOCK), 1)
+    causal = key_pos <= query_pos
+    for h in range(head_count):
+        cols = slice(h * HD, (h + 1) * HD)
+        sc = lax.dot_general(
+            q_ref[:, cols], k_ref[:, cols], (((1,), (1,)), ((), ())),
+            preferred_element_type=jnp.float32,
+        ) * scaling
+        sc = jnp.where(causal, sc, neg_fill)
+        row_max = jnp.max(sc, axis=1, keepdims=True)
+        e = jnp.exp(sc - row_max)
+        max_ref[h] = row_max
+        sum_ref[h] = jnp.sum(e, axis=1, keepdims=True)
+        acc_ref[:, cols] = jnp.dot(
+            e.astype(jnp.bfloat16), v_ref[:, cols], preferred_element_type=jnp.float32
+        )
+
+
 def attend_kernel(meta_ref, q_ref, *refs, topk, head_count):
-    k_refs = refs[:topk]
-    v_refs = refs[topk : 2 * topk]
-    att_ref = refs[2 * topk]
-    if True:
-        scaling = 1.0 / jnp.sqrt(jnp.float32(HD))
-        q_block = meta_ref[topk]
-        query_pos = q_block * BLOCK + lax.broadcasted_iota(jnp.int32, (BLOCK, BLOCK), 0)
-        key_pos = meta_ref[0] * BLOCK + lax.broadcasted_iota(jnp.int32, (BLOCK, BLOCK), 1)
-        causal = key_pos <= query_pos
-        usable = [None] + [
-            (meta_ref[s] != meta_ref[0]) & (meta_ref[s] < q_block) for s in range(1, topk)
-        ]
-        for h in range(head_count):
-            cols = slice(h * HD, (h + 1) * HD)
-            q = q_ref[:, cols]
-            scores = []
-            for s in range(topk):
-                sc = lax.dot_general(
-                    q, k_refs[s][:, cols], (((1,), (1,)), ((), ())),
-                    preferred_element_type=jnp.float32,
-                ) * scaling
-                if s == 0:
-                    sc = jnp.where(causal, sc, neg_fill)
-                else:
-                    sc = jnp.where(usable[s], sc, neg_fill)
-                scores.append(sc)
-            row_max = jnp.max(scores[0], axis=1, keepdims=True)
-            for s in range(1, topk):
-                row_max = jnp.maximum(row_max, jnp.max(scores[s], axis=1, keepdims=True))
-            row_sum = jnp.zeros((BLOCK, 1), jnp.float32)
-            acc = jnp.zeros((BLOCK, HD), jnp.float32)
-            for s in range(topk):
-                e = jnp.exp(scores[s] - row_max)
-                row_sum = row_sum + jnp.sum(e, axis=1, keepdims=True)
-                acc = acc + jnp.dot(
-                    e.astype(jnp.bfloat16), v_refs[s][:, cols],
-                    preferred_element_type=jnp.float32,
-                )
-            att_ref[:, cols] = (acc / row_sum).astype(att_ref.dtype)
+    k_refs = refs[: topk - 1]
+    v_refs = refs[topk - 1 : 2 * topk - 2]
+    acc0_ref, max0_ref, sum0_ref, att_ref = refs[2 * topk - 2 :]
+    scaling = 1.0 / jnp.sqrt(jnp.float32(HD))
+    q_block = meta_ref[topk]
+    usable = [(meta_ref[s] != meta_ref[0]) & (meta_ref[s] < q_block) for s in range(1, topk)]
+    for h in range(head_count):
+        cols = slice(h * HD, (h + 1) * HD)
+        q = q_ref[:, cols]
+        scores = []
+        for s in range(topk - 1):
+            sc = lax.dot_general(
+                q, k_refs[s][:, cols], (((1,), (1,)), ((), ())),
+                preferred_element_type=jnp.float32,
+            ) * scaling
+            scores.append(jnp.where(usable[s], sc, neg_fill))
+        max0 = max0_ref[h]
+        row_max = max0
+        for sc in scores:
+            row_max = jnp.maximum(row_max, jnp.max(sc, axis=1, keepdims=True))
+        rescale = jnp.exp(max0 - row_max)
+        row_sum = sum0_ref[h] * rescale
+        acc = acc0_ref[:, cols] * rescale
+        for s in range(topk - 1):
+            e = jnp.exp(scores[s] - row_max)
+            row_sum = row_sum + jnp.sum(e, axis=1, keepdims=True)
+            acc = acc + jnp.dot(
+                e.astype(jnp.bfloat16), v_refs[s][:, cols], preferred_element_type=jnp.float32
+            )
+        att_ref[:, cols] = (acc / row_sum).astype(att_ref.dtype)
 
 
 def project_kernel(y_ref, *refs, shifts):
@@ -65,9 +77,39 @@
     o_ref[...] = acc.astype(o_ref.dtype)
 
 
-def attend(meta, queries, kv_piece, topk):
+def attend_own(meta, queries, key_rows, value_rows):
     row_count, feat_width = queries.shape
     head_count = feat_width // HD
+    full = pl.BlockSpec((row_count, feat_width), lambda j, m: (0, 0))
+    grid_spec = pltpu.PrefetchScalarGridSpec(
+        num_scalar_prefetch=1,
+        grid=(1,),
+        in_specs=[full, full, full],
+        out_specs=[
+            full,
+            pl.BlockSpec((head_count, row_count, 1), lambda j, m: (0, 0, 0)),
+            pl.BlockSpec((head_count, row_count, 1), lambda j, m: (0, 0, 0)),
+        ],
+    )
+    return pl.pallas_call(
+        functools.partial(own_kernel, head_count=head_count),
+        grid_spec=grid_spec,
+        out_shape=[
+            jax.ShapeDtypeStruct((row_count, feat_width), jnp.float32),
+            jax.ShapeDtypeStruct((head_count, row_count, 1), jnp.float32),
+            jax.ShapeDtypeStruct((head_count, row_count, 1), jnp.float32),
+        ],
+        cost_estimate=pl.CostEstimate(
+            flops=4 * head_count * BLOCK * BLOCK * HD,
+            transcendentals=head_count * BLOCK * BLOCK,
+            bytes_accessed=queries.size * 2 * 3 + queries.size * 4,
+        ),
+    )(meta, queries, key_rows, value_rows)
+
+
+def attend(meta, queries, kv_piece, own_part, topk):
+    row_count, feat_width = queries.shape
+    head_count = feat_width // HD
 
     def k_map(s):
         return lambda j, m: (m[s], 0)
@@ -76,12 +118,14 @@
         return lambda j, m: (m[s], 1)
 
     blk = (BLOCK, feat_width)
+    stat = pl.BlockSpec((head_count, row_count, 1), lambda j, m: (0, 0, 0))
     grid_spec = pltpu.PrefetchScalarGridSpec(
         num_scalar_prefetch=1,
         grid=(1,),
         in_specs=[pl.BlockSpec(blk, lambda j, m: (0, 0))]
-        + [pl.BlockSpec(blk, k_map(s)) for s in range(topk)]
-        + [pl.BlockSpec(blk, v_map(s)) for s in range(topk)],
+        + [pl.BlockSpec(blk, k_map(s)) for s in range(1, topk)]
+        + [pl.BlockSpec(blk, v_map(s)) for s in range(1, topk)]
+        + [pl.BlockSpec(blk, lambda j, m: (0, 0)), stat, stat],
         out_specs=pl.BlockSpec(blk, lambda j, m: (0, 0)),
     )
     return pl.pallas_call(
@@ -89,11 +133,11 @@
         grid_spec=grid_spec,
         out_shape=jax.ShapeDtypeStruct((row_count, feat_width), queries.dtype),
         cost_estimate=pl.CostEstimate(
-            flops=4 * head_count * BLOCK * topk * BLOCK * HD,
-            transcendentals=head_count * BLOCK * topk * BLOCK,
-            bytes_accessed=queries.size * 2 * (2 + 2 * topk),
+            flops=4 * head_count * BLOCK * (topk - 1) * BLOCK * HD,
+            transcendentals=head_count * BLOCK * (topk - 1) * BLOCK,
+            bytes_accessed=queries.size * 2 * (2 + 2 * topk) + queries.size * 4,
         ),
-    )(meta, queries, *([kv_piece] * (2 * topk)))
+    )(meta, queries, *([kv_piece] * (2 * topk - 2)), *own_part)
 
 
 def project(meta, pieces, out_weight, received, halves, out_dtype):
@@ -145,8 +189,9 @@
         received.append(
             lax.ppermute(sent, "y", [(i, (i + shift) % y_size) for i in range(y_size)])
         )
-    kv_piece, received = lax.optimization_barrier((kv_piece, received))
-    attended = attend(meta, queries, kv_piece, topk)
+    own_part = attend_own(meta[topk:topk + 1].repeat(2), queries, key_rows, value_rows)
+    kv_piece, received, own_part = lax.optimization_barrier((kv_piece, received, own_part))
+    attended = attend(meta, queries, kv_piece, own_part, topk)
     pieces = [attended] + [
         lax.ppermute(attended, "y", [(i, (i + shift) % y_size) for i in range(y_size)])
         for shift in range(1, y_size)

time: 181 us -> 184 us (1.017)
  Pallas kernels: 22.5 us -> 30.5 us
  waiting for transfers between devices: 116 us -> 111 us
    ppermute x3, waiting for transfers between devices: 77.2 us -> 71.4 us  [per_device(): lax.ppermute(sent, 'y', [(i, (i + shift) % y_size) for i in range(y_size)])]
    pallas_call x0 -> x1, Pallas kernels: none -> 5.27 us  [attend_own(): pl.pallas_call(functools.partial(own_kernel, head_count=head_count), grid...]
    pallas_call x1, Pallas kernels: 9.02 us -> 11.7 us  [attend(): pl.pallas_call(functools.partial(attend_kernel, topk=topk, head_count=hea...]
  transfers between devices with their start and end apart: 8 -> 8, of which waited for: 6 -> 6; matrix products, arithmetic and copies ran while one was open for 4% -> 4% of each run, Pallas kernels for 4% -> 7%
where the time goes in v10:
time: 184 us
  waiting for transfers between devices  111 us (60%)
  Pallas kernels  30.5 us (17%)
  starting transfers between devices  14.5 us (8%)
  between operations  13.5 us (7%)
  local copies, waits for them, and re-layouts  7.55 us (4%)
  other arithmetic  6.8 us (4%)
    ppermute x3, waiting for transfers between devices, per_device(): lax.ppermute(sent, 'y', [(i, (i + shift) % y_size) for i in range(y_size)])  71.4 us
    ppermute x3, waiting for transfers between devices, per_device(): lax.ppermute(attended, 'y', [(i, (i + shift) % y_size) for i in range(y_s...  21.4 us
    pallas_call x2, Pallas kernels, project(): pl.pallas_call(functools.partial(project_kernel, shifts=shifts), grid_spe...  13.5 us
    ppermute x1, waiting for transfers between devices, per_device(): lax.ppermute(sent, 'xh', [(i, xh_size - 1 - i) for i in range(xh_size)])  12.9 us
    pallas_call x1, Pallas kernels, attend(): pl.pallas_call(functools.partial(attend_kernel, topk=topk, head_count=hea...  11.7 us
    ppermute x3, starting transfers between devices, per_device(): lax.ppermute(sent, 'y', [(i, (i + shift) % y_size) for i in range(y_size)])  5.91 us
    ppermute x3, starting transfers between devices, per_device(): lax.ppermute(attended, 'y', [(i, (i + shift) % y_size) for i in range(y_s...  5.64 us
    pallas_call x1, Pallas kernels, attend_own(): pl.pallas_call(functools.partial(own_kernel, head_count=head_count), grid...  5.27 us
  transfers between devices with their start and end apart: 8, of which 6 were waited for; matrix products, arithmetic and copies ran while one was open for 4% of the time, Pallas kernels for 7%

profile of v10, /device:TPU:0, one launch (start us, length us, event | category | flops | bytes accessed | tf_op | source)
XLA Modules:
  0.0 183.7 jit_solution(655435359939739020)
XLA Ops:
  6.5 2.3 %pad_maximum_fusion = bf16[512,1024]{1,0:T(8,128)(2,1)} fusion(bf16[512,512]{1,0:T(8,128)(2,1)} %v_ref.1, bf16[512,512]{1,0:T(8,128)(2,1)} %k_ref.1), kind=kLoop, calls=%fused_computation.1 | loop fusion | flops 2097152 | bytes 2097152 | tf_op jit(solution)/shard_map/concatenate | solution.py:182
  8.9 5.2 %constant_dynamic-slice_fusion = (bf16[512,1792]{1,0:T(8,128)(2,1)}, bf16[512,1792]{1,0:T(8,128)(2,1)}, bf16[512,1792]{1,0:T(8,128)(2,1)}) fusion(bf16[512,7168]{1,0:T(8,128)(2,1)} %refs_4_.3, s32[]{:T(128)S(6)} %select_n.33, s32[]{:T(128)S(6)} %select_n.31, s32[]{:T(128)S(6)} %select_n.29), kind=kLoop, calls=%fused_computation.3 | loop fusion | bytes 11010060 | tf_op jit(solution)/shard_map/dynamic_slice | solution.py:188
  14.1 1.7 collective-permute-start
  15.8 2.9 %collective-permute-start.1 = (bf16[512,1792]{1,0:T(8,128)(2,1)}, bf16[512,1792]{1,0:T(8,128)(2,1)}, u32[]{:S(2)}, u32[]{:S(2)}) collective-permute-start(bf16[512,1792]{1,0:T(8,128)(2,1)} %get-tuple-element.26), channel_id=1, source_target_pairs={{0,4},{2,6},{4,0},{6,2},{1,5},{3,7},{5,1},{7,3},{8,12},{10,14},{12... | collective-permute-start | bytes 5505032 | tf_op jit(solution)/shard_map/ppermute | solution.py:190
  18.7 1.3 collective-permute-start.2
  20.8 5.3 %shard_map.55 = (f32[512,512]{1,0:T(8,128)}, f32[4,512,1]{2,1,0:T(8,128)}, f32[4,512,1]{2,1,0:T(8,128)}) custom-call(s32[2]{0:T(128)} %reshape.3.meta_ref, bf16[512,512]{1,0:T(8,128)(2,1)} %q_ref.3, bf16[512,512]{1,0:T(8,128)(2,1)} %k_ref.1, bf16[512,512]{1,0:T(8,128)(2,1)} %v_ref.1), custom_call_target="tpu_custom_call" | custom-call | flops 536870912 | bytes 2621440 | tf_op jit(solution)/shard_map/pallas_call | solution.py:94
  26.0 0.6 pad_add_fusion.1.meta_ref
  26.7 30.8 %collective-permute-done.refs_5_ = bf16[512,1792]{1,0:T(8,128)(2,1)S(1)} collective-permute-done((bf16[512,1792]{1,0:T(8,128)(2,1)}, bf16[512,1792]{1,0:T(8,128)(2,1)S(1)}, u32[]{:S(2)}, u32[]{:S(2)}) %collective-permute-start) | collective-permute-done | bytes 1835040 | tf_op jit(solution)/shard_map/ppermute | solution.py:190
  57.4 40.6 %collective-permute-done.1.refs_6_ = bf16[512,1792]{1,0:T(8,128)(2,1)} collective-permute-done((bf16[512,1792]{1,0:T(8,128)(2,1)}, bf16[512,1792]{1,0:T(8,128)(2,1)}, u32[]{:S(2)}, u32[]{:S(2)}) %collective-permute-start.1) | collective-permute-done | bytes 1835040 | tf_op jit(solution)/shard_map/ppermute | solution.py:190
  98.1 5.2 %all-gather.2.cloned.1.call-done.refs_0_.refs_1_.refs_2_.refs_3_ = bf16[8192,1024]{1,0:T(8,128)(2,1)} async-done(((bf16[512,1024]{1,0:T(8,128)(2,1)}), bf16[8192,1024]{1,0:T(8,128)(2,1)}) %all-gather.2.cloned.1.call-update) | async-done | bytes 16777232 | tf_op jit(solution)/shard_map/all_gather | solution.py:181
  103.2 11.7 %shard_map.56.refs_0_ = bf16[512,512]{1,0:T(8,128)(2,1)} custom-call(s32[4]{0:T(128)} %pad_add_fusion.1.meta_ref, bf16[512,512]{1,0:T(8,128)(2,1)} %q_ref.3, bf16[8192,1024]{1,0:T(8,128)(2,1)} %all-gather.2.cloned.1.call-done.refs_0_.refs_1_.refs_2_.refs_3_, bf16[8192,1024]{1,0:T(8,128)(2,1)} %all-gather.2.cloned.1.call-done.refs_0_.refs_1_.refs_2_.refs_3_, ...), custom_call_target="tpu_custom_call" | custom-call | flops 1073741824 | bytes 5242880 | tf_op jit(solution)/shard_map/pallas_call | solution.py:131
  114.9 1.5 collective-permute-start.3
  116.4 2.7 %collective-permute-start.4 = (bf16[512,512]{1,0:T(8,128)(2,1)}, bf16[512,512]{1,0:T(8,128)(2,1)S(1)}, u32[]{:S(2)}, u32[]{:S(2)}) collective-permute-start(bf16[512,512]{1,0:T(8,128)(2,1)} %shard_map.56.refs_0_), channel_id=1, source_target_pairs={{0,4},{2,6},{4,0},{6,2},{1,5},{3,7},{5,1},{7,3},{8,12},{10,14},{12... | collective-permute-start | bytes 1572872 | tf_op jit(solution)/shard_map/ppermute | solution.py:196
  119.2 1.4 collective-permute-start.5
  120.6 0.6 pad_add_fusion.2.y_ref
  121.2 9.2 %collective-permute-done.3.refs_1_ = bf16[512,512]{1,0:T(8,128)(2,1)S(1)} collective-permute-done((bf16[512,512]{1,0:T(8,128)(2,1)}, bf16[512,512]{1,0:T(8,128)(2,1)S(1)}, u32[]{:S(2)}, u32[]{:S(2)}) %collective-permute-start.3) | collective-permute-done | bytes 524320 | tf_op jit(solution)/shard_map/ppermute | solution.py:196
  130.5 12.2 %collective-permute-done.4.refs_2_ = bf16[512,512]{1,0:T(8,128)(2,1)S(1)} collective-permute-done((bf16[512,512]{1,0:T(8,128)(2,1)}, bf16[512,512]{1,0:T(8,128)(2,1)S(1)}, u32[]{:S(2)}, u32[]{:S(2)}) %collective-permute-start.4) | collective-permute-done | bytes 524320 | tf_op jit(solution)/shard_map/ppermute | solution.py:196
  142.7 0.8 copy-done.3
  143.5 0.8 copy-done.4
  144.3 6.6 %shard_map.58 = bf16[512,896]{1,0:T(8,128)(2,1)} custom-call(s32[2]{0:T(128)} %pad_add_fusion.2.y_ref, bf16[512,512]{1,0:T(8,128)(2,1)} %shard_map.56.refs_0_, bf16[512,512]{1,0:T(8,128)(2,1)} %copy-done.2, bf16[512,512]{1,0:T(8,128)(2,1)} %copy-done.3, bf16[512,512]{1,0:T(8,128)(2,1)} %copy-done.4, bf16[512,7168]{1,0:T(8,128)(2,1)} %refs_4_.3, ...), custom_call_target="tpu_custom_call" | custom-call | flops 1879048192 | bytes 6684672 | tf_op jit(solution)/shard_map/pallas_call | solution.py:155
  150.8 3.0 %collective-permute-start.6 = (bf16[512,896]{1,0:T(8,128)(2,1)}, bf16[512,896]{1,0:T(8,128)(2,1)S(1)}, u32[]{:S(2)}, u32[]{:S(2)}) collective-permute-start(bf16[512,896]{1,0:T(8,128)(2,1)} %shard_map.58), channel_id=1, source_target_pairs={{0,1},{1,0},{2,3},{3,2},{4,5},{5,4},{6,7},{7,6},{8,9},{9,8},{10,11... | collective-permute-start | bytes 2752520 | tf_op jit(solution)/shard_map/ppermute | solution.py:203
  154.4 6.9 %shard_map.57 = f32[512,896]{1,0:T(8,128)} custom-call(s32[2]{0:T(128)} %pad_add_fusion.y_ref, bf16[512,512]{1,0:T(8,128)(2,1)} %shard_map.56.refs_0_, bf16[512,512]{1,0:T(8,128)(2,1)} %copy-done.2, bf16[512,512]{1,0:T(8,128)(2,1)} %copy-done.3, bf16[512,512]{1,0:T(8,128)(2,1)} %copy-done.4, bf16[512,7168]{1,0:T(8,128)(2,1)} %refs_4_.3, ...), custom_call_target="tpu_custom_call" | custom-call | flops 1879048192 | bytes 7602176 | tf_op jit(solution)/shard_map/pallas_call | solution.py:155
  161.3 12.9 %collective-permute-done.6 = bf16[512,896]{1,0:T(8,128)(2,1)S(1)} collective-permute-done((bf16[512,896]{1,0:T(8,128)(2,1)}, bf16[512,896]{1,0:T(8,128)(2,1)S(1)}, u32[]{:S(2)}, u32[]{:S(2)}) %collective-permute-start.6) | collective-permute-done | bytes 917536 | tf_op jit(solution)/shard_map/ppermute | solution.py:203
  174.2 2.6 %add_convert_fusion = bf16[512,896]{1,0:T(8,128)(2,1)} fusion(f32[512,896]{1,0:T(8,128)} %shard_map.57, bf16[512,896]{1,0:T(8,128)(2,1)S(1)} %collective-permute-done.6), kind=kLoop, calls=%fused_computation | loop fusion | flops 1376256 | bytes 3670016 | tf_op jit(solution)/shard_map/convert_element_type | solution.py:205
  (15 shorter events, 1.4 us)
Async XLA Ops:
  6.5 13.5 %copy-start = (s32[16,3]{0,1:T(4,128)S(1)}, s32[16,3]{0,1:T(4,128)}, u32[]{:S(2)}) copy-start(s32[16,3]{0,1:T(4,128)} %param.8) | copy-start | bytes 580
  6.5 96.7 %all-gather.2.cloned.1.call-start = ((), (), s32[]{:S(2)}) async-start(), calls=%async_computation | async-start | bytes 17825792 | tf_op jit(solution)/shard_map/all_gather | solution.py:181
  14.1 43.3 %collective-permute-start = (bf16[512,1792]{1,0:T(8,128)(2,1)}, bf16[512,1792]{1,0:T(8,128)(2,1)S(1)}, u32[]{:S(2)}, u32[]{:S(2)}) collective-permute-start(bf16[512,1792]{1,0:T(8,128)(2,1)} %get-tuple-element.27), channel_id=1, source_target_pairs={{0,2},{2,4},{4,6},{6,0},{1,3},{3,5},{5,7},{7,1},{8,10},{10,12},{12... | collective-permute-start | bytes 5505032 | tf_op jit(solution)/shard_map/ppermute | solution.py:190
  15.8 82.3 %collective-permute-start.1 = (bf16[512,1792]{1,0:T(8,128)(2,1)}, bf16[512,1792]{1,0:T(8,128)(2,1)}, u32[]{:S(2)}, u32[]{:S(2)}) collective-permute-start(bf16[512,1792]{1,0:T(8,128)(2,1)} %get-tuple-element.26), channel_id=1, source_target_pairs={{0,4},{2,6},{4,0},{6,2},{1,5},{3,7},{5,1},{7,3},{8,12},{10,14},{12... | collective-permute-start | bytes 5505032 | tf_op jit(solution)/shard_map/ppermute | solution.py:190
  18.7 79.4 %collective-permute-start.2 = (bf16[512,1792]{1,0:T(8,128)(2,1)}, bf16[512,1792]{1,0:T(8,128)(2,1)}, u32[]{:S(2)}, u32[]{:S(2)}) collective-permute-start(bf16[512,1792]{1,0:T(8,128)(2,1)} %get-tuple-element.25), channel_id=1, source_target_pairs={{0,6},{2,0},{4,2},{6,4},{1,7},{3,1},{5,3},{7,5},{8,14},{10,8},{12,... | collective-permute-start | bytes 5505032 | tf_op jit(solution)/shard_map/ppermute | solution.py:190
  57.4 57.5 %copy-start.1 = (bf16[512,1792]{1,0:T(8,128)(2,1)}, bf16[512,1792]{1,0:T(8,128)(2,1)S(1)}, u32[]{:S(2)}) copy-start(bf16[512,1792]{1,0:T(8,128)(2,1)S(1)} %collective-permute-done.refs_5_) | copy-start | bytes 5505028
  114.9 15.5 %collective-permute-start.3 = (bf16[512,512]{1,0:T(8,128)(2,1)}, bf16[512,512]{1,0:T(8,128)(2,1)S(1)}, u32[]{:S(2)}, u32[]{:S(2)}) collective-permute-start(bf16[512,512]{1,0:T(8,128)(2,1)} %shard_map.56.refs_0_), channel_id=1, source_target_pairs={{0,2},{2,4},{4,6},{6,0},{1,3},{3,5},{5,7},{7,1},{8,10},{10,12},{12... | collective-permute-start | bytes 1572872 | tf_op jit(solution)/shard_map/ppermute | solution.py:196
  116.4 26.2 %collective-permute-start.4 = (bf16[512,512]{1,0:T(8,128)(2,1)}, bf16[512,512]{1,0:T(8,128)(2,1)S(1)}, u32[]{:S(2)}, u32[]{:S(2)}) collective-permute-start(bf16[512,512]{1,0:T(8,128)(2,1)} %shard_map.56.refs_0_), channel_id=1, source_target_pairs={{0,4},{2,6},{4,0},{6,2},{1,5},{3,7},{5,1},{7,3},{8,12},{10,14},{12... | collective-permute-start | bytes 1572872 | tf_op jit(solution)/shard_map/ppermute | solution.py:196
  119.2 23.5 %collective-permute-start.5 = (bf16[512,512]{1,0:T(8,128)(2,1)}, bf16[512,512]{1,0:T(8,128)(2,1)S(1)}, u32[]{:S(2)}, u32[]{:S(2)}) collective-permute-start(bf16[512,512]{1,0:T(8,128)(2,1)} %shard_map.56.refs_0_), channel_id=1, source_target_pairs={{0,6},{2,0},{4,2},{6,4},{1,7},{3,1},{5,3},{7,5},{8,14},{10,8},{12,... | collective-permute-start | bytes 1572872 | tf_op jit(solution)/shard_map/ppermute | solution.py:196
  130.5 12.2 %copy-start.2 = (bf16[512,512]{1,0:T(8,128)(2,1)}, bf16[512,512]{1,0:T(8,128)(2,1)S(1)}, u32[]{:S(2)}) copy-start(bf16[512,512]{1,0:T(8,128)(2,1)S(1)} %collective-permute-done.3.refs_1_) | copy-start | bytes 1572868
  142.7 0.8 copy-start.3
  143.5 0.8 copy-start.4
  150.8 23.4 %collective-permute-start.6 = (bf16[512,896]{1,0:T(8,128)(2,1)}, bf16[512,896]{1,0:T(8,128)(2,1)S(1)}, u32[]{:S(2)}, u32[]{:S(2)}) collective-permute-start(bf16[512,896]{1,0:T(8,128)(2,1)} %shard_map.58), channel_id=1, source_target_pairs={{0,1},{1,0},{2,3},{3,2},{4,5},{5,4},{6,7},{7,6},{8,9},{9,8},{10,11... | collective-permute-start | bytes 2752520 | tf_op jit(solution)/shard_map/ppermute | solution.py:203
Sparse Core Ops, SparseCore 0:
  9.1 94.1 all-gather.1

commit v11 on v9

--- a/solution.py
+++ b/solution.py
@@ -155,9 +155,11 @@
     other = jnp.stack([y_place, xh_size - 1 - xh_place]).astype(jnp.int32)
     mine = jnp.stack([y_place, xh_place]).astype(jnp.int32)
     sent = project(other, pieces, out_weight, received, xh_size, queries.dtype)
-    got = lax.ppermute(sent, "xh", [(i, xh_size - 1 - i) for i in range(xh_size)])
+    swap = [(i, xh_size - 1 - i) for i in range(xh_size)]
+    split = row_count // 2
+    got = [lax.ppermute(sent[:split], "xh", swap), lax.ppermute(sent[split:], "xh", swap)]
     own = project(mine, pieces, out_weight, received, xh_size, jnp.float32)
-    return (own + got.astype(jnp.float32)).astype(queries.dtype)
+    return (own + jnp.concatenate(got).astype(jnp.float32)).astype(queries.dtype)
 
 
 def solution(mesh):

time: 181 us -> 182 us (level)
    ppermute x1 -> x2, waiting for transfers between devices: 12.7 us -> 11.9 us  [the longest x1 8 us: per_device(): lax.ppermute(sent[split:], 'xh', swap)]
  transfers between devices with their start and end apart: 8 -> 9, of which waited for: 6 -> 7; matrix products, arithmetic and copies ran while one was open for 4% -> 4% of each run, Pallas kernels for 4% -> 4%
where the time goes in v11:
time: 182 us
  waiting for transfers between devices  115 us (63%)
  Pallas kernels  22.6 us (12%)
  starting transfers between devices  15.2 us (8%)
  between operations  13.5 us (7%)
  local copies, waits for them, and re-layouts  8.23 us (5%)
  other arithmetic  6.76 us (4%)
    ppermute x3, waiting for transfers between devices, per_device(): lax.ppermute(sent, 'y', [(i, (i + shift) % y_size) for i in range(y_size)])  77.2 us
    ppermute x3, waiting for transfers between devices, per_device(): lax.ppermute(attended, 'y', [(i, (i + shift) % y_size) for i in range(y_s...  21.3 us
    pallas_call x2, Pallas kernels, project(): pl.pallas_call(functools.partial(project_kernel, shifts=shifts), grid_spe...  13.5 us
    pallas_call x1, Pallas kernels, attend(): pl.pallas_call(functools.partial(attend_kernel, topk=topk, head_count=hea...  9.03 us
    ppermute x1, waiting for transfers between devices, per_device(): lax.ppermute(sent[split:], 'xh', swap)  8 us
    ppermute x3, starting transfers between devices, per_device(): lax.ppermute(sent, 'y', [(i, (i + shift) % y_size) for i in range(y_size)])  5.91 us
    ppermute x3, starting transfers between devices, per_device(): lax.ppermute(attended, 'y', [(i, (i + shift) % y_size) for i in range(y_s...  5.65 us
    dynamic_slice x1, local copies, waits for them, and re-layouts, per_device(): lax.dynamic_slice_in_dim(out_weight, dest * group_width, group_width, 1)  5.22 us
  transfers between devices with their start and end apart: 9, of which 7 were waited for; matrix products, arithmetic and copies ran while one was open for 4% of the time, Pallas kernels for 4%

profile of v11, /device:TPU:0, one launch (start us, length us, event | category | flops | bytes accessed | tf_op | source)
XLA Modules:
  0.0 181.7 jit_solution(13359859195183182810)
XLA Ops:
  6.5 2.3 %pad_maximum_fusion = bf16[512,1024]{1,0:T(8,128)(2,1)} fusion(bf16[512,512]{1,0:T(8,128)(2,1)} %param.7, bf16[512,512]{1,0:T(8,128)(2,1)} %param.6), kind=kLoop, calls=%fused_computation.1 | loop fusion | flops 2097152 | bytes 2097152 | tf_op jit(solution)/shard_map/concatenate | solution.py:138
  8.9 5.2 %constant_dynamic-slice_fusion = (bf16[512,1792]{1,0:T(8,128)(2,1)}, bf16[512,1792]{1,0:T(8,128)(2,1)}, bf16[512,1792]{1,0:T(8,128)(2,1)}) fusion(bf16[512,7168]{1,0:T(8,128)(2,1)} %refs_4_.3, s32[]{:T(128)S(6)} %select_n.33, s32[]{:T(128)S(6)} %select_n.31, s32[]{:T(128)S(6)} %select_n.29), kind=kLoop, calls=%fused_computation.3 | loop fusion | bytes 11010060 | tf_op jit(solution)/shard_map/dynamic_slice | solution.py:144
  14.1 1.7 collective-permute-start
  15.8 2.9 %collective-permute-start.1 = (bf16[512,1792]{1,0:T(8,128)(2,1)}, bf16[512,1792]{1,0:T(8,128)(2,1)}, u32[]{:S(2)}, u32[]{:S(2)}) collective-permute-start(bf16[512,1792]{1,0:T(8,128)(2,1)} %get-tuple-element.14), channel_id=1, source_target_pairs={{0,4},{2,6},{4,0},{6,2},{1,5},{3,7},{5,1},{7,3},{8,12},{10,14},{12... | collective-permute-start | bytes 5505032 | tf_op jit(solution)/shard_map/ppermute | solution.py:146
  18.7 1.3 collective-permute-start.2
  20.2 0.7 pad_add_fusion.1.meta_ref
  20.9 36.6 %collective-permute-done.refs_5_ = bf16[512,1792]{1,0:T(8,128)(2,1)S(1)} collective-permute-done((bf16[512,1792]{1,0:T(8,128)(2,1)}, bf16[512,1792]{1,0:T(8,128)(2,1)S(1)}, u32[]{:S(2)}, u32[]{:S(2)}) %collective-permute-start) | collective-permute-done | bytes 1835040 | tf_op jit(solution)/shard_map/ppermute | solution.py:146
  57.4 40.6 %collective-permute-done.1.refs_6_ = bf16[512,1792]{1,0:T(8,128)(2,1)} collective-permute-done((bf16[512,1792]{1,0:T(8,128)(2,1)}, bf16[512,1792]{1,0:T(8,128)(2,1)}, u32[]{:S(2)}, u32[]{:S(2)}) %collective-permute-start.1) | collective-permute-done | bytes 1835040 | tf_op jit(solution)/shard_map/ppermute | solution.py:146
  98.0 5.2 %all-gather.2.cloned.1.call-done.refs_0_.refs_1_.refs_2_.refs_3_.refs_4_.refs_5_ = bf16[8192,1024]{1,0:T(8,128)(2,1)} async-done(((bf16[512,1024]{1,0:T(8,128)(2,1)}), bf16[8192,1024]{1,0:T(8,128)(2,1)}) %all-gather.2.cloned.1.call-update) | async-done | bytes 16777232 | tf_op jit(solution)/shard_map/all_gather | solution.py:137
  103.2 9.0 %shard_map.55.refs_0_ = bf16[512,512]{1,0:T(8,128)(2,1)} custom-call(s32[4]{0:T(128)} %pad_add_fusion.1.meta_ref, bf16[512,512]{1,0:T(8,128)(2,1)} %q_ref.1, bf16[8192,1024]{1,0:T(8,128)(2,1)} %all-gather.2.cloned.1.call-done.refs_0_.refs_1_.refs_2_.refs_3_.refs_4_.refs_5_, ...), custom_call_target="tpu_custom_call" | custom-call | flops 1610612736 | bytes 4194304 | tf_op jit(solution)/shard_map/pallas_call | solution.py:87
  112.3 1.5 collective-permute-start.3
  113.7 2.7 %collective-permute-start.4 = (bf16[512,512]{1,0:T(8,128)(2,1)}, bf16[512,512]{1,0:T(8,128)(2,1)S(1)}, u32[]{:S(2)}, u32[]{:S(2)}) collective-permute-start(bf16[512,512]{1,0:T(8,128)(2,1)} %shard_map.55.refs_0_), channel_id=1, source_target_pairs={{0,4},{2,6},{4,0},{6,2},{1,5},{3,7},{5,1},{7,3},{8,12},{10,14},{12... | collective-permute-start | bytes 1572872 | tf_op jit(solution)/shard_map/ppermute | solution.py:151
  116.5 1.4 collective-permute-start.5
  118.5 9.0 %collective-permute-done.3.refs_1_ = bf16[512,512]{1,0:T(8,128)(2,1)S(1)} collective-permute-done((bf16[512,512]{1,0:T(8,128)(2,1)}, bf16[512,512]{1,0:T(8,128)(2,1)S(1)}, u32[]{:S(2)}, u32[]{:S(2)}) %collective-permute-start.3) | collective-permute-done | bytes 524320 | tf_op jit(solution)/shard_map/ppermute | solution.py:151
  127.6 12.2 %collective-permute-done.4.refs_2_ = bf16[512,512]{1,0:T(8,128)(2,1)S(1)} collective-permute-done((bf16[512,512]{1,0:T(8,128)(2,1)}, bf16[512,512]{1,0:T(8,128)(2,1)S(1)}, u32[]{:S(2)}, u32[]{:S(2)}) %collective-permute-start.4) | collective-permute-done | bytes 524320 | tf_op jit(solution)/shard_map/ppermute | solution.py:151
  139.8 0.8 copy-done.3
  140.6 0.8 copy-done.4
  141.4 6.6 %shard_map.57 = bf16[512,896]{1,0:T(8,128)(2,1)} custom-call(s32[2]{0:T(128)} %pad_add_fusion.2.y_ref, bf16[512,512]{1,0:T(8,128)(2,1)} %shard_map.55.refs_0_, bf16[512,512]{1,0:T(8,128)(2,1)} %copy-done.2, bf16[512,512]{1,0:T(8,128)(2,1)} %copy-done.3, bf16[512,512]{1,0:T(8,128)(2,1)} %copy-done.4, bf16[512,7168]{1,0:T(8,128)(2,1)} %refs_4_.3, ...), custom_call_target="tpu_custom_call" | custom-call | flops 1879048192 | bytes 6684672 | tf_op jit(solution)/shard_map/pallas_call | solution.py:111
  147.9 1.2 fusion
  149.2 3.1 %collective-permute-start.6 = (bf16[256,896]{1,0:T(8,128)(2,1)S(1)}, bf16[256,896]{1,0:T(8,128)(2,1)S(1)}, u32[]{:S(2)}, u32[]{:S(2)}) collective-permute-start(bf16[256,896]{1,0:T(8,128)(2,1)S(1)} %get-tuple-element.16), channel_id=1, source_target_pairs={{0,1},{1,0},{2,3},{3,2},{4,5},{5,4},{6,7},{7,6},{8,9},{9,8},{10,11... | collective-permute-start | bytes 1376264 | tf_op jit(solution)/shard_map/ppermute | solution.py:160
  153.4 7.0 %shard_map.56 = f32[512,896]{1,0:T(8,128)} custom-call(s32[2]{0:T(128)} %pad_add_fusion.y_ref, bf16[512,512]{1,0:T(8,128)(2,1)} %shard_map.55.refs_0_, bf16[512,512]{1,0:T(8,128)(2,1)} %copy-done.2, bf16[512,512]{1,0:T(8,128)(2,1)} %copy-done.3, bf16[512,512]{1,0:T(8,128)(2,1)} %copy-done.4, bf16[512,7168]{1,0:T(8,128)(2,1)} %refs_4_.3, ...), custom_call_target="tpu_custom_call" | custom-call | flops 1879048192 | bytes 7602176 | tf_op jit(solution)/shard_map/pallas_call | solution.py:111
  160.3 3.9 %collective-permute-done.6 = bf16[256,896]{1,0:T(8,128)(2,1)S(1)} collective-permute-done((bf16[256,896]{1,0:T(8,128)(2,1)S(1)}, bf16[256,896]{1,0:T(8,128)(2,1)S(1)}, u32[]{:S(2)}, u32[]{:S(2)}) %collective-permute-start.6) | collective-permute-done | bytes 458784 | tf_op jit(solution)/shard_map/ppermute | solution.py:160
  164.2 8.0 %collective-permute-done.7 = bf16[256,896]{1,0:T(8,128)(2,1)S(1)} collective-permute-done((bf16[256,896]{1,0:T(8,128)(2,1)S(1)}, bf16[256,896]{1,0:T(8,128)(2,1)S(1)}, u32[]{:S(2)}, u32[]{:S(2)}) %collective-permute-start.7) | collective-permute-done | bytes 458784 | tf_op jit(solution)/shard_map/ppermute | solution.py:160
  172.2 2.6 %add_convert_fusion = bf16[512,896]{1,0:T(8,128)(2,1)} fusion(f32[512,896]{1,0:T(8,128)} %shard_map.56, bf16[256,896]{1,0:T(8,128)(2,1)S(1)} %collective-permute-done.7, bf16[256,896]{1,0:T(8,128)(2,1)S(1)} %collective-permute-done.6), kind=kLoop, calls=%fused_computation | loop fusion | flops 2752512 | bytes 3670016 | tf_op jit(solution)/shard_map/convert_element_type | solution.py:162
  (16 shorter events, 1.9 us)
Async XLA Ops:
  6.5 13.5 %copy-start = (s32[16,3]{0,1:T(4,128)S(1)}, s32[16,3]{0,1:T(4,128)}, u32[]{:S(2)}) copy-start(s32[16,3]{0,1:T(4,128)} %param.8) | copy-start | bytes 580
  6.5 96.7 %all-gather.2.cloned.1.call-start = ((), (), s32[]{:S(2)}) async-start(), calls=%async_computation | async-start | bytes 17825792 | tf_op jit(solution)/shard_map/all_gather | solution.py:137
  14.1 43.3 %collective-permute-start = (bf16[512,1792]{1,0:T(8,128)(2,1)}, bf16[512,1792]{1,0:T(8,128)(2,1)S(1)}, u32[]{:S(2)}, u32[]{:S(2)}) collective-permute-start(bf16[512,1792]{1,0:T(8,128)(2,1)} %get-tuple-element.15), channel_id=1, source_target_pairs={{0,2},{2,4},{4,6},{6,0},{1,3},{3,5},{5,7},{7,1},{8,10},{10,12},{12... | collective-permute-start | bytes 5505032 | tf_op jit(solution)/shard_map/ppermute | solution.py:146
  15.8 82.3 %collective-permute-start.1 = (bf16[512,1792]{1,0:T(8,128)(2,1)}, bf16[512,1792]{1,0:T(8,128)(2,1)}, u32[]{:S(2)}, u32[]{:S(2)}) collective-permute-start(bf16[512,1792]{1,0:T(8,128)(2,1)} %get-tuple-element.14), channel_id=1, source_target_pairs={{0,4},{2,6},{4,0},{6,2},{1,5},{3,7},{5,1},{7,3},{8,12},{10,14},{12... | collective-permute-start | bytes 5505032 | tf_op jit(solution)/shard_map/ppermute | solution.py:146
  18.7 79.4 %collective-permute-start.2 = (bf16[512,1792]{1,0:T(8,128)(2,1)}, bf16[512,1792]{1,0:T(8,128)(2,1)}, u32[]{:S(2)}, u32[]{:S(2)}) collective-permute-start(bf16[512,1792]{1,0:T(8,128)(2,1)} %get-tuple-element.13), channel_id=1, source_target_pairs={{0,6},{2,0},{4,2},{6,4},{1,7},{3,1},{5,3},{7,5},{8,14},{10,8},{12,... | collective-permute-start | bytes 5505032 | tf_op jit(solution)/shard_map/ppermute | solution.py:146
  57.4 54.8 %copy-start.1 = (bf16[512,1792]{1,0:T(8,128)(2,1)}, bf16[512,1792]{1,0:T(8,128)(2,1)S(1)}, u32[]{:S(2)}) copy-start(bf16[512,1792]{1,0:T(8,128)(2,1)S(1)} %collective-permute-done.refs_5_) | copy-start | bytes 5505028
  112.3 15.3 %collective-permute-start.3 = (bf16[512,512]{1,0:T(8,128)(2,1)}, bf16[512,512]{1,0:T(8,128)(2,1)S(1)}, u32[]{:S(2)}, u32[]{:S(2)}) collective-permute-start(bf16[512,512]{1,0:T(8,128)(2,1)} %shard_map.55.refs_0_), channel_id=1, source_target_pairs={{0,2},{2,4},{4,6},{6,0},{1,3},{3,5},{5,7},{7,1},{8,10},{10,12},{12... | collective-permute-start | bytes 1572872 | tf_op jit(solution)/shard_map/ppermute | solution.py:151
  113.7 26.0 %collective-permute-start.4 = (bf16[512,512]{1,0:T(8,128)(2,1)}, bf16[512,512]{1,0:T(8,128)(2,1)S(1)}, u32[]{:S(2)}, u32[]{:S(2)}) collective-permute-start(bf16[512,512]{1,0:T(8,128)(2,1)} %shard_map.55.refs_0_), channel_id=1, source_target_pairs={{0,4},{2,6},{4,0},{6,2},{1,5},{3,7},{5,1},{7,3},{8,12},{10,14},{12... | collective-permute-start | bytes 1572872 | tf_op jit(solution)/shard_map/ppermute | solution.py:151
  116.5 23.3 %collective-permute-start.5 = (bf16[512,512]{1,0:T(8,128)(2,1)}, bf16[512,512]{1,0:T(8,128)(2,1)S(1)}, u32[]{:S(2)}, u32[]{:S(2)}) collective-permute-start(bf16[512,512]{1,0:T(8,128)(2,1)} %shard_map.55.refs_0_), channel_id=1, source_target_pairs={{0,6},{2,0},{4,2},{6,4},{1,7},{3,1},{5,3},{7,5},{8,14},{10,8},{12,... | collective-permute-start | bytes 1572872 | tf_op jit(solution)/shard_map/ppermute | solution.py:151
  127.6 12.2 %copy-start.2 = (bf16[512,512]{1,0:T(8,128)(2,1)}, bf16[512,512]{1,0:T(8,128)(2,1)S(1)}, u32[]{:S(2)}) copy-start(bf16[512,512]{1,0:T(8,128)(2,1)S(1)} %collective-permute-done.3.refs_1_) | copy-start | bytes 1572868
  139.8 0.8 copy-start.3
  140.6 0.8 copy-start.4
  149.2 15.0 %collective-permute-start.6 = (bf16[256,896]{1,0:T(8,128)(2,1)S(1)}, bf16[256,896]{1,0:T(8,128)(2,1)S(1)}, u32[]{:S(2)}, u32[]{:S(2)}) collective-permute-start(bf16[256,896]{1,0:T(8,128)(2,1)S(1)} %get-tuple-element.16), channel_id=1, source_target_pairs={{0,1},{1,0},{2,3},{3,2},{4,5},{5,4},{6,7},{7,6},{8,9},{9,8},{10,11... | collective-permute-start | bytes 1376264 | tf_op jit(solution)/shard_map/ppermute | solution.py:160
  152.3 19.9 %collective-permute-start.7 = (bf16[256,896]{1,0:T(8,128)(2,1)S(1)}, bf16[256,896]{1,0:T(8,128)(2,1)S(1)}, u32[]{:S(2)}, u32[]{:S(2)}) collective-permute-start(bf16[256,896]{1,0:T(8,128)(2,1)S(1)} %get-tuple-element.17), channel_id=1, source_target_pairs={{0,1},{1,0},{2,3},{3,2},{4,5},{5,4},{6,7},{7,6},{8,9},{9,8},{10,11... | collective-permute-start | bytes 1376264 | tf_op jit(solution)/shard_map/ppermute | solution.py:160
Sparse Core Ops, SparseCore 0:
  9.1 94.1 all-gather.1

commit v12 on v9

--- a/solution.py
+++ b/solution.py
@@ -121,6 +121,49 @@
     )(meta, *pieces, out_weight, *received)
 
 
+def join_kernel(k_hbm, v_hbm, o_hbm, sems):
+    width = k_hbm.shape[1]
+    first = pltpu.make_async_copy(k_hbm, o_hbm.at[:, pl.ds(0, width)], sems.at[0])
+    second = pltpu.make_async_copy(v_hbm, o_hbm.at[:, pl.ds(width, width)], sems.at[1])
+    first.start()
+    second.start()
+    first.wait()
+    second.wait()
+
+
+def join(key_rows, value_rows):
+    rows, width = key_rows.shape
+    return pl.pallas_call(
+        join_kernel,
+        in_specs=[pl.BlockSpec(memory_space=pl.ANY), pl.BlockSpec(memory_space=pl.ANY)],
+        out_specs=pl.BlockSpec(memory_space=pl.ANY),
+        out_shape=jax.ShapeDtypeStruct((rows, 2 * width), key_rows.dtype),
+        scratch_shapes=[pltpu.SemaphoreType.DMA((2,))],
+        cost_estimate=pl.CostEstimate(
+            flops=0, transcendentals=0, bytes_accessed=4 * key_rows.size * key_rows.dtype.itemsize
+        ),
+    )(key_rows, value_rows)
+
+
+def finish_kernel(own_ref, got_ref, o_ref):
+    o_ref[...] = (own_ref[...] + got_ref[...].astype(jnp.float32)).astype(o_ref.dtype)
+
+
+def finish(own, got, chunks=4):
+    rows, width = own.shape
+    blk = pl.BlockSpec((rows // chunks, width), lambda i: (i, 0))
+    return pl.pallas_call(
+        finish_kernel,
+        grid=(chunks,),
+        in_specs=[blk, blk],
+        out_specs=blk,
+        out_shape=jax.ShapeDtypeStruct((rows, width), got.dtype),
+        cost_estimate=pl.CostEstimate(
+            flops=own.size, transcendentals=0, bytes_accessed=own.size * 4 + got.size * 4
+        ),
+    )(own, got)
+
+
 CTX = ("xl", "z", "core")
 TP = ("y", "xh")
 
@@ -135,7 +178,7 @@
     own_choice = lax.dynamic_slice_in_dim(selection, ctx_place, 1, 0)[0]
     meta = jnp.concatenate([own_choice, ctx_place.astype(jnp.int32)[None]])
     kv_piece = lax.all_gather(
-        jnp.concatenate([key_rows, value_rows], axis=1), CTX, axis=0, tiled=True
+        join(key_rows, value_rows), CTX, axis=0, tiled=True
     )
     group_width = out_weight.shape[1] // y_size
     received = []
@@ -157,7 +200,7 @@
     sent = project(other, pieces, out_weight, received, xh_size, queries.dtype)
     got = lax.ppermute(sent, "xh", [(i, xh_size - 1 - i) for i in range(xh_size)])
     own = project(mine, pieces, out_weight, received, xh_size, jnp.float32)
-    return (own + got.astype(jnp.float32)).astype(queries.dtype)
+    return finish(own, got)
 
 
 def solution(mesh):

time: 181 us -> 213 us (1.18)
  Pallas kernels: 22.5 us -> 59.1 us
  other arithmetic: 6.8 us -> 1.81 us
    pallas_call x0 -> x2, Pallas kernels: none -> 36.5 us  [the longest x1 32.9 us: join(): pl.pallas_call(join_kernel, in_specs=[pl.BlockSpec(memory_space=pl.ANY),...]
    convert_element_type x1 -> x0, other arithmetic: 2.64 us -> none  [per_device(): return (own + got.astype(jnp.float32)).astype(queries.dtype)]
    concatenate x1 -> x0, other arithmetic: 2.28 us -> none  [per_device(): jnp.concatenate([key_rows, value_rows], axis=1)]
  transfers between devices with their start and end apart: 8 -> 8, of which waited for: 6 -> 6; matrix products, arithmetic and copies ran while one was open for 4% -> 3% of each run, Pallas kernels for 4% -> 3%
where the time goes in v12:
time: 213 us
  waiting for transfers between devices  116 us (54%)
  Pallas kernels  59.1 us (28%)
  starting transfers between devices  14.5 us (7%)
  between operations  13.5 us (6%)
  local copies, waits for them, and re-layouts  7.94 us (4%)
    ppermute x3, waiting for transfers between devices, per_device(): lax.ppermute(sent, 'y', [(i, (i + shift) % y_size) for i in range(y_size)])  77.3 us
    pallas_call x1, Pallas kernels, join(): pl.pallas_call(join_kernel, in_specs=[pl.BlockSpec(memory_space=pl.ANY),...  32.9 us
    ppermute x3, waiting for transfers between devices, per_device(): lax.ppermute(attended, 'y', [(i, (i + shift) % y_size) for i in range(y_s...  21.2 us
    pallas_call x2, Pallas kernels, project(): pl.pallas_call(functools.partial(project_kernel, shifts=shifts), grid_spe...  13.5 us
    ppermute x1, waiting for transfers between devices, per_device(): lax.ppermute(sent, 'xh', [(i, xh_size - 1 - i) for i in range(xh_size)])  12.6 us
    pallas_call x1, Pallas kernels, attend(): pl.pallas_call(functools.partial(attend_kernel, topk=topk, head_count=hea...  9.07 us
    ppermute x3, starting transfers between devices, per_device(): lax.ppermute(sent, 'y', [(i, (i + shift) % y_size) for i in range(y_size)])  5.91 us
    ppermute x3, starting transfers between devices, per_device(): lax.ppermute(attended, 'y', [(i, (i + shift) % y_size) for i in range(y_s...  5.65 us
  transfers between devices with their start and end apart: 8, of which 6 were waited for; matrix products, arithmetic and copies ran while one was open for 3% of the time, Pallas kernels for 3%

profile of v12, /device:TPU:0, one launch (start us, length us, event | category | flops | bytes accessed | tf_op | source)
XLA Modules:
  0.0 213.0 jit_solution(14611517339637174697)
XLA Ops:
  6.5 32.9 %shard_map.55 = bf16[512,1024]{1,0:T(8,128)(2,1)} custom-call(bf16[512,512]{1,0:T(8,128)(2,1)} %k_hbm.1, bf16[512,512]{1,0:T(8,128)(2,1)} %v_hbm.1), custom_call_target="tpu_custom_call" | custom-call | bytes 2097152 | tf_op jit(solution)/shard_map/pallas_call | solution.py:136
  39.5 5.2 %constant_dynamic-slice_fusion = (bf16[512,1792]{1,0:T(8,128)(2,1)}, bf16[512,1792]{1,0:T(8,128)(2,1)}, bf16[512,1792]{1,0:T(8,128)(2,1)}) fusion(bf16[512,7168]{1,0:T(8,128)(2,1)} %refs_4_.3, s32[]{:T(128)S(6)} %select_n.33, s32[]{:T(128)S(6)} %select_n.31, s32[]{:T(128)S(6)} %select_n.29), kind=kLoop, calls=%fused_computation.1 | loop fusion | bytes 11010060 | tf_op jit(solution)/shard_map/dynamic_slice | solution.py:187
  44.7 1.7 collective-permute-start
  46.4 2.9 %collective-permute-start.1 = (bf16[512,1792]{1,0:T(8,128)(2,1)}, bf16[512,1792]{1,0:T(8,128)(2,1)}, u32[]{:S(2)}, u32[]{:S(2)}) collective-permute-start(bf16[512,1792]{1,0:T(8,128)(2,1)} %get-tuple-element.14), channel_id=1, source_target_pairs={{0,4},{2,6},{4,0},{6,2},{1,5},{3,7},{5,1},{7,3},{8,12},{10,14},{12... | collective-permute-start | bytes 5505032 | tf_op jit(solution)/shard_map/ppermute | solution.py:189
  49.3 1.3 collective-permute-start.2
  51.4 36.7 %collective-permute-done.refs_5_ = bf16[512,1792]{1,0:T(8,128)(2,1)S(1)} collective-permute-done((bf16[512,1792]{1,0:T(8,128)(2,1)}, bf16[512,1792]{1,0:T(8,128)(2,1)S(1)}, u32[]{:S(2)}, u32[]{:S(2)}) %collective-permute-start) | collective-permute-done | bytes 1835040 | tf_op jit(solution)/shard_map/ppermute | solution.py:189
  88.0 40.6 %collective-permute-done.1.refs_6_ = bf16[512,1792]{1,0:T(8,128)(2,1)} collective-permute-done((bf16[512,1792]{1,0:T(8,128)(2,1)}, bf16[512,1792]{1,0:T(8,128)(2,1)}, u32[]{:S(2)}, u32[]{:S(2)}) %collective-permute-start.1) | collective-permute-done | bytes 1835040 | tf_op jit(solution)/shard_map/ppermute | solution.py:189
  128.7 5.1 %all-gather.2.cloned.1.call-done.refs_0_.refs_1_.refs_2_.refs_3_.refs_4_.refs_5_ = bf16[8192,1024]{1,0:T(8,128)(2,1)} async-done(((bf16[512,1024]{1,0:T(8,128)(2,1)}), bf16[8192,1024]{1,0:T(8,128)(2,1)}) %all-gather.2.cloned.1.call-update) | async-done | bytes 16777232 | tf_op jit(solution)/shard_map/all_gather | solution.py:180
  133.7 9.1 %shard_map.56.refs_0_ = bf16[512,512]{1,0:T(8,128)(2,1)} custom-call(s32[4]{0:T(128)} %pad_add_fusion.1.meta_ref, bf16[512,512]{1,0:T(8,128)(2,1)} %q_ref.1, bf16[8192,1024]{1,0:T(8,128)(2,1)} %all-gather.2.cloned.1.call-done.refs_0_.refs_1_.refs_2_.refs_3_.refs_4_.refs_5_, ...), custom_call_target="tpu_custom_call" | custom-call | flops 1610612736 | bytes 4194304 | tf_op jit(solution)/shard_map/pallas_call | solution.py:87
  142.8 1.5 collective-permute-start.3
  144.3 2.7 %collective-permute-start.4 = (bf16[512,512]{1,0:T(8,128)(2,1)}, bf16[512,512]{1,0:T(8,128)(2,1)S(1)}, u32[]{:S(2)}, u32[]{:S(2)}) collective-permute-start(bf16[512,512]{1,0:T(8,128)(2,1)} %shard_map.56.refs_0_), channel_id=1, source_target_pairs={{0,4},{2,6},{4,0},{6,2},{1,5},{3,7},{5,1},{7,3},{8,12},{10,14},{12... | collective-permute-start | bytes 1572872 | tf_op jit(solution)/shard_map/ppermute | solution.py:194
  147.0 1.4 collective-permute-start.5
  148.5 0.6 pad_add_fusion.2.y_ref
  149.1 9.0 %collective-permute-done.3.refs_1_ = bf16[512,512]{1,0:T(8,128)(2,1)S(1)} collective-permute-done((bf16[512,512]{1,0:T(8,128)(2,1)}, bf16[512,512]{1,0:T(8,128)(2,1)S(1)}, u32[]{:S(2)}, u32[]{:S(2)}) %collective-permute-start.3) | collective-permute-done | bytes 524320 | tf_op jit(solution)/shard_map/ppermute | solution.py:194
  158.1 12.2 %collective-permute-done.4.refs_2_ = bf16[512,512]{1,0:T(8,128)(2,1)S(1)} collective-permute-done((bf16[512,512]{1,0:T(8,128)(2,1)}, bf16[512,512]{1,0:T(8,128)(2,1)S(1)}, u32[]{:S(2)}, u32[]{:S(2)}) %collective-permute-start.4) | collective-permute-done | bytes 524320 | tf_op jit(solution)/shard_map/ppermute | solution.py:194
  170.3 0.8 copy-done.3
  171.1 0.8 copy-done.4
  171.9 6.6 %shard_map.58 = bf16[512,896]{1,0:T(8,128)(2,1)} custom-call(s32[2]{0:T(128)} %pad_add_fusion.2.y_ref, bf16[512,512]{1,0:T(8,128)(2,1)} %shard_map.56.refs_0_, bf16[512,512]{1,0:T(8,128)(2,1)} %copy-done.2, bf16[512,512]{1,0:T(8,128)(2,1)} %copy-done.3, bf16[512,512]{1,0:T(8,128)(2,1)} %copy-done.4, bf16[512,7168]{1,0:T(8,128)(2,1)} %refs_4_.3, ...), custom_call_target="tpu_custom_call" | custom-call | flops 1879048192 | bytes 6684672 | tf_op jit(solution)/shard_map/pallas_call | solution.py:111
  178.4 3.0 %collective-permute-start.6 = (bf16[512,896]{1,0:T(8,128)(2,1)}, bf16[512,896]{1,0:T(8,128)(2,1)S(1)}, u32[]{:S(2)}, u32[]{:S(2)}) collective-permute-start(bf16[512,896]{1,0:T(8,128)(2,1)} %shard_map.58), channel_id=1, source_target_pairs={{0,1},{1,0},{2,3},{3,2},{4,5},{5,4},{6,7},{7,6},{8,9},{9,8},{10,11... | collective-permute-start | bytes 2752520 | tf_op jit(solution)/shard_map/ppermute | solution.py:201
  181.4 0.6 pad_add_fusion.y_ref
  182.0 6.9 %shard_map.57.own_ref = f32[512,896]{1,0:T(8,128)} custom-call(s32[2]{0:T(128)} %pad_add_fusion.y_ref, bf16[512,512]{1,0:T(8,128)(2,1)} %shard_map.56.refs_0_, bf16[512,512]{1,0:T(8,128)(2,1)} %copy-done.2, bf16[512,512]{1,0:T(8,128)(2,1)} %copy-done.3, bf16[512,512]{1,0:T(8,128)(2,1)} %copy-done.4, bf16[512,7168]{1,0:T(8,128)(2,1)} %refs_4_.3, ...), custom_call_target="tpu_custom_call" | custom-call | flops 1879048192 | bytes 7602176 | tf_op jit(solution)/shard_map/pallas_call | solution.py:111
  188.9 12.6 %collective-permute-done.6.got_ref = bf16[512,896]{1,0:T(8,128)(2,1)S(1)} collective-permute-done((bf16[512,896]{1,0:T(8,128)(2,1)}, bf16[512,896]{1,0:T(8,128)(2,1)S(1)}, u32[]{:S(2)}, u32[]{:S(2)}) %collective-permute-start.6) | collective-permute-done | bytes 917536 | tf_op jit(solution)/shard_map/ppermute | solution.py:201
  201.5 0.9 copy-done.5
  202.5 3.7 %shard_map.59 = bf16[512,896]{1,0:T(8,128)(2,1)} custom-call(f32[512,896]{1,0:T(8,128)} %shard_map.57.own_ref, bf16[512,896]{1,0:T(8,128)(2,1)} %copy-done.5), custom_call_target="tpu_custom_call" | custom-call | flops 458752 | bytes 3670016 | tf_op jit(solution)/shard_map/pallas_call | solution.py:155
  (15 shorter events, 0.8 us)
Async XLA Ops:
  6.5 44.1 %copy-start = (s32[16,3]{0,1:T(4,128)S(1)}, s32[16,3]{0,1:T(4,128)}, u32[]{:S(2)}) copy-start(s32[16,3]{0,1:T(4,128)} %param.8) | copy-start | bytes 580
  6.5 127.2 %all-gather.2.cloned.1.call-start = ((), (), s32[]{:S(2)}) async-start(), calls=%async_computation | async-start | bytes 17825792 | tf_op jit(solution)/shard_map/all_gather | solution.py:180
  44.7 43.3 %collective-permute-start = (bf16[512,1792]{1,0:T(8,128)(2,1)}, bf16[512,1792]{1,0:T(8,128)(2,1)S(1)}, u32[]{:S(2)}, u32[]{:S(2)}) collective-permute-start(bf16[512,1792]{1,0:T(8,128)(2,1)} %get-tuple-element.15), channel_id=1, source_target_pairs={{0,2},{2,4},{4,6},{6,0},{1,3},{3,5},{5,7},{7,1},{8,10},{10,12},{12... | collective-permute-start | bytes 5505032 | tf_op jit(solution)/shard_map/ppermute | solution.py:189
  46.4 82.3 %collective-permute-start.1 = (bf16[512,1792]{1,0:T(8,128)(2,1)}, bf16[512,1792]{1,0:T(8,128)(2,1)}, u32[]{:S(2)}, u32[]{:S(2)}) collective-permute-start(bf16[512,1792]{1,0:T(8,128)(2,1)} %get-tuple-element.14), channel_id=1, source_target_pairs={{0,4},{2,6},{4,0},{6,2},{1,5},{3,7},{5,1},{7,3},{8,12},{10,14},{12... | collective-permute-start | bytes 5505032 | tf_op jit(solution)/shard_map/ppermute | solution.py:189
  49.3 79.4 %collective-permute-start.2 = (bf16[512,1792]{1,0:T(8,128)(2,1)}, bf16[512,1792]{1,0:T(8,128)(2,1)}, u32[]{:S(2)}, u32[]{:S(2)}) collective-permute-start(bf16[512,1792]{1,0:T(8,128)(2,1)} %get-tuple-element.13), channel_id=1, source_target_pairs={{0,6},{2,0},{4,2},{6,4},{1,7},{3,1},{5,3},{7,5},{8,14},{10,8},{12,... | collective-permute-start | bytes 5505032 | tf_op jit(solution)/shard_map/ppermute | solution.py:189
  88.0 54.8 %copy-start.1 = (bf16[512,1792]{1,0:T(8,128)(2,1)}, bf16[512,1792]{1,0:T(8,128)(2,1)S(1)}, u32[]{:S(2)}) copy-start(bf16[512,1792]{1,0:T(8,128)(2,1)S(1)} %collective-permute-done.refs_5_) | copy-start | bytes 5505028
  142.8 15.2 %collective-permute-start.3 = (bf16[512,512]{1,0:T(8,128)(2,1)}, bf16[512,512]{1,0:T(8,128)(2,1)S(1)}, u32[]{:S(2)}, u32[]{:S(2)}) collective-permute-start(bf16[512,512]{1,0:T(8,128)(2,1)} %shard_map.56.refs_0_), channel_id=1, source_target_pairs={{0,2},{2,4},{4,6},{6,0},{1,3},{3,5},{5,7},{7,1},{8,10},{10,12},{12... | collective-permute-start | bytes 1572872 | tf_op jit(solution)/shard_map/ppermute | solution.py:194
  144.3 26.0 %collective-permute-start.4 = (bf16[512,512]{1,0:T(8,128)(2,1)}, bf16[512,512]{1,0:T(8,128)(2,1)S(1)}, u32[]{:S(2)}, u32[]{:S(2)}) collective-permute-start(bf16[512,512]{1,0:T(8,128)(2,1)} %shard_map.56.refs_0_), channel_id=1, source_target_pairs={{0,4},{2,6},{4,0},{6,2},{1,5},{3,7},{5,1},{7,3},{8,12},{10,14},{12... | collective-permute-start | bytes 1572872 | tf_op jit(solution)/shard_map/ppermute | solution.py:194
  147.0 23.2 %collective-permute-start.5 = (bf16[512,512]{1,0:T(8,128)(2,1)}, bf16[512,512]{1,0:T(8,128)(2,1)S(1)}, u32[]{:S(2)}, u32[]{:S(2)}) collective-permute-start(bf16[512,512]{1,0:T(8,128)(2,1)} %shard_map.56.refs_0_), channel_id=1, source_target_pairs={{0,6},{2,0},{4,2},{6,4},{1,7},{3,1},{5,3},{7,5},{8,14},{10,8},{12,... | collective-permute-start | bytes 1572872 | tf_op jit(solution)/shard_map/ppermute | solution.py:194
  158.1 12.2 %copy-start.2 = (bf16[512,512]{1,0:T(8,128)(2,1)}, bf16[512,512]{1,0:T(8,128)(2,1)S(1)}, u32[]{:S(2)}) copy-start(bf16[512,512]{1,0:T(8,128)(2,1)S(1)} %collective-permute-done.3.refs_1_) | copy-start | bytes 1572868
  170.3 0.8 copy-start.3
  171.1 0.8 copy-start.4
  178.4 23.1 %collective-permute-start.6 = (bf16[512,896]{1,0:T(8,128)(2,1)}, bf16[512,896]{1,0:T(8,128)(2,1)S(1)}, u32[]{:S(2)}, u32[]{:S(2)}) collective-permute-start(bf16[512,896]{1,0:T(8,128)(2,1)} %shard_map.58), channel_id=1, source_target_pairs={{0,1},{1,0},{2,3},{3,2},{4,5},{5,4},{6,7},{7,6},{8,9},{9,8},{10,11... | collective-permute-start | bytes 2752520 | tf_op jit(solution)/shard_map/ppermute | solution.py:201
  201.5 0.9 copy-start.5
Sparse Core Ops, SparseCore 0:
  39.6 94.1 all-gather.1

commit v13 on v9

--- a/solution.py
+++ b/solution.py
@@ -121,6 +121,47 @@
     )(meta, *pieces, out_weight, *received)
 
 
+def part_kernel(meta_ref, *refs, count, has_partial):
+    start = 1 if has_partial else 0
+    a_refs = refs[start : start + count]
+    w_refs = refs[start + count : start + 2 * count]
+    o_ref = refs[start + 2 * count]
+    acc = refs[0][...] if has_partial else None
+    for a_ref, w_ref in zip(a_refs, w_refs):
+        term = jnp.dot(a_ref[...], w_ref[...], preferred_element_type=jnp.float32)
+        acc = term if acc is None else acc + term
+    o_ref[...] = acc.astype(o_ref.dtype)
+
+
+def project_part(meta, partial, pieces, weights, local_first, halves, out_dtype):
+    rows, inner = pieces[0].shape
+    col_width = weights[-1].shape[1] // halves
+    w_specs = [pl.BlockSpec((inner, col_width), lambda i, m: (0, m[1])) for _ in weights]
+    if local_first:
+        w_specs[0] = pl.BlockSpec((inner, col_width), lambda i, m: (0, m[0] * halves + m[1]))
+    full = pl.BlockSpec((rows, col_width), lambda i, m: (0, 0))
+    grid_spec = pltpu.PrefetchScalarGridSpec(
+        num_scalar_prefetch=1,
+        grid=(1,),
+        in_specs=([full] if partial is not None else [])
+        + [pl.BlockSpec((rows, inner), lambda i, m: (0, 0)) for _ in pieces]
+        + w_specs,
+        out_specs=full,
+    )
+    extra = [partial] if partial is not None else []
+    return pl.pallas_call(
+        functools.partial(part_kernel, count=len(pieces), has_partial=partial is not None),
+        grid_spec=grid_spec,
+        out_shape=jax.ShapeDtypeStruct((rows, col_width), out_dtype),
+        cost_estimate=pl.CostEstimate(
+            flops=2 * rows * inner * len(pieces) * col_width,
+            transcendentals=0,
+            bytes_accessed=rows * inner * len(pieces) * 2 + len(pieces) * inner * col_width * 2
+            + rows * col_width * (4 * len(extra) + jnp.dtype(out_dtype).itemsize),
+        ),
+    )(meta, *extra, *pieces, *weights)
+
+
 CTX = ("xl", "z", "core")
 TP = ("y", "xh")
 
@@ -154,7 +195,12 @@
     xh_place = lax.axis_index("xh")
     other = jnp.stack([y_place, xh_size - 1 - xh_place]).astype(jnp.int32)
     mine = jnp.stack([y_place, xh_place]).astype(jnp.int32)
-    sent = project(other, pieces, out_weight, received, xh_size, queries.dtype)
+    early = project_part(
+        other, None, pieces[:2], [out_weight, received[0]], True, xh_size, jnp.float32
+    )
+    sent = project_part(
+        other, early, pieces[2:], list(received[1:]), False, xh_size, queries.dtype
+    )
     got = lax.ppermute(sent, "xh", [(i, xh_size - 1 - i) for i in range(xh_size)])
     own = project(mine, pieces, out_weight, received, xh_size, jnp.float32)
     return (own + got.astype(jnp.float32)).astype(queries.dtype)

time: 181 us -> 179 us (0.989)
  waiting for transfers between devices: 116 us -> 111 us
  Pallas kernels: 22.5 us -> 26 us
    pallas_call x0 -> x2, Pallas kernels: none -> 10.1 us  [project_part(): pl.pallas_call(functools.partial(part_kernel, count=len(pieces), has_part...]
    pallas_call x2 -> x1, Pallas kernels: 13.5 us -> 6.9 us  [project(): pl.pallas_call(functools.partial(project_kernel, shifts=shifts), grid_spe...]
    ppermute x3, waiting for transfers between devices: 21.2 us -> 15.5 us  [per_device(): lax.ppermute(attended, 'y', [(i, (i + shift) % y_size) for i in range(y_s...]
  transfers between devices with their start and end apart: 8 -> 8, of which waited for: 6 -> 6; matrix products, arithmetic and copies ran while one was open for 4% -> 4% of each run, Pallas kernels for 4% -> 7%
where the time goes in v13:
time: 179 us
  waiting for transfers between devices  111 us (62%)
  Pallas kernels  26 us (15%)
  starting transfers between devices  14.5 us (8%)
  between operations  13.5 us (8%)
  local copies, waits for them, and re-layouts  7.77 us (4%)
  other arithmetic  6.82 us (4%)
    ppermute x3, waiting for transfers between devices, per_device(): lax.ppermute(sent, 'y', [(i, (i + shift) % y_size) for i in range(y_size)])  77.2 us
    ppermute x3, waiting for transfers between devices, per_device(): lax.ppermute(attended, 'y', [(i, (i + shift) % y_size) for i in range(y_s...  15.5 us
    ppermute x1, waiting for transfers between devices, per_device(): lax.ppermute(sent, 'xh', [(i, xh_size - 1 - i) for i in range(xh_size)])  12.7 us
    pallas_call x2, Pallas kernels, project_part(): pl.pallas_call(functools.partial(part_kernel, count=len(pieces), has_part...  10.1 us
    pallas_call x1, Pallas kernels, attend(): pl.pallas_call(functools.partial(attend_kernel, topk=topk, head_count=hea...  9.02 us
    pallas_call x1, Pallas kernels, project(): pl.pallas_call(functools.partial(project_kernel, shifts=shifts), grid_spe...  6.9 us
    ppermute x3, starting transfers between devices, per_device(): lax.ppermute(sent, 'y', [(i, (i + shift) % y_size) for i in range(y_size)])  5.91 us
    ppermute x3, starting transfers between devices, per_device(): lax.ppermute(attended, 'y', [(i, (i + shift) % y_size) for i in range(y_s...  5.65 us
  transfers between devices with their start and end apart: 8, of which 6 were waited for; matrix products, arithmetic and copies ran while one was open for 4% of the time, Pallas kernels for 7%

profile of v13, /device:TPU:0, one launch (start us, length us, event | category | flops | bytes accessed | tf_op | source)
XLA Modules:
  0.0 179.2 jit_solution(2674224810829944407)
XLA Ops:
  6.5 2.3 %pad_maximum_fusion = bf16[512,1024]{1,0:T(8,128)(2,1)} fusion(bf16[512,512]{1,0:T(8,128)(2,1)} %param.7, bf16[512,512]{1,0:T(8,128)(2,1)} %param.6), kind=kLoop, calls=%fused_computation.1 | loop fusion | flops 2097152 | bytes 2097152 | tf_op jit(solution)/shard_map/concatenate | solution.py:179
  8.9 5.2 %constant_dynamic-slice_fusion = (bf16[512,1792]{1,0:T(8,128)(2,1)}, bf16[512,1792]{1,0:T(8,128)(2,1)}, bf16[512,1792]{1,0:T(8,128)(2,1)}) fusion(bf16[512,7168]{1,0:T(8,128)(2,1)} %refs_2_.1, s32[]{:T(128)S(6)} %select_n.33, s32[]{:T(128)S(6)} %select_n.31, s32[]{:T(128)S(6)} %select_n.29), kind=kLoop, calls=%fused_computation.3 | loop fusion | bytes 11010060 | tf_op jit(solution)/shard_map/dynamic_slice | solution.py:185
  14.1 1.7 collective-permute-start
  15.7 2.9 %collective-permute-start.1 = (bf16[512,1792]{1,0:T(8,128)(2,1)}, bf16[512,1792]{1,0:T(8,128)(2,1)}, u32[]{:S(2)}, u32[]{:S(2)}) collective-permute-start(bf16[512,1792]{1,0:T(8,128)(2,1)} %get-tuple-element.14), channel_id=1, source_target_pairs={{0,4},{2,6},{4,0},{6,2},{1,5},{3,7},{5,1},{7,3},{8,12},{10,14},{12... | collective-permute-start | bytes 5505032 | tf_op jit(solution)/shard_map/ppermute | solution.py:187
  18.6 1.3 collective-permute-start.2
  20.8 36.6 %collective-permute-done.refs_5_.refs_3_ = bf16[512,1792]{1,0:T(8,128)(2,1)S(1)} collective-permute-done((bf16[512,1792]{1,0:T(8,128)(2,1)}, bf16[512,1792]{1,0:T(8,128)(2,1)S(1)}, u32[]{:S(2)}, u32[]{:S(2)}) %collective-permute-start) | collective-permute-done | bytes 1835040 | tf_op jit(solution)/shard_map/ppermute | solution.py:187
  57.4 40.6 %collective-permute-done.1.refs_6_.refs_3_ = bf16[512,1792]{1,0:T(8,128)(2,1)} collective-permute-done((bf16[512,1792]{1,0:T(8,128)(2,1)}, bf16[512,1792]{1,0:T(8,128)(2,1)}, u32[]{:S(2)}, u32[]{:S(2)}) %collective-permute-start.1) | collective-permute-done | bytes 1835040 | tf_op jit(solution)/shard_map/ppermute | solution.py:187
  98.0 5.2 %all-gather.2.cloned.1.call-done.refs_0_.refs_1_.refs_2_.refs_3_.refs_4_.refs_5_ = bf16[8192,1024]{1,0:T(8,128)(2,1)} async-done(((bf16[512,1024]{1,0:T(8,128)(2,1)}), bf16[8192,1024]{1,0:T(8,128)(2,1)}) %all-gather.2.cloned.1.call-update) | async-done | bytes 16777232 | tf_op jit(solution)/shard_map/all_gather | solution.py:178
  103.2 9.0 %shard_map.55.refs_0_ = bf16[512,512]{1,0:T(8,128)(2,1)} custom-call(s32[4]{0:T(128)} %pad_add_fusion.1.meta_ref, bf16[512,512]{1,0:T(8,128)(2,1)} %q_ref.1, bf16[8192,1024]{1,0:T(8,128)(2,1)} %all-gather.2.cloned.1.call-done.refs_0_.refs_1_.refs_2_.refs_3_.refs_4_.refs_5_, ...), custom_call_target="tpu_custom_call" | custom-call | flops 1610612736 | bytes 4194304 | tf_op jit(solution)/shard_map/pallas_call | solution.py:87
  112.2 1.5 collective-permute-start.3
  113.7 2.7 %collective-permute-start.4 = (bf16[512,512]{1,0:T(8,128)(2,1)}, bf16[512,512]{1,0:T(8,128)(2,1)S(1)}, u32[]{:S(2)}, u32[]{:S(2)}) collective-permute-start(bf16[512,512]{1,0:T(8,128)(2,1)} %shard_map.55.refs_0_), channel_id=1, source_target_pairs={{0,4},{2,6},{4,0},{6,2},{1,5},{3,7},{5,1},{7,3},{8,12},{10,14},{12... | collective-permute-start | bytes 1572872 | tf_op jit(solution)/shard_map/ppermute | solution.py:192
  116.5 1.4 collective-permute-start.5
  117.9 0.6 pad_add_fusion.2.meta_ref
  118.5 9.0 %collective-permute-done.3.refs_1_ = bf16[512,512]{1,0:T(8,128)(2,1)S(1)} collective-permute-done((bf16[512,512]{1,0:T(8,128)(2,1)}, bf16[512,512]{1,0:T(8,128)(2,1)S(1)}, u32[]{:S(2)}, u32[]{:S(2)}) %collective-permute-start.3) | collective-permute-done | bytes 524320 | tf_op jit(solution)/shard_map/ppermute | solution.py:192
  127.5 0.8 copy-done.2
  128.3 5.0 %shard_map.57.refs_0_ = f32[512,896]{1,0:T(8,128)} custom-call(s32[2]{0:T(128)} %pad_add_fusion.2.meta_ref, bf16[512,512]{1,0:T(8,128)(2,1)} %shard_map.55.refs_0_, bf16[512,512]{1,0:T(8,128)(2,1)} %copy-done.2, bf16[512,7168]{1,0:T(8,128)(2,1)} %refs_2_.1, bf16[512,1792]{1,0:T(8,128)(2,1)} %copy-done.1), custom_call_target="tpu_custom_call" | custom-call | flops 939524096 | bytes 4718592 | tf_op jit(solution)/shard_map/pallas_call | solution.py:152
  133.3 6.5 %collective-permute-done.4.refs_2_.refs_1_ = bf16[512,512]{1,0:T(8,128)(2,1)S(1)} collective-permute-done((bf16[512,512]{1,0:T(8,128)(2,1)}, bf16[512,512]{1,0:T(8,128)(2,1)S(1)}, u32[]{:S(2)}, u32[]{:S(2)}) %collective-permute-start.4) | collective-permute-done | bytes 524320 | tf_op jit(solution)/shard_map/ppermute | solution.py:192
  139.8 0.8 copy-done.3
  140.6 0.8 copy-done.4
  141.4 5.2 %shard_map.58 = bf16[512,896]{1,0:T(8,128)(2,1)} custom-call(s32[2]{0:T(128)} %pad_add_fusion.2.meta_ref, f32[512,896]{1,0:T(8,128)} %shard_map.57.refs_0_, bf16[512,512]{1,0:T(8,128)(2,1)} %copy-done.3, bf16[512,512]{1,0:T(8,128)(2,1)} %copy-done.4, bf16[512,1792]{1,0:T(8,128)(2,1)} %collective-permute-done.1.refs_6_.refs_3_, ...), custom_call_target="tpu_custom_call" | custom-call | flops 939524096 | bytes 5636096 | tf_op jit(solution)/shard_map/pallas_call | solution.py:152
  146.5 3.0 %collective-permute-start.6 = (bf16[512,896]{1,0:T(8,128)(2,1)}, bf16[512,896]{1,0:T(8,128)(2,1)S(1)}, u32[]{:S(2)}, u32[]{:S(2)}) collective-permute-start(bf16[512,896]{1,0:T(8,128)(2,1)} %shard_map.58), channel_id=1, source_target_pairs={{0,1},{1,0},{2,3},{3,2},{4,5},{5,4},{6,7},{7,6},{8,9},{9,8},{10,11... | collective-permute-start | bytes 2752520 | tf_op jit(solution)/shard_map/ppermute | solution.py:204
  150.1 6.9 %shard_map.56 = f32[512,896]{1,0:T(8,128)} custom-call(s32[2]{0:T(128)} %pad_add_fusion.y_ref, bf16[512,512]{1,0:T(8,128)(2,1)} %shard_map.55.refs_0_, bf16[512,512]{1,0:T(8,128)(2,1)} %copy-done.2, bf16[512,512]{1,0:T(8,128)(2,1)} %copy-done.3, bf16[512,512]{1,0:T(8,128)(2,1)} %copy-done.4, bf16[512,7168]{1,0:T(8,128)(2,1)} %refs_2_.1, ...), custom_call_target="tpu_custom_call" | custom-call | flops 1879048192 | bytes 7602176 | tf_op jit(solution)/shard_map/pallas_call | solution.py:111
  157.0 12.7 %collective-permute-done.6 = bf16[512,896]{1,0:T(8,128)(2,1)S(1)} collective-permute-done((bf16[512,896]{1,0:T(8,128)(2,1)}, bf16[512,896]{1,0:T(8,128)(2,1)S(1)}, u32[]{:S(2)}, u32[]{:S(2)}) %collective-permute-start.6) | collective-permute-done | bytes 917536 | tf_op jit(solution)/shard_map/ppermute | solution.py:204
  169.7 2.6 %add_convert_fusion = bf16[512,896]{1,0:T(8,128)(2,1)} fusion(f32[512,896]{1,0:T(8,128)} %shard_map.56, bf16[512,896]{1,0:T(8,128)(2,1)S(1)} %collective-permute-done.6), kind=kLoop, calls=%fused_computation | loop fusion | flops 1376256 | bytes 3670016 | tf_op jit(solution)/shard_map/convert_element_type | solution.py:206
  (14 shorter events, 1.5 us)
Async XLA Ops:
  6.5 13.5 %copy-start = (s32[16,3]{0,1:T(4,128)S(1)}, s32[16,3]{0,1:T(4,128)}, u32[]{:S(2)}) copy-start(s32[16,3]{0,1:T(4,128)} %param.8) | copy-start | bytes 580
  6.5 96.7 %all-gather.2.cloned.1.call-start = ((), (), s32[]{:S(2)}) async-start(), calls=%async_computation | async-start | bytes 17825792 | tf_op jit(solution)/shard_map/all_gather | solution.py:178
  14.1 43.3 %collective-permute-start = (bf16[512,1792]{1,0:T(8,128)(2,1)}, bf16[512,1792]{1,0:T(8,128)(2,1)S(1)}, u32[]{:S(2)}, u32[]{:S(2)}) collective-permute-start(bf16[512,1792]{1,0:T(8,128)(2,1)} %get-tuple-element.15), channel_id=1, source_target_pairs={{0,2},{2,4},{4,6},{6,0},{1,3},{3,5},{5,7},{7,1},{8,10},{10,12},{12... | collective-permute-start | bytes 5505032 | tf_op jit(solution)/shard_map/ppermute | solution.py:187
  15.7 82.3 %collective-permute-start.1 = (bf16[512,1792]{1,0:T(8,128)(2,1)}, bf16[512,1792]{1,0:T(8,128)(2,1)}, u32[]{:S(2)}, u32[]{:S(2)}) collective-permute-start(bf16[512,1792]{1,0:T(8,128)(2,1)} %get-tuple-element.14), channel_id=1, source_target_pairs={{0,4},{2,6},{4,0},{6,2},{1,5},{3,7},{5,1},{7,3},{8,12},{10,14},{12... | collective-permute-start | bytes 5505032 | tf_op jit(solution)/shard_map/ppermute | solution.py:187
  18.6 79.4 %collective-permute-start.2 = (bf16[512,1792]{1,0:T(8,128)(2,1)}, bf16[512,1792]{1,0:T(8,128)(2,1)}, u32[]{:S(2)}, u32[]{:S(2)}) collective-permute-start(bf16[512,1792]{1,0:T(8,128)(2,1)} %get-tuple-element.13), channel_id=1, source_target_pairs={{0,6},{2,0},{4,2},{6,4},{1,7},{3,1},{5,3},{7,5},{8,14},{10,8},{12,... | collective-permute-start | bytes 5505032 | tf_op jit(solution)/shard_map/ppermute | solution.py:187
  57.4 54.8 %copy-start.1 = (bf16[512,1792]{1,0:T(8,128)(2,1)}, bf16[512,1792]{1,0:T(8,128)(2,1)S(1)}, u32[]{:S(2)}) copy-start(bf16[512,1792]{1,0:T(8,128)(2,1)S(1)} %collective-permute-done.refs_5_.refs_3_) | copy-start | bytes 5505028
  112.2 15.3 %collective-permute-start.3 = (bf16[512,512]{1,0:T(8,128)(2,1)}, bf16[512,512]{1,0:T(8,128)(2,1)S(1)}, u32[]{:S(2)}, u32[]{:S(2)}) collective-permute-start(bf16[512,512]{1,0:T(8,128)(2,1)} %shard_map.55.refs_0_), channel_id=1, source_target_pairs={{0,2},{2,4},{4,6},{6,0},{1,3},{3,5},{5,7},{7,1},{8,10},{10,12},{12... | collective-permute-start | bytes 1572872 | tf_op jit(solution)/shard_map/ppermute | solution.py:192
  113.7 26.0 %collective-permute-start.4 = (bf16[512,512]{1,0:T(8,128)(2,1)}, bf16[512,512]{1,0:T(8,128)(2,1)S(1)}, u32[]{:S(2)}, u32[]{:S(2)}) collective-permute-start(bf16[512,512]{1,0:T(8,128)(2,1)} %shard_map.55.refs_0_), channel_id=1, source_target_pairs={{0,4},{2,6},{4,0},{6,2},{1,5},{3,7},{5,1},{7,3},{8,12},{10,14},{12... | collective-permute-start | bytes 1572872 | tf_op jit(solution)/shard_map/ppermute | solution.py:192
  116.5 23.3 %collective-permute-start.5 = (bf16[512,512]{1,0:T(8,128)(2,1)}, bf16[512,512]{1,0:T(8,128)(2,1)S(1)}, u32[]{:S(2)}, u32[]{:S(2)}) collective-permute-start(bf16[512,512]{1,0:T(8,128)(2,1)} %shard_map.55.refs_0_), channel_id=1, source_target_pairs={{0,6},{2,0},{4,2},{6,4},{1,7},{3,1},{5,3},{7,5},{8,14},{10,8},{12,... | collective-permute-start | bytes 1572872 | tf_op jit(solution)/shard_map/ppermute | solution.py:192
  127.5 0.8 copy-start.2
  139.8 0.8 copy-start.3
  140.6 0.8 copy-start.4
  146.5 23.2 %collective-permute-start.6 = (bf16[512,896]{1,0:T(8,128)(2,1)}, bf16[512,896]{1,0:T(8,128)(2,1)S(1)}, u32[]{:S(2)}, u32[]{:S(2)}) collective-permute-start(bf16[512,896]{1,0:T(8,128)(2,1)} %shard_map.58), channel_id=1, source_target_pairs={{0,1},{1,0},{2,3},{3,2},{4,5},{5,4},{6,7},{7,6},{8,9},{9,8},{10,11... | collective-permute-start | bytes 2752520 | tf_op jit(solution)/shard_map/ppermute | solution.py:204
Sparse Core Ops, SparseCore 0:
  9.1 94.1 all-gather.1

commit v14 on v13

--- a/solution.py
+++ b/solution.py
@@ -162,6 +162,27 @@
     )(meta, *extra, *pieces, *weights)
 
 
+def join_kernel(k_ref, v_ref, o_ref):
+    width = k_ref.shape[1]
+    o_ref[:, :width] = k_ref[...]
+    o_ref[:, width:] = v_ref[...]
+
+
+def join(key_rows, value_rows, chunks=4):
+    rows, width = key_rows.shape
+    part = pl.BlockSpec((rows // chunks, width), lambda i: (i, 0))
+    return pl.pallas_call(
+        join_kernel,
+        grid=(chunks,),
+        in_specs=[part, part],
+        out_specs=pl.BlockSpec((rows // chunks, 2 * width), lambda i: (i, 0)),
+        out_shape=jax.ShapeDtypeStruct((rows, 2 * width), key_rows.dtype),
+        cost_estimate=pl.CostEstimate(
+            flops=0, transcendentals=0, bytes_accessed=4 * key_rows.size * key_rows.dtype.itemsize
+        ),
+    )(key_rows, value_rows)
+
+
 CTX = ("xl", "z", "core")
 TP = ("y", "xh")
 
@@ -176,7 +197,7 @@
     own_choice = lax.dynamic_slice_in_dim(selection, ctx_place, 1, 0)[0]
     meta = jnp.concatenate([own_choice, ctx_place.astype(jnp.int32)[None]])
     kv_piece = lax.all_gather(
-        jnp.concatenate([key_rows, value_rows], axis=1), CTX, axis=0, tiled=True
+        join(key_rows, value_rows), CTX, axis=0, tiled=True
     )
     group_width = out_weight.shape[1] // y_size
     received = []

time: 179 us -> 181 us (1.011)
  Pallas kernels: 26 us -> 29.5 us
  other arithmetic: 6.82 us -> 4.53 us
    pallas_call x0 -> x1, Pallas kernels: none -> 3.42 us  [join(): pl.pallas_call(join_kernel, grid=(chunks,), in_specs=[part, part], out_sp...]
    concatenate x1 -> x0, other arithmetic: 2.28 us -> none  [per_device(): jnp.concatenate([key_rows, value_rows], axis=1)]
where the time goes in v14:
time: 181 us; the launch traced here: 180 us
  waiting for transfers between devices  110 us (61%)
  Pallas kernels  29.5 us (16%)
  starting transfers between devices  14.5 us (8%)
  between operations  13.5 us (7%)
  local copies, waits for them, and re-layouts  7.77 us (4%)
  other arithmetic  4.53 us (3%)
    ppermute x3, waiting for transfers between devices, per_device(): lax.ppermute(sent, 'y', [(i, (i + shift) % y_size) for i in range(y_size)])  77.2 us
    ppermute x3, waiting for transfers between devices, per_device(): lax.ppermute(attended, 'y', [(i, (i + shift) % y_size) for i in range(y_s...  15.5 us
    ppermute x1, waiting for transfers between devices, per_device(): lax.ppermute(sent, 'xh', [(i, xh_size - 1 - i) for i in range(xh_size)])  12.7 us
    pallas_call x2, Pallas kernels, project_part(): pl.pallas_call(functools.partial(part_kernel, count=len(pieces), has_part...  10.1 us
    pallas_call x1, Pallas kernels, attend(): pl.pallas_call(functools.partial(attend_kernel, topk=topk, head_count=hea...  9.02 us
    pallas_call x1, Pallas kernels, project(): pl.pallas_call(functools.partial(project_kernel, shifts=shifts), grid_spe...  6.9 us
    ppermute x3, starting transfers between devices, per_device(): lax.ppermute(sent, 'y', [(i, (i + shift) % y_size) for i in range(y_size)])  5.91 us
    ppermute x3, starting transfers between devices, per_device(): lax.ppermute(attended, 'y', [(i, (i + shift) % y_size) for i in range(y_s...  5.64 us
  transfers between devices with their start and end apart: 8, of which 6 were waited for; matrix products, arithmetic and copies ran while one was open for 4% of the time, Pallas kernels for 7%

profile of v14, /device:TPU:0, one launch (start us, length us, event | category | flops | bytes accessed | tf_op | source)
XLA Modules:
  0.0 180.2 jit_solution(13494072864409615531)
XLA Ops:
  6.5 3.4 %shard_map.55 = bf16[512,1024]{1,0:T(8,128)(2,1)} custom-call(bf16[512,512]{1,0:T(8,128)(2,1)} %k_ref.1, bf16[512,512]{1,0:T(8,128)(2,1)} %v_ref.1), custom_call_target="tpu_custom_call" | custom-call | bytes 2097152 | tf_op jit(solution)/shard_map/pallas_call | solution.py:174
  10.0 5.2 %constant_dynamic-slice_fusion = (bf16[512,1792]{1,0:T(8,128)(2,1)}, bf16[512,1792]{1,0:T(8,128)(2,1)}, bf16[512,1792]{1,0:T(8,128)(2,1)}) fusion(bf16[512,7168]{1,0:T(8,128)(2,1)} %refs_2_.1, s32[]{:T(128)S(6)} %select_n.33, s32[]{:T(128)S(6)} %select_n.31, s32[]{:T(128)S(6)} %select_n.29), kind=kLoop, calls=%fused_computation.2 | loop fusion | bytes 11010060 | tf_op jit(solution)/shard_map/dynamic_slice | solution.py:206
  15.2 1.7 collective-permute-start
  16.9 2.9 %collective-permute-start.1 = (bf16[512,1792]{1,0:T(8,128)(2,1)}, bf16[512,1792]{1,0:T(8,128)(2,1)}, u32[]{:S(2)}, u32[]{:S(2)}) collective-permute-start(bf16[512,1792]{1,0:T(8,128)(2,1)} %get-tuple-element.14), channel_id=1, source_target_pairs={{0,4},{2,6},{4,0},{6,2},{1,5},{3,7},{5,1},{7,3},{8,12},{10,14},{12... | collective-permute-start | bytes 5505032 | tf_op jit(solution)/shard_map/ppermute | solution.py:208
  19.8 1.3 collective-permute-start.2
  21.9 36.6 %collective-permute-done.refs_5_.refs_3_ = bf16[512,1792]{1,0:T(8,128)(2,1)S(1)} collective-permute-done((bf16[512,1792]{1,0:T(8,128)(2,1)}, bf16[512,1792]{1,0:T(8,128)(2,1)S(1)}, u32[]{:S(2)}, u32[]{:S(2)}) %collective-permute-start) | collective-permute-done | bytes 1835040 | tf_op jit(solution)/shard_map/ppermute | solution.py:208
  58.5 40.6 %collective-permute-done.1.refs_6_.refs_3_ = bf16[512,1792]{1,0:T(8,128)(2,1)} collective-permute-done((bf16[512,1792]{1,0:T(8,128)(2,1)}, bf16[512,1792]{1,0:T(8,128)(2,1)}, u32[]{:S(2)}, u32[]{:S(2)}) %collective-permute-start.1) | collective-permute-done | bytes 1835040 | tf_op jit(solution)/shard_map/ppermute | solution.py:208
  99.2 5.1 %all-gather.2.cloned.1.call-done.refs_0_.refs_1_.refs_2_.refs_3_.refs_4_.refs_5_ = bf16[8192,1024]{1,0:T(8,128)(2,1)} async-done(((bf16[512,1024]{1,0:T(8,128)(2,1)}), bf16[8192,1024]{1,0:T(8,128)(2,1)}) %all-gather.2.cloned.1.call-update) | async-done | bytes 16777232 | tf_op jit(solution)/shard_map/all_gather | solution.py:199
  104.3 9.0 %shard_map.56.refs_0_ = bf16[512,512]{1,0:T(8,128)(2,1)} custom-call(s32[4]{0:T(128)} %pad_add_fusion.1.meta_ref, bf16[512,512]{1,0:T(8,128)(2,1)} %q_ref.1, bf16[8192,1024]{1,0:T(8,128)(2,1)} %all-gather.2.cloned.1.call-done.refs_0_.refs_1_.refs_2_.refs_3_.refs_4_.refs_5_, ...), custom_call_target="tpu_custom_call" | custom-call | flops 1610612736 | bytes 4194304 | tf_op jit(solution)/shard_map/pallas_call | solution.py:87
  113.3 1.5 collective-permute-start.3
  114.8 2.7 %collective-permute-start.4 = (bf16[512,512]{1,0:T(8,128)(2,1)}, bf16[512,512]{1,0:T(8,128)(2,1)S(1)}, u32[]{:S(2)}, u32[]{:S(2)}) collective-permute-start(bf16[512,512]{1,0:T(8,128)(2,1)} %shard_map.56.refs_0_), channel_id=1, source_target_pairs={{0,4},{2,6},{4,0},{6,2},{1,5},{3,7},{5,1},{7,3},{8,12},{10,14},{12... | collective-permute-start | bytes 1572872 | tf_op jit(solution)/shard_map/ppermute | solution.py:213
  117.5 1.4 collective-permute-start.5
  118.9 0.6 pad_add_fusion.2.meta_ref
  119.6 9.0 %collective-permute-done.3.refs_1_ = bf16[512,512]{1,0:T(8,128)(2,1)S(1)} collective-permute-done((bf16[512,512]{1,0:T(8,128)(2,1)}, bf16[512,512]{1,0:T(8,128)(2,1)S(1)}, u32[]{:S(2)}, u32[]{:S(2)}) %collective-permute-start.3) | collective-permute-done | bytes 524320 | tf_op jit(solution)/shard_map/ppermute | solution.py:213
  128.6 0.8 copy-done.2
  129.4 5.0 %shard_map.58.refs_0_ = f32[512,896]{1,0:T(8,128)} custom-call(s32[2]{0:T(128)} %pad_add_fusion.2.meta_ref, bf16[512,512]{1,0:T(8,128)(2,1)} %shard_map.56.refs_0_, bf16[512,512]{1,0:T(8,128)(2,1)} %copy-done.2, bf16[512,7168]{1,0:T(8,128)(2,1)} %refs_2_.1, bf16[512,1792]{1,0:T(8,128)(2,1)} %copy-done.1), custom_call_target="tpu_custom_call" | custom-call | flops 939524096 | bytes 4718592 | tf_op jit(solution)/shard_map/pallas_call | solution.py:152
  134.3 6.5 %collective-permute-done.4.refs_2_.refs_1_ = bf16[512,512]{1,0:T(8,128)(2,1)S(1)} collective-permute-done((bf16[512,512]{1,0:T(8,128)(2,1)}, bf16[512,512]{1,0:T(8,128)(2,1)S(1)}, u32[]{:S(2)}, u32[]{:S(2)}) %collective-permute-start.4) | collective-permute-done | bytes 524320 | tf_op jit(solution)/shard_map/ppermute | solution.py:213
  140.8 0.8 copy-done.3
  141.6 0.8 copy-done.4
  142.4 5.2 %shard_map.59 = bf16[512,896]{1,0:T(8,128)(2,1)} custom-call(s32[2]{0:T(128)} %pad_add_fusion.2.meta_ref, f32[512,896]{1,0:T(8,128)} %shard_map.58.refs_0_, bf16[512,512]{1,0:T(8,128)(2,1)} %copy-done.3, bf16[512,512]{1,0:T(8,128)(2,1)} %copy-done.4, bf16[512,1792]{1,0:T(8,128)(2,1)} %collective-permute-done.1.refs_6_.refs_3_, ...), custom_call_target="tpu_custom_call" | custom-call | flops 939524096 | bytes 5636096 | tf_op jit(solution)/shard_map/pallas_call | solution.py:152
  147.6 3.0 %collective-permute-start.6 = (bf16[512,896]{1,0:T(8,128)(2,1)}, bf16[512,896]{1,0:T(8,128)(2,1)S(1)}, u32[]{:S(2)}, u32[]{:S(2)}) collective-permute-start(bf16[512,896]{1,0:T(8,128)(2,1)} %shard_map.59), channel_id=1, source_target_pairs={{0,1},{1,0},{2,3},{3,2},{4,5},{5,4},{6,7},{7,6},{8,9},{9,8},{10,11... | collective-permute-start | bytes 2752520 | tf_op jit(solution)/shard_map/ppermute | solution.py:225
  151.2 6.9 %shard_map.57 = f32[512,896]{1,0:T(8,128)} custom-call(s32[2]{0:T(128)} %pad_add_fusion.y_ref, bf16[512,512]{1,0:T(8,128)(2,1)} %shard_map.56.refs_0_, bf16[512,512]{1,0:T(8,128)(2,1)} %copy-done.2, bf16[512,512]{1,0:T(8,128)(2,1)} %copy-done.3, bf16[512,512]{1,0:T(8,128)(2,1)} %copy-done.4, bf16[512,7168]{1,0:T(8,128)(2,1)} %refs_2_.1, ...), custom_call_target="tpu_custom_call" | custom-call | flops 1879048192 | bytes 7602176 | tf_op jit(solution)/shard_map/pallas_call | solution.py:111
  158.1 12.7 %collective-permute-done.6 = bf16[512,896]{1,0:T(8,128)(2,1)S(1)} collective-permute-done((bf16[512,896]{1,0:T(8,128)(2,1)}, bf16[512,896]{1,0:T(8,128)(2,1)S(1)}, u32[]{:S(2)}, u32[]{:S(2)}) %collective-permute-start.6) | collective-permute-done | bytes 917536 | tf_op jit(solution)/shard_map/ppermute | solution.py:225
  170.7 2.6 %add_convert_fusion = bf16[512,896]{1,0:T(8,128)(2,1)} fusion(f32[512,896]{1,0:T(8,128)} %shard_map.57, bf16[512,896]{1,0:T(8,128)(2,1)S(1)} %collective-permute-done.6), kind=kLoop, calls=%fused_computation | loop fusion | flops 1376256 | bytes 3670016 | tf_op jit(solution)/shard_map/convert_element_type | solution.py:227
  (14 shorter events, 1.5 us)
Async XLA Ops:
  6.5 14.6 %copy-start = (s32[16,3]{0,1:T(4,128)S(1)}, s32[16,3]{0,1:T(4,128)}, u32[]{:S(2)}) copy-start(s32[16,3]{0,1:T(4,128)} %param.8) | copy-start | bytes 580
  6.5 97.7 %all-gather.2.cloned.1.call-start = ((), (), s32[]{:S(2)}) async-start(), calls=%async_computation | async-start | bytes 17825792 | tf_op jit(solution)/shard_map/all_gather | solution.py:199
  15.2 43.3 %collective-permute-start = (bf16[512,1792]{1,0:T(8,128)(2,1)}, bf16[512,1792]{1,0:T(8,128)(2,1)S(1)}, u32[]{:S(2)}, u32[]{:S(2)}) collective-permute-start(bf16[512,1792]{1,0:T(8,128)(2,1)} %get-tuple-element.15), channel_id=1, source_target_pairs={{0,2},{2,4},{4,6},{6,0},{1,3},{3,5},{5,7},{7,1},{8,10},{10,12},{12... | collective-permute-start | bytes 5505032 | tf_op jit(solution)/shard_map/ppermute | solution.py:208
  16.9 82.3 %collective-permute-start.1 = (bf16[512,1792]{1,0:T(8,128)(2,1)}, bf16[512,1792]{1,0:T(8,128)(2,1)}, u32[]{:S(2)}, u32[]{:S(2)}) collective-permute-start(bf16[512,1792]{1,0:T(8,128)(2,1)} %get-tuple-element.14), channel_id=1, source_target_pairs={{0,4},{2,6},{4,0},{6,2},{1,5},{3,7},{5,1},{7,3},{8,12},{10,14},{12... | collective-permute-start | bytes 5505032 | tf_op jit(solution)/shard_map/ppermute | solution.py:208
  19.8 79.4 %collective-permute-start.2 = (bf16[512,1792]{1,0:T(8,128)(2,1)}, bf16[512,1792]{1,0:T(8,128)(2,1)}, u32[]{:S(2)}, u32[]{:S(2)}) collective-permute-start(bf16[512,1792]{1,0:T(8,128)(2,1)} %get-tuple-element.13), channel_id=1, source_target_pairs={{0,6},{2,0},{4,2},{6,4},{1,7},{3,1},{5,3},{7,5},{8,14},{10,8},{12,... | collective-permute-start | bytes 5505032 | tf_op jit(solution)/shard_map/ppermute | solution.py:208
  58.5 54.7 %copy-start.1 = (bf16[512,1792]{1,0:T(8,128)(2,1)}, bf16[512,1792]{1,0:T(8,128)(2,1)S(1)}, u32[]{:S(2)}) copy-start(bf16[512,1792]{1,0:T(8,128)(2,1)S(1)} %collective-permute-done.refs_5_.refs_3_) | copy-start | bytes 5505028
  113.3 15.3 %collective-permute-start.3 = (bf16[512,512]{1,0:T(8,128)(2,1)}, bf16[512,512]{1,0:T(8,128)(2,1)S(1)}, u32[]{:S(2)}, u32[]{:S(2)}) collective-permute-start(bf16[512,512]{1,0:T(8,128)(2,1)} %shard_map.56.refs_0_), channel_id=1, source_target_pairs={{0,2},{2,4},{4,6},{6,0},{1,3},{3,5},{5,7},{7,1},{8,10},{10,12},{12... | collective-permute-start | bytes 1572872 | tf_op jit(solution)/shard_map/ppermute | solution.py:213
  114.8 26.0 %collective-permute-start.4 = (bf16[512,512]{1,0:T(8,128)(2,1)}, bf16[512,512]{1,0:T(8,128)(2,1)S(1)}, u32[]{:S(2)}, u32[]{:S(2)}) collective-permute-start(bf16[512,512]{1,0:T(8,128)(2,1)} %shard_map.56.refs_0_), channel_id=1, source_target_pairs={{0,4},{2,6},{4,0},{6,2},{1,5},{3,7},{5,1},{7,3},{8,12},{10,14},{12... | collective-permute-start | bytes 1572872 | tf_op jit(solution)/shard_map/ppermute | solution.py:213
  117.5 23.3 %collective-permute-start.5 = (bf16[512,512]{1,0:T(8,128)(2,1)}, bf16[512,512]{1,0:T(8,128)(2,1)S(1)}, u32[]{:S(2)}, u32[]{:S(2)}) collective-permute-start(bf16[512,512]{1,0:T(8,128)(2,1)} %shard_map.56.refs_0_), channel_id=1, source_target_pairs={{0,6},{2,0},{4,2},{6,4},{1,7},{3,1},{5,3},{7,5},{8,14},{10,8},{12,... | collective-permute-start | bytes 1572872 | tf_op jit(solution)/shard_map/ppermute | solution.py:213
  128.6 0.8 copy-start.2
  140.8 0.8 copy-start.3
  141.6 0.8 copy-start.4
  147.6 23.2 %collective-permute-start.6 = (bf16[512,896]{1,0:T(8,128)(2,1)}, bf16[512,896]{1,0:T(8,128)(2,1)S(1)}, u32[]{:S(2)}, u32[]{:S(2)}) collective-permute-start(bf16[512,896]{1,0:T(8,128)(2,1)} %shard_map.59), channel_id=1, source_target_pairs={{0,1},{1,0},{2,3},{3,2},{4,5},{5,4},{6,7},{7,6},{8,9},{9,8},{10,11... | collective-permute-start | bytes 2752520 | tf_op jit(solution)/shard_map/ppermute | solution.py:225
Sparse Core Ops, SparseCore 0:
  10.1 94.1 all-gather.1

commit v15 on v13

--- a/solution.py
+++ b/solution.py
@@ -198,8 +198,11 @@
     early = project_part(
         other, None, pieces[:2], [out_weight, received[0]], True, xh_size, jnp.float32
     )
+    near = project_part(
+        other, early, pieces[3:], list(received[2:]), False, xh_size, jnp.float32
+    )
     sent = project_part(
-        other, early, pieces[2:], list(received[1:]), False, xh_size, queries.dtype
+        other, near, pieces[2:3], list(received[1:2]), False, xh_size, queries.dtype
     )
     got = lax.ppermute(sent, "xh", [(i, xh_size - 1 - i) for i in range(xh_size)])
     own = project(mine, pieces, out_weight, received, xh_size, jnp.float32)

time: 179 us -> 178 us (level)
  waiting for transfers between devices: 111 us -> 106 us
  Pallas kernels: 26 us -> 29.6 us
    ppermute x1, waiting for transfers between devices: 12.7 us -> 8.95 us  [per_device(): lax.ppermute(sent, 'xh', [(i, xh_size - 1 - i) for i in range(xh_size)])]
    pallas_call x2 -> x3, Pallas kernels: 10.1 us -> 13.7 us  [project_part(): pl.pallas_call(functools.partial(part_kernel, count=len(pieces), has_part...]
  transfers between devices with their start and end apart: 8 -> 8, of which waited for: 6 -> 6; matrix products, arithmetic and copies ran while one was open for 4% -> 4% of each run, Pallas kernels for 7% -> 9%
where the time goes in v15:
time: 178 us; the launch traced here: 177 us
  waiting for transfers between devices  106 us (60%)
  Pallas kernels  29.6 us (17%)
  starting transfers between devices  13.9 us (8%)
  between operations  13.5 us (8%)
  local copies, waits for them, and re-layouts  7.7 us (4%)
  other arithmetic  6.72 us (4%)
    ppermute x3, waiting for transfers between devices, per_device(): lax.ppermute(sent, 'y', [(i, (i + shift) % y_size) for i in range(y_size)])  77.1 us
    ppermute x3, waiting for transfers between devices, per_device(): lax.ppermute(attended, 'y', [(i, (i + shift) % y_size) for i in range(y_s...  14.6 us
    pallas_call x3, Pallas kernels, project_part(): pl.pallas_call(functools.partial(part_kernel, count=len(pieces), has_part...  13.7 us
    pallas_call x1, Pallas kernels, attend(): pl.pallas_call(functools.partial(attend_kernel, topk=topk, head_count=hea...  9.02 us
    ppermute x1, waiting for transfers between devices, per_device(): lax.ppermute(sent, 'xh', [(i, xh_size - 1 - i) for i in range(xh_size)])  8.95 us
    pallas_call x1, Pallas kernels, project(): pl.pallas_call(functools.partial(project_kernel, shifts=shifts), grid_spe...  6.9 us
    ppermute x3, starting transfers between devices, per_device(): lax.ppermute(sent, 'y', [(i, (i + shift) % y_size) for i in range(y_size)])  5.91 us
    all_gather x1, waiting for transfers between devices, per_device(): lax.all_gather(jnp.concatenate([key_rows, value_rows], axis=1), CTX, axis...  5.36 us
  transfers between devices with their start and end apart: 8, of which 6 were waited for; matrix products, arithmetic and copies ran while one was open for 4% of the time, Pallas kernels for 9%

profile of v15, /device:TPU:0, one launch (start us, length us, event | category | flops | bytes accessed | tf_op | source)
XLA Modules:
  0.0 177.4 jit_solution(18136854109925038561)
XLA Ops:
  6.5 2.3 %pad_maximum_fusion = bf16[512,1024]{1,0:T(8,128)(2,1)} fusion(bf16[512,512]{1,0:T(8,128)(2,1)} %param.7, bf16[512,512]{1,0:T(8,128)(2,1)} %param.6), kind=kLoop, calls=%fused_computation.1 | loop fusion | flops 2097152 | bytes 2097152 | tf_op jit(solution)/shard_map/concatenate | solution.py:179
  8.9 5.1 %constant_dynamic-slice_fusion = (bf16[512,1792]{1,0:T(8,128)(2,1)}, bf16[512,1792]{1,0:T(8,128)(2,1)}, bf16[512,1792]{1,0:T(8,128)(2,1)}) fusion(bf16[512,7168]{1,0:T(8,128)(2,1)} %refs_2_.1, s32[]{:T(128)S(6)} %select_n.33, s32[]{:T(128)S(6)} %select_n.31, s32[]{:T(128)S(6)} %select_n.29), kind=kLoop, calls=%fused_computation.3 | loop fusion | bytes 11010060 | tf_op jit(solution)/shard_map/dynamic_slice | solution.py:185
  14.0 1.7 collective-permute-start
  15.7 2.9 %collective-permute-start.1 = (bf16[512,1792]{1,0:T(8,128)(2,1)}, bf16[512,1792]{1,0:T(8,128)(2,1)S(1)}, u32[]{:S(2)}, u32[]{:S(2)}) collective-permute-start(bf16[512,1792]{1,0:T(8,128)(2,1)} %get-tuple-element.14), channel_id=1, source_target_pairs={{0,4},{2,6},{4,0},{6,2},{1,5},{3,7},{5,1},{7,3},{8,12},{10,14},{12... | collective-permute-start | bytes 5505032 | tf_op jit(solution)/shard_map/ppermute | solution.py:187
  18.6 1.3 collective-permute-start.2
  20.8 36.7 %collective-permute-done.refs_5_.refs_3_ = bf16[512,1792]{1,0:T(8,128)(2,1)} collective-permute-done((bf16[512,1792]{1,0:T(8,128)(2,1)}, bf16[512,1792]{1,0:T(8,128)(2,1)}, u32[]{:S(2)}, u32[]{:S(2)}) %collective-permute-start) | collective-permute-done | bytes 1835040 | tf_op jit(solution)/shard_map/ppermute | solution.py:187
  57.5 40.4 %collective-permute-done.1.refs_6_.refs_2_ = bf16[512,1792]{1,0:T(8,128)(2,1)S(1)} collective-permute-done((bf16[512,1792]{1,0:T(8,128)(2,1)}, bf16[512,1792]{1,0:T(8,128)(2,1)S(1)}, u32[]{:S(2)}, u32[]{:S(2)}) %collective-permute-start.1) | collective-permute-done | bytes 1835040 | tf_op jit(solution)/shard_map/ppermute | solution.py:187
  97.9 5.4 %all-gather.2.cloned.1.call-done.refs_0_.refs_1_.refs_2_.refs_3_.refs_4_.refs_5_ = bf16[8192,1024]{1,0:T(8,128)(2,1)} async-done(((bf16[512,1024]{1,0:T(8,128)(2,1)}), bf16[8192,1024]{1,0:T(8,128)(2,1)}) %all-gather.2.cloned.1.call-update) | async-done | bytes 16777232 | tf_op jit(solution)/shard_map/all_gather | solution.py:178
  103.2 9.0 %shard_map.55.refs_0_ = bf16[512,512]{1,0:T(8,128)(2,1)} custom-call(s32[4]{0:T(128)} %pad_add_fusion.1.meta_ref, bf16[512,512]{1,0:T(8,128)(2,1)} %q_ref.1, bf16[8192,1024]{1,0:T(8,128)(2,1)} %all-gather.2.cloned.1.call-done.refs_0_.refs_1_.refs_2_.refs_3_.refs_4_.refs_5_, ...), custom_call_target="tpu_custom_call" | custom-call | flops 1610612736 | bytes 4194304 | tf_op jit(solution)/shard_map/pallas_call | solution.py:87
  112.2 1.5 collective-permute-start.3
  113.7 1.7 collective-permute-start.5
  115.5 1.8 %collective-permute-start.4 = (bf16[512,512]{1,0:T(8,128)(2,1)}, bf16[512,512]{1,0:T(8,128)(2,1)S(1)}, u32[]{:S(2)}, u32[]{:S(2)}) collective-permute-start(bf16[512,512]{1,0:T(8,128)(2,1)} %shard_map.55.refs_0_), channel_id=1, source_target_pairs={{0,4},{2,6},{4,0},{6,2},{1,5},{3,7},{5,1},{7,3},{8,12},{10,14},{12... | collective-permute-start | bytes 1572872 | tf_op jit(solution)/shard_map/ppermute | solution.py:192
  117.9 9.7 %collective-permute-done.3.refs_1_ = bf16[512,512]{1,0:T(8,128)(2,1)S(1)} collective-permute-done((bf16[512,512]{1,0:T(8,128)(2,1)}, bf16[512,512]{1,0:T(8,128)(2,1)S(1)}, u32[]{:S(2)}, u32[]{:S(2)}) %collective-permute-start.3) | collective-permute-done | bytes 524320 | tf_op jit(solution)/shard_map/ppermute | solution.py:192
  127.5 0.8 copy-done.2
  128.3 4.9 %shard_map.57.refs_0_ = f32[512,896]{1,0:T(8,128)} custom-call(s32[2]{0:T(128)} %pad_add_fusion.2.meta_ref, bf16[512,512]{1,0:T(8,128)(2,1)} %shard_map.55.refs_0_, bf16[512,512]{1,0:T(8,128)(2,1)} %copy-done.2, bf16[512,7168]{1,0:T(8,128)(2,1)} %refs_2_.1, bf16[512,1792]{1,0:T(8,128)(2,1)} %collective-permute-done.refs_5_.refs_3_), custom_call_target="tpu_custom_call" | custom-call | flops 939524096 | bytes 4718592 | tf_op jit(solution)/shard_map/pallas_call | solution.py:152
  133.3 4.9 %collective-permute-done.5.refs_3_.refs_1_ = bf16[512,512]{1,0:T(8,128)(2,1)S(1)} collective-permute-done((bf16[512,512]{1,0:T(8,128)(2,1)}, bf16[512,512]{1,0:T(8,128)(2,1)S(1)}, u32[]{:S(2)}, u32[]{:S(2)}) %collective-permute-start.5) | collective-permute-done | bytes 524320 | tf_op jit(solution)/shard_map/ppermute | solution.py:192
  138.2 0.8 copy-done.3
  139.0 4.5 %shard_map.58.refs_0_ = f32[512,896]{1,0:T(8,128)} custom-call(s32[2]{0:T(128)} %pad_add_fusion.2.meta_ref, f32[512,896]{1,0:T(8,128)} %shard_map.57.refs_0_, bf16[512,512]{1,0:T(8,128)(2,1)} %copy-done.3, bf16[512,1792]{1,0:T(8,128)(2,1)} %collective-permute-done.2.refs_7_.refs_2_), custom_call_target="tpu_custom_call" | custom-call | flops 469762048 | bytes 5111808 | tf_op jit(solution)/shard_map/pallas_call | solution.py:152
  143.5 0.8 copy-done.4
  144.3 4.2 %shard_map.59 = bf16[512,896]{1,0:T(8,128)(2,1)} custom-call(s32[2]{0:T(128)} %pad_add_fusion.2.meta_ref, f32[512,896]{1,0:T(8,128)} %shard_map.58.refs_0_, bf16[512,512]{1,0:T(8,128)(2,1)} %copy-done.4, bf16[512,1792]{1,0:T(8,128)(2,1)} %copy-done.1), custom_call_target="tpu_custom_call" | custom-call | flops 469762048 | bytes 4194304 | tf_op jit(solution)/shard_map/pallas_call | solution.py:152
  148.5 3.0 %collective-permute-start.6 = (bf16[512,896]{1,0:T(8,128)(2,1)}, bf16[512,896]{1,0:T(8,128)(2,1)S(1)}, u32[]{:S(2)}, u32[]{:S(2)}) collective-permute-start(bf16[512,896]{1,0:T(8,128)(2,1)} %shard_map.59), channel_id=1, source_target_pairs={{0,1},{1,0},{2,3},{3,2},{4,5},{5,4},{6,7},{7,6},{8,9},{9,8},{10,11... | collective-permute-start | bytes 2752520 | tf_op jit(solution)/shard_map/ppermute | solution.py:207
  152.1 6.9 %shard_map.56 = f32[512,896]{1,0:T(8,128)} custom-call(s32[2]{0:T(128)} %pad_add_fusion.y_ref, bf16[512,512]{1,0:T(8,128)(2,1)} %shard_map.55.refs_0_, bf16[512,512]{1,0:T(8,128)(2,1)} %copy-done.2, bf16[512,512]{1,0:T(8,128)(2,1)} %copy-done.4, bf16[512,512]{1,0:T(8,128)(2,1)} %copy-done.3, bf16[512,7168]{1,0:T(8,128)(2,1)} %refs_2_.1, ...), custom_call_target="tpu_custom_call" | custom-call | flops 1879048192 | bytes 7602176 | tf_op jit(solution)/shard_map/pallas_call | solution.py:111
  159.0 9.0 %collective-permute-done.6 = bf16[512,896]{1,0:T(8,128)(2,1)S(1)} collective-permute-done((bf16[512,896]{1,0:T(8,128)(2,1)}, bf16[512,896]{1,0:T(8,128)(2,1)S(1)}, u32[]{:S(2)}, u32[]{:S(2)}) %collective-permute-start.6) | collective-permute-done | bytes 917536 | tf_op jit(solution)/shard_map/ppermute | solution.py:207
  167.9 2.6 %add_convert_fusion = bf16[512,896]{1,0:T(8,128)(2,1)} fusion(f32[512,896]{1,0:T(8,128)} %shard_map.56, bf16[512,896]{1,0:T(8,128)(2,1)S(1)} %collective-permute-done.6), kind=kLoop, calls=%fused_computation | loop fusion | flops 1376256 | bytes 3670016 | tf_op jit(solution)/shard_map/convert_element_type | solution.py:209
  (15 shorter events, 2.0 us)
Async XLA Ops:
  6.5 13.4 %copy-start = (s32[16,3]{0,1:T(4,128)S(1)}, s32[16,3]{0,1:T(4,128)}, u32[]{:S(2)}) copy-start(s32[16,3]{0,1:T(4,128)} %param.8) | copy-start | bytes 580
  6.5 96.7 %all-gather.2.cloned.1.call-start = ((), (), s32[]{:S(2)}) async-start(), calls=%async_computation | async-start | bytes 17825792 | tf_op jit(solution)/shard_map/all_gather | solution.py:178
  14.0 43.4 %collective-permute-start = (bf16[512,1792]{1,0:T(8,128)(2,1)}, bf16[512,1792]{1,0:T(8,128)(2,1)}, u32[]{:S(2)}, u32[]{:S(2)}) collective-permute-start(bf16[512,1792]{1,0:T(8,128)(2,1)} %get-tuple-element.15), channel_id=1, source_target_pairs={{0,2},{2,4},{4,6},{6,0},{1,3},{3,5},{5,7},{7,1},{8,10},{10,12},{12... | collective-permute-start | bytes 5505032 | tf_op jit(solution)/shard_map/ppermute | solution.py:187
  15.7 82.2 %collective-permute-start.1 = (bf16[512,1792]{1,0:T(8,128)(2,1)}, bf16[512,1792]{1,0:T(8,128)(2,1)S(1)}, u32[]{:S(2)}, u32[]{:S(2)}) collective-permute-start(bf16[512,1792]{1,0:T(8,128)(2,1)} %get-tuple-element.14), channel_id=1, source_target_pairs={{0,4},{2,6},{4,0},{6,2},{1,5},{3,7},{5,1},{7,3},{8,12},{10,14},{12... | collective-permute-start | bytes 5505032 | tf_op jit(solution)/shard_map/ppermute | solution.py:187
  18.6 79.3 %collective-permute-start.2 = (bf16[512,1792]{1,0:T(8,128)(2,1)}, bf16[512,1792]{1,0:T(8,128)(2,1)}, u32[]{:S(2)}, u32[]{:S(2)}) collective-permute-start(bf16[512,1792]{1,0:T(8,128)(2,1)} %get-tuple-element.13), channel_id=1, source_target_pairs={{0,6},{2,0},{4,2},{6,4},{1,7},{3,1},{5,3},{7,5},{8,14},{10,8},{12,... | collective-permute-start | bytes 5505032 | tf_op jit(solution)/shard_map/ppermute | solution.py:187
  97.9 14.4 %copy-start.1 = (bf16[512,1792]{1,0:T(8,128)(2,1)}, bf16[512,1792]{1,0:T(8,128)(2,1)S(1)}, u32[]{:S(2)}) copy-start(bf16[512,1792]{1,0:T(8,128)(2,1)S(1)} %collective-permute-done.1.refs_6_.refs_2_) | copy-start | bytes 5505028
  112.2 15.3 %collective-permute-start.3 = (bf16[512,512]{1,0:T(8,128)(2,1)}, bf16[512,512]{1,0:T(8,128)(2,1)S(1)}, u32[]{:S(2)}, u32[]{:S(2)}) collective-permute-start(bf16[512,512]{1,0:T(8,128)(2,1)} %shard_map.55.refs_0_), channel_id=1, source_target_pairs={{0,2},{2,4},{4,6},{6,0},{1,3},{3,5},{5,7},{7,1},{8,10},{10,12},{12... | collective-permute-start | bytes 1572872 | tf_op jit(solution)/shard_map/ppermute | solution.py:192
  113.7 24.5 %collective-permute-start.5 = (bf16[512,512]{1,0:T(8,128)(2,1)}, bf16[512,512]{1,0:T(8,128)(2,1)S(1)}, u32[]{:S(2)}, u32[]{:S(2)}) collective-permute-start(bf16[512,512]{1,0:T(8,128)(2,1)} %shard_map.55.refs_0_), channel_id=1, source_target_pairs={{0,6},{2,0},{4,2},{6,4},{1,7},{3,1},{5,3},{7,5},{8,14},{10,8},{12,... | collective-permute-start | bytes 1572872 | tf_op jit(solution)/shard_map/ppermute | solution.py:192
  115.5 28.0 %collective-permute-start.4 = (bf16[512,512]{1,0:T(8,128)(2,1)}, bf16[512,512]{1,0:T(8,128)(2,1)S(1)}, u32[]{:S(2)}, u32[]{:S(2)}) collective-permute-start(bf16[512,512]{1,0:T(8,128)(2,1)} %shard_map.55.refs_0_), channel_id=1, source_target_pairs={{0,4},{2,6},{4,0},{6,2},{1,5},{3,7},{5,1},{7,3},{8,12},{10,14},{12... | collective-permute-start | bytes 1572872 | tf_op jit(solution)/shard_map/ppermute | solution.py:192
  127.5 0.8 copy-start.2
  138.2 0.8 copy-start.3
  143.5 0.8 copy-start.4
  148.5 19.4 %collective-permute-start.6 = (bf16[512,896]{1,0:T(8,128)(2,1)}, bf16[512,896]{1,0:T(8,128)(2,1)S(1)}, u32[]{:S(2)}, u32[]{:S(2)}) collective-permute-start(bf16[512,896]{1,0:T(8,128)(2,1)} %shard_map.59), channel_id=1, source_target_pairs={{0,1},{1,0},{2,3},{3,2},{4,5},{5,4},{6,7},{7,6},{8,9},{9,8},{10,11... | collective-permute-start | bytes 2752520 | tf_op jit(solution)/shard_map/ppermute | solution.py:207
Sparse Core Ops, SparseCore 0:
  9.1 94.1 all-gather.1

commit v16 on v15

--- a/solution.py
+++ b/solution.py
@@ -133,20 +133,21 @@
     o_ref[...] = acc.astype(o_ref.dtype)
 
 
-def project_part(meta, partial, pieces, weights, local_first, halves, out_dtype):
+def project_part(meta, partial, pieces, weights, local_first, halves, out_dtype, part=(0, 1)):
     rows, inner = pieces[0].shape
+    rows = rows // part[1]
     col_width = weights[-1].shape[1] // halves
     w_specs = [pl.BlockSpec((inner, col_width), lambda i, m: (0, m[1])) for _ in weights]
     if local_first:
         w_specs[0] = pl.BlockSpec((inner, col_width), lambda i, m: (0, m[0] * halves + m[1]))
-    full = pl.BlockSpec((rows, col_width), lambda i, m: (0, 0))
+    full = pl.BlockSpec((rows, col_width), lambda i, m: (part[0], 0))
     grid_spec = pltpu.PrefetchScalarGridSpec(
         num_scalar_prefetch=1,
         grid=(1,),
         in_specs=([full] if partial is not None else [])
-        + [pl.BlockSpec((rows, inner), lambda i, m: (0, 0)) for _ in pieces]
+        + [pl.BlockSpec((rows, inner), lambda i, m: (part[0], 0)) for _ in pieces]
         + w_specs,
-        out_specs=full,
+        out_specs=pl.BlockSpec((rows, col_width), lambda i, m: (0, 0)),
     )
     extra = [partial] if partial is not None else []
     return pl.pallas_call(
@@ -201,10 +202,19 @@
     near = project_part(
         other, early, pieces[3:], list(received[2:]), False, xh_size, jnp.float32
     )
-    sent = project_part(
-        other, near, pieces[2:3], list(received[1:2]), False, xh_size, queries.dtype
-    )
-    got = lax.ppermute(sent, "xh", [(i, xh_size - 1 - i) for i in range(xh_size)])
+    swap = [(i, xh_size - 1 - i) for i in range(xh_size)]
+    got = [
+        lax.ppermute(
+            project_part(
+                other, near, pieces[2:3], list(received[1:2]), False, xh_size, queries.dtype,
+                (r, 2),
+            ),
+            "xh",
+            swap,
+        )
+        for r in range(2)
+    ]
+    got = jnp.concatenate(got)
     own = project(mine, pieces, out_weight, received, xh_size, jnp.float32)
     return (own + got.astype(jnp.float32)).astype(queries.dtype)
 

time: 178 us -> 178 us (level)
  waiting for transfers between devices: 106 us -> 103 us
  Pallas kernels: 29.6 us -> 32.3 us
    ppermute x1 -> x2, waiting for transfers between devices: 8.95 us -> 5.55 us  [per_device(): lax.ppermute(project_part(other, near, pieces[2:3], list(received[1:2]),...]
    pallas_call x3 -> x4, Pallas kernels: 13.7 us -> 16.3 us  [project_part(): pl.pallas_call(functools.partial(part_kernel, count=len(pieces), has_part...]
  transfers between devices with their start and end apart: 8 -> 9, of which waited for: 6 -> 7; matrix products, arithmetic and copies ran while one was open for 4% -> 4% of each run, Pallas kernels for 9% -> 11%
where the time goes in v16:
time: 178 us; the launch traced here: 177 us
  waiting for transfers between devices  103 us (58%)
  Pallas kernels  32.3 us (18%)
  starting transfers between devices  14.5 us (8%)
  between operations  13.5 us (8%)
  local copies, waits for them, and re-layouts  7.73 us (4%)
  other arithmetic  6.66 us (4%)
    ppermute x3, waiting for transfers between devices, per_device(): lax.ppermute(sent, 'y', [(i, (i + shift) % y_size) for i in range(y_size)])  77.2 us
    pallas_call x4, Pallas kernels, project_part(): pl.pallas_call(functools.partial(part_kernel, count=len(pieces), has_part...  16.3 us
    ppermute x3, waiting for transfers between devices, per_device(): lax.ppermute(attended, 'y', [(i, (i + shift) % y_size) for i in range(y_s...  14.5 us
    pallas_call x1, Pallas kernels, attend(): pl.pallas_call(functools.partial(attend_kernel, topk=topk, head_count=hea...  9.06 us
    pallas_call x1, Pallas kernels, project(): pl.pallas_call(functools.partial(project_kernel, shifts=shifts), grid_spe...  6.92 us
    ppermute x3, starting transfers between devices, per_device(): lax.ppermute(sent, 'y', [(i, (i + shift) % y_size) for i in range(y_size)])  5.91 us
    ppermute x2, waiting for transfers between devices, per_device(): lax.ppermute(project_part(other, near, pieces[2:3], list(received[1:2]),...  5.55 us
    all_gather x1, waiting for transfers between devices, per_device(): lax.all_gather(jnp.concatenate([key_rows, value_rows], axis=1), CTX, axis...  5.34 us
  transfers between devices with their start and end apart: 9, of which 7 were waited for; matrix products, arithmetic and copies ran while one was open for 4% of the time, Pallas kernels for 11%

profile of v16, /device:TPU:0, one launch (start us, length us, event | category | flops | bytes accessed | tf_op | source)
XLA Modules:
  0.0 177.2 jit_solution(3170685075760018504)
XLA Ops:
  6.5 2.3 %pad_maximum_fusion = bf16[512,1024]{1,0:T(8,128)(2,1)} fusion(bf16[512,512]{1,0:T(8,128)(2,1)} %param.7, bf16[512,512]{1,0:T(8,128)(2,1)} %param.6), kind=kLoop, calls=%fused_computation.1 | loop fusion | flops 2097152 | bytes 2097152 | tf_op jit(solution)/shard_map/concatenate | solution.py:180
  8.9 5.2 %constant_dynamic-slice_fusion = (bf16[512,1792]{1,0:T(8,128)(2,1)}, bf16[512,1792]{1,0:T(8,128)(2,1)}, bf16[512,1792]{1,0:T(8,128)(2,1)}) fusion(bf16[512,7168]{1,0:T(8,128)(2,1)} %refs_2_.1, s32[]{:T(128)S(6)} %select_n.33, s32[]{:T(128)S(6)} %select_n.31, s32[]{:T(128)S(6)} %select_n.29), kind=kLoop, calls=%fused_computation.3 | loop fusion | bytes 11010060 | tf_op jit(solution)/shard_map/dynamic_slice | solution.py:186
  14.1 1.7 collective-permute-start
  15.7 2.9 %collective-permute-start.1 = (bf16[512,1792]{1,0:T(8,128)(2,1)}, bf16[512,1792]{1,0:T(8,128)(2,1)S(1)}, u32[]{:S(2)}, u32[]{:S(2)}) collective-permute-start(bf16[512,1792]{1,0:T(8,128)(2,1)} %get-tuple-element.14), channel_id=1, source_target_pairs={{0,4},{2,6},{4,0},{6,2},{1,5},{3,7},{5,1},{7,3},{8,12},{10,14},{12... | collective-permute-start | bytes 5505032 | tf_op jit(solution)/shard_map/ppermute | solution.py:188
  18.6 1.3 collective-permute-start.2
  20.7 36.8 %collective-permute-done.refs_5_.refs_3_ = bf16[512,1792]{1,0:T(8,128)(2,1)} collective-permute-done((bf16[512,1792]{1,0:T(8,128)(2,1)}, bf16[512,1792]{1,0:T(8,128)(2,1)}, u32[]{:S(2)}, u32[]{:S(2)}) %collective-permute-start) | collective-permute-done | bytes 1835040 | tf_op jit(solution)/shard_map/ppermute | solution.py:188
  57.5 40.4 %collective-permute-done.1.refs_6_.refs_2_ = bf16[512,1792]{1,0:T(8,128)(2,1)S(1)} collective-permute-done((bf16[512,1792]{1,0:T(8,128)(2,1)}, bf16[512,1792]{1,0:T(8,128)(2,1)S(1)}, u32[]{:S(2)}, u32[]{:S(2)}) %collective-permute-start.1) | collective-permute-done | bytes 1835040 | tf_op jit(solution)/shard_map/ppermute | solution.py:188
  97.9 5.3 %all-gather.2.cloned.1.call-done.refs_0_.refs_1_.refs_2_.refs_3_.refs_4_.refs_5_ = bf16[8192,1024]{1,0:T(8,128)(2,1)} async-done(((bf16[512,1024]{1,0:T(8,128)(2,1)}), bf16[8192,1024]{1,0:T(8,128)(2,1)}) %all-gather.2.cloned.1.call-update) | async-done | bytes 16777232 | tf_op jit(solution)/shard_map/all_gather | solution.py:179
  103.2 9.1 %shard_map.55.refs_0_ = bf16[512,512]{1,0:T(8,128)(2,1)} custom-call(s32[4]{0:T(128)} %pad_add_fusion.1.meta_ref, bf16[512,512]{1,0:T(8,128)(2,1)} %q_ref.1, bf16[8192,1024]{1,0:T(8,128)(2,1)} %all-gather.2.cloned.1.call-done.refs_0_.refs_1_.refs_2_.refs_3_.refs_4_.refs_5_, ...), custom_call_target="tpu_custom_call" | custom-call | flops 1610612736 | bytes 4194304 | tf_op jit(solution)/shard_map/pallas_call | solution.py:87
  112.3 1.5 collective-permute-start.3
  113.8 1.8 collective-permute-start.5
  115.5 1.8 %collective-permute-start.4 = (bf16[512,512]{1,0:T(8,128)(2,1)}, bf16[512,512]{1,0:T(8,128)(2,1)S(1)}, u32[]{:S(2)}, u32[]{:S(2)}) collective-permute-start(bf16[512,512]{1,0:T(8,128)(2,1)} %shard_map.55.refs_0_), channel_id=1, source_target_pairs={{0,4},{2,6},{4,0},{6,2},{1,5},{3,7},{5,1},{7,3},{8,12},{10,14},{12... | collective-permute-start | bytes 1572872 | tf_op jit(solution)/shard_map/ppermute | solution.py:193
  117.9 9.6 %collective-permute-done.3.refs_1_ = bf16[512,512]{1,0:T(8,128)(2,1)S(1)} collective-permute-done((bf16[512,512]{1,0:T(8,128)(2,1)}, bf16[512,512]{1,0:T(8,128)(2,1)S(1)}, u32[]{:S(2)}, u32[]{:S(2)}) %collective-permute-start.3) | collective-permute-done | bytes 524320 | tf_op jit(solution)/shard_map/ppermute | solution.py:193
  128.3 4.9 %shard_map.57.refs_0_ = f32[512,896]{1,0:T(8,128)} custom-call(s32[2]{0:T(128)} %pad_add_fusion.2.meta_ref, bf16[512,512]{1,0:T(8,128)(2,1)} %shard_map.55.refs_0_, bf16[512,512]{1,0:T(8,128)(2,1)} %copy-done.3, bf16[512,7168]{1,0:T(8,128)(2,1)} %refs_2_.1, bf16[512,1792]{1,0:T(8,128)(2,1)} %collective-permute-done.refs_5_.refs_3_), custom_call_target="tpu_custom_call" | custom-call | flops 939524096 | bytes 4718592 | tf_op jit(solution)/shard_map/pallas_call | solution.py:153
  133.3 4.9 %collective-permute-done.5.refs_3_.refs_1_ = bf16[512,512]{1,0:T(8,128)(2,1)S(1)} collective-permute-done((bf16[512,512]{1,0:T(8,128)(2,1)}, bf16[512,512]{1,0:T(8,128)(2,1)S(1)}, u32[]{:S(2)}, u32[]{:S(2)}) %collective-permute-start.5) | collective-permute-done | bytes 524320 | tf_op jit(solution)/shard_map/ppermute | solution.py:193
  138.2 0.8 copy-done.4
  139.0 4.5 %shard_map.58.refs_0_ = f32[512,896]{1,0:T(8,128)} custom-call(s32[2]{0:T(128)} %pad_add_fusion.2.meta_ref, f32[512,896]{1,0:T(8,128)} %shard_map.57.refs_0_, bf16[512,512]{1,0:T(8,128)(2,1)} %copy-done.4, bf16[512,1792]{1,0:T(8,128)(2,1)} %collective-permute-done.2.refs_7_.refs_2_), custom_call_target="tpu_custom_call" | custom-call | flops 469762048 | bytes 5111808 | tf_op jit(solution)/shard_map/pallas_call | solution.py:153
  143.5 0.8 copy-done.2
  144.3 3.4 %shard_map.59 = bf16[256,896]{1,0:T(8,128)(2,1)} custom-call(s32[2]{0:T(128)} %pad_add_fusion.2.meta_ref, f32[512,896]{1,0:T(8,128)} %shard_map.58.refs_0_, bf16[512,512]{1,0:T(8,128)(2,1)} %copy-done.2, bf16[512,1792]{1,0:T(8,128)(2,1)} %copy-done.1), custom_call_target="tpu_custom_call" | custom-call | flops 234881024 | bytes 2555904 | tf_op jit(solution)/shard_map/pallas_call | solution.py:153
  147.7 3.0 %collective-permute-start.6 = (bf16[256,896]{1,0:T(8,128)(2,1)}, bf16[256,896]{1,0:T(8,128)(2,1)S(1)}, u32[]{:S(2)}, u32[]{:S(2)}) collective-permute-start(bf16[256,896]{1,0:T(8,128)(2,1)} %shard_map.59), channel_id=1, source_target_pairs={{0,1},{1,0},{2,3},{3,2},{4,5},{5,4},{6,7},{7,6},{8,9},{9,8},{10,11... | collective-permute-start | bytes 1376264 | tf_op jit(solution)/shard_map/ppermute | solution.py:207
  150.7 3.4 %shard_map.60 = bf16[256,896]{1,0:T(8,128)(2,1)} custom-call(s32[2]{0:T(128)} %pad_add_fusion.2.meta_ref, f32[512,896]{1,0:T(8,128)} %shard_map.58.refs_0_, bf16[512,512]{1,0:T(8,128)(2,1)} %copy-done.2, bf16[512,1792]{1,0:T(8,128)(2,1)} %copy-done.1), custom_call_target="tpu_custom_call" | custom-call | flops 234881024 | bytes 2555904 | tf_op jit(solution)/shard_map/pallas_call | solution.py:153
  155.3 6.9 %shard_map.56 = f32[512,896]{1,0:T(8,128)} custom-call(s32[2]{0:T(128)} %pad_add_fusion.y_ref, bf16[512,512]{1,0:T(8,128)(2,1)} %shard_map.55.refs_0_, bf16[512,512]{1,0:T(8,128)(2,1)} %copy-done.3, bf16[512,512]{1,0:T(8,128)(2,1)} %copy-done.2, bf16[512,512]{1,0:T(8,128)(2,1)} %copy-done.4, bf16[512,7168]{1,0:T(8,128)(2,1)} %refs_2_.1, ...), custom_call_target="tpu_custom_call" | custom-call | flops 1879048192 | bytes 7602176 | tf_op jit(solution)/shard_map/pallas_call | solution.py:111
  162.4 5.4 %collective-permute-done.7 = bf16[256,896]{1,0:T(8,128)(2,1)S(1)} collective-permute-done((bf16[256,896]{1,0:T(8,128)(2,1)}, bf16[256,896]{1,0:T(8,128)(2,1)S(1)}, u32[]{:S(2)}, u32[]{:S(2)}) %collective-permute-start.7) | collective-permute-done | bytes 458784 | tf_op jit(solution)/shard_map/ppermute | solution.py:207
  167.8 2.6 %add_convert_fusion = bf16[512,896]{1,0:T(8,128)(2,1)} fusion(f32[512,896]{1,0:T(8,128)} %shard_map.56, bf16[256,896]{1,0:T(8,128)(2,1)S(1)} %collective-permute-done.7, bf16[256,896]{1,0:T(8,128)(2,1)S(1)} %collective-permute-done.6), kind=kLoop, calls=%fused_computation | loop fusion | flops 2752512 | bytes 3670016 | tf_op jit(solution)/shard_map/convert_element_type | solution.py:219
  (18 shorter events, 3.5 us)
Async XLA Ops:
  6.5 13.4 %copy-start = (s32[16,3]{0,1:T(4,128)S(1)}, s32[16,3]{0,1:T(4,128)}, u32[]{:S(2)}) copy-start(s32[16,3]{0,1:T(4,128)} %param.8) | copy-start | bytes 580
  6.5 96.7 %all-gather.2.cloned.1.call-start = ((), (), s32[]{:S(2)}) async-start(), calls=%async_computation | async-start | bytes 17825792 | tf_op jit(solution)/shard_map/all_gather | solution.py:179
  14.1 43.4 %collective-permute-start = (bf16[512,1792]{1,0:T(8,128)(2,1)}, bf16[512,1792]{1,0:T(8,128)(2,1)}, u32[]{:S(2)}, u32[]{:S(2)}) collective-permute-start(bf16[512,1792]{1,0:T(8,128)(2,1)} %get-tuple-element.15), channel_id=1, source_target_pairs={{0,2},{2,4},{4,6},{6,0},{1,3},{3,5},{5,7},{7,1},{8,10},{10,12},{12... | collective-permute-start | bytes 5505032 | tf_op jit(solution)/shard_map/ppermute | solution.py:188
  15.7 82.2 %collective-permute-start.1 = (bf16[512,1792]{1,0:T(8,128)(2,1)}, bf16[512,1792]{1,0:T(8,128)(2,1)S(1)}, u32[]{:S(2)}, u32[]{:S(2)}) collective-permute-start(bf16[512,1792]{1,0:T(8,128)(2,1)} %get-tuple-element.14), channel_id=1, source_target_pairs={{0,4},{2,6},{4,0},{6,2},{1,5},{3,7},{5,1},{7,3},{8,12},{10,14},{12... | collective-permute-start | bytes 5505032 | tf_op jit(solution)/shard_map/ppermute | solution.py:188
  18.6 79.3 %collective-permute-start.2 = (bf16[512,1792]{1,0:T(8,128)(2,1)}, bf16[512,1792]{1,0:T(8,128)(2,1)}, u32[]{:S(2)}, u32[]{:S(2)}) collective-permute-start(bf16[512,1792]{1,0:T(8,128)(2,1)} %get-tuple-element.13), channel_id=1, source_target_pairs={{0,6},{2,0},{4,2},{6,4},{1,7},{3,1},{5,3},{7,5},{8,14},{10,8},{12,... | collective-permute-start | bytes 5505032 | tf_op jit(solution)/shard_map/ppermute | solution.py:188
  97.9 14.4 %copy-start.1 = (bf16[512,1792]{1,0:T(8,128)(2,1)}, bf16[512,1792]{1,0:T(8,128)(2,1)S(1)}, u32[]{:S(2)}) copy-start(bf16[512,1792]{1,0:T(8,128)(2,1)S(1)} %collective-permute-done.1.refs_6_.refs_2_) | copy-start | bytes 5505028
  112.3 15.2 %collective-permute-start.3 = (bf16[512,512]{1,0:T(8,128)(2,1)}, bf16[512,512]{1,0:T(8,128)(2,1)S(1)}, u32[]{:S(2)}, u32[]{:S(2)}) collective-permute-start(bf16[512,512]{1,0:T(8,128)(2,1)} %shard_map.55.refs_0_), channel_id=1, source_target_pairs={{0,2},{2,4},{4,6},{6,0},{1,3},{3,5},{5,7},{7,1},{8,10},{10,12},{12... | collective-permute-start | bytes 1572872 | tf_op jit(solution)/shard_map/ppermute | solution.py:193
  113.8 24.4 %collective-permute-start.5 = (bf16[512,512]{1,0:T(8,128)(2,1)}, bf16[512,512]{1,0:T(8,128)(2,1)S(1)}, u32[]{:S(2)}, u32[]{:S(2)}) collective-permute-start(bf16[512,512]{1,0:T(8,128)(2,1)} %shard_map.55.refs_0_), channel_id=1, source_target_pairs={{0,6},{2,0},{4,2},{6,4},{1,7},{3,1},{5,3},{7,5},{8,14},{10,8},{12,... | collective-permute-start | bytes 1572872 | tf_op jit(solution)/shard_map/ppermute | solution.py:193
  115.5 28.0 %collective-permute-start.4 = (bf16[512,512]{1,0:T(8,128)(2,1)}, bf16[512,512]{1,0:T(8,128)(2,1)S(1)}, u32[]{:S(2)}, u32[]{:S(2)}) collective-permute-start(bf16[512,512]{1,0:T(8,128)(2,1)} %shard_map.55.refs_0_), channel_id=1, source_target_pairs={{0,4},{2,6},{4,0},{6,2},{1,5},{3,7},{5,1},{7,3},{8,12},{10,14},{12... | collective-permute-start | bytes 1572872 | tf_op jit(solution)/shard_map/ppermute | solution.py:193
  127.5 0.8 copy-start.3
  138.2 0.8 copy-start.4
  143.5 0.8 copy-start.2
  147.7 14.7 %collective-permute-start.6 = (bf16[256,896]{1,0:T(8,128)(2,1)}, bf16[256,896]{1,0:T(8,128)(2,1)S(1)}, u32[]{:S(2)}, u32[]{:S(2)}) collective-permute-start(bf16[256,896]{1,0:T(8,128)(2,1)} %shard_map.59), channel_id=1, source_target_pairs={{0,1},{1,0},{2,3},{3,2},{4,5},{5,4},{6,7},{7,6},{8,9},{9,8},{10,11... | collective-permute-start | bytes 1376264 | tf_op jit(solution)/shard_map/ppermute | solution.py:207
  154.1 13.6 %collective-permute-start.7 = (bf16[256,896]{1,0:T(8,128)(2,1)}, bf16[256,896]{1,0:T(8,128)(2,1)S(1)}, u32[]{:S(2)}, u32[]{:S(2)}) collective-permute-start(bf16[256,896]{1,0:T(8,128)(2,1)} %shard_map.60), channel_id=1, source_target_pairs={{0,1},{1,0},{2,3},{3,2},{4,5},{5,4},{6,7},{7,6},{8,9},{9,8},{10,11... | collective-permute-start | bytes 1376264 | tf_op jit(solution)/shard_map/ppermute | solution.py:207
Sparse Core Ops, SparseCore 0:
  9.1 94.1 all-gather.1

commit v17 on v9

--- a/solution.py
+++ b/solution.py
@@ -55,31 +55,22 @@
             att_ref[:, cols] = (acc / row_sum).astype(att_ref.dtype)
 
 
-def project_kernel(y_ref, *refs, shifts):
-    a_refs = refs[:shifts]
-    w_refs = refs[shifts : 2 * shifts]
-    o_ref = refs[2 * shifts]
-    acc = jnp.dot(a_refs[0][...], w_refs[0][...], preferred_element_type=jnp.float32)
-    for sh in range(1, shifts):
-        acc = acc + jnp.dot(a_refs[sh][...], w_refs[sh][...], preferred_element_type=jnp.float32)
-    o_ref[...] = acc.astype(o_ref.dtype)
-
-
-def attend(meta, queries, kv_piece, topk):
+def attend(meta, queries, kv_piece, topk, half, parts):
     row_count, feat_width = queries.shape
-    head_count = feat_width // HD
+    width = feat_width // parts
+    head_count = width // HD
 
     def k_map(s):
-        return lambda j, m: (m[s], 0)
+        return lambda j, m: (m[s], half)
 
     def v_map(s):
-        return lambda j, m: (m[s], 1)
-
-    blk = (BLOCK, feat_width)
+        return lambda j, m: (m[s], parts + half)
+
+    blk = (BLOCK, width)
     grid_spec = pltpu.PrefetchScalarGridSpec(
         num_scalar_prefetch=1,
         grid=(1,),
-        in_specs=[pl.BlockSpec(blk, lambda j, m: (0, 0))]
+        in_specs=[pl.BlockSpec(blk, lambda j, m: (0, half))]
         + [pl.BlockSpec(blk, k_map(s)) for s in range(topk)]
         + [pl.BlockSpec(blk, v_map(s)) for s in range(topk)],
         out_specs=pl.BlockSpec(blk, lambda j, m: (0, 0)),
@@ -87,38 +78,59 @@
     return pl.pallas_call(
         functools.partial(attend_kernel, topk=topk, head_count=head_count),
         grid_spec=grid_spec,
-        out_shape=jax.ShapeDtypeStruct((row_count, feat_width), queries.dtype),
+        out_shape=jax.ShapeDtypeStruct((row_count, width), queries.dtype),
         cost_estimate=pl.CostEstimate(
             flops=4 * head_count * BLOCK * topk * BLOCK * HD,
             transcendentals=head_count * BLOCK * topk * BLOCK,
-            bytes_accessed=queries.size * 2 * (2 + 2 * topk),
+            bytes_accessed=row_count * width * 2 * (2 + 2 * topk),
         ),
     )(meta, queries, *([kv_piece] * (2 * topk)))
 
 
-def project(meta, pieces, out_weight, received, halves, out_dtype):
-    rows, inner = pieces[0].shape
-    shifts = len(received) + 1
-    col_width = received[0].shape[1] // halves
+def part_kernel(meta_ref, *refs, count, has_partial):
+    start = 1 if has_partial else 0
+    a_refs = refs[start : start + count]
+    w_refs = refs[start + count : start + 2 * count]
+    o_ref = refs[start + 2 * count]
+    acc = refs[0][...] if has_partial else None
+    for a_ref, w_ref in zip(a_refs, w_refs):
+        term = jnp.dot(a_ref[...], w_ref[...], preferred_element_type=jnp.float32)
+        acc = term if acc is None else acc + term
+    o_ref[...] = acc.astype(o_ref.dtype)
+
+
+def project_part(meta, partial, terms, halves, out_dtype, part=(0, 1)):
+    rows, inner = terms[0][0].shape
+    rows = rows // part[1]
+    col_width = terms[-1][1].shape[1] // halves
+
+    def w_spec(is_local, hp):
+        if is_local:
+            return pl.BlockSpec((inner, col_width), lambda i, m: (hp, m[0] * halves + m[1]))
+        return pl.BlockSpec((inner, col_width), lambda i, m: (hp, m[1]))
+
+    full = pl.BlockSpec((rows, col_width), lambda i, m: (part[0], 0))
     grid_spec = pltpu.PrefetchScalarGridSpec(
         num_scalar_prefetch=1,
         grid=(1,),
-        in_specs=[pl.BlockSpec((rows, inner), lambda i, m: (0, 0)) for _ in range(shifts)]
-        + [pl.BlockSpec((inner, col_width), lambda i, m: (0, m[0] * halves + m[1]))]
-        + [pl.BlockSpec((inner, col_width), lambda i, m: (0, m[1])) for _ in received],
+        in_specs=([full] if partial is not None else [])
+        + [pl.BlockSpec((rows, inner), lambda i, m: (part[0], 0)) for _ in terms]
+        + [w_spec(is_local, hp) for _, _, is_local, hp in terms],
         out_specs=pl.BlockSpec((rows, col_width), lambda i, m: (0, 0)),
     )
+    extra = [partial] if partial is not None else []
+    count = len(terms)
     return pl.pallas_call(
-        functools.partial(project_kernel, shifts=shifts),
+        functools.partial(part_kernel, count=count, has_partial=partial is not None),
         grid_spec=grid_spec,
         out_shape=jax.ShapeDtypeStruct((rows, col_width), out_dtype),
         cost_estimate=pl.CostEstimate(
-            flops=2 * rows * inner * shifts * col_width,
+            flops=2 * rows * inner * count * col_width,
             transcendentals=0,
-            bytes_accessed=rows * inner * shifts * 2 + shifts * inner * col_width * 2
-            + rows * col_width * jnp.dtype(out_dtype).itemsize,
+            bytes_accessed=rows * inner * count * 2 + count * inner * col_width * 2
+            + rows * col_width * (4 * len(extra) + jnp.dtype(out_dtype).itemsize),
         ),
-    )(meta, *pieces, out_weight, *received)
+    )(meta, *extra, *[t[0] for t in terms], *[t[1] for t in terms])
 
 
 CTX = ("xl", "z", "core")
@@ -146,17 +158,36 @@
             lax.ppermute(sent, "y", [(i, (i + shift) % y_size) for i in range(y_size)])
         )
     kv_piece, received = lax.optimization_barrier((kv_piece, received))
-    attended = attend(meta, queries, kv_piece, topk)
-    pieces = [attended] + [
-        lax.ppermute(attended, "y", [(i, (i + shift) % y_size) for i in range(y_size)])
-        for shift in range(1, y_size)
-    ]
+    parts = 2
+    by_shift = [[] for _ in range(y_size)]
+    for half in range(parts):
+        attended = attend(meta, queries, kv_piece, topk, half, parts)
+        by_shift[0].append(attended)
+        for shift in range(1, y_size):
+            by_shift[shift].append(
+                lax.ppermute(attended, "y", [(i, (i + shift) % y_size) for i in range(y_size)])
+            )
+    weight_of = [out_weight] + list(received)
+
+    def terms(shift):
+        return [(by_shift[shift][h], weight_of[shift], shift == 0, h) for h in range(parts)]
+
     xh_place = lax.axis_index("xh")
     other = jnp.stack([y_place, xh_size - 1 - xh_place]).astype(jnp.int32)
     mine = jnp.stack([y_place, xh_place]).astype(jnp.int32)
-    sent = project(other, pieces, out_weight, received, xh_size, queries.dtype)
-    got = lax.ppermute(sent, "xh", [(i, xh_size - 1 - i) for i in range(xh_size)])
-    own = project(mine, pieces, out_weight, received, xh_size, jnp.float32)
+    early = project_part(other, None, terms(0) + terms(1), xh_size, jnp.float32)
+    near = project_part(other, early, terms(3), xh_size, jnp.float32)
+    swap = [(i, xh_size - 1 - i) for i in range(xh_size)]
+    got = [
+        lax.ppermute(
+            project_part(other, near, terms(2), xh_size, queries.dtype, (r, 2)), "xh", swap
+        )
+        for r in range(2)
+    ]
+    got = jnp.concatenate(got)
+    own = project_part(
+        mine, None, terms(0) + terms(1) + terms(2) + terms(3), xh_size, jnp.float32
+    )
     return (own + got.astype(jnp.float32)).astype(queries.dtype)
 
 

time: 181 us -> 180 us (level)
  waiting for transfers between devices: 116 us -> 96.4 us
  Pallas kernels: 22.5 us -> 35.4 us
  starting transfers between devices: 14.5 us -> 18.2 us
    ppermute x1 -> x2, waiting for transfers between devices: 12.7 us -> 2.09 us  [per_device(): lax.ppermute(project_part(other, near, terms(2), xh_size, queries.dtype,...]
    pallas_call x2 -> x5, Pallas kernels: 13.5 us -> 23.1 us  [project_part(): pl.pallas_call(functools.partial(part_kernel, count=count, has_partial=pa...]
    ppermute x3 -> x6, waiting for transfers between devices: 21.2 us -> 11.8 us  [per_device(): lax.ppermute(attended, 'y', [(i, (i + shift) % y_size) for i in range(y_s...]
    pallas_call x1 -> x2, Pallas kernels: 9.02 us -> 12.3 us  [attend(): pl.pallas_call(functools.partial(attend_kernel, topk=topk, head_count=hea...]
    ppermute x3 -> x6, starting transfers between devices: 5.65 us -> 8.79 us  [per_device(): lax.ppermute(attended, 'y', [(i, (i + shift) % y_size) for i in range(y_s...]
  transfers between devices with their start and end apart: 8 -> 12, of which waited for: 6 -> 6; matrix products, arithmetic and copies ran while one was open for 4% -> 4% of each run, Pallas kernels for 4% -> 14%
where the time goes in v17:
time: 180 us; the launch traced here: 178 us
  waiting for transfers between devices  96.4 us (54%)
  Pallas kernels  35.4 us (20%)
  starting transfers between devices  18.2 us (10%)
  between operations  13.5 us (8%)
  local copies, waits for them, and re-layouts  8.18 us (5%)
  other arithmetic  6.82 us (4%)
    ppermute x3, waiting for transfers between devices, per_device(): lax.ppermute(sent, 'y', [(i, (i + shift) % y_size) for i in range(y_size)])  77.1 us
    pallas_call x5, Pallas kernels, project_part(): pl.pallas_call(functools.partial(part_kernel, count=count, has_partial=pa...  23.1 us
    pallas_call x2, Pallas kernels, attend(): pl.pallas_call(functools.partial(attend_kernel, topk=topk, head_count=hea...  12.3 us
    ppermute x6, waiting for transfers between devices, per_device(): lax.ppermute(attended, 'y', [(i, (i + shift) % y_size) for i in range(y_s...  11.8 us
    ppermute x6, starting transfers between devices, per_device(): lax.ppermute(attended, 'y', [(i, (i + shift) % y_size) for i in range(y_s...  8.79 us
    ppermute x3, starting transfers between devices, per_device(): lax.ppermute(sent, 'y', [(i, (i + shift) % y_size) for i in range(y_size)])  5.91 us
    all_gather x1, waiting for transfers between devices, per_device(): lax.all_gather(jnp.concatenate([key_rows, value_rows], axis=1), CTX, axis...  5.37 us
    dynamic_slice x1, local copies, waits for them, and re-layouts, per_device(): lax.dynamic_slice_in_dim(out_weight, dest * group_width, group_width, 1)  5.13 us
  transfers between devices with their start and end apart: 12, of which 6 were waited for; matrix products, arithmetic and copies ran while one was open for 4% of the time, Pallas kernels for 14%

profile of v17, /device:TPU:0, one launch (start us, length us, event | category | flops | bytes accessed | tf_op | source)
XLA Modules:
  0.0 178.5 jit_solution(2810922023653073760)
XLA Ops:
  6.5 2.3 %pad_maximum_fusion = bf16[512,1024]{1,0:T(8,128)(2,1)} fusion(bf16[512,512]{1,0:T(8,128)(2,1)} %param.7, bf16[512,512]{1,0:T(8,128)(2,1)} %param.6), kind=kLoop, calls=%fused_computation.1 | loop fusion | flops 2097152 | bytes 2097152 | tf_op jit(solution)/shard_map/concatenate | solution.py:150
  8.9 5.1 %constant_dynamic-slice_fusion = (bf16[512,1792]{1,0:T(8,128)(2,1)}, bf16[512,1792]{1,0:T(8,128)(2,1)}, bf16[512,1792]{1,0:T(8,128)(2,1)}) fusion(bf16[512,7168]{1,0:T(8,128)(2,1)} %refs_5_.1, s32[]{:T(128)S(6)} %select_n.33, s32[]{:T(128)S(6)} %select_n.31, s32[]{:T(128)S(6)} %select_n.29), kind=kLoop, calls=%fused_computation.3 | loop fusion | bytes 11010060 | tf_op jit(solution)/shard_map/dynamic_slice | solution.py:156
  14.0 1.7 collective-permute-start
  15.7 2.9 %collective-permute-start.1 = (bf16[512,1792]{1,0:T(8,128)(2,1)}, bf16[512,1792]{1,0:T(8,128)(2,1)S(1)}, u32[]{:S(2)}, u32[]{:S(2)}) collective-permute-start(bf16[512,1792]{1,0:T(8,128)(2,1)} %get-tuple-element.14), channel_id=1, source_target_pairs={{0,4},{2,6},{4,0},{6,2},{1,5},{3,7},{5,1},{7,3},{8,12},{10,14},{12... | collective-permute-start | bytes 5505032 | tf_op jit(solution)/shard_map/ppermute | solution.py:158
  20.7 36.7 %collective-permute-done.refs_10_.refs_11_.refs_6_.refs_7_ = bf16[512,1792]{1,0:T(8,128)(2,1)} collective-permute-done((bf16[512,1792]{1,0:T(8,128)(2,1)}, bf16[512,1792]{1,0:T(8,128)(2,1)}, u32[]{:S(2)}, u32[]{:S(2)}) %collective-permute-start) | collective-permute-done | bytes 1835040 | tf_op jit(solution)/shard_map/ppermute | solution.py:158
  57.5 40.4 %collective-permute-done.1.refs_12_.refs_13_.refs_3_.refs_4_ = bf16[512,1792]{1,0:T(8,128)(2,1)S(1)} collective-permute-done((bf16[512,1792]{1,0:T(8,128)(2,1)}, bf16[512,1792]{1,0:T(8,128)(2,1)S(1)}, u32[]{:S(2)}, u32[]{:S(2)}) %collective-permute-start.1) | collective-permute-done | bytes 1835040 | tf_op jit(solution)/shard_map/ppermute | solution.py:158
  97.9 5.4 %all-gather.2.cloned.1.call-done.refs_0_.refs_1_.refs_2_.refs_3_.refs_4_.refs_5_ = bf16[8192,1024]{1,0:T(8,128)(2,1)} async-done(((bf16[512,1024]{1,0:T(8,128)(2,1)}), bf16[8192,1024]{1,0:T(8,128)(2,1)}) %all-gather.2.cloned.1.call-update) | async-done | bytes 16777232 | tf_op jit(solution)/shard_map/all_gather | solution.py:149
  103.2 6.2 %shard_map.56.refs_1_ = bf16[512,256]{1,0:T(8,128)(2,1)} custom-call(s32[4]{0:T(128)} %pad_add_fusion.1.meta_ref, bf16[512,512]{1,0:T(8,128)(2,1)} %q_ref.3, bf16[8192,1024]{1,0:T(8,128)(2,1)} %all-gather.2.cloned.1.call-done.refs_0_.refs_1_.refs_2_.refs_3_.refs_4_.refs_5_, ...), custom_call_target="tpu_custom_call" | custom-call | flops 805306368 | bytes 2097152 | tf_op jit(solution)/shard_map/pallas_call | solution.py:78
  109.4 1.5 collective-permute-start.4
  110.9 6.1 %shard_map.55.refs_0_ = bf16[512,256]{1,0:T(8,128)(2,1)} custom-call(s32[4]{0:T(128)} %pad_add_fusion.1.meta_ref, bf16[512,512]{1,0:T(8,128)(2,1)} %q_ref.3, bf16[8192,1024]{1,0:T(8,128)(2,1)} %all-gather.2.cloned.1.call-done.refs_0_.refs_1_.refs_2_.refs_3_.refs_4_.refs_5_, ...), custom_call_target="tpu_custom_call" | custom-call | flops 805306368 | bytes 2097152 | tf_op jit(solution)/shard_map/pallas_call | solution.py:78
  117.0 1.5 collective-permute-start.3
  118.5 1.8 collective-permute-start.8
  120.8 1.8 %collective-permute-start.6 = (bf16[512,256]{1,0:T(8,128)(2,1)S(1)}, bf16[512,256]{1,0:T(8,128)(2,1)S(1)}, u32[]{:S(2)}, u32[]{:S(2)}) collective-permute-start(bf16[512,256]{1,0:T(8,128)(2,1)S(1)} %copy-done.2), channel_id=1, source_target_pairs={{0,4},{2,6},{4,0},{6,2},{1,5},{3,7},{5,1},{7,3},{8,12},{10,14},{12... | collective-permute-start | bytes 786440 | tf_op jit(solution)/shard_map/ppermute | solution.py:168
  122.6 1.7 collective-permute-start.5
  125.0 2.7 %collective-permute-done.3.refs_2_ = bf16[512,256]{1,0:T(8,128)(2,1)S(1)} collective-permute-done((bf16[512,256]{1,0:T(8,128)(2,1)}, bf16[512,256]{1,0:T(8,128)(2,1)S(1)}, u32[]{:S(2)}, u32[]{:S(2)}) %collective-permute-start.3) | collective-permute-done | bytes 262176 | tf_op jit(solution)/shard_map/ppermute | solution.py:168
  128.3 4.9 %shard_map.58.refs_0_ = f32[512,896]{1,0:T(8,128)} custom-call(s32[2]{0:T(128)} %pad_add_fusion.2.meta_ref, bf16[512,256]{1,0:T(8,128)(2,1)} %shard_map.55.refs_0_, bf16[512,256]{1,0:T(8,128)(2,1)} %shard_map.56.refs_1_, bf16[512,256]{1,0:T(8,128)(2,1)} %copy-done.6, bf16[512,256]{1,0:T(8,128)(2,1)} %copy-done.5, bf16[512,7168]{1,0:T(8,128)(2,1)} %refs_5_.1, ...), custom_call_target="tpu_custom_call" | custom-call | flops 939524096 | bytes 4718592 | tf_op jit(solution)/shard_map/pallas_call | solution.py:123
  133.2 9.1 %collective-permute-done.7.refs_6_.refs_1_ = bf16[512,256]{1,0:T(8,128)(2,1)S(1)} collective-permute-done((bf16[512,256]{1,0:T(8,128)(2,1)}, bf16[512,256]{1,0:T(8,128)(2,1)S(1)}, u32[]{:S(2)}, u32[]{:S(2)}) %collective-permute-start.7) | collective-permute-done | bytes 262176 | tf_op jit(solution)/shard_map/ppermute | solution.py:168
  143.1 4.5 %shard_map.59.refs_0_ = f32[512,896]{1,0:T(8,128)} custom-call(s32[2]{0:T(128)} %pad_add_fusion.2.meta_ref, f32[512,896]{1,0:T(8,128)} %shard_map.58.refs_0_, bf16[512,256]{1,0:T(8,128)(2,1)} %copy-done.8, bf16[512,256]{1,0:T(8,128)(2,1)} %copy-done.7, bf16[512,1792]{1,0:T(8,128)(2,1)} %collective-permute-done.2.refs_14_.refs_15_.refs_3_.refs_4_, ...), custom_call_target="tpu_custom_call" | custom-call | flops 469762048 | bytes 5111808 | tf_op jit(solution)/shard_map/pallas_call | solution.py:123
  149.0 3.4 %shard_map.60 = bf16[256,896]{1,0:T(8,128)(2,1)} custom-call(s32[2]{0:T(128)} %pad_add_fusion.2.meta_ref, f32[512,896]{1,0:T(8,128)} %shard_map.59.refs_0_, bf16[512,256]{1,0:T(8,128)(2,1)} %copy-done.4, bf16[512,256]{1,0:T(8,128)(2,1)} %copy-done.3, bf16[512,1792]{1,0:T(8,128)(2,1)} %copy-done.1, bf16[512,1792]{1,0:T(8,128)(2,1)} %copy-done.1), custom_call_target="tpu_custom_call" | custom-call | flops 234881024 | bytes 2555904 | tf_op jit(solution)/shard_map/pallas_call | solution.py:123
  152.4 3.0 %collective-permute-start.9 = (bf16[256,896]{1,0:T(8,128)(2,1)}, bf16[256,896]{1,0:T(8,128)(2,1)S(1)}, u32[]{:S(2)}, u32[]{:S(2)}) collective-permute-start(bf16[256,896]{1,0:T(8,128)(2,1)} %shard_map.60), channel_id=1, source_target_pairs={{0,1},{1,0},{2,3},{3,2},{4,5},{5,4},{6,7},{7,6},{8,9},{9,8},{10,11... | collective-permute-start | bytes 1376264 | tf_op jit(solution)/shard_map/ppermute | solution.py:182
  155.4 3.4 %shard_map.61 = bf16[256,896]{1,0:T(8,128)(2,1)} custom-call(s32[2]{0:T(128)} %pad_add_fusion.2.meta_ref, f32[512,896]{1,0:T(8,128)} %shard_map.59.refs_0_, bf16[512,256]{1,0:T(8,128)(2,1)} %copy-done.4, bf16[512,256]{1,0:T(8,128)(2,1)} %copy-done.3, bf16[512,1792]{1,0:T(8,128)(2,1)} %copy-done.1, bf16[512,1792]{1,0:T(8,128)(2,1)} %copy-done.1), custom_call_target="tpu_custom_call" | custom-call | flops 234881024 | bytes 2555904 | tf_op jit(solution)/shard_map/pallas_call | solution.py:123
  160.0 6.9 %shard_map.57 = f32[512,896]{1,0:T(8,128)} custom-call(s32[2]{0:T(128)} %pad_add_fusion.meta_ref, bf16[512,256]{1,0:T(8,128)(2,1)} %shard_map.55.refs_0_, bf16[512,256]{1,0:T(8,128)(2,1)} %shard_map.56.refs_1_, bf16[512,256]{1,0:T(8,128)(2,1)} %copy-done.6, bf16[512,256]{1,0:T(8,128)(2,1)} %copy-done.5, bf16[512,256]{1,0:T(8,128)(2,1)} %copy-done.4, ...), custom_call_target="tpu_custom_call" | custom-call | flops 1879048192 | bytes 7602176 | tf_op jit(solution)/shard_map/pallas_call | solution.py:123
  166.9 2.1 %collective-permute-done.10 = bf16[256,896]{1,0:T(8,128)(2,1)S(1)} collective-permute-done((bf16[256,896]{1,0:T(8,128)(2,1)}, bf16[256,896]{1,0:T(8,128)(2,1)S(1)}, u32[]{:S(2)}, u32[]{:S(2)}) %collective-permute-start.10) | collective-permute-done | bytes 458784 | tf_op jit(solution)/shard_map/ppermute | solution.py:182
  169.0 2.6 %add_convert_fusion = bf16[512,896]{1,0:T(8,128)(2,1)} fusion(f32[512,896]{1,0:T(8,128)} %shard_map.57, bf16[256,896]{1,0:T(8,128)(2,1)S(1)} %collective-permute-done.10, bf16[256,896]{1,0:T(8,128)(2,1)S(1)} %collective-permute-done.9), kind=kLoop, calls=%fused_computation | loop fusion | flops 2752512 | bytes 3670016 | tf_op jit(solution)/shard_map/convert_element_type | solution.py:191
  (33 shorter events, 7.4 us)
Async XLA Ops:
  6.5 13.4 %copy-start = (s32[16,3]{0,1:T(4,128)S(1)}, s32[16,3]{0,1:T(4,128)}, u32[]{:S(2)}) copy-start(s32[16,3]{0,1:T(4,128)} %param.8) | copy-start | bytes 580
  6.5 96.7 %all-gather.2.cloned.1.call-start = ((), (), s32[]{:S(2)}) async-start(), calls=%async_computation | async-start | bytes 17825792 | tf_op jit(solution)/shard_map/all_gather | solution.py:149
  14.0 43.4 %collective-permute-start = (bf16[512,1792]{1,0:T(8,128)(2,1)}, bf16[512,1792]{1,0:T(8,128)(2,1)}, u32[]{:S(2)}, u32[]{:S(2)}) collective-permute-start(bf16[512,1792]{1,0:T(8,128)(2,1)} %get-tuple-element.15), channel_id=1, source_target_pairs={{0,2},{2,4},{4,6},{6,0},{1,3},{3,5},{5,7},{7,1},{8,10},{10,12},{12... | collective-permute-start | bytes 5505032 | tf_op jit(solution)/shard_map/ppermute | solution.py:158
  15.7 82.2 %collective-permute-start.1 = (bf16[512,1792]{1,0:T(8,128)(2,1)}, bf16[512,1792]{1,0:T(8,128)(2,1)S(1)}, u32[]{:S(2)}, u32[]{:S(2)}) collective-permute-start(bf16[512,1792]{1,0:T(8,128)(2,1)} %get-tuple-element.14), channel_id=1, source_target_pairs={{0,4},{2,6},{4,0},{6,2},{1,5},{3,7},{5,1},{7,3},{8,12},{10,14},{12... | collective-permute-start | bytes 5505032 | tf_op jit(solution)/shard_map/ppermute | solution.py:158
  18.6 79.3 %collective-permute-start.2 = (bf16[512,1792]{1,0:T(8,128)(2,1)}, bf16[512,1792]{1,0:T(8,128)(2,1)}, u32[]{:S(2)}, u32[]{:S(2)}) collective-permute-start(bf16[512,1792]{1,0:T(8,128)(2,1)} %get-tuple-element.13), channel_id=1, source_target_pairs={{0,6},{2,0},{4,2},{6,4},{1,7},{3,1},{5,3},{7,5},{8,14},{10,8},{12,... | collective-permute-start | bytes 5505032 | tf_op jit(solution)/shard_map/ppermute | solution.py:158
  97.8 11.5 %copy-start.1 = (bf16[512,1792]{1,0:T(8,128)(2,1)}, bf16[512,1792]{1,0:T(8,128)(2,1)S(1)}, u32[]{:S(2)}) copy-start(bf16[512,1792]{1,0:T(8,128)(2,1)S(1)} %collective-permute-done.1.refs_12_.refs_13_.refs_3_.refs_4_) | copy-start | bytes 5505028
  109.4 9.1 %copy-start.2 = (bf16[512,256]{1,0:T(8,128)(2,1)S(1)}, bf16[512,256]{1,0:T(8,128)(2,1)}, u32[]{:S(2)}) copy-start(bf16[512,256]{1,0:T(8,128)(2,1)} %shard_map.56.refs_1_) | copy-start | bytes 786436
  109.4 13.2 %collective-permute-start.4 = (bf16[512,256]{1,0:T(8,128)(2,1)}, bf16[512,256]{1,0:T(8,128)(2,1)S(1)}, u32[]{:S(2)}, u32[]{:S(2)}) collective-permute-start(bf16[512,256]{1,0:T(8,128)(2,1)} %shard_map.56.refs_1_), channel_id=1, source_target_pairs={{0,2},{2,4},{4,6},{6,0},{1,3},{3,5},{5,7},{7,1},{8,10},{10,12},{12... | collective-permute-start | bytes 786440 | tf_op jit(solution)/shard_map/ppermute | solution.py:168
  117.0 10.6 %collective-permute-start.3 = (bf16[512,256]{1,0:T(8,128)(2,1)}, bf16[512,256]{1,0:T(8,128)(2,1)S(1)}, u32[]{:S(2)}, u32[]{:S(2)}) collective-permute-start(bf16[512,256]{1,0:T(8,128)(2,1)} %shard_map.55.refs_0_), channel_id=1, source_target_pairs={{0,2},{2,4},{4,6},{6,0},{1,3},{3,5},{5,7},{7,1},{8,10},{10,12},{12... | collective-permute-start | bytes 786440 | tf_op jit(solution)/shard_map/ppermute | solution.py:168
  118.5 14.7 %collective-permute-start.8 = (bf16[512,256]{1,0:T(8,128)(2,1)S(1)}, bf16[512,256]{1,0:T(8,128)(2,1)S(1)}, u32[]{:S(2)}, u32[]{:S(2)}) collective-permute-start(bf16[512,256]{1,0:T(8,128)(2,1)S(1)} %copy-done.2), channel_id=1, source_target_pairs={{0,6},{2,0},{4,2},{6,4},{1,7},{3,1},{5,3},{7,5},{8,14},{10,8},{12,... | collective-permute-start | bytes 786440 | tf_op jit(solution)/shard_map/ppermute | solution.py:168
  120.2 22.1 %collective-permute-start.7 = (bf16[512,256]{1,0:T(8,128)(2,1)}, bf16[512,256]{1,0:T(8,128)(2,1)S(1)}, u32[]{:S(2)}, u32[]{:S(2)}) collective-permute-start(bf16[512,256]{1,0:T(8,128)(2,1)} %shard_map.55.refs_0_), channel_id=1, source_target_pairs={{0,6},{2,0},{4,2},{6,4},{1,7},{3,1},{5,3},{7,5},{8,14},{10,8},{12,... | collective-permute-start | bytes 786440 | tf_op jit(solution)/shard_map/ppermute | solution.py:168
  120.8 26.8 %collective-permute-start.6 = (bf16[512,256]{1,0:T(8,128)(2,1)S(1)}, bf16[512,256]{1,0:T(8,128)(2,1)S(1)}, u32[]{:S(2)}, u32[]{:S(2)}) collective-permute-start(bf16[512,256]{1,0:T(8,128)(2,1)S(1)} %copy-done.2), channel_id=1, source_target_pairs={{0,4},{2,6},{4,0},{6,2},{1,5},{3,7},{5,1},{7,3},{8,12},{10,14},{12... | collective-permute-start | bytes 786440 | tf_op jit(solution)/shard_map/ppermute | solution.py:168
  122.6 5.1 %copy-start.5 = (bf16[512,256]{1,0:T(8,128)(2,1)}, bf16[512,256]{1,0:T(8,128)(2,1)S(1)}, u32[]{:S(2)}) copy-start(bf16[512,256]{1,0:T(8,128)(2,1)S(1)} %collective-permute-done.4.refs_3_) | copy-start | bytes 786436
  122.6 25.0 %collective-permute-start.5 = (bf16[512,256]{1,0:T(8,128)(2,1)}, bf16[512,256]{1,0:T(8,128)(2,1)S(1)}, u32[]{:S(2)}, u32[]{:S(2)}) collective-permute-start(bf16[512,256]{1,0:T(8,128)(2,1)} %shard_map.55.refs_0_), channel_id=1, source_target_pairs={{0,4},{2,6},{4,0},{6,2},{1,5},{3,7},{5,1},{7,3},{8,12},{10,14},{12... | collective-permute-start | bytes 786440 | tf_op jit(solution)/shard_map/ppermute | solution.py:168
  127.7 0.7 copy-start.6
  133.2 9.1 %copy-start.7 = (bf16[512,256]{1,0:T(8,128)(2,1)}, bf16[512,256]{1,0:T(8,128)(2,1)S(1)}, u32[]{:S(2)}) copy-start(bf16[512,256]{1,0:T(8,128)(2,1)S(1)} %collective-permute-done.8.refs_7_.refs_2_) | copy-start | bytes 786436
  142.3 0.7 copy-start.8
  147.6 0.7 copy-start.3
  148.3 0.7 copy-start.4
  152.4 14.5 %collective-permute-start.9 = (bf16[256,896]{1,0:T(8,128)(2,1)}, bf16[256,896]{1,0:T(8,128)(2,1)S(1)}, u32[]{:S(2)}, u32[]{:S(2)}) collective-permute-start(bf16[256,896]{1,0:T(8,128)(2,1)} %shard_map.60), channel_id=1, source_target_pairs={{0,1},{1,0},{2,3},{3,2},{4,5},{5,4},{6,7},{7,6},{8,9},{9,8},{10,11... | collective-permute-start | bytes 1376264 | tf_op jit(solution)/shard_map/ppermute | solution.py:182
  158.8 10.2 %collective-permute-start.10 = (bf16[256,896]{1,0:T(8,128)(2,1)}, bf16[256,896]{1,0:T(8,128)(2,1)S(1)}, u32[]{:S(2)}, u32[]{:S(2)}) collective-permute-start(bf16[256,896]{1,0:T(8,128)(2,1)} %shard_map.61), channel_id=1, source_target_pairs={{0,1},{1,0},{2,3},{3,2},{4,5},{5,4},{6,7},{7,6},{8,9},{9,8},{10,11... | collective-permute-start | bytes 1376264 | tf_op jit(solution)/shard_map/ppermute | solution.py:182
Sparse Core Ops, SparseCore 0:
  9.1 94.1 all-gather.1

commit v18 on v16

--- a/solution.py
+++ b/solution.py
@@ -215,8 +215,8 @@
         for r in range(2)
     ]
     got = jnp.concatenate(got)
-    own = project(mine, pieces, out_weight, received, xh_size, jnp.float32)
-    return (own + got.astype(jnp.float32)).astype(queries.dtype)
+    own = project(mine, pieces, out_weight, received, xh_size, queries.dtype)
+    return (own.astype(jnp.float32) + got.astype(jnp.float32)).astype(queries.dtype)
 
 
 def solution(mesh):

time: 178 us -> 177 us (level)
  no operation moved by 1% of the time
where the time goes in v18:
time: 177 us
  waiting for transfers between devices  103 us (58%)
  Pallas kernels  32 us (18%)
  starting transfers between devices  14.5 us (8%)
  between operations  13.5 us (8%)
  local copies, waits for them, and re-layouts  7.73 us (4%)
  other arithmetic  6.43 us (4%)
    ppermute x3, waiting for transfers between devices, per_device(): lax.ppermute(sent, 'y', [(i, (i + shift) % y_size) for i in range(y_size)])  77.2 us
    pallas_call x4, Pallas kernels, project_part(): pl.pallas_call(functools.partial(part_kernel, count=len(pieces), has_part...  16.3 us
    ppermute x3, waiting for transfers between devices, per_device(): lax.ppermute(attended, 'y', [(i, (i + shift) % y_size) for i in range(y_s...  14.5 us
    pallas_call x1, Pallas kernels, attend(): pl.pallas_call(functools.partial(attend_kernel, topk=topk, head_count=hea...  9.07 us
    pallas_call x1, Pallas kernels, project(): pl.pallas_call(functools.partial(project_kernel, shifts=shifts), grid_spe...  6.56 us
    ppermute x3, starting transfers between devices, per_device(): lax.ppermute(sent, 'y', [(i, (i + shift) % y_size) for i in range(y_size)])  5.91 us
    ppermute x2, waiting for transfers between devices, per_device(): lax.ppermute(project_part(other, near, pieces[2:3], list(received[1:2]),...  5.9 us
    all_gather x1, waiting for transfers between devices, per_device(): lax.all_gather(jnp.concatenate([key_rows, value_rows], axis=1), CTX, axis...  5.34 us
  transfers between devices with their start and end apart: 9, of which 7 were waited for; matrix products, arithmetic and copies ran while one was open for 4% of the time, Pallas kernels for 11%

profile of v18, /device:TPU:0, one launch (start us, length us, event | category | flops | bytes accessed | tf_op | source)
XLA Modules:
  0.0 177.0 jit_solution(4210399287299389544)
XLA Ops:
  6.5 2.3 %pad_maximum_fusion = bf16[512,1024]{1,0:T(8,128)(2,1)} fusion(bf16[512,512]{1,0:T(8,128)(2,1)} %param.7, bf16[512,512]{1,0:T(8,128)(2,1)} %param.6), kind=kLoop, calls=%fused_computation.1 | loop fusion | flops 2097152 | bytes 2097152 | tf_op jit(solution)/shard_map/concatenate | solution.py:180
  8.9 5.2 %constant_dynamic-slice_fusion = (bf16[512,1792]{1,0:T(8,128)(2,1)}, bf16[512,1792]{1,0:T(8,128)(2,1)}, bf16[512,1792]{1,0:T(8,128)(2,1)}) fusion(bf16[512,7168]{1,0:T(8,128)(2,1)} %refs_2_.1, s32[]{:T(128)S(6)} %select_n.33, s32[]{:T(128)S(6)} %select_n.31, s32[]{:T(128)S(6)} %select_n.29), kind=kLoop, calls=%fused_computation.3 | loop fusion | bytes 11010060 | tf_op jit(solution)/shard_map/dynamic_slice | solution.py:186
  14.1 1.7 collective-permute-start
  15.7 2.9 %collective-permute-start.1 = (bf16[512,1792]{1,0:T(8,128)(2,1)}, bf16[512,1792]{1,0:T(8,128)(2,1)S(1)}, u32[]{:S(2)}, u32[]{:S(2)}) collective-permute-start(bf16[512,1792]{1,0:T(8,128)(2,1)} %get-tuple-element.14), channel_id=1, source_target_pairs={{0,4},{2,6},{4,0},{6,2},{1,5},{3,7},{5,1},{7,3},{8,12},{10,14},{12... | collective-permute-start | bytes 5505032 | tf_op jit(solution)/shard_map/ppermute | solution.py:188
  18.6 1.3 collective-permute-start.2
  20.7 36.8 %collective-permute-done.refs_5_.refs_3_ = bf16[512,1792]{1,0:T(8,128)(2,1)} collective-permute-done((bf16[512,1792]{1,0:T(8,128)(2,1)}, bf16[512,1792]{1,0:T(8,128)(2,1)}, u32[]{:S(2)}, u32[]{:S(2)}) %collective-permute-start) | collective-permute-done | bytes 1835040 | tf_op jit(solution)/shard_map/ppermute | solution.py:188
  57.5 40.4 %collective-permute-done.1.refs_6_.refs_2_ = bf16[512,1792]{1,0:T(8,128)(2,1)S(1)} collective-permute-done((bf16[512,1792]{1,0:T(8,128)(2,1)}, bf16[512,1792]{1,0:T(8,128)(2,1)S(1)}, u32[]{:S(2)}, u32[]{:S(2)}) %collective-permute-start.1) | collective-permute-done | bytes 1835040 | tf_op jit(solution)/shard_map/ppermute | solution.py:188
  97.9 5.3 %all-gather.2.cloned.1.call-done.refs_0_.refs_1_.refs_2_.refs_3_.refs_4_.refs_5_ = bf16[8192,1024]{1,0:T(8,128)(2,1)} async-done(((bf16[512,1024]{1,0:T(8,128)(2,1)}), bf16[8192,1024]{1,0:T(8,128)(2,1)}) %all-gather.2.cloned.1.call-update) | async-done | bytes 16777232 | tf_op jit(solution)/shard_map/all_gather | solution.py:179
  103.2 9.1 %shard_map.55.refs_0_ = bf16[512,512]{1,0:T(8,128)(2,1)} custom-call(s32[4]{0:T(128)} %pad_add_fusion.1.meta_ref, bf16[512,512]{1,0:T(8,128)(2,1)} %q_ref.1, bf16[8192,1024]{1,0:T(8,128)(2,1)} %all-gather.2.cloned.1.call-done.refs_0_.refs_1_.refs_2_.refs_3_.refs_4_.refs_5_, ...), custom_call_target="tpu_custom_call" | custom-call | flops 1610612736 | bytes 4194304 | tf_op jit(solution)/shard_map/pallas_call | solution.py:87
  112.3 1.5 collective-permute-start.3
  113.8 1.8 collective-permute-start.5
  115.5 1.8 %collective-permute-start.4 = (bf16[512,512]{1,0:T(8,128)(2,1)}, bf16[512,512]{1,0:T(8,128)(2,1)S(1)}, u32[]{:S(2)}, u32[]{:S(2)}) collective-permute-start(bf16[512,512]{1,0:T(8,128)(2,1)} %shard_map.55.refs_0_), channel_id=1, source_target_pairs={{0,4},{2,6},{4,0},{6,2},{1,5},{3,7},{5,1},{7,3},{8,12},{10,14},{12... | collective-permute-start | bytes 1572872 | tf_op jit(solution)/shard_map/ppermute | solution.py:193
  117.9 9.6 %collective-permute-done.3.refs_1_ = bf16[512,512]{1,0:T(8,128)(2,1)S(1)} collective-permute-done((bf16[512,512]{1,0:T(8,128)(2,1)}, bf16[512,512]{1,0:T(8,128)(2,1)S(1)}, u32[]{:S(2)}, u32[]{:S(2)}) %collective-permute-start.3) | collective-permute-done | bytes 524320 | tf_op jit(solution)/shard_map/ppermute | solution.py:193
  128.3 4.9 %shard_map.57.refs_0_ = f32[512,896]{1,0:T(8,128)} custom-call(s32[2]{0:T(128)} %pad_add_fusion.2.meta_ref, bf16[512,512]{1,0:T(8,128)(2,1)} %shard_map.55.refs_0_, bf16[512,512]{1,0:T(8,128)(2,1)} %copy-done.3, bf16[512,7168]{1,0:T(8,128)(2,1)} %refs_2_.1, bf16[512,1792]{1,0:T(8,128)(2,1)} %collective-permute-done.refs_5_.refs_3_), custom_call_target="tpu_custom_call" | custom-call | flops 939524096 | bytes 4718592 | tf_op jit(solution)/shard_map/pallas_call | solution.py:153
  133.3 4.9 %collective-permute-done.5.refs_3_.refs_1_ = bf16[512,512]{1,0:T(8,128)(2,1)S(1)} collective-permute-done((bf16[512,512]{1,0:T(8,128)(2,1)}, bf16[512,512]{1,0:T(8,128)(2,1)S(1)}, u32[]{:S(2)}, u32[]{:S(2)}) %collective-permute-start.5) | collective-permute-done | bytes 524320 | tf_op jit(solution)/shard_map/ppermute | solution.py:193
  138.2 0.8 copy-done.4
  139.0 4.5 %shard_map.58.refs_0_ = f32[512,896]{1,0:T(8,128)} custom-call(s32[2]{0:T(128)} %pad_add_fusion.2.meta_ref, f32[512,896]{1,0:T(8,128)} %shard_map.57.refs_0_, bf16[512,512]{1,0:T(8,128)(2,1)} %copy-done.4, bf16[512,1792]{1,0:T(8,128)(2,1)} %collective-permute-done.2.refs_7_.refs_2_), custom_call_target="tpu_custom_call" | custom-call | flops 469762048 | bytes 5111808 | tf_op jit(solution)/shard_map/pallas_call | solution.py:153
  143.5 0.8 copy-done.2
  144.3 3.4 %shard_map.59 = bf16[256,896]{1,0:T(8,128)(2,1)} custom-call(s32[2]{0:T(128)} %pad_add_fusion.2.meta_ref, f32[512,896]{1,0:T(8,128)} %shard_map.58.refs_0_, bf16[512,512]{1,0:T(8,128)(2,1)} %copy-done.2, bf16[512,1792]{1,0:T(8,128)(2,1)} %copy-done.1), custom_call_target="tpu_custom_call" | custom-call | flops 234881024 | bytes 2555904 | tf_op jit(solution)/shard_map/pallas_call | solution.py:153
  147.7 3.0 %collective-permute-start.6 = (bf16[256,896]{1,0:T(8,128)(2,1)}, bf16[256,896]{1,0:T(8,128)(2,1)S(1)}, u32[]{:S(2)}, u32[]{:S(2)}) collective-permute-start(bf16[256,896]{1,0:T(8,128)(2,1)} %shard_map.59), channel_id=1, source_target_pairs={{0,1},{1,0},{2,3},{3,2},{4,5},{5,4},{6,7},{7,6},{8,9},{9,8},{10,11... | collective-permute-start | bytes 1376264 | tf_op jit(solution)/shard_map/ppermute | solution.py:207
  150.7 3.4 %shard_map.60 = bf16[256,896]{1,0:T(8,128)(2,1)} custom-call(s32[2]{0:T(128)} %pad_add_fusion.2.meta_ref, f32[512,896]{1,0:T(8,128)} %shard_map.58.refs_0_, bf16[512,512]{1,0:T(8,128)(2,1)} %copy-done.2, bf16[512,1792]{1,0:T(8,128)(2,1)} %copy-done.1), custom_call_target="tpu_custom_call" | custom-call | flops 234881024 | bytes 2555904 | tf_op jit(solution)/shard_map/pallas_call | solution.py:153
  155.3 6.6 %shard_map.56 = bf16[512,896]{1,0:T(8,128)(2,1)} custom-call(s32[2]{0:T(128)} %pad_add_fusion.y_ref, bf16[512,512]{1,0:T(8,128)(2,1)} %shard_map.55.refs_0_, bf16[512,512]{1,0:T(8,128)(2,1)} %copy-done.3, bf16[512,512]{1,0:T(8,128)(2,1)} %copy-done.2, bf16[512,512]{1,0:T(8,128)(2,1)} %copy-done.4, bf16[512,7168]{1,0:T(8,128)(2,1)} %refs_2_.1, ...), custom_call_target="tpu_custom_call" | custom-call | flops 1879048192 | bytes 6684672 | tf_op jit(solution)/shard_map/pallas_call | solution.py:111
  162.4 5.4 %collective-permute-done.7 = bf16[256,896]{1,0:T(8,128)(2,1)S(1)} collective-permute-done((bf16[256,896]{1,0:T(8,128)(2,1)}, bf16[256,896]{1,0:T(8,128)(2,1)S(1)}, u32[]{:S(2)}, u32[]{:S(2)}) %collective-permute-start.7) | collective-permute-done | bytes 458784 | tf_op jit(solution)/shard_map/ppermute | solution.py:207
  167.8 2.4 %add_convert_fusion = bf16[512,896]{1,0:T(8,128)(2,1)} fusion(bf16[512,896]{1,0:T(8,128)(2,1)} %shard_map.56, bf16[256,896]{1,0:T(8,128)(2,1)S(1)} %collective-permute-done.7, bf16[256,896]{1,0:T(8,128)(2,1)S(1)} %collective-permute-done.6), kind=kLoop, calls=%fused_computation | loop fusion | flops 3211264 | bytes 2752512 | tf_op jit(solution)/shard_map/convert_element_type | solution.py:219
  (18 shorter events, 3.9 us)
Async XLA Ops:
  6.5 13.4 %copy-start = (s32[16,3]{0,1:T(4,128)S(1)}, s32[16,3]{0,1:T(4,128)}, u32[]{:S(2)}) copy-start(s32[16,3]{0,1:T(4,128)} %param.8) | copy-start | bytes 580
  6.5 96.7 %all-gather.2.cloned.1.call-start = ((), (), s32[]{:S(2)}) async-start(), calls=%async_computation | async-start | bytes 17825792 | tf_op jit(solution)/shard_map/all_gather | solution.py:179
  14.1 43.4 %collective-permute-start = (bf16[512,1792]{1,0:T(8,128)(2,1)}, bf16[512,1792]{1,0:T(8,128)(2,1)}, u32[]{:S(2)}, u32[]{:S(2)}) collective-permute-start(bf16[512,1792]{1,0:T(8,128)(2,1)} %get-tuple-element.15), channel_id=1, source_target_pairs={{0,2},{2,4},{4,6},{6,0},{1,3},{3,5},{5,7},{7,1},{8,10},{10,12},{12... | collective-permute-start | bytes 5505032 | tf_op jit(solution)/shard_map/ppermute | solution.py:188
  15.7 82.2 %collective-permute-start.1 = (bf16[512,1792]{1,0:T(8,128)(2,1)}, bf16[512,1792]{1,0:T(8,128)(2,1)S(1)}, u32[]{:S(2)}, u32[]{:S(2)}) collective-permute-start(bf16[512,1792]{1,0:T(8,128)(2,1)} %get-tuple-element.14), channel_id=1, source_target_pairs={{0,4},{2,6},{4,0},{6,2},{1,5},{3,7},{5,1},{7,3},{8,12},{10,14},{12... | collective-permute-start | bytes 5505032 | tf_op jit(solution)/shard_map/ppermute | solution.py:188
  18.6 79.3 %collective-permute-start.2 = (bf16[512,1792]{1,0:T(8,128)(2,1)}, bf16[512,1792]{1,0:T(8,128)(2,1)}, u32[]{:S(2)}, u32[]{:S(2)}) collective-permute-start(bf16[512,1792]{1,0:T(8,128)(2,1)} %get-tuple-element.13), channel_id=1, source_target_pairs={{0,6},{2,0},{4,2},{6,4},{1,7},{3,1},{5,3},{7,5},{8,14},{10,8},{12,... | collective-permute-start | bytes 5505032 | tf_op jit(solution)/shard_map/ppermute | solution.py:188
  97.9 14.4 %copy-start.1 = (bf16[512,1792]{1,0:T(8,128)(2,1)}, bf16[512,1792]{1,0:T(8,128)(2,1)S(1)}, u32[]{:S(2)}) copy-start(bf16[512,1792]{1,0:T(8,128)(2,1)S(1)} %collective-permute-done.1.refs_6_.refs_2_) | copy-start | bytes 5505028
  112.3 15.2 %collective-permute-start.3 = (bf16[512,512]{1,0:T(8,128)(2,1)}, bf16[512,512]{1,0:T(8,128)(2,1)S(1)}, u32[]{:S(2)}, u32[]{:S(2)}) collective-permute-start(bf16[512,512]{1,0:T(8,128)(2,1)} %shard_map.55.refs_0_), channel_id=1, source_target_pairs={{0,2},{2,4},{4,6},{6,0},{1,3},{3,5},{5,7},{7,1},{8,10},{10,12},{12... | collective-permute-start | bytes 1572872 | tf_op jit(solution)/shard_map/ppermute | solution.py:193
  113.8 24.4 %collective-permute-start.5 = (bf16[512,512]{1,0:T(8,128)(2,1)}, bf16[512,512]{1,0:T(8,128)(2,1)S(1)}, u32[]{:S(2)}, u32[]{:S(2)}) collective-permute-start(bf16[512,512]{1,0:T(8,128)(2,1)} %shard_map.55.refs_0_), channel_id=1, source_target_pairs={{0,6},{2,0},{4,2},{6,4},{1,7},{3,1},{5,3},{7,5},{8,14},{10,8},{12,... | collective-permute-start | bytes 1572872 | tf_op jit(solution)/shard_map/ppermute | solution.py:193
  115.5 28.0 %collective-permute-start.4 = (bf16[512,512]{1,0:T(8,128)(2,1)}, bf16[512,512]{1,0:T(8,128)(2,1)S(1)}, u32[]{:S(2)}, u32[]{:S(2)}) collective-permute-start(bf16[512,512]{1,0:T(8,128)(2,1)} %shard_map.55.refs_0_), channel_id=1, source_target_pairs={{0,4},{2,6},{4,0},{6,2},{1,5},{3,7},{5,1},{7,3},{8,12},{10,14},{12... | collective-permute-start | bytes 1572872 | tf_op jit(solution)/shard_map/ppermute | solution.py:193
  127.5 0.8 copy-start.3
  138.2 0.8 copy-start.4
  143.5 0.8 copy-start.2
  147.7 14.7 %collective-permute-start.6 = (bf16[256,896]{1,0:T(8,128)(2,1)}, bf16[256,896]{1,0:T(8,128)(2,1)S(1)}, u32[]{:S(2)}, u32[]{:S(2)}) collective-permute-start(bf16[256,896]{1,0:T(8,128)(2,1)} %shard_map.59), channel_id=1, source_target_pairs={{0,1},{1,0},{2,3},{3,2},{4,5},{5,4},{6,7},{7,6},{8,9},{9,8},{10,11... | collective-permute-start | bytes 1376264 | tf_op jit(solution)/shard_map/ppermute | solution.py:207
  154.2 13.6 %collective-permute-start.7 = (bf16[256,896]{1,0:T(8,128)(2,1)}, bf16[256,896]{1,0:T(8,128)(2,1)S(1)}, u32[]{:S(2)}, u32[]{:S(2)}) collective-permute-start(bf16[256,896]{1,0:T(8,128)(2,1)} %shard_map.60), channel_id=1, source_target_pairs={{0,1},{1,0},{2,3},{3,2},{4,5},{5,4},{6,7},{7,6},{8,9},{9,8},{10,11... | collective-permute-start | bytes 1376264 | tf_op jit(solution)/shard_map/ppermute | solution.py:207
Sparse Core Ops, SparseCore 0:
  9.1 94.1 all-gather.1

commit v19 on v16

--- a/solution.py
+++ b/solution.py
@@ -207,12 +207,12 @@
         lax.ppermute(
             project_part(
                 other, near, pieces[2:3], list(received[1:2]), False, xh_size, queries.dtype,
-                (r, 2),
+                (r, 4),
             ),
             "xh",
             swap,
         )
-        for r in range(2)
+        for r in range(4)
     ]
     got = jnp.concatenate(got)
     own = project(mine, pieces, out_weight, received, xh_size, jnp.float32)

time: 178 us -> 181 us (1.017)
  waiting for transfers between devices: 103 us -> 97 us
  Pallas kernels: 32.3 us -> 37.7 us
  starting transfers between devices: 14.5 us -> 18 us
    ppermute x2 -> x4, waiting for transfers between devices: 5.55 us -> 0.01 us  [per_device(): lax.ppermute(project_part(other, near, pieces[2:3], list(received[1:2]),...]
    pallas_call x4 -> x6, Pallas kernels: 16.3 us -> 21.7 us  [project_part(): pl.pallas_call(functools.partial(part_kernel, count=len(pieces), has_part...]
    ppermute x2 -> x4, starting transfers between devices: 3.53 us -> 7.06 us  [per_device(): lax.ppermute(project_part(other, near, pieces[2:3], list(received[1:2]),...]
  transfers between devices with their start and end apart: 9 -> 11, of which waited for: 7 -> 5; matrix products, arithmetic and copies ran while one was open for 4% -> 4% of each run, Pallas kernels for 11% -> 14%
where the time goes in v19:
time: 181 us
  waiting for transfers between devices  97 us (54%)
  Pallas kernels  37.7 us (21%)
  starting transfers between devices  18 us (10%)
  between operations  13.5 us (7%)
  local copies, waits for them, and re-layouts  7.74 us (4%)
  other arithmetic  6.67 us (4%)
    ppermute x3, waiting for transfers between devices, per_device(): lax.ppermute(sent, 'y', [(i, (i + shift) % y_size) for i in range(y_size)])  77.1 us
    pallas_call x6, Pallas kernels, project_part(): pl.pallas_call(functools.partial(part_kernel, count=len(pieces), has_part...  21.7 us
    ppermute x3, waiting for transfers between devices, per_device(): lax.ppermute(attended, 'y', [(i, (i + shift) % y_size) for i in range(y_s...  14.5 us
    pallas_call x1, Pallas kernels, attend(): pl.pallas_call(functools.partial(attend_kernel, topk=topk, head_count=hea...  9.1 us
    ppermute x4, starting transfers between devices, per_device(): lax.ppermute(project_part(other, near, pieces[2:3], list(received[1:2]),...  7.06 us
    pallas_call x1, Pallas kernels, project(): pl.pallas_call(functools.partial(project_kernel, shifts=shifts), grid_spe...  6.91 us
    ppermute x3, starting transfers between devices, per_device(): lax.ppermute(sent, 'y', [(i, (i + shift) % y_size) for i in range(y_size)])  5.91 us
    all_gather x1, waiting for transfers between devices, per_device(): lax.all_gather(jnp.concatenate([key_rows, value_rows], axis=1), CTX, axis...  5.36 us
  transfers between devices with their start and end apart: 11, of which 5 were waited for; matrix products, arithmetic and copies ran while one was open for 4% of the time, Pallas kernels for 14%

profile of v19, /device:TPU:0, one launch (start us, length us, event | category | flops | bytes accessed | tf_op | source)
XLA Modules:
  0.0 180.6 jit_solution(1629399710930168432)
XLA Ops:
  6.5 2.3 %pad_maximum_fusion = bf16[512,1024]{1,0:T(8,128)(2,1)} fusion(bf16[512,512]{1,0:T(8,128)(2,1)} %param.7, bf16[512,512]{1,0:T(8,128)(2,1)} %param.6), kind=kLoop, calls=%fused_computation.1 | loop fusion | flops 2097152 | bytes 2097152 | tf_op jit(solution)/shard_map/concatenate | solution.py:180
  8.9 5.1 %constant_dynamic-slice_fusion = (bf16[512,1792]{1,0:T(8,128)(2,1)}, bf16[512,1792]{1,0:T(8,128)(2,1)}, bf16[512,1792]{1,0:T(8,128)(2,1)}) fusion(bf16[512,7168]{1,0:T(8,128)(2,1)} %refs_2_.1, s32[]{:T(128)S(6)} %select_n.33, s32[]{:T(128)S(6)} %select_n.31, s32[]{:T(128)S(6)} %select_n.29), kind=kLoop, calls=%fused_computation.3 | loop fusion | bytes 11010060 | tf_op jit(solution)/shard_map/dynamic_slice | solution.py:186
  14.0 1.7 collective-permute-start
  15.7 2.9 %collective-permute-start.1 = (bf16[512,1792]{1,0:T(8,128)(2,1)}, bf16[512,1792]{1,0:T(8,128)(2,1)S(1)}, u32[]{:S(2)}, u32[]{:S(2)}) collective-permute-start(bf16[512,1792]{1,0:T(8,128)(2,1)} %get-tuple-element.14), channel_id=1, source_target_pairs={{0,4},{2,6},{4,0},{6,2},{1,5},{3,7},{5,1},{7,3},{8,12},{10,14},{12... | collective-permute-start | bytes 5505032 | tf_op jit(solution)/shard_map/ppermute | solution.py:188
  18.6 1.3 collective-permute-start.2
  20.8 36.7 %collective-permute-done.refs_5_.refs_3_ = bf16[512,1792]{1,0:T(8,128)(2,1)} collective-permute-done((bf16[512,1792]{1,0:T(8,128)(2,1)}, bf16[512,1792]{1,0:T(8,128)(2,1)}, u32[]{:S(2)}, u32[]{:S(2)}) %collective-permute-start) | collective-permute-done | bytes 1835040 | tf_op jit(solution)/shard_map/ppermute | solution.py:188
  57.5 40.4 %collective-permute-done.1.refs_6_.refs_2_ = bf16[512,1792]{1,0:T(8,128)(2,1)S(1)} collective-permute-done((bf16[512,1792]{1,0:T(8,128)(2,1)}, bf16[512,1792]{1,0:T(8,128)(2,1)S(1)}, u32[]{:S(2)}, u32[]{:S(2)}) %collective-permute-start.1) | collective-permute-done | bytes 1835040 | tf_op jit(solution)/shard_map/ppermute | solution.py:188
  97.9 5.4 %all-gather.2.cloned.1.call-done.refs_0_.refs_1_.refs_2_.refs_3_.refs_4_.refs_5_ = bf16[8192,1024]{1,0:T(8,128)(2,1)} async-done(((bf16[512,1024]{1,0:T(8,128)(2,1)}), bf16[8192,1024]{1,0:T(8,128)(2,1)}) %all-gather.2.cloned.1.call-update) | async-done | bytes 16777232 | tf_op jit(solution)/shard_map/all_gather | solution.py:179
  103.2 9.1 %shard_map.55.refs_0_ = bf16[512,512]{1,0:T(8,128)(2,1)} custom-call(s32[4]{0:T(128)} %pad_add_fusion.1.meta_ref, bf16[512,512]{1,0:T(8,128)(2,1)} %q_ref.1, bf16[8192,1024]{1,0:T(8,128)(2,1)} %all-gather.2.cloned.1.call-done.refs_0_.refs_1_.refs_2_.refs_3_.refs_4_.refs_5_, ...), custom_call_target="tpu_custom_call" | custom-call | flops 1610612736 | bytes 4194304 | tf_op jit(solution)/shard_map/pallas_call | solution.py:87
  112.3 1.5 collective-permute-start.3
  113.8 1.8 collective-permute-start.5
  115.6 1.8 collective-permute-start.4
  117.9 9.6 %collective-permute-done.3.refs_1_ = bf16[512,512]{1,0:T(8,128)(2,1)S(1)} collective-permute-done((bf16[512,512]{1,0:T(8,128)(2,1)}, bf16[512,512]{1,0:T(8,128)(2,1)S(1)}, u32[]{:S(2)}, u32[]{:S(2)}) %collective-permute-start.3) | collective-permute-done | bytes 524320 | tf_op jit(solution)/shard_map/ppermute | solution.py:193
  128.4 4.9 %shard_map.57.refs_0_ = f32[512,896]{1,0:T(8,128)} custom-call(s32[2]{0:T(128)} %pad_add_fusion.2.meta_ref, bf16[512,512]{1,0:T(8,128)(2,1)} %shard_map.55.refs_0_, bf16[512,512]{1,0:T(8,128)(2,1)} %copy-done.3, bf16[512,7168]{1,0:T(8,128)(2,1)} %refs_2_.1, bf16[512,1792]{1,0:T(8,128)(2,1)} %collective-permute-done.refs_5_.refs_3_), custom_call_target="tpu_custom_call" | custom-call | flops 939524096 | bytes 4718592 | tf_op jit(solution)/shard_map/pallas_call | solution.py:153
  133.3 4.9 %collective-permute-done.5.refs_3_.refs_1_ = bf16[512,512]{1,0:T(8,128)(2,1)S(1)} collective-permute-done((bf16[512,512]{1,0:T(8,128)(2,1)}, bf16[512,512]{1,0:T(8,128)(2,1)S(1)}, u32[]{:S(2)}, u32[]{:S(2)}) %collective-permute-start.5) | collective-permute-done | bytes 524320 | tf_op jit(solution)/shard_map/ppermute | solution.py:193
  139.0 4.5 %shard_map.58.refs_0_ = f32[512,896]{1,0:T(8,128)} custom-call(s32[2]{0:T(128)} %pad_add_fusion.2.meta_ref, f32[512,896]{1,0:T(8,128)} %shard_map.57.refs_0_, bf16[512,512]{1,0:T(8,128)(2,1)} %copy-done.4, bf16[512,1792]{1,0:T(8,128)(2,1)} %collective-permute-done.2.refs_7_.refs_2_), custom_call_target="tpu_custom_call" | custom-call | flops 469762048 | bytes 5111808 | tf_op jit(solution)/shard_map/pallas_call | solution.py:153
  144.3 3.1 %shard_map.59 = bf16[128,896]{1,0:T(8,128)(2,1)} custom-call(s32[2]{0:T(128)} %pad_add_fusion.2.meta_ref, f32[512,896]{1,0:T(8,128)} %shard_map.58.refs_0_, bf16[512,512]{1,0:T(8,128)(2,1)} %copy-done.2, bf16[512,1792]{1,0:T(8,128)(2,1)} %copy-done.1), custom_call_target="tpu_custom_call" | custom-call | flops 117440512 | bytes 1736704 | tf_op jit(solution)/shard_map/pallas_call | solution.py:153
  147.4 3.0 %collective-permute-start.6 = (bf16[128,896]{1,0:T(8,128)(2,1)}, bf16[128,896]{1,0:T(8,128)(2,1)S(1)}, u32[]{:S(2)}, u32[]{:S(2)}) collective-permute-start(bf16[128,896]{1,0:T(8,128)(2,1)} %shard_map.59), channel_id=1, source_target_pairs={{0,1},{1,0},{2,3},{3,2},{4,5},{5,4},{6,7},{7,6},{8,9},{9,8},{10,11... | collective-permute-start | bytes 688136 | tf_op jit(solution)/shard_map/ppermute | solution.py:207
  150.4 3.1 %shard_map.60 = bf16[128,896]{1,0:T(8,128)(2,1)} custom-call(s32[2]{0:T(128)} %pad_add_fusion.2.meta_ref, f32[512,896]{1,0:T(8,128)} %shard_map.58.refs_0_, bf16[512,512]{1,0:T(8,128)(2,1)} %copy-done.2, bf16[512,1792]{1,0:T(8,128)(2,1)} %copy-done.1), custom_call_target="tpu_custom_call" | custom-call | flops 117440512 | bytes 1736704 | tf_op jit(solution)/shard_map/pallas_call | solution.py:153
  154.0 3.1 %shard_map.61 = bf16[128,896]{1,0:T(8,128)(2,1)} custom-call(s32[2]{0:T(128)} %pad_add_fusion.2.meta_ref, f32[512,896]{1,0:T(8,128)} %shard_map.58.refs_0_, bf16[512,512]{1,0:T(8,128)(2,1)} %copy-done.2, bf16[512,1792]{1,0:T(8,128)(2,1)} %copy-done.1), custom_call_target="tpu_custom_call" | custom-call | flops 117440512 | bytes 1736704 | tf_op jit(solution)/shard_map/pallas_call | solution.py:153
  157.0 3.0 %collective-permute-start.8 = (bf16[128,896]{1,0:T(8,128)(2,1)}, bf16[128,896]{1,0:T(8,128)(2,1)S(1)}, u32[]{:S(2)}, u32[]{:S(2)}) collective-permute-start(bf16[128,896]{1,0:T(8,128)(2,1)} %shard_map.61), channel_id=1, source_target_pairs={{0,1},{1,0},{2,3},{3,2},{4,5},{5,4},{6,7},{7,6},{8,9},{9,8},{10,11... | collective-permute-start | bytes 688136 | tf_op jit(solution)/shard_map/ppermute | solution.py:207
  160.0 3.1 %shard_map.62 = bf16[128,896]{1,0:T(8,128)(2,1)} custom-call(s32[2]{0:T(128)} %pad_add_fusion.2.meta_ref, f32[512,896]{1,0:T(8,128)} %shard_map.58.refs_0_, bf16[512,512]{1,0:T(8,128)(2,1)} %copy-done.2, bf16[512,1792]{1,0:T(8,128)(2,1)} %copy-done.1), custom_call_target="tpu_custom_call" | custom-call | flops 117440512 | bytes 1736704 | tf_op jit(solution)/shard_map/pallas_call | solution.py:153
  164.2 6.9 %shard_map.56 = f32[512,896]{1,0:T(8,128)} custom-call(s32[2]{0:T(128)} %pad_add_fusion.y_ref, bf16[512,512]{1,0:T(8,128)(2,1)} %shard_map.55.refs_0_, bf16[512,512]{1,0:T(8,128)(2,1)} %copy-done.3, bf16[512,512]{1,0:T(8,128)(2,1)} %copy-done.2, bf16[512,512]{1,0:T(8,128)(2,1)} %copy-done.4, bf16[512,7168]{1,0:T(8,128)(2,1)} %refs_2_.1, ...), custom_call_target="tpu_custom_call" | custom-call | flops 1879048192 | bytes 7602176 | tf_op jit(solution)/shard_map/pallas_call | solution.py:111
  171.1 2.6 %add_convert_fusion = bf16[512,896]{1,0:T(8,128)(2,1)} fusion(f32[512,896]{1,0:T(8,128)} %shard_map.56, bf16[128,896]{1,0:T(8,128)(2,1)S(1)} %collective-permute-done.9, bf16[128,896]{1,0:T(8,128)(2,1)S(1)} %collective-permute-done.8, bf16[128,896]{1,0:T(8,128)(2,1)S(1)} %collective-permute-done.7, bf16[128,896]{1,0:T(8,128)(2,1)S(1)} %collective-permute-done.6), kind=kLoop, calls=%fused_computation | loop fusion | flops 4587520 | bytes 3670016 | tf_op jit(solution)/shard_map/convert_element_type | solution.py:219
  (24 shorter events, 5.5 us)
Async XLA Ops:
  6.5 13.4 %copy-start = (s32[16,3]{0,1:T(4,128)S(1)}, s32[16,3]{0,1:T(4,128)}, u32[]{:S(2)}) copy-start(s32[16,3]{0,1:T(4,128)} %param.8) | copy-start | bytes 580
  6.5 96.7 %all-gather.2.cloned.1.call-start = ((), (), s32[]{:S(2)}) async-start(), calls=%async_computation | async-start | bytes 17825792 | tf_op jit(solution)/shard_map/all_gather | solution.py:179
  14.0 43.4 %collective-permute-start = (bf16[512,1792]{1,0:T(8,128)(2,1)}, bf16[512,1792]{1,0:T(8,128)(2,1)}, u32[]{:S(2)}, u32[]{:S(2)}) collective-permute-start(bf16[512,1792]{1,0:T(8,128)(2,1)} %get-tuple-element.15), channel_id=1, source_target_pairs={{0,2},{2,4},{4,6},{6,0},{1,3},{3,5},{5,7},{7,1},{8,10},{10,12},{12... | collective-permute-start | bytes 5505032 | tf_op jit(solution)/shard_map/ppermute | solution.py:188
  15.7 82.2 %collective-permute-start.1 = (bf16[512,1792]{1,0:T(8,128)(2,1)}, bf16[512,1792]{1,0:T(8,128)(2,1)S(1)}, u32[]{:S(2)}, u32[]{:S(2)}) collective-permute-start(bf16[512,1792]{1,0:T(8,128)(2,1)} %get-tuple-element.14), channel_id=1, source_target_pairs={{0,4},{2,6},{4,0},{6,2},{1,5},{3,7},{5,1},{7,3},{8,12},{10,14},{12... | collective-permute-start | bytes 5505032 | tf_op jit(solution)/shard_map/ppermute | solution.py:188
  18.6 79.3 %collective-permute-start.2 = (bf16[512,1792]{1,0:T(8,128)(2,1)}, bf16[512,1792]{1,0:T(8,128)(2,1)}, u32[]{:S(2)}, u32[]{:S(2)}) collective-permute-start(bf16[512,1792]{1,0:T(8,128)(2,1)} %get-tuple-element.13), channel_id=1, source_target_pairs={{0,6},{2,0},{4,2},{6,4},{1,7},{3,1},{5,3},{7,5},{8,14},{10,8},{12,... | collective-permute-start | bytes 5505032 | tf_op jit(solution)/shard_map/ppermute | solution.py:188
  97.9 14.5 %copy-start.1 = (bf16[512,1792]{1,0:T(8,128)(2,1)}, bf16[512,1792]{1,0:T(8,128)(2,1)S(1)}, u32[]{:S(2)}) copy-start(bf16[512,1792]{1,0:T(8,128)(2,1)S(1)} %collective-permute-done.1.refs_6_.refs_2_) | copy-start | bytes 5505028
  112.3 15.2 %collective-permute-start.3 = (bf16[512,512]{1,0:T(8,128)(2,1)}, bf16[512,512]{1,0:T(8,128)(2,1)S(1)}, u32[]{:S(2)}, u32[]{:S(2)}) collective-permute-start(bf16[512,512]{1,0:T(8,128)(2,1)} %shard_map.55.refs_0_), channel_id=1, source_target_pairs={{0,2},{2,4},{4,6},{6,0},{1,3},{3,5},{5,7},{7,1},{8,10},{10,12},{12... | collective-permute-start | bytes 1572872 | tf_op jit(solution)/shard_map/ppermute | solution.py:193
  113.8 24.4 %collective-permute-start.5 = (bf16[512,512]{1,0:T(8,128)(2,1)}, bf16[512,512]{1,0:T(8,128)(2,1)S(1)}, u32[]{:S(2)}, u32[]{:S(2)}) collective-permute-start(bf16[512,512]{1,0:T(8,128)(2,1)} %shard_map.55.refs_0_), channel_id=1, source_target_pairs={{0,6},{2,0},{4,2},{6,4},{1,7},{3,1},{5,3},{7,5},{8,14},{10,8},{12,... | collective-permute-start | bytes 1572872 | tf_op jit(solution)/shard_map/ppermute | solution.py:193
  115.6 27.9 %collective-permute-start.4 = (bf16[512,512]{1,0:T(8,128)(2,1)}, bf16[512,512]{1,0:T(8,128)(2,1)S(1)}, u32[]{:S(2)}, u32[]{:S(2)}) collective-permute-start(bf16[512,512]{1,0:T(8,128)(2,1)} %shard_map.55.refs_0_), channel_id=1, source_target_pairs={{0,4},{2,6},{4,0},{6,2},{1,5},{3,7},{5,1},{7,3},{8,12},{10,14},{12... | collective-permute-start | bytes 1572872 | tf_op jit(solution)/shard_map/ppermute | solution.py:193
  127.6 0.8 copy-start.3
  138.2 0.8 copy-start.4
  143.5 0.8 copy-start.2
  147.4 23.7 %collective-permute-start.6 = (bf16[128,896]{1,0:T(8,128)(2,1)}, bf16[128,896]{1,0:T(8,128)(2,1)S(1)}, u32[]{:S(2)}, u32[]{:S(2)}) collective-permute-start(bf16[128,896]{1,0:T(8,128)(2,1)} %shard_map.59), channel_id=1, source_target_pairs={{0,1},{1,0},{2,3},{3,2},{4,5},{5,4},{6,7},{7,6},{8,9},{9,8},{10,11... | collective-permute-start | bytes 688136 | tf_op jit(solution)/shard_map/ppermute | solution.py:207
  153.4 17.7 %collective-permute-start.7 = (bf16[128,896]{1,0:T(8,128)(2,1)}, bf16[128,896]{1,0:T(8,128)(2,1)S(1)}, u32[]{:S(2)}, u32[]{:S(2)}) collective-permute-start(bf16[128,896]{1,0:T(8,128)(2,1)} %shard_map.60), channel_id=1, source_target_pairs={{0,1},{1,0},{2,3},{3,2},{4,5},{5,4},{6,7},{7,6},{8,9},{9,8},{10,11... | collective-permute-start | bytes 688136 | tf_op jit(solution)/shard_map/ppermute | solution.py:207
  157.0 14.1 %collective-permute-start.8 = (bf16[128,896]{1,0:T(8,128)(2,1)}, bf16[128,896]{1,0:T(8,128)(2,1)S(1)}, u32[]{:S(2)}, u32[]{:S(2)}) collective-permute-start(bf16[128,896]{1,0:T(8,128)(2,1)} %shard_map.61), channel_id=1, source_target_pairs={{0,1},{1,0},{2,3},{3,2},{4,5},{5,4},{6,7},{7,6},{8,9},{9,8},{10,11... | collective-permute-start | bytes 688136 | tf_op jit(solution)/shard_map/ppermute | solution.py:207
  163.1 8.0 %collective-permute-start.9 = (bf16[128,896]{1,0:T(8,128)(2,1)}, bf16[128,896]{1,0:T(8,128)(2,1)S(1)}, u32[]{:S(2)}, u32[]{:S(2)}) collective-permute-start(bf16[128,896]{1,0:T(8,128)(2,1)} %shard_map.62), channel_id=1, source_target_pairs={{0,1},{1,0},{2,3},{3,2},{4,5},{5,4},{6,7},{7,6},{8,9},{9,8},{10,11... | collective-permute-start | bytes 688136 | tf_op jit(solution)/shard_map/ppermute | solution.py:207
Sparse Core Ops, SparseCore 0:
  9.1 94.1 all-gather.1

commit v20 on v16

--- a/solution.py
+++ b/solution.py
@@ -40,18 +40,20 @@
                 else:
                     sc = jnp.where(usable[s], sc, neg_fill)
                 scores.append(sc)
-            row_max = jnp.max(scores[0], axis=1, keepdims=True)
+            top = scores[0]
             for s in range(1, topk):
-                row_max = jnp.maximum(row_max, jnp.max(scores[s], axis=1, keepdims=True))
-            row_sum = jnp.zeros((BLOCK, 1), jnp.float32)
+                top = jnp.maximum(top, scores[s])
+            row_max = jnp.max(top, axis=1, keepdims=True)
+            total = None
             acc = jnp.zeros((BLOCK, HD), jnp.float32)
             for s in range(topk):
                 e = jnp.exp(scores[s] - row_max)
-                row_sum = row_sum + jnp.sum(e, axis=1, keepdims=True)
+                total = e if total is None else total + e
                 acc = acc + jnp.dot(
                     e.astype(jnp.bfloat16), v_refs[s][:, cols],
                     preferred_element_type=jnp.float32,
                 )
+            row_sum = jnp.sum(total, axis=1, keepdims=True)
             att_ref[:, cols] = (acc / row_sum).astype(att_ref.dtype)
 
 

time: 178 us -> 178 us (level)
  no operation moved by 1% of the time
where the time goes in v20:
time: 178 us
  waiting for transfers between devices  103 us (58%)
  Pallas kernels  32.7 us (18%)
  starting transfers between devices  14.5 us (8%)
  between operations  13.5 us (8%)
  local copies, waits for them, and re-layouts  7.73 us (4%)
  other arithmetic  6.66 us (4%)
    ppermute x3, waiting for transfers between devices, per_device(): lax.ppermute(sent, 'y', [(i, (i + shift) % y_size) for i in range(y_size)])  77.2 us
    pallas_call x4, Pallas kernels, project_part(): pl.pallas_call(functools.partial(part_kernel, count=len(pieces), has_part...  16.3 us
    ppermute x3, waiting for transfers between devices, per_device(): lax.ppermute(attended, 'y', [(i, (i + shift) % y_size) for i in range(y_s...  14.5 us
    pallas_call x1, Pallas kernels, attend(): pl.pallas_call(functools.partial(attend_kernel, topk=topk, head_count=hea...  9.41 us
    pallas_call x1, Pallas kernels, project(): pl.pallas_call(functools.partial(project_kernel, shifts=shifts), grid_spe...  6.92 us
    ppermute x3, starting transfers between devices, per_device(): lax.ppermute(sent, 'y', [(i, (i + shift) % y_size) for i in range(y_size)])  5.91 us
    ppermute x2, waiting for transfers between devices, per_device(): lax.ppermute(project_part(other, near, pieces[2:3], list(received[1:2]),...  5.55 us
    all_gather x1, waiting for transfers between devices, per_device(): lax.all_gather(jnp.concatenate([key_rows, value_rows], axis=1), CTX, axis...  5.34 us
  transfers between devices with their start and end apart: 9, of which 7 were waited for; matrix products, arithmetic and copies ran while one was open for 4% of the time, Pallas kernels for 11%

profile of v20, /device:TPU:0, one launch (start us, length us, event | category | flops | bytes accessed | tf_op | source)
XLA Modules:
  0.0 177.6 jit_solution(6246581727709510557)
XLA Ops:
  6.5 2.3 %pad_maximum_fusion = bf16[512,1024]{1,0:T(8,128)(2,1)} fusion(bf16[512,512]{1,0:T(8,128)(2,1)} %param.7, bf16[512,512]{1,0:T(8,128)(2,1)} %param.6), kind=kLoop, calls=%fused_computation.1 | loop fusion | flops 2097152 | bytes 2097152 | tf_op jit(solution)/shard_map/concatenate | solution.py:182
  8.9 5.2 %constant_dynamic-slice_fusion = (bf16[512,1792]{1,0:T(8,128)(2,1)}, bf16[512,1792]{1,0:T(8,128)(2,1)}, bf16[512,1792]{1,0:T(8,128)(2,1)}) fusion(bf16[512,7168]{1,0:T(8,128)(2,1)} %refs_2_.1, s32[]{:T(128)S(6)} %select_n.33, s32[]{:T(128)S(6)} %select_n.31, s32[]{:T(128)S(6)} %select_n.29), kind=kLoop, calls=%fused_computation.3 | loop fusion | bytes 11010060 | tf_op jit(solution)/shard_map/dynamic_slice | solution.py:188
  14.1 1.7 collective-permute-start
  15.7 2.9 %collective-permute-start.1 = (bf16[512,1792]{1,0:T(8,128)(2,1)}, bf16[512,1792]{1,0:T(8,128)(2,1)S(1)}, u32[]{:S(2)}, u32[]{:S(2)}) collective-permute-start(bf16[512,1792]{1,0:T(8,128)(2,1)} %get-tuple-element.14), channel_id=1, source_target_pairs={{0,4},{2,6},{4,0},{6,2},{1,5},{3,7},{5,1},{7,3},{8,12},{10,14},{12... | collective-permute-start | bytes 5505032 | tf_op jit(solution)/shard_map/ppermute | solution.py:190
  18.6 1.3 collective-permute-start.2
  20.7 36.8 %collective-permute-done.refs_5_.refs_3_ = bf16[512,1792]{1,0:T(8,128)(2,1)} collective-permute-done((bf16[512,1792]{1,0:T(8,128)(2,1)}, bf16[512,1792]{1,0:T(8,128)(2,1)}, u32[]{:S(2)}, u32[]{:S(2)}) %collective-permute-start) | collective-permute-done | bytes 1835040 | tf_op jit(solution)/shard_map/ppermute | solution.py:190
  57.5 40.4 %collective-permute-done.1.refs_6_.refs_2_ = bf16[512,1792]{1,0:T(8,128)(2,1)S(1)} collective-permute-done((bf16[512,1792]{1,0:T(8,128)(2,1)}, bf16[512,1792]{1,0:T(8,128)(2,1)S(1)}, u32[]{:S(2)}, u32[]{:S(2)}) %collective-permute-start.1) | collective-permute-done | bytes 1835040 | tf_op jit(solution)/shard_map/ppermute | solution.py:190
  97.9 5.3 %all-gather.2.cloned.1.call-done.refs_0_.refs_1_.refs_2_.refs_3_.refs_4_.refs_5_ = bf16[8192,1024]{1,0:T(8,128)(2,1)} async-done(((bf16[512,1024]{1,0:T(8,128)(2,1)}), bf16[8192,1024]{1,0:T(8,128)(2,1)}) %all-gather.2.cloned.1.call-update) | async-done | bytes 16777232 | tf_op jit(solution)/shard_map/all_gather | solution.py:181
  103.2 9.4 %shard_map.55.refs_0_ = bf16[512,512]{1,0:T(8,128)(2,1)} custom-call(s32[4]{0:T(128)} %pad_add_fusion.1.meta_ref, bf16[512,512]{1,0:T(8,128)(2,1)} %q_ref.1, bf16[8192,1024]{1,0:T(8,128)(2,1)} %all-gather.2.cloned.1.call-done.refs_0_.refs_1_.refs_2_.refs_3_.refs_4_.refs_5_, ...), custom_call_target="tpu_custom_call" | custom-call | flops 1610612736 | bytes 4194304 | tf_op jit(solution)/shard_map/pallas_call | solution.py:89
  112.6 1.5 collective-permute-start.3
  114.1 1.8 collective-permute-start.5
  115.9 1.8 %collective-permute-start.4 = (bf16[512,512]{1,0:T(8,128)(2,1)}, bf16[512,512]{1,0:T(8,128)(2,1)S(1)}, u32[]{:S(2)}, u32[]{:S(2)}) collective-permute-start(bf16[512,512]{1,0:T(8,128)(2,1)} %shard_map.55.refs_0_), channel_id=1, source_target_pairs={{0,4},{2,6},{4,0},{6,2},{1,5},{3,7},{5,1},{7,3},{8,12},{10,14},{12... | collective-permute-start | bytes 1572872 | tf_op jit(solution)/shard_map/ppermute | solution.py:195
  118.3 9.6 %collective-permute-done.3.refs_1_ = bf16[512,512]{1,0:T(8,128)(2,1)S(1)} collective-permute-done((bf16[512,512]{1,0:T(8,128)(2,1)}, bf16[512,512]{1,0:T(8,128)(2,1)S(1)}, u32[]{:S(2)}, u32[]{:S(2)}) %collective-permute-start.3) | collective-permute-done | bytes 524320 | tf_op jit(solution)/shard_map/ppermute | solution.py:195
  128.7 4.9 %shard_map.57.refs_0_ = f32[512,896]{1,0:T(8,128)} custom-call(s32[2]{0:T(128)} %pad_add_fusion.2.meta_ref, bf16[512,512]{1,0:T(8,128)(2,1)} %shard_map.55.refs_0_, bf16[512,512]{1,0:T(8,128)(2,1)} %copy-done.3, bf16[512,7168]{1,0:T(8,128)(2,1)} %refs_2_.1, bf16[512,1792]{1,0:T(8,128)(2,1)} %collective-permute-done.refs_5_.refs_3_), custom_call_target="tpu_custom_call" | custom-call | flops 939524096 | bytes 4718592 | tf_op jit(solution)/shard_map/pallas_call | solution.py:155
  133.6 4.9 %collective-permute-done.5.refs_3_.refs_1_ = bf16[512,512]{1,0:T(8,128)(2,1)S(1)} collective-permute-done((bf16[512,512]{1,0:T(8,128)(2,1)}, bf16[512,512]{1,0:T(8,128)(2,1)S(1)}, u32[]{:S(2)}, u32[]{:S(2)}) %collective-permute-start.5) | collective-permute-done | bytes 524320 | tf_op jit(solution)/shard_map/ppermute | solution.py:195
  138.5 0.8 copy-done.4
  139.3 4.5 %shard_map.58.refs_0_ = f32[512,896]{1,0:T(8,128)} custom-call(s32[2]{0:T(128)} %pad_add_fusion.2.meta_ref, f32[512,896]{1,0:T(8,128)} %shard_map.57.refs_0_, bf16[512,512]{1,0:T(8,128)(2,1)} %copy-done.4, bf16[512,1792]{1,0:T(8,128)(2,1)} %collective-permute-done.2.refs_7_.refs_2_), custom_call_target="tpu_custom_call" | custom-call | flops 469762048 | bytes 5111808 | tf_op jit(solution)/shard_map/pallas_call | solution.py:155
  143.9 0.8 copy-done.2
  144.7 3.4 %shard_map.59 = bf16[256,896]{1,0:T(8,128)(2,1)} custom-call(s32[2]{0:T(128)} %pad_add_fusion.2.meta_ref, f32[512,896]{1,0:T(8,128)} %shard_map.58.refs_0_, bf16[512,512]{1,0:T(8,128)(2,1)} %copy-done.2, bf16[512,1792]{1,0:T(8,128)(2,1)} %copy-done.1), custom_call_target="tpu_custom_call" | custom-call | flops 234881024 | bytes 2555904 | tf_op jit(solution)/shard_map/pallas_call | solution.py:155
  148.1 3.0 %collective-permute-start.6 = (bf16[256,896]{1,0:T(8,128)(2,1)}, bf16[256,896]{1,0:T(8,128)(2,1)S(1)}, u32[]{:S(2)}, u32[]{:S(2)}) collective-permute-start(bf16[256,896]{1,0:T(8,128)(2,1)} %shard_map.59), channel_id=1, source_target_pairs={{0,1},{1,0},{2,3},{3,2},{4,5},{5,4},{6,7},{7,6},{8,9},{9,8},{10,11... | collective-permute-start | bytes 1376264 | tf_op jit(solution)/shard_map/ppermute | solution.py:209
  151.1 3.4 %shard_map.60 = bf16[256,896]{1,0:T(8,128)(2,1)} custom-call(s32[2]{0:T(128)} %pad_add_fusion.2.meta_ref, f32[512,896]{1,0:T(8,128)} %shard_map.58.refs_0_, bf16[512,512]{1,0:T(8,128)(2,1)} %copy-done.2, bf16[512,1792]{1,0:T(8,128)(2,1)} %copy-done.1), custom_call_target="tpu_custom_call" | custom-call | flops 234881024 | bytes 2555904 | tf_op jit(solution)/shard_map/pallas_call | solution.py:155
  155.6 6.9 %shard_map.56 = f32[512,896]{1,0:T(8,128)} custom-call(s32[2]{0:T(128)} %pad_add_fusion.y_ref, bf16[512,512]{1,0:T(8,128)(2,1)} %shard_map.55.refs_0_, bf16[512,512]{1,0:T(8,128)(2,1)} %copy-done.3, bf16[512,512]{1,0:T(8,128)(2,1)} %copy-done.2, bf16[512,512]{1,0:T(8,128)(2,1)} %copy-done.4, bf16[512,7168]{1,0:T(8,128)(2,1)} %refs_2_.1, ...), custom_call_target="tpu_custom_call" | custom-call | flops 1879048192 | bytes 7602176 | tf_op jit(solution)/shard_map/pallas_call | solution.py:113
  162.7 5.4 %collective-permute-done.7 = bf16[256,896]{1,0:T(8,128)(2,1)S(1)} collective-permute-done((bf16[256,896]{1,0:T(8,128)(2,1)}, bf16[256,896]{1,0:T(8,128)(2,1)S(1)}, u32[]{:S(2)}, u32[]{:S(2)}) %collective-permute-start.7) | collective-permute-done | bytes 458784 | tf_op jit(solution)/shard_map/ppermute | solution.py:209
  168.1 2.6 %add_convert_fusion = bf16[512,896]{1,0:T(8,128)(2,1)} fusion(f32[512,896]{1,0:T(8,128)} %shard_map.56, bf16[256,896]{1,0:T(8,128)(2,1)S(1)} %collective-permute-done.7, bf16[256,896]{1,0:T(8,128)(2,1)S(1)} %collective-permute-done.6), kind=kLoop, calls=%fused_computation | loop fusion | flops 2752512 | bytes 3670016 | tf_op jit(solution)/shard_map/convert_element_type | solution.py:221
  (18 shorter events, 3.5 us)
Async XLA Ops:
  6.5 13.4 %copy-start = (s32[16,3]{0,1:T(4,128)S(1)}, s32[16,3]{0,1:T(4,128)}, u32[]{:S(2)}) copy-start(s32[16,3]{0,1:T(4,128)} %param.8) | copy-start | bytes 580
  6.5 96.7 %all-gather.2.cloned.1.call-start = ((), (), s32[]{:S(2)}) async-start(), calls=%async_computation | async-start | bytes 17825792 | tf_op jit(solution)/shard_map/all_gather | solution.py:181
  14.1 43.4 %collective-permute-start = (bf16[512,1792]{1,0:T(8,128)(2,1)}, bf16[512,1792]{1,0:T(8,128)(2,1)}, u32[]{:S(2)}, u32[]{:S(2)}) collective-permute-start(bf16[512,1792]{1,0:T(8,128)(2,1)} %get-tuple-element.15), channel_id=1, source_target_pairs={{0,2},{2,4},{4,6},{6,0},{1,3},{3,5},{5,7},{7,1},{8,10},{10,12},{12... | collective-permute-start | bytes 5505032 | tf_op jit(solution)/shard_map/ppermute | solution.py:190
  15.7 82.2 %collective-permute-start.1 = (bf16[512,1792]{1,0:T(8,128)(2,1)}, bf16[512,1792]{1,0:T(8,128)(2,1)S(1)}, u32[]{:S(2)}, u32[]{:S(2)}) collective-permute-start(bf16[512,1792]{1,0:T(8,128)(2,1)} %get-tuple-element.14), channel_id=1, source_target_pairs={{0,4},{2,6},{4,0},{6,2},{1,5},{3,7},{5,1},{7,3},{8,12},{10,14},{12... | collective-permute-start | bytes 5505032 | tf_op jit(solution)/shard_map/ppermute | solution.py:190
  18.6 79.3 %collective-permute-start.2 = (bf16[512,1792]{1,0:T(8,128)(2,1)}, bf16[512,1792]{1,0:T(8,128)(2,1)}, u32[]{:S(2)}, u32[]{:S(2)}) collective-permute-start(bf16[512,1792]{1,0:T(8,128)(2,1)} %get-tuple-element.13), channel_id=1, source_target_pairs={{0,6},{2,0},{4,2},{6,4},{1,7},{3,1},{5,3},{7,5},{8,14},{10,8},{12,... | collective-permute-start | bytes 5505032 | tf_op jit(solution)/shard_map/ppermute | solution.py:190
  97.9 14.8 %copy-start.1 = (bf16[512,1792]{1,0:T(8,128)(2,1)}, bf16[512,1792]{1,0:T(8,128)(2,1)S(1)}, u32[]{:S(2)}) copy-start(bf16[512,1792]{1,0:T(8,128)(2,1)S(1)} %collective-permute-done.1.refs_6_.refs_2_) | copy-start | bytes 5505028
  112.6 15.2 %collective-permute-start.3 = (bf16[512,512]{1,0:T(8,128)(2,1)}, bf16[512,512]{1,0:T(8,128)(2,1)S(1)}, u32[]{:S(2)}, u32[]{:S(2)}) collective-permute-start(bf16[512,512]{1,0:T(8,128)(2,1)} %shard_map.55.refs_0_), channel_id=1, source_target_pairs={{0,2},{2,4},{4,6},{6,0},{1,3},{3,5},{5,7},{7,1},{8,10},{10,12},{12... | collective-permute-start | bytes 1572872 | tf_op jit(solution)/shard_map/ppermute | solution.py:195
  114.1 24.4 %collective-permute-start.5 = (bf16[512,512]{1,0:T(8,128)(2,1)}, bf16[512,512]{1,0:T(8,128)(2,1)S(1)}, u32[]{:S(2)}, u32[]{:S(2)}) collective-permute-start(bf16[512,512]{1,0:T(8,128)(2,1)} %shard_map.55.refs_0_), channel_id=1, source_target_pairs={{0,6},{2,0},{4,2},{6,4},{1,7},{3,1},{5,3},{7,5},{8,14},{10,8},{12,... | collective-permute-start | bytes 1572872 | tf_op jit(solution)/shard_map/ppermute | solution.py:195
  115.9 28.0 %collective-permute-start.4 = (bf16[512,512]{1,0:T(8,128)(2,1)}, bf16[512,512]{1,0:T(8,128)(2,1)S(1)}, u32[]{:S(2)}, u32[]{:S(2)}) collective-permute-start(bf16[512,512]{1,0:T(8,128)(2,1)} %shard_map.55.refs_0_), channel_id=1, source_target_pairs={{0,4},{2,6},{4,0},{6,2},{1,5},{3,7},{5,1},{7,3},{8,12},{10,14},{12... | collective-permute-start | bytes 1572872 | tf_op jit(solution)/shard_map/ppermute | solution.py:195
  127.9 0.8 copy-start.3
  138.5 0.8 copy-start.4
  143.9 0.8 copy-start.2
  148.1 14.7 %collective-permute-start.6 = (bf16[256,896]{1,0:T(8,128)(2,1)}, bf16[256,896]{1,0:T(8,128)(2,1)S(1)}, u32[]{:S(2)}, u32[]{:S(2)}) collective-permute-start(bf16[256,896]{1,0:T(8,128)(2,1)} %shard_map.59), channel_id=1, source_target_pairs={{0,1},{1,0},{2,3},{3,2},{4,5},{5,4},{6,7},{7,6},{8,9},{9,8},{10,11... | collective-permute-start | bytes 1376264 | tf_op jit(solution)/shard_map/ppermute | solution.py:209
  154.5 13.6 %collective-permute-start.7 = (bf16[256,896]{1,0:T(8,128)(2,1)}, bf16[256,896]{1,0:T(8,128)(2,1)S(1)}, u32[]{:S(2)}, u32[]{:S(2)}) collective-permute-start(bf16[256,896]{1,0:T(8,128)(2,1)} %shard_map.60), channel_id=1, source_target_pairs={{0,1},{1,0},{2,3},{3,2},{4,5},{5,4},{6,7},{7,6},{8,9},{9,8},{10,11... | collective-permute-start | bytes 1376264 | tf_op jit(solution)/shard_map/ppermute | solution.py:209
Sparse Core Ops, SparseCore 0:
  9.1 94.1 all-gather.1
